TPU v7x, 128 devices: a whole 4x4x4 slice. The times are simulated.
128 devices in a mesh: dp: 8 (over z_hi, y), head: 16 (over z_lo, x, core).
Axes of the slice: x: 4, y: 4, z: 4 (z_hi: 2, z_lo: 2; z = z_hi * 2 + z_lo), core: 2. Of those that a mesh axis runs over, the one named last changes fastest.
Arguments:
- queries: bfloat16 [4096, 128, 192], P('dp', 'head'), may hold values from -6 to 6
- latent: bfloat16 [4096, 576], P('dp'), may hold values from -6 to 6
- prefix: bfloat16 [256, 576], replicated, may hold values from -12 to 12
- kv_up: bfloat16 [512, 128, 256], P(None, 'head'), may hold values from -0.25 to 0.25
- out_grad: bfloat16 [4096, 128, 128], P('dp', 'head'), may hold values from -12 to 12
- lengths: int32 [8], P('dp'), may hold values from 64 to 512, as said below
- positions: int32 [8, 512], P('dp'), may hold values from 0 to 4606, as said below
Outputs:
- query_grad: bfloat16 [4096, 128, 192], P('dp', 'head')
- latent_grad: float32 [4096, 576], P(('dp', 'head'))
- up_grad: float32 [512, 128, 256], P('dp', 'head')
- prefix_grad: float32 [256, 576], replicated
Inputs may be any that keep to these rules, and one draw needn't show every extreme that they name: Sequence b's valid tokens are its first lengths[b] tokens. Within a sequence the positions rise by one from token to token.
All inputs are finite; a program needn't handle non-finite values.
Results may differ from a plain program's by a relative error of at most 0.018.
Values may be sent and summed in bfloat16 or wider, within the bound.
No kernel may reach another device: no remote copies, remote signals or barrier semaphores. Data moves between devices by JAX's collectives and lax.ppermute only.
A program may use at most 128 MiB of HBM per device.

v0:
```python
import jax
import jax.numpy as jnp
from jax import lax
from jax.sharding import PartitionSpec as P


def angles_of(positions, rope_dim):
    halfway = rope_dim // 2
    frequency = 10000.0 ** (-(jnp.arange(halfway, dtype=jnp.float32) * 2.0 / rope_dim))
    angles = positions.astype(jnp.float32)[:, None] * frequency[None, :]
    return (jnp.cos(angles), jnp.sin(angles))


def rotate(values, cosine, sine):
    halfway = values.shape[-1] // 2
    leading = values[..., :halfway]
    trailing = values[..., halfway:]
    return jnp.concatenate(
        [leading * cosine - trailing * sine, trailing * cosine + leading * sine], axis=-1
    )


def unrotate(values, cosine, sine):
    halfway = values.shape[-1] // 2
    leading = values[..., :halfway]
    trailing = values[..., halfway:]
    return jnp.concatenate(
        [leading * cosine + trailing * sine, trailing * cosine - leading * sine], axis=-1
    )


def block_gradients(
    query_nope, query_rope, key_nope, key_rope, values, cotangent, first_row, length, prefix_rows
):
    score_scale = (query_nope.shape[-1] + query_rope.shape[-1]) ** (-0.5)
    scores = (
        jnp.einsum("qhd,khd->hqk", query_nope, key_nope, preferred_element_type=jnp.float32)
        + jnp.einsum("qhr,kr->hqk", query_rope, key_rope, preferred_element_type=jnp.float32)
    ) * score_scale
    row_index = first_row + jnp.arange(query_nope.shape[0])
    col_index = jnp.arange(key_nope.shape[0]) - prefix_rows
    allowed = (col_index[None, :] < 0) | (col_index[None, :] <= row_index[:, None]) & (
        col_index[None, :] < length
    )
    scores = jnp.where(allowed[None], scores, -jnp.inf)
    highest = jnp.max(scores, axis=-1, keepdims=True)
    exponent = jnp.exp(scores - highest)
    probability = exponent / jnp.sum(exponent, axis=-1, keepdims=True)
    weights = probability.astype(jnp.bfloat16)
    output = jnp.einsum("hqk,khv->qhv", weights, values, preferred_element_type=jnp.float32)
    row_delta = jnp.sum(cotangent.astype(jnp.float32) * output, axis=-1)
    prob_grad = jnp.einsum("qhv,khv->hqk", cotangent, values, preferred_element_type=jnp.float32)
    score_grad = (
        probability * (prob_grad - jnp.transpose(row_delta)[:, :, None]) * score_scale
    ).astype(jnp.bfloat16)
    nope_query = jnp.einsum(
        "hqk,khd->qhd", score_grad, key_nope, preferred_element_type=jnp.float32
    )
    rope_query = jnp.einsum("hqk,kr->qhr", score_grad, key_rope, preferred_element_type=jnp.float32)
    nope_key = jnp.einsum(
        "hqk,qhd->khd", score_grad, query_nope, preferred_element_type=jnp.float32
    )
    rope_key = jnp.einsum("hqk,qhr->kr", score_grad, query_rope, preferred_element_type=jnp.float32)
    value_grad = jnp.einsum("hqk,qhv->khv", weights, cotangent, preferred_element_type=jnp.float32)
    return (nope_query, rope_query, nope_key, rope_key, value_grad)


def on_device(queries, latent, prefix, kv_up, out_grad, lengths, positions):
    seq_len = queries.shape[0]
    latent_dim = kv_up.shape[0]
    value_dim = out_grad.shape[2]
    nope_dim = kv_up.shape[2] - value_dim
    rope_dim = latent.shape[1] - latent_dim
    prefix_rows = prefix.shape[0]
    length = lengths[0]
    cosine, sine = angles_of(positions[0], rope_dim)
    query_nope = queries[:, :, :nope_dim]
    query_rope = rotate(
        queries[:, :, nope_dim:].astype(jnp.float32), cosine[:, None], sine[:, None]
    ).astype(jnp.bfloat16)
    token_rope = rotate(latent[:, latent_dim:].astype(jnp.float32), cosine, sine).astype(
        jnp.bfloat16
    )
    source = jnp.concatenate(
        [prefix, jnp.concatenate([latent[:, :latent_dim], token_rope], axis=1)], axis=0
    )
    source_latent = source[:, :latent_dim]
    key_rope = source[:, latent_dim:]
    key_total = source.shape[0]
    live_rows = jnp.arange(seq_len) < length
    cotangent = jnp.where(live_rows[:, None, None], out_grad, jnp.zeros_like(out_grad))
    block_rows = min(seq_len, 256)
    head_part = kv_up.shape[1]
    projected = jnp.einsum(
        "kl,lhd->khd", source_latent, kv_up, preferred_element_type=jnp.float32
    ).astype(jnp.bfloat16)
    key_nope = projected[:, :, :nope_dim]
    values = projected[:, :, nope_dim:]
    nope_total = jnp.zeros((key_total, head_part, nope_dim), jnp.float32)
    rope_total = jnp.zeros((key_total, rope_dim), jnp.float32)
    value_total = jnp.zeros((key_total, head_part, value_dim), jnp.float32)
    query_pieces = []
    for block_number in range(seq_len // block_rows):
        first_row = block_number * block_rows
        last_row = first_row + block_rows
        pieces = block_gradients(
            query_nope[first_row:last_row],
            query_rope[first_row:last_row],
            key_nope,
            key_rope,
            values,
            cotangent[first_row:last_row],
            first_row,
            length,
            prefix_rows,
        )
        nope_query, rope_query, nope_key, rope_key, value_grad = pieces
        nope_total = nope_total.at[:key_total].add(nope_key)
        rope_total = rope_total.at[:key_total].add(rope_key)
        value_total = value_total.at[:key_total].add(value_grad)
        query_pieces.append(
            jnp.concatenate(
                [
                    nope_query,
                    unrotate(
                        rope_query, cosine[first_row:last_row, None], sine[first_row:last_row, None]
                    ),
                ],
                axis=-1,
            ).astype(jnp.bfloat16)
        )
    head_projected_grad = jnp.concatenate([nope_total, value_total], axis=-1).astype(jnp.bfloat16)
    up_part = jnp.einsum(
        "kl,khd->lhd", source_latent, head_projected_grad, preferred_element_type=jnp.float32
    )
    query_grad, projected_grad, rope_grad, up_part = (
        jnp.concatenate(query_pieces, axis=0),
        head_projected_grad,
        rope_total,
        up_part,
    )
    up_grad = lax.psum_scatter(
        up_part.astype(jnp.bfloat16), "dp", scatter_dimension=0, tiled=True
    ).astype(jnp.float32)
    token_grad = projected_grad[prefix_rows:]
    token_rope_grad = rope_grad[prefix_rows:]
    latent_part = jnp.einsum("khd,lhd->kl", token_grad, kv_up, preferred_element_type=jnp.float32)
    latent_grad = lax.psum_scatter(
        jnp.concatenate([latent_part, unrotate(token_rope_grad, cosine, sine)], axis=1).astype(
            jnp.bfloat16
        ),
        "head",
        scatter_dimension=0,
        tiled=True,
    ).astype(jnp.float32)
    latent_part = jnp.einsum(
        "khd,lhd->kl", projected_grad[:prefix_rows], kv_up, preferred_element_type=jnp.float32
    )
    prefix_grad = lax.psum(
        jnp.concatenate([latent_part, rope_grad[:prefix_rows]], axis=1), ("dp", "head")
    )
    return (query_grad, latent_grad, up_grad, prefix_grad)


def solution(mesh):
    placed = (
        P("dp", "head", None),
        P("dp", None),
        P(),
        P(None, "head", None),
        P("dp", "head", None),
        P("dp"),
        P("dp", None),
    )
    return jax.shard_map(
        on_device,
        mesh=mesh,
        in_specs=placed,
        out_specs=(P("dp", "head", None), P(("dp", "head"), None), P("dp", "head", None), P()),
        check_vma=False,
    )
```

profile of v0, /device:TPU:1, one launch (start us, length us, event | category | flops | bytes accessed | tf_op | source)
XLA Modules:
  0.0 243.2 jit_solution(17686090707486672726)
XLA Ops:
  8.0 0.0 all-reduce.2.cloned.1.call-start
  8.1 0.6 iota_add_fusion.1
  8.6 0.8 slice_convert_fusion.1
  9.5 1.1 slice.200
  10.6 0.7 convert_element_type.53
  11.2 0.3 multiply_cosine_fusion
  11.6 0.1 copy.121
  11.7 0.1 copy.120
  11.8 1.2 copy.122
  13.0 0.2 copy.204
  13.2 0.0 copy-start.22
  13.2 0.8 maximum_bitcast_fusion
  14.0 0.1 maximum_maximum_fusion.1
  14.2 1.5 slice_convert_fusion
  15.7 1.8 convolution_convert_fusion
  17.6 3.6 %fusion.46 = f32[8,768,256]{2,1,0:T(8,128)} fusion(bf16[768,8,256]{2,0,1:T(8,128)(2,1)S(1)} %convolution_convert_fusion, bf16[512,8,192]{0,2,1:T(8,128)(2,1)S(1)} %copy-done.11), kind=kOutput, calls=%fused_computation.60 | convolution fusion | flops 402653184 | bytes 8388608 | tf_op jit(solution)/shard_map/qhd,khd->hqk/dot_general | solution.py:37
  21.2 3.6 %fusion.49 = f32[8,768,256]{2,1,0:T(8,128)} fusion(bf16[768,8,256]{2,0,1:T(8,128)(2,1)S(1)} %convolution_convert_fusion, bf16[512,8,192]{0,2,1:T(8,128)(2,1)S(1)} %copy-done.11), kind=kOutput, calls=%fused_computation.63 | convolution fusion | flops 402653184 | bytes 8388608 | tf_op jit(solution)/shard_map/qhd,khd->hqk/dot_general | solution.py:37
  25.5 1.2 copy_select_fusion
  26.6 0.9 subtract_convert_fusion
  27.5 1.4 fusion.52
  28.9 7.7 %fusion.92 = (f32[8,256]{1,0:T(8,128)S(1)}, f32[8,256,768]{1,2,0:T(8,128)}) fusion(f32[8,768,256]{2,1,0:T(8,128)} %fusion.49, pred[256,768]{0,1:T(8,128)(4,1)} %get-tuple-element.150, bf16[768,64,1]{1,0,2:T(8,128)(2,1)} %maximum_bitcast_fusion, bf16[512,8,32]{0,2,1:T(8,128)(2,1)S(1)} %get-tuple-element.136, bf16[512,8,32]{0,2,1:T(8,128)(2,1)} %get-tuple-element.137), kind=kOutput, calls=%fused_computation.128 | convolution fusion | flops 209715968 | bytes 13410304 | tf_op jit(solution)/shard_map/sub | solution.py:47
  36.6 3.5 %fusion.7 = bf16[8,256,768]{1,2,0:T(8,128)(2,1)S(1)} fusion(f32[8,256,768]{1,2,0:T(8,128)} %get-tuple-element.159, f32[8,256]{1,0:T(8,128)S(1)} %get-tuple-element.158), kind=kLoop, calls=%fused_computation.22 | loop fusion | flops 3145728 | bytes 9445376 | tf_op jit(solution)/shard_map/convert_element_type | solution.py:49
  40.2 1.2 fusion.31
  41.4 2.9 %fusion.60 = f32[8,128,768]{2,1,0:T(8,128)} fusion(bf16[8,256,768]{1,2,0:T(8,128)(2,1)S(1)} %fusion.7, bf16[512,8,128]{2,0,1:T(8,128)(2,1)S(1)} %copy-done.12), kind=kOutput, calls=%fused_computation.85 | convolution fusion | flops 402653184 | bytes 6815744 | tf_op jit(solution)/shard_map/hqk,qhv->khv/dot_general | solution.py:64
  44.3 1.2 multiply_convert_fusion.1
  45.5 1.7 convolution_bitcast_fusion.5
  47.3 3.8 %fusion.56 = f32[8,768,128]{1,2,0:T(8,128)} fusion(bf16[8,256,768]{1,2,0:T(8,128)(2,1)S(1)} %multiply_convert_fusion.1, bf16[512,8,192]{0,2,1:T(8,128)(2,1)} %param.31), kind=kOutput, calls=%fused_computation.81 | convolution fusion | flops 402653184 | bytes 6815744 | tf_op jit(solution)/shard_map/hqk,qhd->khd/dot_general | solution.py:60
  51.1 7.7 %fusion.91 = (f32[8,256]{1,0:T(8,128)S(1)}, f32[8,256,768]{1,2,0:T(8,128)}) fusion(f32[8,768,256]{2,1,0:T(8,128)} %fusion.46, pred[256,768]{0,1:T(8,128)(4,1)} %get-tuple-element.151, bf16[768,64,1]{1,0,2:T(8,128)(2,1)} %maximum_bitcast_fusion, bf16[512,8,32]{0,2,1:T(8,128)(2,1)} %get-tuple-element.137, bf16[512,8,32]{0,2,1:T(8,128)(2,1)S(1)} %get-tuple-element.136), kind=kOutput, calls=%fused_computation.127 | convolution fusion | flops 209715968 | bytes 13410304 | tf_op jit(solution)/shard_map/sub | solution.py:47
  58.8 3.5 %fusion.8 = bf16[8,256,768]{1,2,0:T(8,128)(2,1)S(1)} fusion(f32[8,256,768]{1,2,0:T(8,128)} %get-tuple-element.157, f32[8,256]{1,0:T(8,128)S(1)} %get-tuple-element.156), kind=kLoop, calls=%fused_computation.23 | loop fusion | flops 3145728 | bytes 9445376 | tf_op jit(solution)/shard_map/convert_element_type | solution.py:49
  62.3 0.2 copy-done.5
  62.5 3.0 %fusion.32 = f32[256,8]{0,1:T(8,128)S(1)} fusion(bf16[8,256,768]{1,2,0:T(8,128)(2,1)S(1)} %fusion.8, bf16[768,8,256]{2,0,1:T(8,128)(2,1)S(1)} %copy-done.5, bf16[512,8,128]{2,0,1:T(8,128)(2,1)} %copy_select_fusion), kind=kOutput, calls=%fused_computation.44 | convolution fusion | flops 403437568 | bytes 5251072 | tf_op jit(solution)/shard_map/hqk,khv->qhv/dot_general | solution.py:50
  65.6 1.2 multiply_convert_fusion
  66.8 0.6 copy-done.7
  67.5 2.4 fusion.18
  69.9 1.1 fusion.38
  70.9 0.7 copy-done.17
  71.6 0.1 copy.161
  71.7 4.3 %fusion.17 = bf16[768,8,128]{0,2,1:T(8,128)(2,1)S(1)} fusion(f32[8,768,128]{1,2,0:T(8,128)} %fusion.56, bf16[8,256,768]{1,2,0:T(8,128)(2,1)} %copy-done, bf16[512,8,192]{0,2,1:T(8,128)(2,1)} %param.31), kind=kOutput, calls=%fused_computation.33 | convolution fusion | flops 404226048 | bytes 8388608 | tf_op jit(solution)/shard_map/hqk,qhd->khd/dot_general | solution.py:60
  76.1 0.8 fusion.33
  76.9 0.3 copy-done.15
  77.2 0.9 pad_maximum_fusion.4
  78.1 0.0 all-reduce.2.cloned.1.call-update
  78.2 0.0 reduce-scatter.7.cloned.1.call-start
  78.2 3.5 %fusion.26 = bf16[512,512]{0,1:T(8,128)(2,1)S(1)} fusion(bf16[768,8,128]{0,2,1:T(8,128)(2,1)} %copy-done.15, bf16[768,8,128]{0,2,1:T(8,128)(2,1)} %fusion.18, bf16[512,8,256]{2,1,0:T(8,128)(2,1)} %param.34), kind=kOutput, calls=%fused_computation.40 | convolution fusion | flops 1078198272 | bytes 5767168 | tf_op jit(solution)/shard_map/khd,lhd->kl/dot_general | solution.py:147
  81.7 0.3 fusion.77
  82.1 0.9 pad_maximum_fusion.5
  82.9 2.1 copy.202
  85.1 0.0 reduce-scatter.7.cloned.1.call-update
  85.1 0.0 reduce-scatter.5.cloned.1.call-start
  85.1 5.4 %fusion.12 = bf16[512,8,256]{2,0,1:T(8,128)(2,1)} fusion(bf16[768,8,128]{0,2,1:T(8,128)(2,1)} %fusion.18, bf16[768,8,128]{0,2,1:T(8,128)(2,1)} %copy-done.15, bf16[768,576]{1,0:T(8,128)(2,1)} %copy-done.20), kind=kOutput, calls=%fused_computation.27 | convolution fusion | flops 1617952768 | bytes 6029312 | tf_op jit(solution)/shard_map/kl,khd->lhd/dot_general | solution.py:133
  90.5 0.0 reduce-scatter.5.cloned.1.call-update
  90.6 2.7 %convolution_bitcast_fusion.2 = f32[256,8,64]{0,2,1:T(8,128)S(1)} fusion(bf16[768,64,1]{1,0,2:T(8,128)(2,1)S(1)} %copy-done.10, bf16[8,256,768]{1,2,0:T(8,128)(2,1)} %copy-done), kind=kOutput, calls=%fused_computation.46 | convolution fusion | flops 201326592 | bytes 3768320 | tf_op jit(solution)/shard_map/hqk,kr->qhr/dot_general | solution.py:59
  93.3 0.1 add_convert_fusion.3
  93.4 0.7 convolution_bitcast_fusion.3
  94.1 0.1 add_convert_fusion.4
  94.2 1.1 copy-done.1
  95.2 0.7 fusion.37
  95.9 0.7 fusion.36
  96.7 1.3 maximum_maximum_fusion
  97.9 132.1 %all-reduce.2.cloned.1.call-done = f32[256,576]{1,0:T(8,128)} async-done(((f32[256,576]{1,0:T(8,128)}), f32[256,576]{1,0:T(8,128)}) %all-reduce.2.cloned.1.call-update) | async-done | bytes 589840 | tf_op jit(solution)/shard_map/psum | solution.py:159
  230.1 2.1 copy.164
  232.2 0.9 copy.203
  233.1 0.8 copy.162
  233.9 1.9 copy.163
  (55 shorter events, 0.1 us)
Async XLA Ops:
  8.0 222.1 %all-reduce.2.cloned.1.call-start = ((), (), s32[]{:S(2)}) async-start(), calls=%async_computation.3 | async-start | bytes 1310720 | tf_op jit(solution)/shard_map/psum | solution.py:159
  13.2 2.5 %copy-start.22 = (bf16[512,8,256]{2,1,0:T(8,128)(2,1)S(1)}, bf16[512,8,256]{2,1,0:T(8,128)(2,1)}, u32[]{:S(2)}) copy-start(bf16[512,8,256]{2,1,0:T(8,128)(2,1)} %param.34) | copy-start | bytes 6291460
  14.2 3.4 %copy-start.20 = (bf16[768,576]{1,0:T(8,128)(2,1)}, bf16[768,576]{1,0:T(8,128)(2,1)S(1)}, u32[]{:S(2)}) copy-start(bf16[768,576]{1,0:T(8,128)(2,1)S(1)} %maximum_maximum_fusion.1) | copy-start | bytes 2654212
  15.7 1.8 copy-start.11
  17.6 22.6 %copy-start.3 = (bf16[768,8,256]{2,0,1:T(8,128)(2,1)}, bf16[768,8,256]{2,0,1:T(8,128)(2,1)S(1)}, u32[]{:S(2)}) copy-start(bf16[768,8,256]{2,0,1:T(8,128)(2,1)S(1)} %convolution_convert_fusion) | copy-start | bytes 9437188
  21.2 4.3 %copy-start.19 = (bf16[512,8,128]{2,1,0:T(8,128)(2,1)S(1)}, bf16[512,8,128]{2,1,0:T(8,128)(2,1)}, u32[]{:S(2)}) copy-start(bf16[512,8,128]{2,1,0:T(8,128)(2,1)} %param.35) | copy-start | bytes 3145732
  24.8 2.7 %copy-start.21 = (s32[256]{0:T(256)S(1)}, s32[256]{0:T(256)}, u32[]{:S(2)}) copy-start(s32[256]{0:T(256)} %iota_add_fusion.1) | copy-start | bytes 3076
  36.6 3.5 %copy-start.12 = (bf16[512,8,128]{2,0,1:T(8,128)(2,1)S(1)}, bf16[512,8,128]{2,0,1:T(8,128)(2,1)}, u32[]{:S(2)}) copy-start(bf16[512,8,128]{2,0,1:T(8,128)(2,1)} %copy_select_fusion) | copy-start | bytes 3145732
  36.6 7.6 %slice-start = ((s8[6291456]{0:T(1024)(128)(4,1)}), s8[2097152]{0:T(1024)(128)(4,1)S(1)}, s32[]{:S(2)}) async-start(s8[6291456]{0:T(1024)(128)(4,1)} %bitcast.93), calls=%async_computation.5 | async-start | bytes 4194304
  40.1 4.1 %slice-start.1 = ((s8[6291456]{0:T(1024)(128)(4,1)}), s8[4194304]{0:T(1024)(128)(4,1)S(1)}, s32[]{:S(2)}) async-start(s8[6291456]{0:T(1024)(128)(4,1)} %bitcast.93), calls=%async_computation.6 | async-start | bytes 8388608
  41.4 2.9 %copy-start.4 = (bf16[768,8,256]{2,0,1:T(8,128)(2,1)S(1)}, bf16[768,8,256]{2,0,1:T(8,128)(2,1)}, u32[]{:S(2)}) copy-start(bf16[768,8,256]{2,0,1:T(8,128)(2,1)} %copy-done.3) | copy-start | bytes 9437188
  44.3 1.3 copy-start.8
  58.8 3.7 %copy-start.5 = (bf16[768,8,256]{2,0,1:T(8,128)(2,1)S(1)}, bf16[768,8,256]{2,0,1:T(8,128)(2,1)}, u32[]{:S(2)}) copy-start(bf16[768,8,256]{2,0,1:T(8,128)(2,1)} %copy-done.3) | copy-start | bytes 9437188
  58.8 6.7 %copy-start.2 = (f32[8,256,768]{1,2,0:T(8,128)S(1)}, f32[8,256,768]{1,2,0:T(8,128)}, u32[]{:S(2)}) copy-start(f32[8,256,768]{1,2,0:T(8,128)} %get-tuple-element.157) | copy-start | bytes 18874372
  62.5 3.0 %copy-start.13 = (bf16[512,8,128]{2,0,1:T(8,128)(2,1)S(1)}, bf16[512,8,128]{2,0,1:T(8,128)(2,1)}, u32[]{:S(2)}) copy-start(bf16[512,8,128]{2,0,1:T(8,128)(2,1)} %copy_select_fusion) | copy-start | bytes 3145732
  65.6 1.9 copy-start.7
  67.5 2.4 copy-start
  67.5 2.4 copy-start.9
  67.5 2.4 copy-start.16
  70.9 0.7 copy-start.17
  71.7 4.3 %copy-start.14 = (bf16[768,8,128]{0,2,1:T(8,128)(2,1)S(1)}, bf16[768,8,128]{0,2,1:T(8,128)(2,1)}, u32[]{:S(2)}) copy-start(bf16[768,8,128]{0,2,1:T(8,128)(2,1)} %fusion.18) | copy-start | bytes 4718596
  71.7 4.3 %copy-start.23 = (bf16[512,8,256]{2,1,0:T(8,128)(2,1)S(1)}, bf16[512,8,256]{2,1,0:T(8,128)(2,1)}, u32[]{:S(2)}) copy-start(bf16[512,8,256]{2,1,0:T(8,128)(2,1)} %param.34) | copy-start | bytes 6291460
  76.1 1.1 copy-start.15
  78.2 3.6 %copy-start.18 = (f32[768,64]{0,1:T(8,128)S(1)}, f32[768,64]{0,1:T(8,128)}, u32[]{:S(2)}) copy-start(f32[768,64]{0,1:T(8,128)} %copy-done.17) | copy-start | bytes 589828
  78.2 154.0 %reduce-scatter.7.cloned.1.call-start = ((), (), s32[]{:S(2)}) async-start(), calls=%async_computation.4 | async-start | bytes 696320
  85.1 5.5 %copy-start.10 = (bf16[768,64,1]{1,0,2:T(8,128)(2,1)S(1)}, bf16[768,64,1]{1,0,2:T(8,128)(2,1)}, u32[]{:S(2)}) copy-start(bf16[768,64,1]{1,0,2:T(8,128)(2,1)} %maximum_bitcast_fusion) | copy-start | bytes 294916
  85.1 148.8 %reduce-scatter.5.cloned.1.call-start = ((), (), s32[]{:S(2)}) async-start(), calls=%async_computation.2 | async-start | bytes 2359296 | tf_op jit(solution)/shard_map/reduce_scatter | solution.py:142
  90.6 3.6 %copy-start.6 = (bf16[768,8,256]{2,0,1:T(8,128)(2,1)S(1)}, bf16[768,8,256]{2,0,1:T(8,128)(2,1)}, u32[]{:S(2)}) copy-start(bf16[768,8,256]{2,0,1:T(8,128)(2,1)} %copy-done.3) | copy-start | bytes 9437188
  93.3 1.9 copy-start.1
Sparse Core Ops, SparseCore 0:
  78.3 151.7 all-reduce.1
Sparse Core Ops, SparseCore 1:
  85.2 61.4 reduce-scatter.6
  150.3 77.0 reduce-scatter.4
where the time goes:
time: 244 us; the launch traced here: 243 us
  waiting for transfers between devices  132 us (54%)
  matrix products  61.9 us (25%)
  other arithmetic  18.8 us (8%)
  between operations  16.6 us (7%)
  local copies, waits for them, and re-layouts  13.6 us (6%)
    psum x1, waiting for transfers between devices, on_device(): lax.psum(jnp.concatenate([latent_part, rope_grad[:prefix_rows]], axis=1),...  132 us
    sub x2, matrix products, block_gradients(): exponent = jnp.exp(scores - highest)  15.4 us
    unnamed x59, local copies, waits for them, and re-layouts  12.2 us
    dot_general x2, matrix products, block_gradients(): jnp.einsum('hqk,qhd->khd', score_grad, query_nope, preferred_element_type...  8.15 us
    dot_general x2, matrix products, block_gradients(): jnp.einsum('qhd,khd->hqk', query_nope, key_nope, preferred_element_type=j...  7.21 us
    convert_element_type x2, other arithmetic, block_gradients(): weights = probability.astype(jnp.bfloat16)  6.97 us
    dot_general x1, matrix products, on_device(): jnp.einsum('kl,khd->lhd', source_latent, head_projected_grad, preferred_e...  5.36 us
    dot_general x2, matrix products, block_gradients(): jnp.einsum('hqk,qhv->khv', weights, cotangent, preferred_element_type=jnp...  5.23 us
  transfers between devices with their start and end apart: 3, of which 1 were waited for; matrix products, arithmetic and copies ran while one was open for 9% of the time, Pallas kernels for 0%

commit v1 on v0

--- a/solution.py
+++ b/solution.py
@@ -139,25 +139,34 @@
         rope_total,
         up_part,
     )
-    up_grad = lax.psum_scatter(
-        up_part.astype(jnp.bfloat16), "dp", scatter_dimension=0, tiled=True
-    ).astype(jnp.float32)
+    dp_size = lax.axis_size("dp")
+    head_size = lax.axis_size("head")
+    up_pieces = lax.all_to_all(
+        up_part.astype(jnp.bfloat16).reshape((dp_size, -1) + up_part.shape[1:]), "dp", 0, 0, tiled=False
+    )
+    up_grad = jnp.sum(up_pieces.astype(jnp.float32), axis=0)
     token_grad = projected_grad[prefix_rows:]
     token_rope_grad = rope_grad[prefix_rows:]
     latent_part = jnp.einsum("khd,lhd->kl", token_grad, kv_up, preferred_element_type=jnp.float32)
-    latent_grad = lax.psum_scatter(
-        jnp.concatenate([latent_part, unrotate(token_rope_grad, cosine, sine)], axis=1).astype(
-            jnp.bfloat16
-        ),
-        "head",
-        scatter_dimension=0,
-        tiled=True,
-    ).astype(jnp.float32)
+    token_part = jnp.concatenate(
+        [latent_part, unrotate(token_rope_grad, cosine, sine)], axis=1
+    ).astype(jnp.bfloat16)
+    token_pieces = lax.all_to_all(
+        token_part.reshape((head_size, -1) + token_part.shape[1:]), "head", 0, 0, tiled=False
+    )
+    latent_grad = jnp.sum(token_pieces.astype(jnp.float32), axis=0)
     latent_part = jnp.einsum(
         "khd,lhd->kl", projected_grad[:prefix_rows], kv_up, preferred_element_type=jnp.float32
     )
-    prefix_grad = lax.psum(
-        jnp.concatenate([latent_part, rope_grad[:prefix_rows]], axis=1), ("dp", "head")
+    prefix_part = jnp.concatenate([latent_part, rope_grad[:prefix_rows]], axis=1)
+    world = dp_size * head_size
+    prefix_pieces = lax.all_to_all(
+        prefix_part.reshape((world, -1) + prefix_part.shape[1:]), ("dp", "head"), 0, 0, tiled=False
+    )
+    prefix_own = jnp.sum(prefix_pieces, axis=0)
+    prefix_copies = jnp.broadcast_to(prefix_own[None], (world,) + prefix_own.shape)
+    prefix_grad = lax.all_to_all(prefix_copies, ("dp", "head"), 0, 0, tiled=False).reshape(
+        prefix_part.shape
     )
     return (query_grad, latent_grad, up_grad, prefix_grad)
 

time: 244 us -> 172 us (0.70)
  waiting for transfers between devices: 132 us -> 46.5 us
  starting transfers between devices: 0.13 us -> 25.6 us
  between operations: 16.6 us -> 1.79 us
  local copies, waits for them, and re-layouts: 13.6 us -> 18 us
    psum x1 -> x0, waiting for transfers between devices: 132 us -> none  [on_device(): lax.psum(jnp.concatenate([latent_part, rope_grad[:prefix_rows]], axis=1),...]
    all_to_all x0 -> x4, waiting for transfers between devices: none -> 46.5 us  [the longest x1 17.6 us: on_device(): lax.all_to_all(up_part.astype(jnp.bfloat16).reshape((dp_size, -1) + up_pa...]
    all_to_all x0 -> x4, starting transfers between devices: none -> 25.6 us  [the longest x1 11.5 us: on_device(): lax.all_to_all(prefix_part.reshape((world, -1) + prefix_part.shape[1:]),...]
    reshape x0 -> x3, local copies, waits for them, and re-layouts: none -> 4.35 us  [the longest x1 1.58 us: on_device(): up_part.astype(jnp.bfloat16).reshape((dp_size, -1) + up_part.shape[1:])]
    reduce_sum x0 -> x3, other arithmetic: none -> 4.09 us  [the longest x1 2.02 us: on_device(): up_grad = jnp.sum(up_pieces.astype(jnp.float32), axis=0)]
    unnamed x59 -> x64, local copies, waits for them, and re-layouts: 12.2 us -> 9.56 us
  transfers between devices with their start and end apart: 3 -> 4, of which waited for: 1 -> 4; matrix products, arithmetic and copies ran while one was open for 9% -> 14% of each run, Pallas kernels for 0% -> 0%
where the time goes in v1:
time: 172 us; the launch traced here: 171 us
  matrix products  60.6 us (35%)
  waiting for transfers between devices  46.5 us (27%)
  starting transfers between devices  25.6 us (15%)
  other arithmetic  18.5 us (11%)
  local copies, waits for them, and re-layouts  18 us (10%)
  between operations  1.79 us (1%)
    all_to_all x1, waiting for transfers between devices, on_device(): lax.all_to_all(up_part.astype(jnp.bfloat16).reshape((dp_size, -1) + up_pa...  17.6 us
    sub x2, matrix products, block_gradients(): exponent = jnp.exp(scores - highest)  15.1 us
    all_to_all x1, starting transfers between devices, on_device(): lax.all_to_all(prefix_part.reshape((world, -1) + prefix_part.shape[1:]),...  11.5 us
    all_to_all x1, waiting for transfers between devices, on_device(): lax.all_to_all(prefix_part.reshape((world, -1) + prefix_part.shape[1:]),...  11 us
    all_to_all x1, waiting for transfers between devices, on_device(): lax.all_to_all(token_part.reshape((head_size, -1) + token_part.shape[1:])...  9.96 us
    unnamed x64, local copies, waits for them, and re-layouts  9.56 us
    dot_general x2, matrix products, block_gradients(): jnp.einsum('hqk,qhd->khd', score_grad, query_nope, preferred_element_type...  8.18 us
    all_to_all x1, waiting for transfers between devices, on_device(): lax.all_to_all(prefix_copies, ('dp', 'head'), 0, 0, tiled=False)  7.88 us
  transfers between devices with their start and end apart: 4, of which 4 were waited for; matrix products, arithmetic and copies ran while one was open for 14% of the time, Pallas kernels for 0%

profile of v1, /device:TPU:1, one launch (start us, length us, event | category | flops | bytes accessed | tf_op | source)
XLA Modules:
  0.0 170.9 jit_solution(10199901937560176659)
XLA Ops:
  0.7 1.0 slice_convert_fusion.1
  1.7 1.9 %slice.200 = bf16[512,512]{0,1:T(8,128)(2,1)} slice(bf16[512,576]{0,1:T(8,128)(2,1)} %param.32), slice={[0:512], [0:512]} | slice | bytes 1048576 | tf_op jit(solution)/shard_map/slice | solution.py:85
  3.5 0.7 convert_element_type.54
  4.2 0.3 multiply_cosine_fusion
  4.8 1.2 copy.166
  6.0 1.3 copy.252
  7.5 1.1 copy-done.12
  8.8 1.8 %convolution_convert_fusion = bf16[768,8,256]{2,0,1:T(8,128)(2,1)S(1)} fusion(bf16[512,8,256]{2,1,0:T(8,128)(2,1)S(1)} %copy-done, bf16[768,576]{1,0:T(8,128)(2,1)S(1)} %maximum_maximum_fusion.1), kind=kOutput, calls=%fused_computation.25 | convolution fusion | flops 1612185600 | bytes 6029312 | tf_op jit(solution)/shard_map/kl,lhd->khd/dot_general | solution.py:94
  10.6 3.6 %fusion.46 = f32[8,768,256]{2,1,0:T(8,128)} fusion(bf16[768,8,256]{2,0,1:T(8,128)(2,1)S(1)} %convolution_convert_fusion, bf16[512,8,192]{0,2,1:T(8,128)(2,1)S(1)} %copy-done.12), kind=kOutput, calls=%fused_computation.62 | convolution fusion | flops 402653184 | bytes 8388608 | tf_op jit(solution)/shard_map/qhd,khd->hqk/dot_general | solution.py:37
  14.3 3.6 %fusion.49 = f32[8,768,256]{2,1,0:T(8,128)} fusion(bf16[768,8,256]{2,0,1:T(8,128)(2,1)S(1)} %convolution_convert_fusion, bf16[512,8,192]{0,2,1:T(8,128)(2,1)S(1)} %copy-done.12), kind=kOutput, calls=%fused_computation.65 | convolution fusion | flops 402653184 | bytes 8388608 | tf_op jit(solution)/shard_map/qhd,khd->hqk/dot_general | solution.py:37
  18.5 1.2 copy_select_fusion
  19.7 0.2 subtract_convert_fusion
  19.8 0.9 fusion.52
  20.8 7.5 %fusion.92 = (f32[8,256]{1,0:T(8,128)S(1)}, f32[8,256,768]{1,2,0:T(8,128)}) fusion(f32[8,768,256]{2,1,0:T(8,128)} %fusion.49, pred[256,768]{0,1:T(8,128)(4,1)S(1)} %get-tuple-element.150, bf16[768,64,1]{1,0,2:T(8,128)(2,1)S(1)} %maximum_bitcast_fusion, bf16[512,8,32]{0,2,1:T(8,128)(2,1)S(1)} %get-tuple-element.136, ...), kind=kOutput, calls=%fused_computation.130 | convolution fusion | flops 209715968 | bytes 13410304 | tf_op jit(solution)/shard_map/sub | solution.py:47
  28.3 3.5 %fusion.7 = bf16[8,256,768]{1,2,0:T(8,128)(2,1)S(1)} fusion(f32[8,256,768]{1,2,0:T(8,128)} %get-tuple-element.159, f32[8,256]{1,0:T(8,128)S(1)} %get-tuple-element.158), kind=kLoop, calls=%fused_computation.23 | loop fusion | flops 3145728 | bytes 9445376 | tf_op jit(solution)/shard_map/convert_element_type | solution.py:49
  31.8 0.2 copy-done.8
  32.0 0.3 copy-done.13
  32.3 1.2 fusion.31
  33.5 2.8 %fusion.60 = f32[8,128,768]{2,1,0:T(8,128)} fusion(bf16[8,256,768]{1,2,0:T(8,128)(2,1)S(1)} %fusion.7, bf16[512,8,128]{2,0,1:T(8,128)(2,1)S(1)} %copy-done.13), kind=kOutput, calls=%fused_computation.87 | convolution fusion | flops 402653184 | bytes 6815744 | tf_op jit(solution)/shard_map/hqk,qhv->khv/dot_general | solution.py:64
  36.3 1.2 multiply_convert_fusion.1
  37.6 1.1 convolution_bitcast_fusion.5
  38.7 3.9 %fusion.56 = f32[8,768,128]{1,2,0:T(8,128)} fusion(bf16[8,256,768]{1,2,0:T(8,128)(2,1)S(1)} %multiply_convert_fusion.1, bf16[512,8,192]{0,2,1:T(8,128)(2,1)} %param.31), kind=kOutput, calls=%fused_computation.83 | convolution fusion | flops 402653184 | bytes 6815744 | tf_op jit(solution)/shard_map/hqk,qhd->khd/dot_general | solution.py:60
  42.6 7.5 %fusion.91 = (f32[8,256]{1,0:T(8,128)S(1)}, f32[8,256,768]{1,2,0:T(8,128)}) fusion(f32[8,768,256]{2,1,0:T(8,128)} %fusion.46, pred[256,768]{0,1:T(8,128)(4,1)S(1)} %get-tuple-element.151, bf16[768,64,1]{1,0,2:T(8,128)(2,1)S(1)} %maximum_bitcast_fusion, bf16[512,8,32]{0,2,1:T(8,128)(2,1)S(1)} %get-tuple-element.137, ...), kind=kOutput, calls=%fused_computation.129 | convolution fusion | flops 209715968 | bytes 13410304 | tf_op jit(solution)/shard_map/sub | solution.py:47
  50.1 3.5 %fusion.8 = bf16[8,256,768]{1,2,0:T(8,128)(2,1)S(1)} fusion(f32[8,256,768]{1,2,0:T(8,128)} %get-tuple-element.157, f32[8,256]{1,0:T(8,128)S(1)} %get-tuple-element.156), kind=kLoop, calls=%fused_computation.24 | loop fusion | flops 3145728 | bytes 9445376 | tf_op jit(solution)/shard_map/convert_element_type | solution.py:49
  53.6 0.2 copy-done.9
  53.8 3.0 %fusion.32 = f32[256,8]{0,1:T(8,128)S(1)} fusion(bf16[8,256,768]{1,2,0:T(8,128)(2,1)S(1)} %fusion.8, bf16[768,8,256]{2,0,1:T(8,128)(2,1)S(1)} %copy-done.9, bf16[512,8,128]{2,0,1:T(8,128)(2,1)} %copy_select_fusion), kind=kOutput, calls=%fused_computation.46 | convolution fusion | flops 403437568 | bytes 5251072 | tf_op jit(solution)/shard_map/hqk,khv->qhv/dot_general | solution.py:50
  56.9 1.2 multiply_convert_fusion
  58.1 0.6 copy-done.11
  58.7 2.6 %fusion.18 = bf16[768,8,128]{0,2,1:T(8,128)(2,1)} fusion(f32[8,128,768]{2,1,0:T(8,128)S(1)} %copy-done.11, bf16[8,256,768]{1,2,0:T(8,128)(2,1)S(1)} %fusion.8, bf16[512,8,128]{2,0,1:T(8,128)(2,1)S(1)} %copy-done.14), kind=kOutput, calls=%fused_computation.35 | convolution fusion | flops 404226048 | bytes 8388608 | tf_op jit(solution)/shard_map/hqk,qhv->khv/dot_general | solution.py:64
  61.3 1.1 fusion.38
  62.4 0.7 copy-done.18
  63.2 4.3 %fusion.17 = bf16[768,8,128]{0,2,1:T(8,128)(2,1)S(1)} fusion(f32[8,768,128]{1,2,0:T(8,128)} %fusion.56, bf16[8,256,768]{1,2,0:T(8,128)(2,1)} %copy-done.3, bf16[512,8,192]{0,2,1:T(8,128)(2,1)} %param.31), kind=kOutput, calls=%fused_computation.34 | convolution fusion | flops 404226048 | bytes 8388608 | tf_op jit(solution)/shard_map/hqk,qhd->khd/dot_general | solution.py:60
  67.5 0.8 fusion.33
  68.3 0.3 copy-done.17
  68.7 1.2 reshape.400
  69.9 11.5 %all-to-all-start.2 = ((f32[128,2,576]{2,1,0:T(2,128)}), f32[128,2,576]{2,1,0:T(2,128)S(1)}, u32[]{:S(2)}, u32[]{:S(2)}) async-start(f32[128,2,576]{2,1,0:T(2,128)} %reshape.400), calls=%async_computation.2 | async-start | bytes 1310720 | tf_op jit(solution)/shard_map/all_to_all | solution.py:163
  81.4 0.3 fusion.77
  82.0 2.9 %fusion.26 = bf16[512,512]{1,0:T(8,128)(2,1)S(1)} fusion(bf16[512,8,256]{2,1,0:T(8,128)(2,1)S(1)} %copy-done, bf16[768,8,128]{0,2,1:T(8,128)(2,1)} %copy-done.17, bf16[768,8,128]{0,2,1:T(8,128)(2,1)} %fusion.18), kind=kOutput, calls=%fused_computation.42 | convolution fusion | flops 1078198272 | bytes 5767168 | tf_op jit(solution)/shard_map/khd,lhd->kl/dot_general | solution.py:150
  84.9 1.0 pad_maximum_fusion.4
  85.9 11.0 %all-to-all-done.2 = f32[128,2,576]{2,1,0:T(2,128)S(1)} async-done(((f32[128,2,576]{2,1,0:T(2,128)}), f32[128,2,576]{2,1,0:T(2,128)S(1)}, u32[]{:S(2)}, u32[]{:S(2)}) %all-to-all-start.2) | async-done | bytes 589856 | tf_op jit(solution)/shard_map/all_to_all | solution.py:163
  96.9 0.8 copy-done.15
  97.7 4.0 %all-to-all-start = ((bf16[16,32,576]{2,1,0:T(8,128)(2,1)}), bf16[16,32,576]{2,1,0:T(8,128)(2,1)S(1)}, u32[]{:S(2)}, u32[]{:S(2)}) async-start(bf16[16,32,576]{2,1,0:T(8,128)(2,1)} %pad_maximum_fusion.4), calls=%async_computation | async-start | bytes 1310720 | tf_op jit(solution)/shard_map/all_to_all | solution.py:154
  101.7 1.3 reduce_sum.69
  103.0 10.0 %all-to-all-done = bf16[16,32,576]{2,1,0:T(8,128)(2,1)S(1)} async-done(((bf16[16,32,576]{2,1,0:T(8,128)(2,1)}), bf16[16,32,576]{2,1,0:T(8,128)(2,1)S(1)}, u32[]{:S(2)}, u32[]{:S(2)}) %all-to-all-start) | async-done | bytes 589856 | tf_op jit(solution)/shard_map/all_to_all | solution.py:154
  113.0 1.0 broadcast_in_dim.35
  114.0 5.5 %all-to-all-start.3 = ((f32[128,2,576]{2,1,0:T(2,128)}), f32[128,2,576]{2,1,0:T(2,128)}, u32[]{:S(2)}, u32[]{:S(2)}) async-start(f32[128,2,576]{2,1,0:T(2,128)} %broadcast_in_dim.35), calls=%async_computation.3 | async-start | bytes 1310720 | tf_op jit(solution)/shard_map/all_to_all | solution.py:168
  119.5 4.0 %fusion.12 = bf16[512,8,256]{2,0,1:T(8,128)(2,1)S(1)} fusion(bf16[768,8,128]{0,2,1:T(8,128)(2,1)} %fusion.18, bf16[768,8,128]{0,2,1:T(8,128)(2,1)} %copy-done.17, bf16[768,576]{1,0:T(8,128)(2,1)} %copy-done.21), kind=kOutput, calls=%fused_computation.28 | convolution fusion | flops 1617952768 | bytes 6029312 | tf_op jit(solution)/shard_map/kl,khd->lhd/dot_general | solution.py:133
  123.5 1.6 copy.205
  125.1 0.7 fusion.89
  125.8 0.5 copy-done.4
  126.2 0.7 convolution_bitcast_fusion.2
  126.9 7.9 %all-to-all-done.3 = f32[128,2,576]{2,1,0:T(2,128)} async-done(((f32[128,2,576]{2,1,0:T(2,128)}), f32[128,2,576]{2,1,0:T(2,128)}, u32[]{:S(2)}, u32[]{:S(2)}) %all-to-all-start.3) | async-done | bytes 589856 | tf_op jit(solution)/shard_map/all_to_all | solution.py:168
  134.8 4.6 %all-to-all-start.1 = ((bf16[8,64,8,256]{3,1,2,0:T(8,128)(2,1)}), bf16[8,64,8,256]{3,1,2,0:T(8,128)(2,1)}, u32[]{:S(2)}, u32[]{:S(2)}) async-start(bf16[8,64,8,256]{3,1,2,0:T(8,128)(2,1)} %copy.205), calls=%async_computation.1 | async-start | bytes 4194304 | tf_op jit(solution)/shard_map/all_to_all | solution.py:144
  139.6 2.7 %convolution_bitcast_fusion.3 = f32[256,8,64]{0,2,1:T(8,128)S(1)} fusion(bf16[768,64,1]{1,0,2:T(8,128)(2,1)S(1)} %maximum_bitcast_fusion, bf16[8,256,768]{1,2,0:T(8,128)(2,1)} %copy-done.1), kind=kOutput, calls=%fused_computation.49 | convolution fusion | flops 201326592 | bytes 3768320 | tf_op jit(solution)/shard_map/hqk,kr->qhr/dot_general | solution.py:59
  142.4 2.3 %fusion.37 = bf16[256,8,128]{0,2,1:T(8,128)(2,1)S(1)} fusion(bf16[8,256,768]{1,2,0:T(8,128)(2,1)S(1)} %copy-done.5, bf16[768,8,256]{2,0,1:T(8,128)(2,1)} %copy-done.7), kind=kOutput, calls=%fused_computation.51 | convolution fusion | flops 402915328 | bytes 5242880 | tf_op jit(solution)/shard_map/hqk,khd->qhd/dot_general | solution.py:56
  144.8 0.1 copy-done.2
  144.9 0.7 fusion.36
  145.6 1.3 maximum_maximum_fusion
  146.9 0.7 convert_reduce_fusion.1
  147.6 1.5 reshape.401
  149.1 1.0 copy.211
  150.2 17.6 %all-to-all-done.1 = bf16[8,64,8,256]{3,1,2,0:T(8,128)(2,1)} async-done(((bf16[8,64,8,256]{3,1,2,0:T(8,128)(2,1)}), bf16[8,64,8,256]{3,1,2,0:T(8,128)(2,1)}, u32[]{:S(2)}, u32[]{:S(2)}) %all-to-all-start.1) | async-done | bytes 2097184 | tf_op jit(solution)/shard_map/all_to_all | solution.py:144
  167.8 2.0 %convert_reduce_fusion = f32[64,8,256]{2,0,1:T(8,128)S(1)} fusion(bf16[8,64,8,256]{3,1,2,0:T(8,128)(2,1)} %all-to-all-done.1), kind=kLoop, calls=%fused_computation.12 | loop fusion | flops 1966080 | bytes 2621440 | tf_op jit(solution)/shard_map/reduce_sum | solution.py:147
  169.8 1.1 copy.210
  (68 shorter events, 1.3 us)
Async XLA Ops:
  0.6 8.2 %copy-start = (bf16[512,8,256]{2,1,0:T(8,128)(2,1)S(1)}, bf16[512,8,256]{2,1,0:T(8,128)(2,1)}, u32[]{:S(2)}) copy-start(bf16[512,8,256]{2,1,0:T(8,128)(2,1)} %param.34) | copy-start | bytes 6291460
  4.6 15.1 %copy-start.22 = (f32[512,32]{0,1:T(8,128)}, f32[512,32]{0,1:T(8,128)S(1)}, u32[]{:S(2)}) copy-start(f32[512,32]{0,1:T(8,128)S(1)} %get-tuple-element.153) | copy-start | bytes 196612
  7.3 1.4 copy-start.12
  8.7 2.0 %copy-start.21 = (bf16[768,576]{1,0:T(8,128)(2,1)}, bf16[768,576]{1,0:T(8,128)(2,1)S(1)}, u32[]{:S(2)}) copy-start(bf16[768,576]{1,0:T(8,128)(2,1)S(1)} %maximum_maximum_fusion.1) | copy-start | bytes 2654212
  10.6 3.6 %copy-start.7 = (bf16[768,8,256]{2,0,1:T(8,128)(2,1)}, bf16[768,8,256]{2,0,1:T(8,128)(2,1)S(1)}, u32[]{:S(2)}) copy-start(bf16[768,8,256]{2,0,1:T(8,128)(2,1)S(1)} %convolution_convert_fusion) | copy-start | bytes 9437188
  14.3 4.2 %copy-start.20 = (bf16[512,8,128]{2,1,0:T(8,128)(2,1)S(1)}, bf16[512,8,128]{2,1,0:T(8,128)(2,1)}, u32[]{:S(2)}) copy-start(bf16[512,8,128]{2,1,0:T(8,128)(2,1)} %param.35) | copy-start | bytes 3145732
  28.3 3.7 %copy-start.8 = (bf16[768,8,256]{2,0,1:T(8,128)(2,1)S(1)}, bf16[768,8,256]{2,0,1:T(8,128)(2,1)}, u32[]{:S(2)}) copy-start(bf16[768,8,256]{2,0,1:T(8,128)(2,1)} %copy-done.7) | copy-start | bytes 9437188
  28.3 4.0 %copy-start.13 = (bf16[512,8,128]{2,0,1:T(8,128)(2,1)S(1)}, bf16[512,8,128]{2,0,1:T(8,128)(2,1)}, u32[]{:S(2)}) copy-start(bf16[512,8,128]{2,0,1:T(8,128)(2,1)} %copy_select_fusion) | copy-start | bytes 3145732
  28.3 8.0 %slice-start = ((s8[6291456]{0:T(1024)(128)(4,1)}), s8[4194304]{0:T(1024)(128)(4,1)S(1)}, s32[]{:S(2)}) async-start(s8[6291456]{0:T(1024)(128)(4,1)} %bitcast.96), calls=%async_computation.4 | async-start | bytes 8388608
  32.3 4.1 %slice-start.1 = ((s8[6291456]{0:T(1024)(128)(4,1)}), s8[2097152]{0:T(1024)(128)(4,1)S(1)}, s32[]{:S(2)}) async-start(s8[6291456]{0:T(1024)(128)(4,1)} %bitcast.96), calls=%async_computation.5 | async-start | bytes 4194304
  37.6 5.0 %copy-start.1 = (bf16[8,256,768]{1,2,0:T(8,128)(2,1)}, bf16[8,256,768]{1,2,0:T(8,128)(2,1)S(1)}, u32[]{:S(2)}) copy-start(bf16[8,256,768]{1,2,0:T(8,128)(2,1)S(1)} %multiply_convert_fusion.1) | copy-start | bytes 9437188
  50.1 3.7 %copy-start.9 = (bf16[768,8,256]{2,0,1:T(8,128)(2,1)S(1)}, bf16[768,8,256]{2,0,1:T(8,128)(2,1)}, u32[]{:S(2)}) copy-start(bf16[768,8,256]{2,0,1:T(8,128)(2,1)} %copy-done.7) | copy-start | bytes 9437188
  50.1 6.7 %copy-start.6 = (f32[8,256,768]{1,2,0:T(8,128)S(1)}, f32[8,256,768]{1,2,0:T(8,128)}, u32[]{:S(2)}) copy-start(f32[8,256,768]{1,2,0:T(8,128)} %get-tuple-element.157) | copy-start | bytes 18874372
  53.8 3.0 %copy-start.14 = (bf16[512,8,128]{2,0,1:T(8,128)(2,1)S(1)}, bf16[512,8,128]{2,0,1:T(8,128)(2,1)}, u32[]{:S(2)}) copy-start(bf16[512,8,128]{2,0,1:T(8,128)(2,1)} %copy_select_fusion) | copy-start | bytes 3145732
  56.8 1.9 %copy-start.11 = (f32[8,128,768]{2,1,0:T(8,128)S(1)}, f32[8,128,768]{2,1,0:T(8,128)}, u32[]{:S(2)}) copy-start(f32[8,128,768]{2,1,0:T(8,128)} %fusion.60) | copy-start | bytes 9437188
  58.7 2.6 %copy-start.3 = (bf16[8,256,768]{1,2,0:T(8,128)(2,1)}, bf16[8,256,768]{1,2,0:T(8,128)(2,1)S(1)}, u32[]{:S(2)}) copy-start(bf16[8,256,768]{1,2,0:T(8,128)(2,1)S(1)} %multiply_convert_fusion) | copy-start | bytes 9437188
  62.4 0.7 copy-start.18
  63.2 4.3 %copy-start.16 = (bf16[768,8,128]{0,2,1:T(8,128)(2,1)S(1)}, bf16[768,8,128]{0,2,1:T(8,128)(2,1)}, u32[]{:S(2)}) copy-start(bf16[768,8,128]{0,2,1:T(8,128)(2,1)} %fusion.18) | copy-start | bytes 4718596
  67.5 1.1 copy-start.17
  68.6 12.8 %copy-start.19 = (f32[768,64]{0,1:T(8,128)S(1)}, f32[768,64]{0,1:T(8,128)}, u32[]{:S(2)}) copy-start(f32[768,64]{0,1:T(8,128)} %copy-done.18) | copy-start | bytes 589828
  69.9 26.9 %all-to-all-start.2 = ((f32[128,2,576]{2,1,0:T(2,128)}), f32[128,2,576]{2,1,0:T(2,128)S(1)}, u32[]{:S(2)}, u32[]{:S(2)}) async-start(f32[128,2,576]{2,1,0:T(2,128)} %reshape.400), calls=%async_computation.2 | async-start | bytes 1310720 | tf_op jit(solution)/shard_map/all_to_all | solution.py:163
  96.9 0.9 copy-start.15
  97.7 15.2 %all-to-all-start = ((bf16[16,32,576]{2,1,0:T(8,128)(2,1)}), bf16[16,32,576]{2,1,0:T(8,128)(2,1)S(1)}, u32[]{:S(2)}, u32[]{:S(2)}) async-start(bf16[16,32,576]{2,1,0:T(8,128)(2,1)} %pad_maximum_fusion.4), calls=%async_computation | async-start | bytes 1310720 | tf_op jit(solution)/shard_map/all_to_all | solution.py:154
  114.0 20.8 %all-to-all-start.3 = ((f32[128,2,576]{2,1,0:T(2,128)}), f32[128,2,576]{2,1,0:T(2,128)}, u32[]{:S(2)}, u32[]{:S(2)}) async-start(f32[128,2,576]{2,1,0:T(2,128)} %broadcast_in_dim.35), calls=%async_computation.3 | async-start | bytes 1310720 | tf_op jit(solution)/shard_map/all_to_all | solution.py:168
  123.5 1.6 copy-start.23
  123.5 2.7 %copy-start.4 = (bf16[8,256,768]{1,2,0:T(8,128)(2,1)S(1)}, bf16[8,256,768]{1,2,0:T(8,128)(2,1)}, u32[]{:S(2)}) copy-start(bf16[8,256,768]{1,2,0:T(8,128)(2,1)} %copy-done.3) | copy-start | bytes 9437188
  126.2 13.2 %copy-start.26 = (f32[256,32]{0,1:T(8,128)S(1)}, f32[256,32]{0,1:T(8,128)}, u32[]{:S(2)}) copy-start(f32[256,32]{0,1:T(8,128)} %get-tuple-element.147) | copy-start | bytes 98308
  126.2 13.2 %copy-start.27 = (f32[256,32]{0,1:T(8,128)S(1)}, f32[256,32]{0,1:T(8,128)}, u32[]{:S(2)}) copy-start(f32[256,32]{0,1:T(8,128)} %get-tuple-element.160) | copy-start | bytes 98308
  134.8 33.0 %all-to-all-start.1 = ((bf16[8,64,8,256]{3,1,2,0:T(8,128)(2,1)}), bf16[8,64,8,256]{3,1,2,0:T(8,128)(2,1)}, u32[]{:S(2)}, u32[]{:S(2)}) async-start(bf16[8,64,8,256]{3,1,2,0:T(8,128)(2,1)} %copy.205), calls=%async_computation.1 | async-start | bytes 4194304 | tf_op jit(solution)/shard_map/all_to_all | solution.py:144
  139.4 2.9 %copy-start.24 = (f32[256,32]{0,1:T(8,128)S(1)}, f32[256,32]{0,1:T(8,128)}, u32[]{:S(2)}) copy-start(f32[256,32]{0,1:T(8,128)} %get-tuple-element.146) | copy-start | bytes 98308
  139.4 2.9 %copy-start.25 = (f32[256,32]{0,1:T(8,128)S(1)}, f32[256,32]{0,1:T(8,128)}, u32[]{:S(2)}) copy-start(f32[256,32]{0,1:T(8,128)} %get-tuple-element.161) | copy-start | bytes 98308
  139.5 3.0 %copy-start.5 = (bf16[8,256,768]{1,2,0:T(8,128)(2,1)S(1)}, bf16[8,256,768]{1,2,0:T(8,128)(2,1)}, u32[]{:S(2)}) copy-start(bf16[8,256,768]{1,2,0:T(8,128)(2,1)} %copy-done.3) | copy-start | bytes 9437188
  139.6 5.2 %copy-start.10 = (bf16[768,8,256]{2,0,1:T(8,128)(2,1)S(1)}, bf16[768,8,256]{2,0,1:T(8,128)(2,1)}, u32[]{:S(2)}) copy-start(bf16[768,8,256]{2,0,1:T(8,128)(2,1)} %copy-done.7) | copy-start | bytes 9437188
  142.3 2.6 %copy-start.2 = (bf16[8,256,768]{1,2,0:T(8,128)(2,1)S(1)}, bf16[8,256,768]{1,2,0:T(8,128)(2,1)}, u32[]{:S(2)}) copy-start(bf16[8,256,768]{1,2,0:T(8,128)(2,1)} %copy-done.1) | copy-start | bytes 9437188

commit v2 on v1

--- a/solution.py
+++ b/solution.py
@@ -1,7 +1,7 @@
 import jax
 import jax.numpy as jnp
 from jax import lax
-from jax.sharding import PartitionSpec as P
+from jax.sharding import Mesh, PartitionSpec as P
 
 
 def angles_of(positions, rope_dim):
@@ -65,6 +65,10 @@
     return (nope_query, rope_query, nope_key, rope_key, value_grad)
 
 
+def swap_pair(values):
+    return lax.ppermute(values, "core", [(0, 1), (1, 0)])
+
+
 def on_device(queries, latent, prefix, kv_up, out_grad, lengths, positions):
     seq_len = queries.shape[0]
     latent_dim = kv_up.shape[0]
@@ -103,21 +107,22 @@
     for block_number in range(seq_len // block_rows):
         first_row = block_number * block_rows
         last_row = first_row + block_rows
+        seen = prefix_rows + last_row
         pieces = block_gradients(
             query_nope[first_row:last_row],
             query_rope[first_row:last_row],
-            key_nope,
-            key_rope,
-            values,
+            key_nope[:seen],
+            key_rope[:seen],
+            values[:seen],
             cotangent[first_row:last_row],
             first_row,
             length,
             prefix_rows,
         )
         nope_query, rope_query, nope_key, rope_key, value_grad = pieces
-        nope_total = nope_total.at[:key_total].add(nope_key)
-        rope_total = rope_total.at[:key_total].add(rope_key)
-        value_total = value_total.at[:key_total].add(value_grad)
+        nope_total = nope_total.at[:seen].add(nope_key)
+        rope_total = rope_total.at[:seen].add(rope_key)
+        value_total = value_total.at[:seen].add(value_grad)
         query_pieces.append(
             jnp.concatenate(
                 [
@@ -140,7 +145,6 @@
         up_part,
     )
     dp_size = lax.axis_size("dp")
-    head_size = lax.axis_size("head")
     up_pieces = lax.all_to_all(
         up_part.astype(jnp.bfloat16).reshape((dp_size, -1) + up_part.shape[1:]), "dp", 0, 0, tiled=False
     )
@@ -151,40 +155,61 @@
     token_part = jnp.concatenate(
         [latent_part, unrotate(token_rope_grad, cosine, sine)], axis=1
     ).astype(jnp.bfloat16)
-    token_pieces = lax.all_to_all(
-        token_part.reshape((head_size, -1) + token_part.shape[1:]), "head", 0, 0, tiled=False
-    )
+    core = lax.axis_index("core")
+    pair_size = lax.axis_size("core")
+    row_size = lax.axis_size("hr")
+    token_blocks = token_part.reshape((row_size, pair_size, -1) + token_part.shape[1:])
+    token_mine = jnp.where(core == 0, token_blocks[:, 0], token_blocks[:, 1])
+    token_other = jnp.where(core == 0, token_blocks[:, 1], token_blocks[:, 0])
+    token_pair = (
+        token_mine.astype(jnp.float32) + swap_pair(token_other).astype(jnp.float32)
+    ).astype(jnp.bfloat16)
+    token_pieces = lax.all_to_all(token_pair, "hr", 0, 0, tiled=False)
     latent_grad = jnp.sum(token_pieces.astype(jnp.float32), axis=0)
     latent_part = jnp.einsum(
         "khd,lhd->kl", projected_grad[:prefix_rows], kv_up, preferred_element_type=jnp.float32
     )
     prefix_part = jnp.concatenate([latent_part, rope_grad[:prefix_rows]], axis=1)
-    world = dp_size * head_size
+    half_rows = prefix_part.shape[0] // 2
+    prefix_mine = lax.dynamic_slice_in_dim(prefix_part, core * half_rows, half_rows)
+    prefix_other = lax.dynamic_slice_in_dim(prefix_part, (1 - core) * half_rows, half_rows)
+    prefix_half = prefix_mine + swap_pair(prefix_other)
+    outer = ("dp", "hr")
+    outer_size = dp_size * row_size
     prefix_pieces = lax.all_to_all(
-        prefix_part.reshape((world, -1) + prefix_part.shape[1:]), ("dp", "head"), 0, 0, tiled=False
+        prefix_half.reshape((outer_size, -1) + prefix_half.shape[1:]), outer, 0, 0, tiled=False
     )
     prefix_own = jnp.sum(prefix_pieces, axis=0)
-    prefix_copies = jnp.broadcast_to(prefix_own[None], (world,) + prefix_own.shape)
-    prefix_grad = lax.all_to_all(prefix_copies, ("dp", "head"), 0, 0, tiled=False).reshape(
-        prefix_part.shape
+    prefix_copies = jnp.broadcast_to(prefix_own[None], (outer_size,) + prefix_own.shape)
+    prefix_gathered = lax.all_to_all(prefix_copies, outer, 0, 0, tiled=False).reshape(
+        prefix_half.shape
+    )
+    prefix_partner = swap_pair(prefix_gathered)
+    prefix_grad = jnp.where(
+        core == 0,
+        jnp.concatenate([prefix_gathered, prefix_partner], axis=0),
+        jnp.concatenate([prefix_partner, prefix_gathered], axis=0),
     )
     return (query_grad, latent_grad, up_grad, prefix_grad)
 
 
 def solution(mesh):
+    dp_size, head_size = mesh.shape["dp"], mesh.shape["head"]
+    split = Mesh(mesh.devices.reshape(dp_size, head_size // 2, 2), ("dp", "hr", "core"))
+    head = ("hr", "core")
     placed = (
-        P("dp", "head", None),
+        P("dp", head, None),
         P("dp", None),
         P(),
-        P(None, "head", None),
-        P("dp", "head", None),
+        P(None, head, None),
+        P("dp", head, None),
         P("dp"),
         P("dp", None),
     )
     return jax.shard_map(
         on_device,
-        mesh=mesh,
+        mesh=split,
         in_specs=placed,
-        out_specs=(P("dp", "head", None), P(("dp", "head"), None), P("dp", "head", None), P()),
+        out_specs=(P("dp", head, None), P(("dp",) + head, None), P("dp", head, None), P()),
         check_vma=False,
     )

time: 172 us -> 167 us (0.971)
  waiting for transfers between devices: 46.5 us -> 28 us
  other arithmetic: 18.5 us -> 25.3 us
  starting transfers between devices: 25.6 us -> 29.6 us
  matrix products: 60.6 us -> 63.4 us
    all_to_all x3, waiting for transfers between devices: 28.8 us -> 16.8 us  [the longest x1 8.49 us: on_device(): lax.all_to_all(prefix_half.reshape((outer_size, -1) + prefix_half.shape[1...]
    all_to_all x1, waiting for transfers between devices: 17.6 us -> 11.2 us  [on_device(): lax.all_to_all(up_part.astype(jnp.bfloat16).reshape((dp_size, -1) + up_pa...]
    ppermute x0 -> x3, starting transfers between devices: none -> 4.79 us  [swap_pair(): return lax.ppermute(values, 'core', [(0, 1), (1, 0)])]
    dot_general x2, matrix products: 2.48 us -> 4.89 us  [block_gradients(): jnp.einsum('qhv,khv->hqk', cotangent, values, preferred_element_type=jnp....]
    unnamed x64 -> x68, local copies, waits for them, and re-layouts: 9.56 us -> 7.5 us
    convert_element_type x0 -> x1, other arithmetic: none -> 1.82 us  [on_device(): token_pair = (token_mine.astype(jnp.float32) + swap_pair(token_other).ast...]
    sub x2, matrix products: 15.1 us -> 13.3 us  [block_gradients(): exponent = jnp.exp(scores - highest)]
    add x0 -> x1, other arithmetic: none -> 1.73 us  [on_device(): prefix_half = prefix_mine + swap_pair(prefix_other)]
  transfers between devices with their start and end apart: 4 -> 7, of which waited for: 4 -> 4; matrix products, arithmetic and copies ran while one was open for 14% -> 20% of each run, Pallas kernels for 0% -> 0%
where the time goes in v2:
time: 167 us; the launch traced here: 166 us
  matrix products  63.4 us (38%)
  starting transfers between devices  29.6 us (18%)
  waiting for transfers between devices  28 us (17%)
  other arithmetic  25.3 us (15%)
  local copies, waits for them, and re-layouts  17.5 us (10%)
  between operations  1.84 us (1%)
    sub x2, matrix products, block_gradients(): exponent = jnp.exp(scores - highest)  13.3 us
    all_to_all x1, starting transfers between devices, on_device(): lax.all_to_all(prefix_half.reshape((outer_size, -1) + prefix_half.shape[1...  11.5 us
    all_to_all x1, waiting for transfers between devices, on_device(): lax.all_to_all(up_part.astype(jnp.bfloat16).reshape((dp_size, -1) + up_pa...  11.2 us
    all_to_all x1, waiting for transfers between devices, on_device(): lax.all_to_all(prefix_half.reshape((outer_size, -1) + prefix_half.shape[1...  8.49 us
    unnamed x68, local copies, waits for them, and re-layouts  7.5 us
    all_to_all x1, waiting for transfers between devices, on_device(): lax.all_to_all(prefix_copies, outer, 0, 0, tiled=False)  7.26 us
    dot_general x2, matrix products, block_gradients(): jnp.einsum('hqk,qhd->khd', score_grad, query_nope, preferred_element_type...  6.79 us
    dot_general x2, matrix products, block_gradients(): jnp.einsum('qhd,khd->hqk', query_nope, key_nope, preferred_element_type=j...  6.38 us
  transfers between devices with their start and end apart: 7, of which 4 were waited for; matrix products, arithmetic and copies ran while one was open for 20% of the time, Pallas kernels for 0%

profile of v2, /device:TPU:1, one launch (start us, length us, event | category | flops | bytes accessed | tf_op | source)
XLA Modules:
  0.0 165.7 jit_solution(15621060437868061803)
XLA Ops:
  0.7 1.0 slice_convert_fusion.1
  1.7 1.9 %slice.226 = bf16[512,512]{0,1:T(8,128)(2,1)} slice(bf16[512,576]{0,1:T(8,128)(2,1)} %param.26), slice={[0:512], [0:512]} | slice | bytes 1048576 | tf_op jit(solution)/shard_map/slice | solution.py:89
  3.5 1.2 copy.178
  4.7 0.7 convert_element_type.66
  5.4 0.3 multiply_cosine_fusion
  6.0 1.3 copy.268
  7.5 0.7 maximum_bitcast_fusion.1
  8.3 0.8 copy-done.13
  9.2 1.8 %convolution_convert_fusion = bf16[768,8,256]{2,0,1:T(8,128)(2,1)S(1)} fusion(bf16[512,8,256]{2,1,0:T(8,128)(2,1)S(1)} %copy-done, bf16[768,576]{1,0:T(8,128)(2,1)S(1)} %maximum_maximum_fusion.1), kind=kOutput, calls=%fused_computation.25 | convolution fusion | flops 1612185600 | bytes 6029312 | tf_op jit(solution)/shard_map/kl,lhd->khd/dot_general | solution.py:98
  11.0 3.6 %fusion.24 = f32[8,768,256]{2,1,0:T(8,128)} fusion(bf16[768,8,256]{2,0,1:T(8,128)(2,1)S(1)} %convolution_convert_fusion, bf16[512,8,192]{0,2,1:T(8,128)(2,1)S(1)} %copy-done.13), kind=kOutput, calls=%fused_computation.43 | convolution fusion | flops 402653184 | bytes 8388608 | tf_op jit(solution)/shard_map/qhd,khd->hqk/dot_general | solution.py:37
  14.6 2.8 %fusion.63 = f32[8,512,256]{2,1,0:T(8,128)} fusion(bf16[768,8,256]{2,0,1:T(8,128)(2,1)S(1)} %convolution_convert_fusion, bf16[512,8,192]{0,2,1:T(8,128)(2,1)S(1)} %copy-done.13), kind=kOutput, calls=%fused_computation.69 | convolution fusion | flops 268435456 | bytes 5767168 | tf_op jit(solution)/shard_map/qhd,khd->hqk/dot_general | solution.py:37
  18.1 1.2 copy_select_fusion
  19.7 5.7 %fusion.112 = (f32[8,256]{1,0:T(8,128)S(1)}, f32[8,256,512]{1,2,0:T(8,128)}) fusion(f32[8,512,256]{2,1,0:T(8,128)} %fusion.63, bf16[512,64,1]{1,0,2:T(8,128)(2,1)S(1)} %copy-done.26, pred[256,512]{0,1:T(8,128)(4,1)S(1)} %fusion.67, bf16[512,8,32]{0,2,1:T(8,128)(2,1)S(1)} %get-tuple-element.112, bf16[512,8,32]{0,2,1:T(8,128)(2,1)S(1)} %get-tuple-element.113), kind=kOutput, calls=%fused_computation.149 | convolution fusion | flops 139985408 | bytes 9117696 | tf_op jit(solution)/shard_map/sub | solution.py:47
  25.5 2.7 %fusion.14 = bf16[8,256,512]{1,2,0:T(8,128)(2,1)S(1)} fusion(f32[8,256,512]{1,2,0:T(8,128)} %get-tuple-element.133, f32[8,256]{1,0:T(8,128)S(1)} %get-tuple-element.132), kind=kLoop, calls=%fused_computation.30 | loop fusion | flops 2097152 | bytes 6299648 | tf_op jit(solution)/shard_map/convert_element_type | solution.py:49
  28.2 2.2 %fusion.46 = f32[256,8]{0,1:T(8,128)S(1)} fusion(bf16[8,256,512]{1,2,0:T(8,128)(2,1)S(1)} %fusion.14, bf16[768,8,256]{2,0,1:T(8,128)(2,1)} %copy-done.9, bf16[512,8,128]{2,0,1:T(8,128)(2,1)S(1)} %copy-done.14), kind=kOutput, calls=%fused_computation.53 | convolution fusion | flops 269219840 | bytes 3678208 | tf_op jit(solution)/shard_map/hqk,khv->qhv/dot_general | solution.py:50
  30.4 2.0 %multiply_convert_fusion.1 = bf16[8,256,512]{1,2,0:T(8,128)(2,1)S(1)} fusion(f32[8,256]{1,0:T(8,128)S(1)} %bitcast.132, f32[8,256,512]{1,2,0:T(8,128)S(1)} %copy-done.6, f32[8,256]{1,0:T(8,128)S(1)} %get-tuple-element.132, bf16[768,8,256]{2,0,1:T(8,128)(2,1)} %copy-done.9, bf16[512,8,128]{2,0,1:T(8,128)(2,1)S(1)} %copy-done.14), kind=kOutput, calls=%fused_computation.11 | convolution fusion | flops 273678336 | bytes 7880704 | tf_op jit(solution)/shard_map/qhv,khv->hqk/dot_general | solution.py:52
  32.5 0.7 convolution_bitcast_fusion.6
  33.2 3.3 %convolution_bitcast_fusion.1 = f32[512,8,128]{0,2,1:T(8,128)} fusion(bf16[8,256,512]{1,2,0:T(8,128)(2,1)S(1)} %multiply_convert_fusion.1, bf16[512,8,192]{0,2,1:T(8,128)(2,1)} %param.25), kind=kOutput, calls=%fused_computation.32 | convolution fusion | flops 268435456 | bytes 4718592 | tf_op jit(solution)/shard_map/hqk,qhd->khd/dot_general | solution.py:60
  36.5 2.1 %convolution_bitcast_fusion = f32[512,8,128]{0,2,1:T(8,128)} fusion(bf16[8,256,512]{1,2,0:T(8,128)(2,1)S(1)} %fusion.14, bf16[512,8,128]{2,0,1:T(8,128)(2,1)S(1)} %copy-done.14), kind=kOutput, calls=%fused_computation.31 | convolution fusion | flops 268435456 | bytes 4718592 | tf_op jit(solution)/shard_map/hqk,qhv->khv/dot_general | solution.py:64
  38.6 0.7 and_or_fusion
  39.3 7.5 %fusion.111 = (f32[8,256]{1,0:T(8,128)S(1)}, f32[8,256,768]{1,2,0:T(8,128)}) fusion(f32[8,768,256]{2,1,0:T(8,128)} %fusion.24, pred[256,768]{0,1:T(8,128)(4,1)S(1)} %and_or_fusion, bf16[768,64,1]{1,0,2:T(8,128)(2,1)S(1)} %maximum_bitcast_fusion, bf16[512,8,32]{0,2,1:T(8,128)(2,1)S(1)} %get-tuple-element.113, bf16[512,8,32]{0,2,1:T(8,128)(2,1)S(1)} %get-tuple-element.112), kind=kOutput, calls=%fused_computation.148 | convolution fusion | flops 209715968 | bytes 13410304 | tf_op jit(solution)/shard_map/sub | solution.py:47
  46.9 3.5 %fusion.9 = bf16[8,256,768]{1,2,0:T(8,128)(2,1)S(1)} fusion(f32[8,256,768]{1,2,0:T(8,128)} %get-tuple-element.131, f32[8,256]{1,0:T(8,128)S(1)} %get-tuple-element.130), kind=kLoop, calls=%fused_computation.24 | loop fusion | flops 3145728 | bytes 9445376 | tf_op jit(solution)/shard_map/convert_element_type | solution.py:49
  50.4 1.7 %copy-done.7 = bf16[8,256,768]{1,2,0:T(8,128)(2,1)} copy-done((bf16[8,256,768]{1,2,0:T(8,128)(2,1)}, bf16[8,256,768]{1,2,0:T(8,128)(2,1)S(1)}, u32[]{:S(2)}) %copy-start.7) | copy-done | bytes 3145752
  52.0 2.7 %fusion.47 = f32[256,8]{0,1:T(8,128)S(1)} fusion(bf16[8,256,768]{1,2,0:T(8,128)(2,1)S(1)} %fusion.9, bf16[768,8,256]{2,0,1:T(8,128)(2,1)S(1)} %copy-done.10, bf16[512,8,128]{2,0,1:T(8,128)(2,1)} %copy_select_fusion), kind=kOutput, calls=%fused_computation.54 | convolution fusion | flops 403437568 | bytes 5251072 | tf_op jit(solution)/shard_map/hqk,khv->qhv/dot_general | solution.py:50
  54.8 2.9 %multiply_convert_fusion = bf16[8,256,768]{1,2,0:T(8,128)(2,1)} fusion(f32[8,256]{1,0:T(8,128)S(1)} %bitcast.133, f32[8,256,768]{1,2,0:T(8,128)S(1)} %copy-done.5, f32[8,256]{1,0:T(8,128)S(1)} %get-tuple-element.130, bf16[768,8,256]{2,0,1:T(8,128)(2,1)S(1)} %copy-done.10, bf16[512,8,128]{2,0,1:T(8,128)(2,1)S(1)} %copy-done.15), kind=kOutput, calls=%fused_computation.5 | convolution fusion | flops 410517504 | bytes 11550720 | tf_op jit(solution)/shard_map/qhv,khv->hqk/dot_general | solution.py:52
  57.7 3.1 %fusion.57 = f32[768,64]{0,1:T(8,128)S(1)} fusion(bf16[8,256,768]{1,2,0:T(8,128)(2,1)} %multiply_convert_fusion, f32[512,64]{0,1:T(8,128)S(1)} %convolution_bitcast_fusion.6, bf16[512,8,32]{0,2,1:T(8,128)(2,1)S(1)} %get-tuple-element.113, bf16[512,8,32]{0,2,1:T(8,128)(2,1)S(1)} %get-tuple-element.112), kind=kOutput, calls=%fused_computation.61 | convolution fusion | flops 201900032 | bytes 3997696 | tf_op jit(solution)/shard_map/hqk,qhr->kr/dot_general | solution.py:63
  60.8 0.4 copy-done.12
  61.2 3.5 %fusion.8 = bf16[768,8,128]{0,2,1:T(8,128)(2,1)} fusion(f32[512,8,128]{0,2,1:T(8,128)S(1)} %copy-done.12, bf16[8,256,768]{1,2,0:T(8,128)(2,1)S(1)} %copy-done.1, bf16[512,8,192]{0,2,1:T(8,128)(2,1)} %param.25), kind=kOutput, calls=%fused_computation.22 | convolution fusion | flops 404226048 | bytes 7340032 | tf_op jit(solution)/shard_map/hqk,qhd->khd/dot_general | solution.py:60
  64.7 2.3 %fusion.7 = bf16[768,8,128]{0,2,1:T(8,128)(2,1)} fusion(f32[512,8,128]{0,2,1:T(8,128)S(1)} %copy-done.11, bf16[8,256,768]{1,2,0:T(8,128)(2,1)S(1)} %copy-done.8, bf16[512,8,128]{2,0,1:T(8,128)(2,1)S(1)} %copy-done.16), kind=kOutput, calls=%fused_computation.20 | convolution fusion | flops 404226048 | bytes 7340032 | tf_op jit(solution)/shard_map/hqk,qhv->khv/dot_general | solution.py:64
  67.2 2.2 %fusion.51 = f32[256,512]{1,0:T(8,128)S(1)} fusion(bf16[512,8,256]{2,1,0:T(8,128)(2,1)S(1)} %copy-done, bf16[768,8,128]{0,2,1:T(8,128)(2,1)} %fusion.8, bf16[768,8,128]{0,2,1:T(8,128)(2,1)} %fusion.7), kind=kOutput, calls=%fused_computation.56 | convolution fusion | flops 538968064 | bytes 5767168 | tf_op jit(solution)/shard_map/khd,lhd->kl/dot_general | solution.py:169
  69.5 0.8 fusion.77
  70.2 1.4 collective-permute-start.1
  71.9 2.1 %fusion.38 = bf16[512,512]{1,0:T(8,128)(2,1)} fusion(bf16[512,8,256]{2,1,0:T(8,128)(2,1)S(1)} %copy-done, bf16[768,8,128]{0,2,1:T(8,128)(2,1)S(1)} %copy-done.17, bf16[768,8,128]{0,2,1:T(8,128)(2,1)S(1)} %copy-done.18), kind=kOutput, calls=%fused_computation.50 | convolution fusion | flops 1078198272 | bytes 5767168 | tf_op jit(solution)/shard_map/khd,lhd->kl/dot_general | solution.py:154
  74.0 0.7 copy.265
  74.8 0.8 copy.264
  75.6 1.3 pad_maximum_fusion.4
  76.9 0.8 fusion.76
  77.6 1.7 %fusion.79 = f32[128,576]{1,0:T(8,128)} fusion(f32[128,576]{1,0:T(8,128)} %collective-permute-done.1, s32[]{:T(128)S(6)} %select_n.50, f32[256,512]{1,0:T(8,128)S(1)} %fusion.51, f32[256,64]{1,0:T(8,128)} %copy-done.25), kind=kLoop, calls=%fused_computation.102 | loop fusion | flops 147456 | bytes 1179652 | tf_op jit(solution)/shard_map/add | solution.py:176
  79.4 1.9 %reshape.413 = f32[64,2,576]{2,1,0:T(2,128)} reshape(f32[128,576]{1,0:T(8,128)} %fusion.79) | data formatting | bytes 589824 | tf_op jit(solution)/shard_map/reshape | solution.py:180
  81.3 11.5 %all-to-all-start.2 = ((f32[64,2,576]{2,1,0:T(2,128)}), f32[64,2,576]{2,1,0:T(2,128)S(1)}, u32[]{:S(2)}, u32[]{:S(2)}) async-start(f32[64,2,576]{2,1,0:T(2,128)} %reshape.413), calls=%async_computation.2 | async-start | bytes 655360 | tf_op jit(solution)/shard_map/all_to_all | solution.py:179
  92.8 1.8 %fusion.65 = bf16[8,32,576]{2,1,0:T(8,128)(2,1)} fusion(bf16[8,32,576]{2,1,0:T(8,128)(2,1)} %collective-permute-done, pred[]{:T(512)S(6)} %eq.2, bf16[8,2,32,576]{3,2,1,0:T(8,128)(2,1)S(1)} %pad_maximum_fusion.4), kind=kLoop, calls=%fused_computation.80 | loop fusion | flops 737280 | bytes 1179649 | tf_op jit(solution)/shard_map/convert_element_type | solution.py:166
  94.6 8.5 %all-to-all-done.2 = f32[64,2,576]{2,1,0:T(2,128)S(1)} async-done(((f32[64,2,576]{2,1,0:T(2,128)}), f32[64,2,576]{2,1,0:T(2,128)S(1)}, u32[]{:S(2)}, u32[]{:S(2)}) %all-to-all-start.2) | async-done | bytes 294944 | tf_op jit(solution)/shard_map/all_to_all | solution.py:179
  103.1 3.4 %all-to-all-start = ((bf16[8,32,576]{2,1,0:T(8,128)(2,1)}), bf16[8,32,576]{2,1,0:T(8,128)(2,1)S(1)}, u32[]{:S(2)}, u32[]{:S(2)}) async-start(bf16[8,32,576]{2,1,0:T(8,128)(2,1)} %fusion.65), calls=%async_computation | async-start | bytes 655360 | tf_op jit(solution)/shard_map/all_to_all | solution.py:167
  106.5 4.0 %fusion.13 = bf16[512,8,256]{2,0,1:T(8,128)(2,1)S(1)} fusion(bf16[768,8,128]{0,2,1:T(8,128)(2,1)} %fusion.7, bf16[768,8,128]{0,2,1:T(8,128)(2,1)} %fusion.8, bf16[768,576]{1,0:T(8,128)(2,1)} %copy-done.29), kind=kOutput, calls=%fused_computation.29 | convolution fusion | flops 1617952768 | bytes 6029312 | tf_op jit(solution)/shard_map/kl,khd->lhd/dot_general | solution.py:138
  110.5 1.6 copy.221
  112.2 1.1 all-to-all-done
  113.3 0.8 broadcast_in_dim.38
  114.2 5.5 %all-to-all-start.3 = ((f32[64,2,576]{2,1,0:T(2,128)}), f32[64,2,576]{2,1,0:T(2,128)S(1)}, u32[]{:S(2)}, u32[]{:S(2)}) async-start(f32[64,2,576]{2,1,0:T(2,128)} %broadcast_in_dim.38), calls=%async_computation.3 | async-start | bytes 655360 | tf_op jit(solution)/shard_map/all_to_all | solution.py:184
  119.7 2.6 %convolution_bitcast_fusion.3 = f32[256,8,64]{0,2,1:T(8,128)S(1)} fusion(bf16[768,64,1]{1,0,2:T(8,128)(2,1)S(1)} %maximum_bitcast_fusion, bf16[8,256,768]{1,2,0:T(8,128)(2,1)} %multiply_convert_fusion), kind=kOutput, calls=%fused_computation.57 | convolution fusion | flops 201326592 | bytes 3768320 | tf_op jit(solution)/shard_map/hqk,kr->qhr/dot_general | solution.py:59
  122.3 7.3 %all-to-all-done.3 = f32[64,2,576]{2,1,0:T(2,128)S(1)} async-done(((f32[64,2,576]{2,1,0:T(2,128)}), f32[64,2,576]{2,1,0:T(2,128)S(1)}, u32[]{:S(2)}, u32[]{:S(2)}) %all-to-all-start.3) | async-done | bytes 294944 | tf_op jit(solution)/shard_map/all_to_all | solution.py:184
  129.6 4.4 %all-to-all-start.1 = ((bf16[8,64,8,256]{3,1,2,0:T(8,128)(2,1)}), bf16[8,64,8,256]{3,1,2,0:T(8,128)(2,1)}, u32[]{:S(2)}, u32[]{:S(2)}) async-start(bf16[8,64,8,256]{3,1,2,0:T(8,128)(2,1)} %copy.221), calls=%async_computation.1 | async-start | bytes 4194304 | tf_op jit(solution)/shard_map/all_to_all | solution.py:148
  133.9 0.8 add_convert_fusion.1
  134.7 2.2 %convolution_bitcast_fusion.4 = f32[256,8,64]{0,2,1:T(8,128)S(1)} fusion(bf16[512,64,1]{1,0,2:T(8,128)(2,1)S(1)} %copy-done.27, bf16[8,256,512]{1,2,0:T(8,128)(2,1)} %copy-done.3), kind=kOutput, calls=%fused_computation.58 | convolution fusion | flops 134217728 | bytes 2686976 | tf_op jit(solution)/shard_map/hqk,kr->qhr/dot_general | solution.py:59
  137.0 0.8 add_convert_fusion.2
  137.7 1.8 %fusion.50 = bf16[256,8,128]{0,2,1:T(8,128)(2,1)S(1)} fusion(bf16[8,256,512]{1,2,0:T(8,128)(2,1)S(1)} %copy-done.4, bf16[768,8,256]{2,0,1:T(8,128)(2,1)} %copy-done.9), kind=kOutput, calls=%fused_computation.55 | convolution fusion | flops 268697600 | bytes 3670016 | tf_op jit(solution)/shard_map/hqk,khd->qhd/dot_general | solution.py:56
  139.5 2.2 %fusion.54 = bf16[256,8,128]{0,2,1:T(8,128)(2,1)S(1)} fusion(bf16[8,256,768]{1,2,0:T(8,128)(2,1)S(1)} %copy-done.2, bf16[768,8,256]{2,0,1:T(8,128)(2,1)} %copy-done.9), kind=kOutput, calls=%fused_computation.59 | convolution fusion | flops 402915328 | bytes 5242880 | tf_op jit(solution)/shard_map/hqk,khd->qhd/dot_general | solution.py:56
  141.7 2.0 %reshape.414 = f32[128,576]{1,0:T(8,128)} reshape(f32[64,2,576]{2,1,0:T(2,128)} %copy-done.23) | data formatting | bytes 589824 | tf_op jit(solution)/shard_map/reshape | solution.py:184
  143.7 3.4 %collective-permute-start.2 = (f32[128,576]{1,0:T(8,128)}, f32[128,576]{1,0:T(8,128)S(1)}, u32[]{:S(2)}, u32[]{:S(2)}) collective-permute-start(f32[128,576]{1,0:T(8,128)} %reshape.414), channel_id=1, source_target_pairs={{0,1},{1,0},{2,3},{3,2},{4,5},{5,4},{6,7},{7,6},{8,9},{9,8},{10,11... | collective-permute-start | bytes 884744 | tf_op jit(solution)/shard_map/ppermute | solution.py:69
  147.1 2.5 %maximum_maximum_fusion = bf16[512,8,192]{0,2,1:T(8,128)(2,1)} fusion(bf16[256,8,32]{0,2,1:T(8,128)(2,1)} %get-tuple-element.117, bf16[256,8,32]{0,2,1:T(8,128)(2,1)} %get-tuple-element.116, bf16[256,8,128]{0,2,1:T(8,128)(2,1)S(1)} %fusion.54, bf16[256,8,32]{0,2,1:T(8,128)(2,1)} %get-tuple-element.115, bf16[256,8,32]{0,2,1:T(8,128)(2,1)} %get-tuple-element.114, ...), kind=kLoop, calls=%fused_computation.37 | loop fusion | flops 9437184 | bytes 3145728 | tf_op jit(solution)/shard_map/concatenate | solution.py:142
  149.6 0.7 convert_reduce_fusion.1
  150.3 1.0 copy.227
  151.4 11.2 %all-to-all-done.1 = bf16[8,64,8,256]{3,1,2,0:T(8,128)(2,1)} async-done(((bf16[8,64,8,256]{3,1,2,0:T(8,128)(2,1)}), bf16[8,64,8,256]{3,1,2,0:T(8,128)(2,1)}, u32[]{:S(2)}, u32[]{:S(2)}) %all-to-all-start.1) | async-done | bytes 2097184 | tf_op jit(solution)/shard_map/all_to_all | solution.py:148
  162.5 2.0 %convert_reduce_fusion = f32[64,8,256]{2,0,1:T(8,128)S(1)} fusion(bf16[8,64,8,256]{3,1,2,0:T(8,128)(2,1)} %all-to-all-done.1), kind=kLoop, calls=%fused_computation.10 | loop fusion | flops 1966080 | bytes 2621440 | tf_op jit(solution)/shard_map/reduce_sum | solution.py:151
  164.6 1.1 copy.226
  (85 shorter events, 1.8 us)
Async XLA Ops:
  0.6 8.5 %copy-start = (bf16[512,8,256]{2,1,0:T(8,128)(2,1)S(1)}, bf16[512,8,256]{2,1,0:T(8,128)(2,1)}, u32[]{:S(2)}) copy-start(bf16[512,8,256]{2,1,0:T(8,128)(2,1)} %param.28) | copy-start | bytes 6291460
  5.7 13.6 %copy-start.30 = (f32[512,32]{0,1:T(8,128)}, f32[512,32]{0,1:T(8,128)S(1)}, u32[]{:S(2)}) copy-start(f32[512,32]{0,1:T(8,128)S(1)} %get-tuple-element.127) | copy-start | bytes 196612
  7.2 1.8 %copy-start.13 = (bf16[512,8,192]{0,2,1:T(8,128)(2,1)S(1)}, bf16[512,8,192]{0,2,1:T(8,128)(2,1)}, u32[]{:S(2)}) copy-start(bf16[512,8,192]{0,2,1:T(8,128)(2,1)} %param.25) | copy-start | bytes 4718596
  7.5 3.5 %copy-start.29 = (bf16[768,576]{1,0:T(8,128)(2,1)}, bf16[768,576]{1,0:T(8,128)(2,1)S(1)}, u32[]{:S(2)}) copy-start(bf16[768,576]{1,0:T(8,128)(2,1)S(1)} %maximum_maximum_fusion.1) | copy-start | bytes 2654212
  11.0 3.6 %copy-start.9 = (bf16[768,8,256]{2,0,1:T(8,128)(2,1)}, bf16[768,8,256]{2,0,1:T(8,128)(2,1)S(1)}, u32[]{:S(2)}) copy-start(bf16[768,8,256]{2,0,1:T(8,128)(2,1)S(1)} %convolution_convert_fusion) | copy-start | bytes 9437188
  14.6 3.5 %copy-start.28 = (bf16[512,8,128]{2,1,0:T(8,128)(2,1)S(1)}, bf16[512,8,128]{2,1,0:T(8,128)(2,1)}, u32[]{:S(2)}) copy-start(bf16[512,8,128]{2,1,0:T(8,128)(2,1)} %param.29) | copy-start | bytes 3145732
  17.4 2.3 %copy-start.26 = (bf16[512,64,1]{1,0,2:T(8,128)(2,1)S(1)}, bf16[512,64,1]{1,0,2:T(8,128)(2,1)}, u32[]{:S(2)}) copy-start(bf16[512,64,1]{1,0,2:T(8,128)(2,1)} %maximum_bitcast_fusion.1) | copy-start | bytes 196612
  25.5 2.7 %copy-start.14 = (bf16[512,8,128]{2,0,1:T(8,128)(2,1)S(1)}, bf16[512,8,128]{2,0,1:T(8,128)(2,1)}, u32[]{:S(2)}) copy-start(bf16[512,8,128]{2,0,1:T(8,128)(2,1)} %copy_select_fusion) | copy-start | bytes 3145732
  25.5 4.9 %copy-start.6 = (f32[8,256,512]{1,2,0:T(8,128)S(1)}, f32[8,256,512]{1,2,0:T(8,128)}, u32[]{:S(2)}) copy-start(f32[8,256,512]{1,2,0:T(8,128)} %get-tuple-element.133) | copy-start | bytes 12582916
  32.4 4.0 %copy-start.3 = (bf16[8,256,512]{1,2,0:T(8,128)(2,1)}, bf16[8,256,512]{1,2,0:T(8,128)(2,1)S(1)}, u32[]{:S(2)}) copy-start(bf16[8,256,512]{1,2,0:T(8,128)(2,1)S(1)} %multiply_convert_fusion.1) | copy-start | bytes 6291460
  46.9 5.2 %copy-start.10 = (bf16[768,8,256]{2,0,1:T(8,128)(2,1)S(1)}, bf16[768,8,256]{2,0,1:T(8,128)(2,1)}, u32[]{:S(2)}) copy-start(bf16[768,8,256]{2,0,1:T(8,128)(2,1)} %copy-done.9) | copy-start | bytes 9437188
  46.9 7.9 %copy-start.5 = (f32[8,256,768]{1,2,0:T(8,128)S(1)}, f32[8,256,768]{1,2,0:T(8,128)}, u32[]{:S(2)}) copy-start(f32[8,256,768]{1,2,0:T(8,128)} %get-tuple-element.131) | copy-start | bytes 18874372
  50.4 1.7 %copy-start.7 = (bf16[8,256,768]{1,2,0:T(8,128)(2,1)}, bf16[8,256,768]{1,2,0:T(8,128)(2,1)S(1)}, u32[]{:S(2)}) copy-start(bf16[8,256,768]{1,2,0:T(8,128)(2,1)S(1)} %fusion.9) | copy-start | bytes 9437188
  52.0 2.8 %copy-start.15 = (bf16[512,8,128]{2,0,1:T(8,128)(2,1)S(1)}, bf16[512,8,128]{2,0,1:T(8,128)(2,1)}, u32[]{:S(2)}) copy-start(bf16[512,8,128]{2,0,1:T(8,128)(2,1)} %copy_select_fusion) | copy-start | bytes 3145732
  57.7 3.1 %copy-start.1 = (bf16[8,256,768]{1,2,0:T(8,128)(2,1)S(1)}, bf16[8,256,768]{1,2,0:T(8,128)(2,1)}, u32[]{:S(2)}) copy-start(bf16[8,256,768]{1,2,0:T(8,128)(2,1)} %multiply_convert_fusion) | copy-start | bytes 9437188
  57.7 3.5 %copy-start.12 = (f32[512,8,128]{0,2,1:T(8,128)S(1)}, f32[512,8,128]{0,2,1:T(8,128)}, u32[]{:S(2)}) copy-start(f32[512,8,128]{0,2,1:T(8,128)} %convolution_bitcast_fusion.1) | copy-start | bytes 6291460
  61.2 5.9 %copy-start.19 = (f32[768,64]{0,1:T(8,128)}, f32[768,64]{0,1:T(8,128)S(1)}, u32[]{:S(2)}) copy-start(f32[768,64]{0,1:T(8,128)S(1)} %fusion.57) | copy-start | bytes 589828
  61.2 3.5 %copy-start.8 = (bf16[8,256,768]{1,2,0:T(8,128)(2,1)S(1)}, bf16[8,256,768]{1,2,0:T(8,128)(2,1)}, u32[]{:S(2)}) copy-start(bf16[8,256,768]{1,2,0:T(8,128)(2,1)} %copy-done.7) | copy-start | bytes 9437188
  61.2 3.5 %copy-start.11 = (f32[512,8,128]{0,2,1:T(8,128)S(1)}, f32[512,8,128]{0,2,1:T(8,128)}, u32[]{:S(2)}) copy-start(f32[512,8,128]{0,2,1:T(8,128)} %convolution_bitcast_fusion) | copy-start | bytes 6291460
  61.2 3.5 %copy-start.16 = (bf16[512,8,128]{2,0,1:T(8,128)(2,1)S(1)}, bf16[512,8,128]{2,0,1:T(8,128)(2,1)}, u32[]{:S(2)}) copy-start(bf16[512,8,128]{2,0,1:T(8,128)(2,1)} %copy_select_fusion) | copy-start | bytes 3145732
  67.2 2.3 %copy-start.25 = (f32[256,64]{1,0:T(8,128)}, f32[256,64]{1,0:T(8,128)S(1)}, u32[]{:S(2)}) copy-start(f32[256,64]{1,0:T(8,128)S(1)} %copy.225) | copy-start | bytes 196612
  67.2 4.4 %copy-start.20 = (f32[768,64]{0,1:T(8,128)S(1)}, f32[768,64]{0,1:T(8,128)}, u32[]{:S(2)}) copy-start(f32[768,64]{0,1:T(8,128)} %copy-done.19) | copy-start | bytes 589828
  67.2 4.7 %copy-start.17 = (bf16[768,8,128]{0,2,1:T(8,128)(2,1)S(1)}, bf16[768,8,128]{0,2,1:T(8,128)(2,1)}, u32[]{:S(2)}) copy-start(bf16[768,8,128]{0,2,1:T(8,128)(2,1)} %fusion.8) | copy-start | bytes 4718596
  67.2 4.7 %copy-start.18 = (bf16[768,8,128]{0,2,1:T(8,128)(2,1)S(1)}, bf16[768,8,128]{0,2,1:T(8,128)(2,1)}, u32[]{:S(2)}) copy-start(bf16[768,8,128]{0,2,1:T(8,128)(2,1)} %fusion.7) | copy-start | bytes 4718596
  70.2 7.4 %collective-permute-start.1 = (f32[128,576]{1,0:T(8,128)}, f32[128,576]{1,0:T(8,128)}, u32[]{:S(2)}, u32[]{:S(2)}) collective-permute-start(f32[128,576]{1,0:T(8,128)} %fusion.77), channel_id=1, source_target_pairs={{0,1},{1,0},{2,3},{3,2},{4,5},{5,4},{6,7},{7,6},{8,9},{9,8},{10,11... | collective-permute-start | bytes 884744 | tf_op jit(solution)/shard_map/ppermute | solution.py:69
  77.6 15.1 %collective-permute-start = (bf16[8,32,576]{2,1,0:T(8,128)(2,1)}, bf16[8,32,576]{2,1,0:T(8,128)(2,1)}, u32[]{:S(2)}, u32[]{:S(2)}) collective-permute-start(bf16[8,32,576]{2,1,0:T(8,128)(2,1)} %fusion.76), channel_id=1, source_target_pairs={{0,1},{1,0},{2,3},{3,2},{4,5},{5,4},{6,7},{7,6},{8,9},{9,8},{10,11... | collective-permute-start | bytes 884744 | tf_op jit(solution)/shard_map/ppermute | solution.py:69
  81.3 21.8 %all-to-all-start.2 = ((f32[64,2,576]{2,1,0:T(2,128)}), f32[64,2,576]{2,1,0:T(2,128)S(1)}, u32[]{:S(2)}, u32[]{:S(2)}) async-start(f32[64,2,576]{2,1,0:T(2,128)} %reshape.413), calls=%async_computation.2 | async-start | bytes 655360 | tf_op jit(solution)/shard_map/all_to_all | solution.py:179
  103.1 10.2 %all-to-all-start = ((bf16[8,32,576]{2,1,0:T(8,128)(2,1)}), bf16[8,32,576]{2,1,0:T(8,128)(2,1)S(1)}, u32[]{:S(2)}, u32[]{:S(2)}) async-start(bf16[8,32,576]{2,1,0:T(8,128)(2,1)} %fusion.65), calls=%async_computation | async-start | bytes 655360 | tf_op jit(solution)/shard_map/all_to_all | solution.py:167
  110.5 1.6 copy-start.31
  113.3 0.8 copy-start.21
  114.2 15.4 %all-to-all-start.3 = ((f32[64,2,576]{2,1,0:T(2,128)}), f32[64,2,576]{2,1,0:T(2,128)S(1)}, u32[]{:S(2)}, u32[]{:S(2)}) async-start(f32[64,2,576]{2,1,0:T(2,128)} %broadcast_in_dim.38), calls=%async_computation.3 | async-start | bytes 655360 | tf_op jit(solution)/shard_map/all_to_all | solution.py:184
  122.3 12.4 %copy-start.27 = (bf16[512,64,1]{1,0,2:T(8,128)(2,1)S(1)}, bf16[512,64,1]{1,0,2:T(8,128)(2,1)}, u32[]{:S(2)}) copy-start(bf16[512,64,1]{1,0,2:T(8,128)(2,1)} %maximum_bitcast_fusion.1) | copy-start | bytes 196612
  129.6 7.4 %copy-start.23 = (f32[64,2,576]{2,1,0:T(2,128)}, f32[64,2,576]{2,1,0:T(2,128)S(1)}, u32[]{:S(2)}) copy-start(f32[64,2,576]{2,1,0:T(2,128)S(1)} %all-to-all-done.3) | copy-start | bytes 884740
  129.6 33.0 %all-to-all-start.1 = ((bf16[8,64,8,256]{3,1,2,0:T(8,128)(2,1)}), bf16[8,64,8,256]{3,1,2,0:T(8,128)(2,1)}, u32[]{:S(2)}, u32[]{:S(2)}) async-start(bf16[8,64,8,256]{3,1,2,0:T(8,128)(2,1)} %copy.221), calls=%async_computation.1 | async-start | bytes 4194304 | tf_op jit(solution)/shard_map/all_to_all | solution.py:148
  133.9 3.8 %copy-start.4 = (bf16[8,256,512]{1,2,0:T(8,128)(2,1)S(1)}, bf16[8,256,512]{1,2,0:T(8,128)(2,1)}, u32[]{:S(2)}) copy-start(bf16[8,256,512]{1,2,0:T(8,128)(2,1)} %copy-done.3) | copy-start | bytes 6291460
  134.7 4.8 %copy-start.2 = (bf16[8,256,768]{1,2,0:T(8,128)(2,1)S(1)}, bf16[8,256,768]{1,2,0:T(8,128)(2,1)}, u32[]{:S(2)}) copy-start(bf16[8,256,768]{1,2,0:T(8,128)(2,1)} %multiply_convert_fusion) | copy-start | bytes 9437188
  141.7 7.9 %copy-start.22 = (bf16[8,32,576]{2,1,0:T(8,128)(2,1)S(1)}, bf16[8,32,576]{2,1,0:T(8,128)(2,1)}, u32[]{:S(2)}) copy-start(bf16[8,32,576]{2,1,0:T(8,128)(2,1)} %copy-done.21) | copy-start | bytes 884740
  143.7 6.6 %copy-start.24 = (f32[128,576]{1,0:T(8,128)S(1)}, f32[128,576]{1,0:T(8,128)}, u32[]{:S(2)}) copy-start(f32[128,576]{1,0:T(8,128)} %reshape.414) | copy-start | bytes 884740
  143.7 6.6 %collective-permute-start.2 = (f32[128,576]{1,0:T(8,128)}, f32[128,576]{1,0:T(8,128)S(1)}, u32[]{:S(2)}, u32[]{:S(2)}) collective-permute-start(f32[128,576]{1,0:T(8,128)} %reshape.414), channel_id=1, source_target_pairs={{0,1},{1,0},{2,3},{3,2},{4,5},{5,4},{6,7},{7,6},{8,9},{9,8},{10,11... | collective-permute-start | bytes 884744 | tf_op jit(solution)/shard_map/ppermute | solution.py:69

commit v3 on v2

--- a/solution.py
+++ b/solution.py
@@ -67,6 +67,12 @@
 
 def swap_pair(values):
     return lax.ppermute(values, "core", [(0, 1), (1, 0)])
+
+
+def gather_copies(values, axis, size):
+    copies = jnp.broadcast_to(values[None], (size,) + values.shape)
+    gathered = lax.all_to_all(copies, axis, 0, 0, tiled=False)
+    return gathered.reshape((size * values.shape[0],) + values.shape[1:])
 
 
 def on_device(queries, latent, prefix, kv_up, out_grad, lengths, positions):
@@ -174,16 +180,24 @@
     prefix_mine = lax.dynamic_slice_in_dim(prefix_part, core * half_rows, half_rows)
     prefix_other = lax.dynamic_slice_in_dim(prefix_part, (1 - core) * half_rows, half_rows)
     prefix_half = prefix_mine + swap_pair(prefix_other)
-    outer = ("dp", "hr")
-    outer_size = dp_size * row_size
-    prefix_pieces = lax.all_to_all(
-        prefix_half.reshape((outer_size, -1) + prefix_half.shape[1:]), outer, 0, 0, tiled=False
-    )
-    prefix_own = jnp.sum(prefix_pieces, axis=0)
-    prefix_copies = jnp.broadcast_to(prefix_own[None], (outer_size,) + prefix_own.shape)
-    prefix_gathered = lax.all_to_all(prefix_copies, outer, 0, 0, tiled=False).reshape(
-        prefix_half.shape
-    )
+    prefix_rows_part = jnp.sum(
+        lax.all_to_all(
+            prefix_half.reshape((row_size, -1) + prefix_half.shape[1:]), "hr", 0, 0, tiled=False
+        ),
+        axis=0,
+    )
+    prefix_own = jnp.sum(
+        lax.all_to_all(
+            prefix_rows_part.reshape((dp_size, -1) + prefix_rows_part.shape[1:]),
+            "dp",
+            0,
+            0,
+            tiled=False,
+        ),
+        axis=0,
+    )
+    prefix_rows_full = gather_copies(prefix_own, "dp", dp_size)
+    prefix_gathered = gather_copies(prefix_rows_full, "hr", row_size)
     prefix_partner = swap_pair(prefix_gathered)
     prefix_grad = jnp.where(
         core == 0,

time: 167 us -> 174 us (1.042)
  blocking collectives: 0 us -> 26.7 us
  waiting for transfers between devices: 28 us -> 20.5 us
  starting transfers between devices: 29.6 us -> 22.4 us
  other arithmetic: 25.3 us -> 21.9 us
  local copies, waits for them, and re-layouts: 17.5 us -> 14.8 us
    all_to_all x0 -> x2, blocking collectives: none -> 26.7 us  [the longest x1 13.6 us: on_device(): lax.all_to_all(prefix_rows_part.reshape((dp_size, -1) + prefix_rows_part....]
    all_to_all x2, starting transfers between devices: 17 us -> 7.37 us  [gather_copies(): gathered = lax.all_to_all(copies, axis, 0, 0, tiled=False)]
    all_to_all x2, waiting for transfers between devices: 15.8 us -> 6.34 us  [gather_copies(): gathered = lax.all_to_all(copies, axis, 0, 0, tiled=False)]
    reshape x2 -> x1, local copies, waits for them, and re-layouts: 3.89 us -> 0.03 us  [on_device(): prefix_rows_part.reshape((dp_size, -1) + prefix_rows_part.shape[1:])]
    ppermute x3, starting transfers between devices: 4.79 us -> 7.02 us  [swap_pair(): return lax.ppermute(values, 'core', [(0, 1), (1, 0)])]
    all_to_all x1, waiting for transfers between devices: 11.2 us -> 13.3 us  [on_device(): lax.all_to_all(up_part.astype(jnp.bfloat16).reshape((dp_size, -1) + up_pa...]
    unnamed x68 -> x66, local copies, waits for them, and re-layouts: 7.5 us -> 7.49 us
  transfers between devices with their start and end apart: 7 -> 7, of which waited for: 4 -> 4; matrix products, arithmetic and copies ran while one was open for 20% -> 17% of each run, Pallas kernels for 0% -> 0%
where the time goes in v3:
time: 174 us; the launch traced here: 173 us
  matrix products  64.9 us (37%)
  blocking collectives  26.7 us (15%)
  starting transfers between devices  22.4 us (13%)
  other arithmetic  21.9 us (13%)
  waiting for transfers between devices  20.5 us (12%)
  local copies, waits for them, and re-layouts  14.8 us (9%)
  between operations  1.86 us (1%)
    all_to_all x1, blocking collectives, on_device(): lax.all_to_all(prefix_rows_part.reshape((dp_size, -1) + prefix_rows_part....  13.6 us
    all_to_all x1, waiting for transfers between devices, on_device(): lax.all_to_all(up_part.astype(jnp.bfloat16).reshape((dp_size, -1) + up_pa...  13.3 us
    sub x2, matrix products, block_gradients(): exponent = jnp.exp(scores - highest)  13.3 us
    all_to_all x1, blocking collectives, on_device(): lax.all_to_all(prefix_half.reshape((row_size, -1) + prefix_half.shape[1:]...  13.1 us
    unnamed x66, local copies, waits for them, and re-layouts  7.49 us
    all_to_all x2, starting transfers between devices, gather_copies(): gathered = lax.all_to_all(copies, axis, 0, 0, tiled=False)  7.37 us
    ppermute x3, starting transfers between devices, swap_pair(): return lax.ppermute(values, 'core', [(0, 1), (1, 0)])  7.02 us
    dot_general x2, matrix products, block_gradients(): jnp.einsum('hqk,qhd->khd', score_grad, query_nope, preferred_element_type...  6.77 us
  transfers between devices with their start and end apart: 7, of which 4 were waited for; matrix products, arithmetic and copies ran while one was open for 17% of the time, Pallas kernels for 0%

profile of v3, /device:TPU:1, one launch (start us, length us, event | category | flops | bytes accessed | tf_op | source)
XLA Modules:
  0.0 173.0 jit_solution(6585585851846131597)
XLA Ops:
  0.7 1.0 slice_convert_fusion.1
  1.7 1.9 %slice.226 = bf16[512,512]{0,1:T(8,128)(2,1)} slice(bf16[512,576]{0,1:T(8,128)(2,1)} %param.26), slice={[0:512], [0:512]} | slice | bytes 1048576 | tf_op jit(solution)/shard_map/slice | solution.py:95
  3.5 1.2 copy.293
  4.7 0.7 convert_element_type.66
  5.4 0.3 multiply_cosine_fusion
  6.0 1.3 copy.385
  7.5 0.7 maximum_bitcast_fusion.1
  8.3 0.8 copy-done.13
  9.2 1.8 %convolution_convert_fusion = bf16[768,8,256]{2,0,1:T(8,128)(2,1)S(1)} fusion(bf16[512,8,256]{2,1,0:T(8,128)(2,1)S(1)} %copy-done, bf16[768,576]{1,0:T(8,128)(2,1)S(1)} %maximum_maximum_fusion.1), kind=kOutput, calls=%fused_computation.25 | convolution fusion | flops 1612185600 | bytes 6029312 | tf_op jit(solution)/shard_map/kl,lhd->khd/dot_general | solution.py:104
  11.0 3.6 %fusion.24 = f32[8,768,256]{2,1,0:T(8,128)} fusion(bf16[768,8,256]{2,0,1:T(8,128)(2,1)S(1)} %convolution_convert_fusion, bf16[512,8,192]{0,2,1:T(8,128)(2,1)S(1)} %copy-done.13), kind=kOutput, calls=%fused_computation.43 | convolution fusion | flops 402653184 | bytes 8388608 | tf_op jit(solution)/shard_map/qhd,khd->hqk/dot_general | solution.py:37
  14.6 2.7 %fusion.63 = f32[8,512,256]{2,1,0:T(8,128)} fusion(bf16[768,8,256]{2,0,1:T(8,128)(2,1)S(1)} %convolution_convert_fusion, bf16[512,8,192]{0,2,1:T(8,128)(2,1)S(1)} %copy-done.13), kind=kOutput, calls=%fused_computation.69 | convolution fusion | flops 268435456 | bytes 5767168 | tf_op jit(solution)/shard_map/qhd,khd->hqk/dot_general | solution.py:37
  18.1 1.2 copy_select_fusion
  19.8 5.7 %fusion.112 = (f32[8,256]{1,0:T(8,128)S(1)}, f32[8,256,512]{1,2,0:T(8,128)}) fusion(f32[8,512,256]{2,1,0:T(8,128)} %fusion.63, bf16[512,64,1]{1,0,2:T(8,128)(2,1)S(1)} %copy-done.23, pred[256,512]{0,1:T(8,128)(4,1)S(1)} %fusion.67, bf16[512,8,32]{0,2,1:T(8,128)(2,1)S(1)} %get-tuple-element.120, bf16[512,8,32]{0,2,1:T(8,128)(2,1)S(1)} %get-tuple-element.121), kind=kOutput, calls=%fused_computation.149 | convolution fusion | flops 139985408 | bytes 9117696 | tf_op jit(solution)/shard_map/sub | solution.py:47
  25.5 2.7 %fusion.14 = bf16[8,256,512]{1,2,0:T(8,128)(2,1)S(1)} fusion(f32[8,256,512]{1,2,0:T(8,128)} %get-tuple-element.141, f32[8,256]{1,0:T(8,128)S(1)} %get-tuple-element.140), kind=kLoop, calls=%fused_computation.30 | loop fusion | flops 2097152 | bytes 6299648 | tf_op jit(solution)/shard_map/convert_element_type | solution.py:49
  28.2 2.2 %fusion.46 = f32[256,8]{0,1:T(8,128)S(1)} fusion(bf16[8,256,512]{1,2,0:T(8,128)(2,1)S(1)} %fusion.14, bf16[768,8,256]{2,0,1:T(8,128)(2,1)} %copy-done.9, bf16[512,8,128]{2,0,1:T(8,128)(2,1)S(1)} %copy-done.14), kind=kOutput, calls=%fused_computation.53 | convolution fusion | flops 269219840 | bytes 3678208 | tf_op jit(solution)/shard_map/hqk,khv->qhv/dot_general | solution.py:50
  30.4 2.0 %multiply_convert_fusion.1 = bf16[8,256,512]{1,2,0:T(8,128)(2,1)S(1)} fusion(f32[8,256]{1,0:T(8,128)S(1)} %bitcast.137, f32[8,256,512]{1,2,0:T(8,128)S(1)} %copy-done.6, f32[8,256]{1,0:T(8,128)S(1)} %get-tuple-element.140, bf16[768,8,256]{2,0,1:T(8,128)(2,1)} %copy-done.9, bf16[512,8,128]{2,0,1:T(8,128)(2,1)S(1)} %copy-done.14), kind=kOutput, calls=%fused_computation.11 | convolution fusion | flops 273678336 | bytes 7880704 | tf_op jit(solution)/shard_map/qhv,khv->hqk/dot_general | solution.py:52
  32.5 0.7 convolution_bitcast_fusion.6
  33.2 3.2 %convolution_bitcast_fusion.1 = f32[512,8,128]{0,2,1:T(8,128)} fusion(bf16[8,256,512]{1,2,0:T(8,128)(2,1)S(1)} %multiply_convert_fusion.1, bf16[512,8,192]{0,2,1:T(8,128)(2,1)} %param.25), kind=kOutput, calls=%fused_computation.32 | convolution fusion | flops 268435456 | bytes 4718592 | tf_op jit(solution)/shard_map/hqk,qhd->khd/dot_general | solution.py:60
  36.5 2.1 %convolution_bitcast_fusion = f32[512,8,128]{0,2,1:T(8,128)} fusion(bf16[8,256,512]{1,2,0:T(8,128)(2,1)S(1)} %fusion.14, bf16[512,8,128]{2,0,1:T(8,128)(2,1)S(1)} %copy-done.14), kind=kOutput, calls=%fused_computation.31 | convolution fusion | flops 268435456 | bytes 4718592 | tf_op jit(solution)/shard_map/hqk,qhv->khv/dot_general | solution.py:64
  38.6 0.7 and_or_fusion
  39.3 7.5 %fusion.111 = (f32[8,256]{1,0:T(8,128)S(1)}, f32[8,256,768]{1,2,0:T(8,128)}) fusion(f32[8,768,256]{2,1,0:T(8,128)} %fusion.24, pred[256,768]{0,1:T(8,128)(4,1)S(1)} %and_or_fusion, bf16[768,64,1]{1,0,2:T(8,128)(2,1)S(1)} %maximum_bitcast_fusion, bf16[512,8,32]{0,2,1:T(8,128)(2,1)S(1)} %get-tuple-element.121, bf16[512,8,32]{0,2,1:T(8,128)(2,1)S(1)} %get-tuple-element.120), kind=kOutput, calls=%fused_computation.148 | convolution fusion | flops 209715968 | bytes 13410304 | tf_op jit(solution)/shard_map/sub | solution.py:47
  46.9 3.5 %fusion.9 = bf16[8,256,768]{1,2,0:T(8,128)(2,1)S(1)} fusion(f32[8,256,768]{1,2,0:T(8,128)} %get-tuple-element.139, f32[8,256]{1,0:T(8,128)S(1)} %get-tuple-element.138), kind=kLoop, calls=%fused_computation.24 | loop fusion | flops 3145728 | bytes 9445376 | tf_op jit(solution)/shard_map/convert_element_type | solution.py:49
  50.4 1.7 copy-done.7
  52.0 2.8 %fusion.47 = f32[256,8]{0,1:T(8,128)S(1)} fusion(bf16[8,256,768]{1,2,0:T(8,128)(2,1)S(1)} %fusion.9, bf16[768,8,256]{2,0,1:T(8,128)(2,1)S(1)} %copy-done.10, bf16[512,8,128]{2,0,1:T(8,128)(2,1)} %copy_select_fusion), kind=kOutput, calls=%fused_computation.54 | convolution fusion | flops 403437568 | bytes 5251072 | tf_op jit(solution)/shard_map/hqk,khv->qhv/dot_general | solution.py:50
  54.8 2.9 %multiply_convert_fusion = bf16[8,256,768]{1,2,0:T(8,128)(2,1)} fusion(f32[8,256]{1,0:T(8,128)S(1)} %bitcast.138, f32[8,256,768]{1,2,0:T(8,128)S(1)} %copy-done.5, f32[8,256]{1,0:T(8,128)S(1)} %get-tuple-element.138, bf16[768,8,256]{2,0,1:T(8,128)(2,1)S(1)} %copy-done.10, bf16[512,8,128]{2,0,1:T(8,128)(2,1)S(1)} %copy-done.15), kind=kOutput, calls=%fused_computation.5 | convolution fusion | flops 410517504 | bytes 11550720 | tf_op jit(solution)/shard_map/qhv,khv->hqk/dot_general | solution.py:52
  57.7 3.1 %fusion.57 = f32[768,64]{0,1:T(8,128)S(1)} fusion(bf16[8,256,768]{1,2,0:T(8,128)(2,1)} %multiply_convert_fusion, f32[512,64]{0,1:T(8,128)S(1)} %convolution_bitcast_fusion.6, bf16[512,8,32]{0,2,1:T(8,128)(2,1)S(1)} %get-tuple-element.121, bf16[512,8,32]{0,2,1:T(8,128)(2,1)S(1)} %get-tuple-element.120), kind=kOutput, calls=%fused_computation.61 | convolution fusion | flops 201900032 | bytes 3997696 | tf_op jit(solution)/shard_map/hqk,qhr->kr/dot_general | solution.py:63
  60.8 0.4 copy-done.12
  61.2 3.5 %fusion.8 = bf16[768,8,128]{0,2,1:T(8,128)(2,1)} fusion(f32[512,8,128]{0,2,1:T(8,128)S(1)} %copy-done.12, bf16[8,256,768]{1,2,0:T(8,128)(2,1)S(1)} %copy-done.1, bf16[512,8,192]{0,2,1:T(8,128)(2,1)} %param.25), kind=kOutput, calls=%fused_computation.22 | convolution fusion | flops 404226048 | bytes 7340032 | tf_op jit(solution)/shard_map/hqk,qhd->khd/dot_general | solution.py:60
  64.7 2.3 %fusion.7 = bf16[768,8,128]{0,2,1:T(8,128)(2,1)} fusion(f32[512,8,128]{0,2,1:T(8,128)S(1)} %copy-done.11, bf16[8,256,768]{1,2,0:T(8,128)(2,1)S(1)} %copy-done.8, bf16[512,8,128]{2,0,1:T(8,128)(2,1)S(1)} %copy-done.16), kind=kOutput, calls=%fused_computation.20 | convolution fusion | flops 404226048 | bytes 7340032 | tf_op jit(solution)/shard_map/hqk,qhv->khv/dot_general | solution.py:64
  67.2 2.2 %fusion.51 = f32[256,512]{1,0:T(8,128)S(1)} fusion(bf16[512,8,256]{2,1,0:T(8,128)(2,1)S(1)} %copy-done, bf16[768,8,128]{0,2,1:T(8,128)(2,1)} %fusion.8, bf16[768,8,128]{0,2,1:T(8,128)(2,1)} %fusion.7), kind=kOutput, calls=%fused_computation.56 | convolution fusion | flops 538968064 | bytes 5767168 | tf_op jit(solution)/shard_map/khd,lhd->kl/dot_general | solution.py:175
  69.5 0.8 fusion.77
  70.2 1.4 collective-permute-start.1
  71.9 2.1 %fusion.38 = bf16[512,512]{1,0:T(8,128)(2,1)} fusion(bf16[512,8,256]{2,1,0:T(8,128)(2,1)S(1)} %copy-done, bf16[768,8,128]{0,2,1:T(8,128)(2,1)S(1)} %copy-done.18, bf16[768,8,128]{0,2,1:T(8,128)(2,1)S(1)} %copy-done.19), kind=kOutput, calls=%fused_computation.50 | convolution fusion | flops 1078198272 | bytes 5767168 | tf_op jit(solution)/shard_map/khd,lhd->kl/dot_general | solution.py:160
  74.1 0.8 copy.381
  74.8 0.8 copy.380
  75.6 1.3 pad_maximum_fusion.4
  76.9 0.8 fusion.76
  77.7 1.0 fusion.79
  78.7 13.1 %all_to_all.30 = f32[8,16,576]{2,1,0:T(8,128)S(1)} all-to-all(f32[8,16,576]{2,1,0:T(8,128)S(1)} %bitcast.131), channel_id=1, replica_groups=mesh['dp'=8,'hr'=8,'core'=2] {'hr'}, dimensions={0} | all-to-all | bytes 589824 | tf_op jit(solution)/shard_map/all_to_all | solution.py:184
  91.8 13.6 %all_to_all.31 = f32[8,2,576]{2,1,0:T(2,128)S(1)} all-to-all(f32[8,2,576]{2,1,0:T(2,128)S(1)} %reshape.418), channel_id=1, replica_groups=mesh['dp'=8,'hr'=8,'core'=2] {'dp'}, dimensions={0} | all-to-all | bytes 73728 | tf_op jit(solution)/shard_map/all_to_all | solution.py:190
  105.4 0.6 broadcast_in_dim.46
  106.1 3.3 %all-to-all-start.4 = ((f32[8,2,576]{2,1,0:T(2,128)}), f32[8,2,576]{2,1,0:T(2,128)S(1)}, u32[]{:S(2)}, u32[]{:S(2)}) async-start(f32[8,2,576]{2,1,0:T(2,128)} %broadcast_in_dim.46), calls=%async_computation.4 | async-start | bytes 81920 | tf_op jit(solution)/shard_map/all_to_all | solution.py:74
  109.4 1.8 %fusion.65 = bf16[8,32,576]{2,1,0:T(8,128)(2,1)} fusion(bf16[8,32,576]{2,1,0:T(8,128)(2,1)} %collective-permute-done, pred[]{:T(512)S(6)} %eq.2, bf16[8,2,32,576]{3,2,1,0:T(8,128)(2,1)S(1)} %pad_maximum_fusion.4), kind=kLoop, calls=%fused_computation.80 | loop fusion | flops 737280 | bytes 1179649 | tf_op jit(solution)/shard_map/convert_element_type | solution.py:172
  111.3 4.7 %all-to-all-done.4 = f32[8,2,576]{2,1,0:T(2,128)S(1)} async-done(((f32[8,2,576]{2,1,0:T(2,128)}), f32[8,2,576]{2,1,0:T(2,128)S(1)}, u32[]{:S(2)}, u32[]{:S(2)}) %all-to-all-start.4) | async-done | bytes 36896 | tf_op jit(solution)/shard_map/all_to_all | solution.py:74
  116.0 3.7 %all-to-all-start = ((bf16[8,32,576]{2,1,0:T(8,128)(2,1)}), bf16[8,32,576]{2,1,0:T(8,128)(2,1)S(1)}, u32[]{:S(2)}, u32[]{:S(2)}) async-start(bf16[8,32,576]{2,1,0:T(8,128)(2,1)} %fusion.65), calls=%async_computation | async-start | bytes 655360 | tf_op jit(solution)/shard_map/all_to_all | solution.py:173
  119.7 5.3 %fusion.13 = bf16[512,8,256]{2,0,1:T(8,128)(2,1)} fusion(bf16[768,8,128]{0,2,1:T(8,128)(2,1)} %fusion.7, bf16[768,8,128]{0,2,1:T(8,128)(2,1)} %fusion.8, bf16[768,576]{1,0:T(8,128)(2,1)} %copy-done.26), kind=kOutput, calls=%fused_computation.29 | convolution fusion | flops 1617952768 | bytes 6029312 | tf_op jit(solution)/shard_map/kl,khd->lhd/dot_general | solution.py:144
  125.0 0.8 all-to-all-done
  125.9 0.7 broadcast_in_dim.48
  126.6 4.0 %all-to-all-start.5 = ((f32[8,16,576]{2,1,0:T(8,128)}), f32[8,16,576]{2,1,0:T(8,128)S(1)}, u32[]{:S(2)}, u32[]{:S(2)}) async-start(f32[8,16,576]{2,1,0:T(8,128)} %broadcast_in_dim.48), calls=%async_computation.5 | async-start | bytes 655360 | tf_op jit(solution)/shard_map/all_to_all | solution.py:74
  130.7 2.7 %convolution_bitcast_fusion.3 = f32[256,8,64]{0,2,1:T(8,128)S(1)} fusion(bf16[768,64,1]{1,0,2:T(8,128)(2,1)S(1)} %maximum_bitcast_fusion, bf16[8,256,768]{1,2,0:T(8,128)(2,1)} %multiply_convert_fusion), kind=kOutput, calls=%fused_computation.57 | convolution fusion | flops 201326592 | bytes 3768320 | tf_op jit(solution)/shard_map/hqk,kr->qhr/dot_general | solution.py:59
  133.4 1.5 copy.336
  134.9 0.6 fusion.109
  135.5 1.6 all-to-all-done.5
  137.1 4.3 %all-to-all-start.1 = ((bf16[8,64,8,256]{3,1,2,0:T(8,128)(2,1)}), bf16[8,64,8,256]{3,1,2,0:T(8,128)(2,1)}, u32[]{:S(2)}, u32[]{:S(2)}) async-start(bf16[8,64,8,256]{3,1,2,0:T(8,128)(2,1)} %copy.336), calls=%async_computation.1 | async-start | bytes 4194304 | tf_op jit(solution)/shard_map/all_to_all | solution.py:154
  141.6 2.2 %convolution_bitcast_fusion.4 = f32[256,8,64]{0,2,1:T(8,128)S(1)} fusion(bf16[512,64,1]{1,0,2:T(8,128)(2,1)S(1)} %copy-done.24, bf16[8,256,512]{1,2,0:T(8,128)(2,1)} %copy-done.3), kind=kOutput, calls=%fused_computation.58 | convolution fusion | flops 134217728 | bytes 2686976 | tf_op jit(solution)/shard_map/hqk,kr->qhr/dot_general | solution.py:59
  143.9 1.8 %fusion.50 = bf16[256,8,128]{0,2,1:T(8,128)(2,1)S(1)} fusion(bf16[8,256,512]{1,2,0:T(8,128)(2,1)S(1)} %copy-done.4, bf16[768,8,256]{2,0,1:T(8,128)(2,1)} %copy-done.9), kind=kOutput, calls=%fused_computation.55 | convolution fusion | flops 268697600 | bytes 3670016 | tf_op jit(solution)/shard_map/hqk,khd->qhd/dot_general | solution.py:56
  145.7 2.2 %fusion.54 = bf16[256,8,128]{0,2,1:T(8,128)(2,1)S(1)} fusion(bf16[8,256,768]{1,2,0:T(8,128)(2,1)S(1)} %copy-done.2, bf16[768,8,256]{2,0,1:T(8,128)(2,1)} %copy-done.9), kind=kOutput, calls=%fused_computation.59 | convolution fusion | flops 402915328 | bytes 5242880 | tf_op jit(solution)/shard_map/hqk,khd->qhd/dot_general | solution.py:56
  147.9 5.6 %collective-permute-start.2 = (f32[128,576]{1,0:T(8,128)S(1)}, f32[128,576]{1,0:T(8,128)S(1)}, u32[]{:S(2)}, u32[]{:S(2)}) collective-permute-start(f32[128,576]{1,0:T(8,128)S(1)} %bitcast.129), channel_id=1, source_target_pairs={{0,1},{1,0},{2,3},{3,2},{4,5},{5,4},{6,7},{7,6},{8,9},{9,8},{10,11... | collective-permute-start | bytes 884744 | tf_op jit(solution)/shard_map/ppermute | solution.py:69
  153.5 1.3 maximum_maximum_fusion
  154.8 0.7 convert_reduce_fusion.1
  155.5 1.0 copy.343
  156.6 13.3 %all-to-all-done.1 = bf16[8,64,8,256]{3,1,2,0:T(8,128)(2,1)} async-done(((bf16[8,64,8,256]{3,1,2,0:T(8,128)(2,1)}), bf16[8,64,8,256]{3,1,2,0:T(8,128)(2,1)}, u32[]{:S(2)}, u32[]{:S(2)}) %all-to-all-start.1) | async-done | bytes 2097184 | tf_op jit(solution)/shard_map/all_to_all | solution.py:154
  169.9 2.0 %convert_reduce_fusion = f32[64,8,256]{2,0,1:T(8,128)S(1)} fusion(bf16[8,64,8,256]{3,1,2,0:T(8,128)(2,1)} %all-to-all-done.1), kind=kLoop, calls=%fused_computation.10 | loop fusion | flops 1966080 | bytes 2621440 | tf_op jit(solution)/shard_map/reduce_sum | solution.py:157
  171.9 1.1 copy.342
  (87 shorter events, 2.0 us)
Async XLA Ops:
  0.6 8.5 %copy-start = (bf16[512,8,256]{2,1,0:T(8,128)(2,1)S(1)}, bf16[512,8,256]{2,1,0:T(8,128)(2,1)}, u32[]{:S(2)}) copy-start(bf16[512,8,256]{2,1,0:T(8,128)(2,1)} %param.28) | copy-start | bytes 6291460
  5.7 13.6 %copy-start.27 = (f32[512,32]{0,1:T(8,128)}, f32[512,32]{0,1:T(8,128)S(1)}, u32[]{:S(2)}) copy-start(f32[512,32]{0,1:T(8,128)S(1)} %get-tuple-element.135) | copy-start | bytes 196612
  7.2 1.8 %copy-start.13 = (bf16[512,8,192]{0,2,1:T(8,128)(2,1)S(1)}, bf16[512,8,192]{0,2,1:T(8,128)(2,1)}, u32[]{:S(2)}) copy-start(bf16[512,8,192]{0,2,1:T(8,128)(2,1)} %param.25) | copy-start | bytes 4718596
  7.5 3.5 %copy-start.26 = (bf16[768,576]{1,0:T(8,128)(2,1)}, bf16[768,576]{1,0:T(8,128)(2,1)S(1)}, u32[]{:S(2)}) copy-start(bf16[768,576]{1,0:T(8,128)(2,1)S(1)} %maximum_maximum_fusion.1) | copy-start | bytes 2654212
  11.0 3.6 %copy-start.9 = (bf16[768,8,256]{2,0,1:T(8,128)(2,1)}, bf16[768,8,256]{2,0,1:T(8,128)(2,1)S(1)}, u32[]{:S(2)}) copy-start(bf16[768,8,256]{2,0,1:T(8,128)(2,1)S(1)} %convolution_convert_fusion) | copy-start | bytes 9437188
  14.6 3.5 %copy-start.25 = (bf16[512,8,128]{2,1,0:T(8,128)(2,1)S(1)}, bf16[512,8,128]{2,1,0:T(8,128)(2,1)}, u32[]{:S(2)}) copy-start(bf16[512,8,128]{2,1,0:T(8,128)(2,1)} %param.29) | copy-start | bytes 3145732
  17.4 2.4 %copy-start.23 = (bf16[512,64,1]{1,0,2:T(8,128)(2,1)S(1)}, bf16[512,64,1]{1,0,2:T(8,128)(2,1)}, u32[]{:S(2)}) copy-start(bf16[512,64,1]{1,0,2:T(8,128)(2,1)} %maximum_bitcast_fusion.1) | copy-start | bytes 196612
  25.5 2.7 %copy-start.14 = (bf16[512,8,128]{2,0,1:T(8,128)(2,1)S(1)}, bf16[512,8,128]{2,0,1:T(8,128)(2,1)}, u32[]{:S(2)}) copy-start(bf16[512,8,128]{2,0,1:T(8,128)(2,1)} %copy_select_fusion) | copy-start | bytes 3145732
  25.5 4.9 %copy-start.6 = (f32[8,256,512]{1,2,0:T(8,128)S(1)}, f32[8,256,512]{1,2,0:T(8,128)}, u32[]{:S(2)}) copy-start(f32[8,256,512]{1,2,0:T(8,128)} %get-tuple-element.141) | copy-start | bytes 12582916
  32.5 4.0 %copy-start.3 = (bf16[8,256,512]{1,2,0:T(8,128)(2,1)}, bf16[8,256,512]{1,2,0:T(8,128)(2,1)S(1)}, u32[]{:S(2)}) copy-start(bf16[8,256,512]{1,2,0:T(8,128)(2,1)S(1)} %multiply_convert_fusion.1) | copy-start | bytes 6291460
  46.9 5.2 %copy-start.10 = (bf16[768,8,256]{2,0,1:T(8,128)(2,1)S(1)}, bf16[768,8,256]{2,0,1:T(8,128)(2,1)}, u32[]{:S(2)}) copy-start(bf16[768,8,256]{2,0,1:T(8,128)(2,1)} %copy-done.9) | copy-start | bytes 9437188
  46.9 7.9 %copy-start.5 = (f32[8,256,768]{1,2,0:T(8,128)S(1)}, f32[8,256,768]{1,2,0:T(8,128)}, u32[]{:S(2)}) copy-start(f32[8,256,768]{1,2,0:T(8,128)} %get-tuple-element.139) | copy-start | bytes 18874372
  50.4 1.7 copy-start.7
  52.0 2.8 %copy-start.15 = (bf16[512,8,128]{2,0,1:T(8,128)(2,1)S(1)}, bf16[512,8,128]{2,0,1:T(8,128)(2,1)}, u32[]{:S(2)}) copy-start(bf16[512,8,128]{2,0,1:T(8,128)(2,1)} %copy_select_fusion) | copy-start | bytes 3145732
  57.7 3.1 %copy-start.1 = (bf16[8,256,768]{1,2,0:T(8,128)(2,1)S(1)}, bf16[8,256,768]{1,2,0:T(8,128)(2,1)}, u32[]{:S(2)}) copy-start(bf16[8,256,768]{1,2,0:T(8,128)(2,1)} %multiply_convert_fusion) | copy-start | bytes 9437188
  57.7 3.5 %copy-start.12 = (f32[512,8,128]{0,2,1:T(8,128)S(1)}, f32[512,8,128]{0,2,1:T(8,128)}, u32[]{:S(2)}) copy-start(f32[512,8,128]{0,2,1:T(8,128)} %convolution_bitcast_fusion.1) | copy-start | bytes 6291460
  61.2 5.9 %copy-start.20 = (f32[768,64]{0,1:T(8,128)}, f32[768,64]{0,1:T(8,128)S(1)}, u32[]{:S(2)}) copy-start(f32[768,64]{0,1:T(8,128)S(1)} %fusion.57) | copy-start | bytes 589828
  61.2 3.5 %copy-start.8 = (bf16[8,256,768]{1,2,0:T(8,128)(2,1)S(1)}, bf16[8,256,768]{1,2,0:T(8,128)(2,1)}, u32[]{:S(2)}) copy-start(bf16[8,256,768]{1,2,0:T(8,128)(2,1)} %copy-done.7) | copy-start | bytes 9437188
  61.2 3.5 %copy-start.11 = (f32[512,8,128]{0,2,1:T(8,128)S(1)}, f32[512,8,128]{0,2,1:T(8,128)}, u32[]{:S(2)}) copy-start(f32[512,8,128]{0,2,1:T(8,128)} %convolution_bitcast_fusion) | copy-start | bytes 6291460
  61.2 3.5 %copy-start.16 = (bf16[512,8,128]{2,0,1:T(8,128)(2,1)S(1)}, bf16[512,8,128]{2,0,1:T(8,128)(2,1)}, u32[]{:S(2)}) copy-start(bf16[512,8,128]{2,0,1:T(8,128)(2,1)} %copy_select_fusion) | copy-start | bytes 3145732
  67.2 2.3 %copy-start.22 = (f32[256,64]{1,0:T(8,128)}, f32[256,64]{1,0:T(8,128)S(1)}, u32[]{:S(2)}) copy-start(f32[256,64]{1,0:T(8,128)S(1)} %copy.340) | copy-start | bytes 196612
  67.2 4.4 %copy-start.21 = (f32[768,64]{0,1:T(8,128)S(1)}, f32[768,64]{0,1:T(8,128)}, u32[]{:S(2)}) copy-start(f32[768,64]{0,1:T(8,128)} %copy-done.20) | copy-start | bytes 589828
  67.2 4.7 %copy-start.18 = (bf16[768,8,128]{0,2,1:T(8,128)(2,1)S(1)}, bf16[768,8,128]{0,2,1:T(8,128)(2,1)}, u32[]{:S(2)}) copy-start(bf16[768,8,128]{0,2,1:T(8,128)(2,1)} %fusion.8) | copy-start | bytes 4718596
  67.2 4.7 %copy-start.19 = (bf16[768,8,128]{0,2,1:T(8,128)(2,1)S(1)}, bf16[768,8,128]{0,2,1:T(8,128)(2,1)}, u32[]{:S(2)}) copy-start(bf16[768,8,128]{0,2,1:T(8,128)(2,1)} %fusion.7) | copy-start | bytes 4718596
  70.2 7.4 %collective-permute-start.1 = (f32[128,576]{1,0:T(8,128)}, f32[128,576]{1,0:T(8,128)}, u32[]{:S(2)}, u32[]{:S(2)}) collective-permute-start(f32[128,576]{1,0:T(8,128)} %fusion.77), channel_id=1, source_target_pairs={{0,1},{1,0},{2,3},{3,2},{4,5},{5,4},{6,7},{7,6},{8,9},{9,8},{10,11... | collective-permute-start | bytes 884744 | tf_op jit(solution)/shard_map/ppermute | solution.py:69
  77.6 31.8 %collective-permute-start = (bf16[8,32,576]{2,1,0:T(8,128)(2,1)}, bf16[8,32,576]{2,1,0:T(8,128)(2,1)}, u32[]{:S(2)}, u32[]{:S(2)}) collective-permute-start(bf16[8,32,576]{2,1,0:T(8,128)(2,1)} %fusion.76), channel_id=1, source_target_pairs={{0,1},{1,0},{2,3},{3,2},{4,5},{5,4},{6,7},{7,6},{8,9},{9,8},{10,11... | collective-permute-start | bytes 884744 | tf_op jit(solution)/shard_map/ppermute | solution.py:69
  106.1 9.9 %all-to-all-start.4 = ((f32[8,2,576]{2,1,0:T(2,128)}), f32[8,2,576]{2,1,0:T(2,128)S(1)}, u32[]{:S(2)}, u32[]{:S(2)}) async-start(f32[8,2,576]{2,1,0:T(2,128)} %broadcast_in_dim.46), calls=%async_computation.4 | async-start | bytes 81920 | tf_op jit(solution)/shard_map/all_to_all | solution.py:74
  116.0 9.9 %all-to-all-start = ((bf16[8,32,576]{2,1,0:T(8,128)(2,1)}), bf16[8,32,576]{2,1,0:T(8,128)(2,1)S(1)}, u32[]{:S(2)}, u32[]{:S(2)}) async-start(bf16[8,32,576]{2,1,0:T(8,128)(2,1)} %fusion.65), calls=%async_computation | async-start | bytes 655360 | tf_op jit(solution)/shard_map/all_to_all | solution.py:173
  126.6 10.5 %all-to-all-start.5 = ((f32[8,16,576]{2,1,0:T(8,128)}), f32[8,16,576]{2,1,0:T(8,128)S(1)}, u32[]{:S(2)}, u32[]{:S(2)}) async-start(f32[8,16,576]{2,1,0:T(8,128)} %broadcast_in_dim.48), calls=%async_computation.5 | async-start | bytes 655360 | tf_op jit(solution)/shard_map/all_to_all | solution.py:74
  130.6 2.7 %copy-start.17 = (bf16[512,8,256]{2,0,1:T(8,128)(2,1)S(1)}, bf16[512,8,256]{2,0,1:T(8,128)(2,1)}, u32[]{:S(2)}) copy-start(bf16[512,8,256]{2,0,1:T(8,128)(2,1)} %fusion.13) | copy-start | bytes 6291460
  130.6 4.2 %copy-start.28 = (f32[512,32]{0,1:T(8,128)S(1)}, f32[512,32]{0,1:T(8,128)}, u32[]{:S(2)}) copy-start(f32[512,32]{0,1:T(8,128)} %copy-done.27) | copy-start | bytes 196612
  134.9 6.7 %copy-start.24 = (bf16[512,64,1]{1,0,2:T(8,128)(2,1)S(1)}, bf16[512,64,1]{1,0,2:T(8,128)(2,1)}, u32[]{:S(2)}) copy-start(bf16[512,64,1]{1,0,2:T(8,128)(2,1)} %maximum_bitcast_fusion.1) | copy-start | bytes 196612
  135.5 6.0 %copy-start.29 = (f32[256,32]{0,1:T(8,128)S(1)}, f32[256,32]{0,1:T(8,128)}, u32[]{:S(2)}) copy-start(f32[256,32]{0,1:T(8,128)} %get-tuple-element.131) | copy-start | bytes 98308
  135.5 6.0 %copy-start.30 = (f32[256,32]{0,1:T(8,128)S(1)}, f32[256,32]{0,1:T(8,128)}, u32[]{:S(2)}) copy-start(f32[256,32]{0,1:T(8,128)} %get-tuple-element.142) | copy-start | bytes 98308
  137.1 32.8 %all-to-all-start.1 = ((bf16[8,64,8,256]{3,1,2,0:T(8,128)(2,1)}), bf16[8,64,8,256]{3,1,2,0:T(8,128)(2,1)}, u32[]{:S(2)}, u32[]{:S(2)}) async-start(bf16[8,64,8,256]{3,1,2,0:T(8,128)(2,1)} %copy.336), calls=%async_computation.1 | async-start | bytes 4194304 | tf_op jit(solution)/shard_map/all_to_all | solution.py:154
  141.5 2.5 %copy-start.4 = (bf16[8,256,512]{1,2,0:T(8,128)(2,1)S(1)}, bf16[8,256,512]{1,2,0:T(8,128)(2,1)}, u32[]{:S(2)}) copy-start(bf16[8,256,512]{1,2,0:T(8,128)(2,1)} %copy-done.3) | copy-start | bytes 6291460
  141.6 4.1 %copy-start.2 = (bf16[8,256,768]{1,2,0:T(8,128)(2,1)S(1)}, bf16[8,256,768]{1,2,0:T(8,128)(2,1)}, u32[]{:S(2)}) copy-start(bf16[8,256,768]{1,2,0:T(8,128)(2,1)} %multiply_convert_fusion) | copy-start | bytes 9437188
  147.9 7.6 %collective-permute-start.2 = (f32[128,576]{1,0:T(8,128)S(1)}, f32[128,576]{1,0:T(8,128)S(1)}, u32[]{:S(2)}, u32[]{:S(2)}) collective-permute-start(f32[128,576]{1,0:T(8,128)S(1)} %bitcast.129), channel_id=1, source_target_pairs={{0,1},{1,0},{2,3},{3,2},{4,5},{5,4},{6,7},{7,6},{8,9},{9,8},{10,11... | collective-permute-start | bytes 884744 | tf_op jit(solution)/shard_map/ppermute | solution.py:69

commit v4 on v2

--- a/solution.py
+++ b/solution.py
@@ -57,19 +57,34 @@
         "hqk,khd->qhd", score_grad, key_nope, preferred_element_type=jnp.float32
     )
     rope_query = jnp.einsum("hqk,kr->qhr", score_grad, key_rope, preferred_element_type=jnp.float32)
-    nope_key = jnp.einsum(
-        "hqk,qhd->khd", score_grad, query_nope, preferred_element_type=jnp.float32
-    )
-    rope_key = jnp.einsum("hqk,qhr->kr", score_grad, query_rope, preferred_element_type=jnp.float32)
-    value_grad = jnp.einsum("hqk,qhv->khv", weights, cotangent, preferred_element_type=jnp.float32)
-    return (nope_query, rope_query, nope_key, rope_key, value_grad)
+    return (nope_query, rope_query, score_grad, weights)
+
+
+def key_gradients(score_grads, weights, query_nopes, query_ropes, cotangents, first, last):
+    nope_key = rope_key = value_grad = None
+    for score_grad, weight, query_nope, query_rope, cotangent in zip(
+        score_grads, weights, query_nopes, query_ropes, cotangents
+    ):
+        if score_grad.shape[-1] < last:
+            continue
+        part = score_grad[:, :, first:last]
+        nope = jnp.einsum("hqk,qhd->khd", part, query_nope, preferred_element_type=jnp.float32)
+        rope = jnp.einsum("hqk,qhr->kr", part, query_rope, preferred_element_type=jnp.float32)
+        value = jnp.einsum(
+            "hqk,qhv->khv", weight[:, :, first:last], cotangent, preferred_element_type=jnp.float32
+        )
+        if nope_key is None:
+            nope_key, rope_key, value_grad = nope, rope, value
+        else:
+            nope_key, rope_key, value_grad = nope_key + nope, rope_key + rope, value_grad + value
+    return nope_key, rope_key, value_grad
 
 
 def swap_pair(values):
     return lax.ppermute(values, "core", [(0, 1), (1, 0)])
 
 
-def on_device(queries, latent, prefix, kv_up, out_grad, lengths, positions):
+def device_step(queries, latent, prefix, kv_up, out_grad, lengths, positions):
     seq_len = queries.shape[0]
     latent_dim = kv_up.shape[0]
     value_dim = out_grad.shape[2]
@@ -90,39 +105,39 @@
     )
     source_latent = source[:, :latent_dim]
     key_rope = source[:, latent_dim:]
-    key_total = source.shape[0]
     live_rows = jnp.arange(seq_len) < length
     cotangent = jnp.where(live_rows[:, None, None], out_grad, jnp.zeros_like(out_grad))
     block_rows = min(seq_len, 256)
-    head_part = kv_up.shape[1]
     projected = jnp.einsum(
         "kl,lhd->khd", source_latent, kv_up, preferred_element_type=jnp.float32
     ).astype(jnp.bfloat16)
     key_nope = projected[:, :, :nope_dim]
     values = projected[:, :, nope_dim:]
-    nope_total = jnp.zeros((key_total, head_part, nope_dim), jnp.float32)
-    rope_total = jnp.zeros((key_total, rope_dim), jnp.float32)
-    value_total = jnp.zeros((key_total, head_part, value_dim), jnp.float32)
     query_pieces = []
+    score_grads, weight_blocks, nope_blocks, rope_blocks, cot_blocks = [], [], [], [], []
     for block_number in range(seq_len // block_rows):
         first_row = block_number * block_rows
         last_row = first_row + block_rows
         seen = prefix_rows + last_row
-        pieces = block_gradients(
-            query_nope[first_row:last_row],
-            query_rope[first_row:last_row],
+        nope_block = query_nope[first_row:last_row]
+        rope_block = query_rope[first_row:last_row]
+        cot_block = cotangent[first_row:last_row]
+        nope_query, rope_query, score_grad, weights = block_gradients(
+            nope_block,
+            rope_block,
             key_nope[:seen],
             key_rope[:seen],
             values[:seen],
-            cotangent[first_row:last_row],
+            cot_block,
             first_row,
             length,
             prefix_rows,
         )
-        nope_query, rope_query, nope_key, rope_key, value_grad = pieces
-        nope_total = nope_total.at[:seen].add(nope_key)
-        rope_total = rope_total.at[:seen].add(rope_key)
-        value_total = value_total.at[:seen].add(value_grad)
+        score_grads.append(score_grad)
+        weight_blocks.append(weights)
+        nope_blocks.append(nope_block)
+        rope_blocks.append(rope_block)
+        cot_blocks.append(cot_block)
         query_pieces.append(
             jnp.concatenate(
                 [
@@ -134,16 +149,23 @@
                 axis=-1,
             ).astype(jnp.bfloat16)
         )
+    key_inputs = (score_grads, weight_blocks, nope_blocks, rope_blocks, cot_blocks)
+    nope_prefix, rope_prefix, value_prefix = key_gradients(*key_inputs, 0, prefix_rows)
+    prefix_projected_grad = jnp.concatenate([nope_prefix, value_prefix], axis=-1).astype(jnp.bfloat16)
+    token_sets = []
+    for block_number in range(seq_len // block_rows):
+        first = prefix_rows + block_number * block_rows
+        token_sets.append(key_gradients(*key_inputs, first, first + block_rows))
+    nope_total = jnp.concatenate([nope_prefix] + [t[0] for t in token_sets], axis=0)
+    rope_total = jnp.concatenate([rope_prefix] + [t[1] for t in token_sets], axis=0)
+    value_total = jnp.concatenate([value_prefix] + [t[2] for t in token_sets], axis=0)
     head_projected_grad = jnp.concatenate([nope_total, value_total], axis=-1).astype(jnp.bfloat16)
     up_part = jnp.einsum(
         "kl,khd->lhd", source_latent, head_projected_grad, preferred_element_type=jnp.float32
     )
-    query_grad, projected_grad, rope_grad, up_part = (
-        jnp.concatenate(query_pieces, axis=0),
-        head_projected_grad,
-        rope_total,
-        up_part,
-    )
+    query_grad = jnp.concatenate(query_pieces, axis=0)
+    projected_grad = head_projected_grad
+    rope_grad = rope_total
     dp_size = lax.axis_size("dp")
     up_pieces = lax.all_to_all(
         up_part.astype(jnp.bfloat16).reshape((dp_size, -1) + up_part.shape[1:]), "dp", 0, 0, tiled=False
@@ -167,7 +189,7 @@
     token_pieces = lax.all_to_all(token_pair, "hr", 0, 0, tiled=False)
     latent_grad = jnp.sum(token_pieces.astype(jnp.float32), axis=0)
     latent_part = jnp.einsum(
-        "khd,lhd->kl", projected_grad[:prefix_rows], kv_up, preferred_element_type=jnp.float32
+        "khd,lhd->kl", prefix_projected_grad, kv_up, preferred_element_type=jnp.float32
     )
     prefix_part = jnp.concatenate([latent_part, rope_grad[:prefix_rows]], axis=1)
     half_rows = prefix_part.shape[0] // 2
@@ -207,7 +229,7 @@
         P("dp", None),
     )
     return jax.shard_map(
-        on_device,
+        device_step,
         mesh=split,
         in_specs=placed,
         out_specs=(P("dp", head, None), P(("dp",) + head, None), P("dp", head, None), P()),

time: 167 us -> 175 us (1.048)
  matrix products: 63.4 us -> 70.2 us
    dot_general x10 -> x19, matrix products: 25.2 us -> 32.4 us  [the longest x5 10.4 us: key_gradients(): jnp.einsum('hqk,qhv->khv', weight[:, :, first:last], cotangent, preferred...]
    unnamed x68 -> x94, local copies, waits for them, and re-layouts: 7.5 us -> 6.75 us
    concatenate x4 -> x5, other arithmetic: 4.66 us -> 4.26 us  [the longest x1 2.47 us: device_step(): query_grad = jnp.concatenate(query_pieces, axis=0)]
  transfers between devices with their start and end apart: 7 -> 7, of which waited for: 4 -> 4; matrix products, arithmetic and copies ran while one was open for 20% -> 25% of each run, Pallas kernels for 0% -> 0%
where the time goes in v4:
time: 175 us; the launch traced here: 174 us
  matrix products  70.2 us (40%)
  starting transfers between devices  29.8 us (17%)
  waiting for transfers between devices  28.1 us (16%)
  other arithmetic  26.5 us (15%)
  local copies, waits for them, and re-layouts  17.4 us (10%)
  between operations  1.95 us (1%)
    sub x2, matrix products, block_gradients(): exponent = jnp.exp(scores - highest)  13.4 us
    all_to_all x1, waiting for transfers between devices, device_step(): lax.all_to_all(up_part.astype(jnp.bfloat16).reshape((dp_size, -1) + up_pa...  11.4 us
    all_to_all x1, starting transfers between devices, device_step(): lax.all_to_all(prefix_half.reshape((outer_size, -1) + prefix_half.shape[1...  11.2 us
    dot_general x5, matrix products, key_gradients(): jnp.einsum('hqk,qhv->khv', weight[:, :, first:last], cotangent, preferred...  10.4 us
    all_to_all x1, waiting for transfers between devices, device_step(): lax.all_to_all(prefix_half.reshape((outer_size, -1) + prefix_half.shape[1...  8.83 us
    dot_general x5, matrix products, key_gradients(): jnp.einsum('hqk,qhd->khd', part, query_nope, preferred_element_type=jnp.f...  8.81 us
    all_to_all x1, waiting for transfers between devices, device_step(): lax.all_to_all(prefix_copies, outer, 0, 0, tiled=False)  7.26 us
    unnamed x94, local copies, waits for them, and re-layouts  6.75 us
  transfers between devices with their start and end apart: 7, of which 4 were waited for; matrix products, arithmetic and copies ran while one was open for 25% of the time, Pallas kernels for 0%

profile of v4, /device:TPU:1, one launch (start us, length us, event | category | flops | bytes accessed | tf_op | source)
XLA Modules:
  0.0 174.0 jit_solution(16337828884224393094)
XLA Ops:
  0.7 1.0 slice_convert_fusion.1
  1.7 1.9 %slice.137 = bf16[512,512]{0,1:T(8,128)(2,1)} slice(bf16[512,576]{0,1:T(8,128)(2,1)} %param.8), slice={[0:512], [0:512]} | slice | bytes 1048576 | tf_op jit(solution)/shard_map/slice | solution.py:104
  3.5 1.2 copy.208
  5.4 1.0 multiply_cosine_fusion
  6.6 1.3 copy.312
  7.9 0.8 maximum_bitcast_fusion
  9.7 1.8 %convolution_convert_fusion = bf16[768,8,256]{2,0,1:T(8,128)(2,1)S(1)} fusion(bf16[512,8,256]{2,1,0:T(8,128)(2,1)S(1)} %copy-done, bf16[768,576]{1,0:T(8,128)(2,1)S(1)} %maximum_maximum_fusion.1), kind=kOutput, calls=%fused_computation.27 | convolution fusion | flops 1612185600 | bytes 6029312 | tf_op jit(solution)/shard_map/kl,lhd->khd/dot_general | solution.py:111
  11.5 3.6 %fusion.44 = f32[8,768,256]{2,1,0:T(8,128)} fusion(bf16[768,8,256]{2,0,1:T(8,128)(2,1)S(1)} %convolution_convert_fusion, bf16[512,8,192]{0,2,1:T(8,128)(2,1)S(1)} %copy-done.11), kind=kOutput, calls=%fused_computation.53 | convolution fusion | flops 402653184 | bytes 8388608 | tf_op jit(solution)/shard_map/qhd,khd->hqk/dot_general | solution.py:37
  15.2 2.8 %fusion.114 = f32[8,512,256]{2,1,0:T(8,128)} fusion(bf16[768,8,256]{2,0,1:T(8,128)(2,1)S(1)} %convolution_convert_fusion, bf16[512,8,192]{0,2,1:T(8,128)(2,1)S(1)} %copy-done.11), kind=kOutput, calls=%fused_computation.120 | convolution fusion | flops 268435456 | bytes 5767168 | tf_op jit(solution)/shard_map/qhd,khd->hqk/dot_general | solution.py:37
  18.8 0.8 pad_maximum_fusion.1
  19.8 0.9 fusion.118
  20.7 5.7 %fusion.169 = (f32[8,256]{1,0:T(8,128)S(1)}, f32[8,256,512]{1,2,0:T(8,128)}) fusion(f32[8,512,256]{2,1,0:T(8,128)} %fusion.114, bf16[512,64,1]{1,0,2:T(8,128)(2,1)S(1)} %maximum_bitcast_fusion.1, pred[256,512]{0,1:T(8,128)(4,1)} %fusion.118, bf16[512,8,32]{0,2,1:T(8,128)(2,1)S(1)} %get-tuple-element.16, bf16[512,8,32]{0,2,1:T(8,128)(2,1)} %copy-done.16), kind=kOutput, calls=%fused_computation.208 | convolution fusion | flops 139985408 | bytes 9117696 | tf_op jit(solution)/shard_map/sub | solution.py:47
  26.4 2.5 %fusion.34 = bf16[8,256,512]{1,2,0:T(8,128)(2,1)S(1)} fusion(f32[8,256,512]{1,2,0:T(8,128)} %get-tuple-element.37, f32[8,256]{1,0:T(8,128)S(1)} %get-tuple-element.36), kind=kLoop, calls=%fused_computation.42 | loop fusion | flops 2097152 | bytes 6299648 | tf_op jit(solution)/shard_map/convert_element_type | solution.py:49
  29.0 2.9 %fusion.70 = f32[256,8]{0,1:T(8,128)S(1)} fusion(bf16[8,256,512]{1,2,0:T(8,128)(2,1)S(1)} %fusion.34, bf16[768,8,256]{2,0,1:T(8,128)(2,1)} %copy-done.8, bf16[512,8,128]{2,0,1:T(8,128)(2,1)S(1)} %copy_select_fusion), kind=kOutput, calls=%fused_computation.73 | convolution fusion | flops 269219840 | bytes 3678208 | tf_op jit(solution)/shard_map/hqk,khv->qhv/dot_general | solution.py:50
  31.9 1.4 fusion.94
  33.3 1.5 and_or_fusion
  34.8 7.8 %fusion.168 = (f32[8,256]{1,0:T(8,128)S(1)}, f32[8,256,768]{1,2,0:T(8,128)}) fusion(f32[8,768,256]{2,1,0:T(8,128)} %fusion.44, pred[256,768]{0,1:T(8,128)(4,1)} %and_or_fusion, bf16[768,64,1]{1,0,2:T(8,128)(2,1)} %maximum_bitcast_fusion, bf16[256,8,64]{0,2,1:T(8,128)(2,1)} %pad_maximum_fusion.1), kind=kOutput, calls=%fused_computation.207 | convolution fusion | flops 209191680 | bytes 13148160 | tf_op jit(solution)/shard_map/sub | solution.py:47
  42.6 3.5 %fusion.18 = bf16[8,256,768]{1,2,0:T(8,128)(2,1)S(1)} fusion(f32[8,256,768]{1,2,0:T(8,128)} %get-tuple-element.35, f32[8,256]{1,0:T(8,128)S(1)} %get-tuple-element.34), kind=kLoop, calls=%fused_computation.26 | loop fusion | flops 3145728 | bytes 9445376 | tf_op jit(solution)/shard_map/convert_element_type | solution.py:49
  46.3 1.2 fusion.71
  48.0 1.3 copy-done.1
  49.3 2.9 %multiply_convert_fusion = bf16[8,256,768]{1,2,0:T(8,128)(2,1)} fusion(f32[8,256]{1,0:T(8,128)S(1)} %bitcast.139, f32[8,256,768]{1,2,0:T(8,128)S(1)} %copy-done.1, f32[8,256]{1,0:T(8,128)S(1)} %get-tuple-element.34, bf16[768,8,256]{2,0,1:T(8,128)(2,1)S(1)} %copy-done.9, bf16[512,8,128]{2,0,1:T(8,128)(2,1)S(1)} %copy_select_fusion), kind=kOutput, calls=%fused_computation.5 | convolution fusion | flops 410517504 | bytes 11550720 | tf_op jit(solution)/shard_map/qhv,khv->hqk/dot_general | solution.py:52
  52.1 2.3 %multiply_convert_fusion.1 = bf16[8,256,512]{1,2,0:T(8,128)(2,1)} fusion(f32[8,256]{1,0:T(8,128)S(1)} %bitcast.138, f32[8,256,512]{1,2,0:T(8,128)S(1)} %copy-done.7, f32[8,256]{1,0:T(8,128)S(1)} %get-tuple-element.36, bf16[768,8,256]{2,0,1:T(8,128)(2,1)S(1)} %copy-done.9, bf16[512,8,128]{2,0,1:T(8,128)(2,1)S(1)} %copy_select_fusion), kind=kOutput, calls=%fused_computation.11 | convolution fusion | flops 273678336 | bytes 7880704 | tf_op jit(solution)/shard_map/qhv,khv->hqk/dot_general | solution.py:52
  54.4 2.9 %fusion.78 = bf16[256,8,128]{2,0,1:T(8,128)(2,1)} fusion(f32[8,128,256]{1,2,0:T(8,128)} %fusion.94, bf16[8,256,768]{1,2,0:T(8,128)(2,1)} %copy-done.10, bf16[512,8,128]{2,0,1:T(8,128)(2,1)S(1)} %copy_select_fusion), kind=kOutput, calls=%fused_computation.79 | convolution fusion | flops 134742016 | bytes 3145728 | tf_op jit(solution)/shard_map/hqk,qhv->khv/dot_general | solution.py:73
  57.3 1.8 %fusion.109 = f32[8,256,128]{2,1,0:T(8,128)S(1)} fusion(bf16[8,256,512]{1,2,0:T(8,128)(2,1)} %multiply_convert_fusion.1, bf16[512,8,192]{0,2,1:T(8,128)(2,1)} %param.7), kind=kOutput, calls=%fused_computation.115 | convolution fusion | flops 134217728 | bytes 2621440 | tf_op jit(solution)/shard_map/hqk,qhd->khd/dot_general | solution.py:71
  59.6 2.3 %fusion.80 = bf16[256,8,128]{2,0,1:T(8,128)(2,1)} fusion(f32[8,256,128]{2,1,0:T(8,128)S(1)} %fusion.109, bf16[8,256,768]{1,2,0:T(8,128)(2,1)S(1)} %copy-done.2, bf16[512,8,192]{0,2,1:T(8,128)(2,1)} %param.7), kind=kOutput, calls=%fused_computation.81 | convolution fusion | flops 134742016 | bytes 3145728 | tf_op jit(solution)/shard_map/hqk,qhd->khd/dot_general | solution.py:71
  61.9 2.3 %fusion.88 = f32[256,64]{0,1:T(8,128)} fusion(f32[256,64]{0,1:T(8,128)S(1)} %convolution_bitcast_fusion.3, bf16[8,256,512]{1,2,0:T(8,128)(2,1)} %multiply_convert_fusion.1, bf16[512,8,32]{0,2,1:T(8,128)(2,1)S(1)} %get-tuple-element.16, bf16[512,8,32]{0,2,1:T(8,128)(2,1)} %copy-done.16), kind=kOutput, calls=%fused_computation.92 | convolution fusion | flops 67649536 | bytes 1703936 | tf_op jit(solution)/shard_map/hqk,qhr->kr/dot_general | solution.py:72
  64.2 0.9 copy.262
  65.2 2.2 %fusion.81 = f32[256,512]{1,0:T(8,128)S(1)} fusion(bf16[512,8,256]{2,1,0:T(8,128)(2,1)S(1)} %copy-done, bf16[256,8,128]{2,0,1:T(8,128)(2,1)} %fusion.78, bf16[256,8,128]{2,0,1:T(8,128)(2,1)} %fusion.80), kind=kOutput, calls=%fused_computation.82 | convolution fusion | flops 538968064 | bytes 3670016 | tf_op jit(solution)/shard_map/khd,lhd->kl/dot_general | solution.py:191
  67.4 0.8 fusion.130
  68.1 1.4 collective-permute-start.1
  70.4 2.6 %fusion.75 = bf16[256,8,128]{2,0,1:T(8,128)(2,1)} fusion(bf16[8,256,768]{1,2,0:T(8,128)(2,1)} %copy-done.10, bf16[512,8,128]{2,0,1:T(8,128)(2,1)S(1)} %copy_select_fusion), kind=kOutput, calls=%fused_computation.76 | convolution fusion | flops 134479872 | bytes 2097152 | tf_op jit(solution)/shard_map/hqk,qhv->khv/dot_general | solution.py:73
  73.0 1.2 fusion.74
  74.3 1.4 fusion.91
  75.7 1.4 fusion.104
  78.0 0.8 copy.308
  78.8 2.1 %fusion.77 = bf16[256,8,128]{2,0,1:T(8,128)(2,1)S(1)} fusion(f32[8,128,256]{1,2,0:T(8,128)} %fusion.91, bf16[8,256,768]{1,2,0:T(8,128)(2,1)} %copy-done.10, bf16[512,8,128]{2,0,1:T(8,128)(2,1)S(1)} %copy_select_fusion), kind=kOutput, calls=%fused_computation.78 | convolution fusion | flops 134742016 | bytes 3145728 | tf_op jit(solution)/shard_map/hqk,qhv->khv/dot_general | solution.py:73
  80.9 2.0 %fusion.79 = bf16[256,8,128]{2,0,1:T(8,128)(2,1)S(1)} fusion(f32[8,256,128]{2,1,0:T(8,128)S(1)} %copy-done.15, bf16[8,256,768]{1,2,0:T(8,128)(2,1)} %multiply_convert_fusion, bf16[512,8,192]{0,2,1:T(8,128)(2,1)} %param.7), kind=kOutput, calls=%fused_computation.80 | convolution fusion | flops 134742016 | bytes 3145728 | tf_op jit(solution)/shard_map/hqk,qhd->khd/dot_general | solution.py:71
  83.0 1.3 fusion.62
  84.5 0.8 fusion.129
  85.4 1.7 fusion.132
  87.1 1.9 %reshape.240 = f32[64,2,576]{2,1,0:T(2,128)} reshape(f32[128,576]{1,0:T(8,128)} %fusion.132) | data formatting | bytes 589824 | tf_op jit(solution)/shard_map/reshape | solution.py:202
  89.0 11.2 %all-to-all-start.2 = ((f32[64,2,576]{2,1,0:T(2,128)}), f32[64,2,576]{2,1,0:T(2,128)S(1)}, u32[]{:S(2)}, u32[]{:S(2)}) async-start(f32[64,2,576]{2,1,0:T(2,128)} %reshape.240), calls=%async_computation.2 | async-start | bytes 655360 | tf_op jit(solution)/shard_map/all_to_all | solution.py:201
  100.3 1.8 %fusion.116 = bf16[8,32,576]{2,1,0:T(8,128)(2,1)} fusion(bf16[8,32,576]{2,1,0:T(8,128)(2,1)} %collective-permute-done, pred[]{:T(512)S(6)} %eq.2, bf16[8,2,32,576]{3,2,1,0:T(8,128)(2,1)S(1)} %pad_maximum_fusion), kind=kLoop, calls=%fused_computation.131 | loop fusion | flops 737280 | bytes 1179649 | tf_op jit(solution)/shard_map/convert_element_type | solution.py:188
  102.1 8.8 %all-to-all-done.2 = f32[64,2,576]{2,1,0:T(2,128)S(1)} async-done(((f32[64,2,576]{2,1,0:T(2,128)}), f32[64,2,576]{2,1,0:T(2,128)S(1)}, u32[]{:S(2)}, u32[]{:S(2)}) %all-to-all-start.2) | async-done | bytes 294944 | tf_op jit(solution)/shard_map/all_to_all | solution.py:201
  111.0 3.4 %all-to-all-start = ((bf16[8,32,576]{2,1,0:T(8,128)(2,1)}), bf16[8,32,576]{2,1,0:T(8,128)(2,1)S(1)}, u32[]{:S(2)}, u32[]{:S(2)}) async-start(bf16[8,32,576]{2,1,0:T(8,128)(2,1)} %fusion.116), calls=%async_computation | async-start | bytes 655360 | tf_op jit(solution)/shard_map/all_to_all | solution.py:189
  114.4 3.9 %fusion.31 = bf16[512,8,256]{2,0,1:T(8,128)(2,1)S(1)} fusion(bf16[256,8,128]{2,0,1:T(8,128)(2,1)} %fusion.75, bf16[256,8,128]{2,0,1:T(8,128)(2,1)} %copy-done.35, bf16[256,8,128]{2,0,1:T(8,128)(2,1)} %fusion.78, bf16[256,8,128]{2,0,1:T(8,128)(2,1)} %fusion.74, bf16[256,8,128]{2,0,1:T(8,128)(2,1)} %copy-done.36, bf16[256,8,128]{2,0,1:T(8,128)(2,1)} %fusion.80, ...), kind=kOutput, calls=%fused_computation.41 | convolution fusion | flops 1630535680 | bytes 6029312 | tf_op jit(solution)/shard_map/kl,khd->lhd/dot_general | solution.py:163
  118.3 1.5 copy.257
  121.2 0.8 broadcast_in_dim.38
  122.0 6.0 %all-to-all-start.3 = ((f32[64,2,576]{2,1,0:T(2,128)}), f32[64,2,576]{2,1,0:T(2,128)S(1)}, u32[]{:S(2)}, u32[]{:S(2)}) async-start(f32[64,2,576]{2,1,0:T(2,128)} %broadcast_in_dim.38), calls=%async_computation.3 | async-start | bytes 655360 | tf_op jit(solution)/shard_map/all_to_all | solution.py:206
  128.0 2.6 %convolution_bitcast_fusion.1 = f32[256,8,64]{0,2,1:T(8,128)S(1)} fusion(bf16[768,64,1]{1,0,2:T(8,128)(2,1)S(1)} %copy-done.20, bf16[8,256,768]{1,2,0:T(8,128)(2,1)} %multiply_convert_fusion), kind=kOutput, calls=%fused_computation.83 | convolution fusion | flops 201326592 | bytes 3768320 | tf_op jit(solution)/shard_map/hqk,kr->qhr/dot_general | solution.py:59
  130.6 7.3 %all-to-all-done.3 = f32[64,2,576]{2,1,0:T(2,128)S(1)} async-done(((f32[64,2,576]{2,1,0:T(2,128)}), f32[64,2,576]{2,1,0:T(2,128)S(1)}, u32[]{:S(2)}, u32[]{:S(2)}) %all-to-all-start.3) | async-done | bytes 294944 | tf_op jit(solution)/shard_map/all_to_all | solution.py:206
  137.9 4.4 %all-to-all-start.1 = ((bf16[8,64,8,256]{3,1,2,0:T(8,128)(2,1)}), bf16[8,64,8,256]{3,1,2,0:T(8,128)(2,1)}, u32[]{:S(2)}, u32[]{:S(2)}) async-start(bf16[8,64,8,256]{3,1,2,0:T(8,128)(2,1)} %copy.257), calls=%async_computation.1 | async-start | bytes 4194304 | tf_op jit(solution)/shard_map/all_to_all | solution.py:170
  142.3 0.8 add_convert_fusion.1
  143.0 2.2 %convolution_bitcast_fusion.2 = f32[256,8,64]{0,2,1:T(8,128)S(1)} fusion(bf16[512,64,1]{1,0,2:T(8,128)(2,1)S(1)} %copy-done.24, bf16[8,256,512]{1,2,0:T(8,128)(2,1)} %multiply_convert_fusion.1), kind=kOutput, calls=%fused_computation.84 | convolution fusion | flops 134217728 | bytes 2686976 | tf_op jit(solution)/shard_map/hqk,kr->qhr/dot_general | solution.py:59
  145.3 0.8 add_convert_fusion.2
  146.1 1.8 %fusion.76 = bf16[256,8,128]{0,2,1:T(8,128)(2,1)S(1)} fusion(bf16[8,256,512]{1,2,0:T(8,128)(2,1)S(1)} %copy-done.6, bf16[768,8,256]{2,0,1:T(8,128)(2,1)} %copy-done.8), kind=kOutput, calls=%fused_computation.77 | convolution fusion | flops 268697600 | bytes 3670016 | tf_op jit(solution)/shard_map/hqk,khd->qhd/dot_general | solution.py:56
  147.9 2.2 %fusion.84 = bf16[256,8,128]{0,2,1:T(8,128)(2,1)S(1)} fusion(bf16[8,256,768]{1,2,0:T(8,128)(2,1)S(1)} %copy-done.4, bf16[768,8,256]{2,0,1:T(8,128)(2,1)} %copy-done.8), kind=kOutput, calls=%fused_computation.85 | convolution fusion | flops 402915328 | bytes 5242880 | tf_op jit(solution)/shard_map/hqk,khd->qhd/dot_general | solution.py:56
  150.0 1.9 %reshape.241 = f32[128,576]{1,0:T(8,128)} reshape(f32[64,2,576]{2,1,0:T(2,128)} %copy-done.21) | data formatting | bytes 589824 | tf_op jit(solution)/shard_map/reshape | solution.py:206
  152.0 3.3 %collective-permute-start.2 = (f32[128,576]{1,0:T(8,128)}, f32[128,576]{1,0:T(8,128)S(1)}, u32[]{:S(2)}, u32[]{:S(2)}) collective-permute-start(f32[128,576]{1,0:T(8,128)} %reshape.241), channel_id=1, source_target_pairs={{0,1},{1,0},{2,3},{3,2},{4,5},{5,4},{6,7},{7,6},{8,9},{9,8},{10,11... | collective-permute-start | bytes 884744 | tf_op jit(solution)/shard_map/ppermute | solution.py:84
  155.2 2.5 %maximum_maximum_fusion = bf16[512,8,192]{0,2,1:T(8,128)(2,1)} fusion(bf16[256,8,32]{0,2,1:T(8,128)(2,1)} %get-tuple-element.21, bf16[256,8,32]{0,2,1:T(8,128)(2,1)} %get-tuple-element.20, bf16[256,8,128]{0,2,1:T(8,128)(2,1)S(1)} %fusion.84, bf16[256,8,32]{0,2,1:T(8,128)(2,1)} %get-tuple-element.19, bf16[256,8,32]{0,2,1:T(8,128)(2,1)} %get-tuple-element.18, ...), kind=kLoop, calls=%fused_computation.47 | loop fusion | flops 9437184 | bytes 3145728 | tf_op jit(solution)/shard_map/concatenate | solution.py:166
  158.4 1.0 copy.264
  159.5 11.4 %all-to-all-done.1 = bf16[8,64,8,256]{3,1,2,0:T(8,128)(2,1)} async-done(((bf16[8,64,8,256]{3,1,2,0:T(8,128)(2,1)}), bf16[8,64,8,256]{3,1,2,0:T(8,128)(2,1)}, u32[]{:S(2)}, u32[]{:S(2)}) %all-to-all-start.1) | async-done | bytes 2097184 | tf_op jit(solution)/shard_map/all_to_all | solution.py:170
  170.9 2.0 %convert_reduce_fusion = f32[64,8,256]{2,0,1:T(8,128)S(1)} fusion(bf16[8,64,8,256]{3,1,2,0:T(8,128)(2,1)} %all-to-all-done.1), kind=kLoop, calls=%fused_computation.10 | loop fusion | flops 1966080 | bytes 2621440 | tf_op jit(solution)/shard_map/reduce_sum | solution.py:173
  172.9 1.1 copy.263
  (120 shorter events, 7.8 us)
Async XLA Ops:
  0.6 9.1 %copy-start = (bf16[512,8,256]{2,1,0:T(8,128)(2,1)S(1)}, bf16[512,8,256]{2,1,0:T(8,128)(2,1)}, u32[]{:S(2)}) copy-start(bf16[512,8,256]{2,1,0:T(8,128)(2,1)} %param.10) | copy-start | bytes 6291460
  0.7 5.8 %copy-start.40 = (f32[32]{0:T(128)}, f32[32]{0:T(128)S(1)}, u32[]{:S(2)}) copy-start(f32[32]{0:T(128)S(1)} %negate_power_fusion) | copy-start | bytes 388
  7.9 1.7 copy-start.11
  8.8 2.7 %copy-start.28 = (bf16[768,576]{1,0:T(8,128)(2,1)}, bf16[768,576]{1,0:T(8,128)(2,1)S(1)}, u32[]{:S(2)}) copy-start(bf16[768,576]{1,0:T(8,128)(2,1)S(1)} %maximum_maximum_fusion.1) | copy-start | bytes 2654212
  9.6 11.2 %copy-start.23 = (bf16[512,64,1]{1,0,2:T(8,128)(2,1)}, bf16[512,64,1]{1,0,2:T(8,128)(2,1)S(1)}, u32[]{:S(2)}) copy-start(bf16[512,64,1]{1,0,2:T(8,128)(2,1)S(1)} %maximum_bitcast_fusion.1) | copy-start | bytes 196612
  11.5 3.6 %copy-start.8 = (bf16[768,8,256]{2,0,1:T(8,128)(2,1)}, bf16[768,8,256]{2,0,1:T(8,128)(2,1)S(1)}, u32[]{:S(2)}) copy-start(bf16[768,8,256]{2,0,1:T(8,128)(2,1)S(1)} %convolution_convert_fusion) | copy-start | bytes 9437188
  15.2 3.5 %copy-start.29 = (f32[512,32]{0,1:T(8,128)S(1)}, f32[512,32]{0,1:T(8,128)}, u32[]{:S(2)}) copy-start(f32[512,32]{0,1:T(8,128)} %get-tuple-element.30) | copy-start | bytes 196612
  15.2 3.5 %copy-start.31 = (f32[512,32]{0,1:T(8,128)S(1)}, f32[512,32]{0,1:T(8,128)}, u32[]{:S(2)}) copy-start(f32[512,32]{0,1:T(8,128)} %get-tuple-element.31) | copy-start | bytes 196612
  15.2 4.5 %copy-start.27 = (bf16[512,8,128]{2,1,0:T(8,128)(2,1)S(1)}, bf16[512,8,128]{2,1,0:T(8,128)(2,1)}, u32[]{:S(2)}) copy-start(bf16[512,8,128]{2,1,0:T(8,128)(2,1)} %param.11) | copy-start | bytes 3145732
  18.8 0.8 copy-start.16
  29.0 4.3 %copy-start.13 = (bf16[8,256,512]{1,2,0:T(8,128)(2,1)}, bf16[8,256,512]{1,2,0:T(8,128)(2,1)S(1)}, u32[]{:S(2)}) copy-start(bf16[8,256,512]{1,2,0:T(8,128)(2,1)S(1)} %fusion.34) | copy-start | bytes 6291460
  29.0 4.3 %copy-start.42 = (s32[256]{0:T(256)S(1)}, s32[256]{0:T(256)}, u32[]{:S(2)}) copy-start(s32[256]{0:T(256)} %iota_add_fusion.2) | copy-start | bytes 3076
  42.6 3.7 %copy-start.9 = (bf16[768,8,256]{2,0,1:T(8,128)(2,1)S(1)}, bf16[768,8,256]{2,0,1:T(8,128)(2,1)}, u32[]{:S(2)}) copy-start(bf16[768,8,256]{2,0,1:T(8,128)(2,1)} %copy-done.8) | copy-start | bytes 9437188
  42.6 6.7 %copy-start.1 = (f32[8,256,768]{1,2,0:T(8,128)S(1)}, f32[8,256,768]{1,2,0:T(8,128)}, u32[]{:S(2)}) copy-start(f32[8,256,768]{1,2,0:T(8,128)} %get-tuple-element.35) | copy-start | bytes 18874372
  46.3 1.7 copy-start.10
  49.3 2.9 %copy-start.7 = (f32[8,256,512]{1,2,0:T(8,128)S(1)}, f32[8,256,512]{1,2,0:T(8,128)}, u32[]{:S(2)}) copy-start(f32[8,256,512]{1,2,0:T(8,128)} %get-tuple-element.37) | copy-start | bytes 12582916
  54.4 4.7 %copy-start.2 = (bf16[8,256,768]{1,2,0:T(8,128)(2,1)S(1)}, bf16[8,256,768]{1,2,0:T(8,128)(2,1)}, u32[]{:S(2)}) copy-start(bf16[8,256,768]{1,2,0:T(8,128)(2,1)} %multiply_convert_fusion) | copy-start | bytes 9437188
  54.4 4.7 %copy-start.25 = (bf16[256,8,64]{0,2,1:T(8,128)(2,1)S(1)}, bf16[256,8,64]{0,2,1:T(8,128)(2,1)}, u32[]{:S(2)}) copy-start(bf16[256,8,64]{0,2,1:T(8,128)(2,1)} %pad_maximum_fusion.1) | copy-start | bytes 786436
  65.1 4.4 %copy-start.3 = (bf16[8,256,768]{1,2,0:T(8,128)(2,1)S(1)}, bf16[8,256,768]{1,2,0:T(8,128)(2,1)}, u32[]{:S(2)}) copy-start(bf16[8,256,768]{1,2,0:T(8,128)(2,1)} %multiply_convert_fusion) | copy-start | bytes 9437188
  65.2 4.4 %copy-start.26 = (bf16[256,8,64]{0,2,1:T(8,128)(2,1)S(1)}, bf16[256,8,64]{0,2,1:T(8,128)(2,1)}, u32[]{:S(2)}) copy-start(bf16[256,8,64]{0,2,1:T(8,128)(2,1)} %pad_maximum_fusion.1) | copy-start | bytes 786436
  67.3 2.2 %copy-start.18 = (f32[256,512]{1,0:T(8,128)}, f32[256,512]{1,0:T(8,128)S(1)}, u32[]{:S(2)}) copy-start(f32[256,512]{1,0:T(8,128)S(1)} %fusion.81) | copy-start | bytes 1572868
  67.4 5.7 %copy-start.12 = (bf16[512,8,192]{0,2,1:T(8,128)(2,1)S(1)}, bf16[512,8,192]{0,2,1:T(8,128)(2,1)}, u32[]{:S(2)}) copy-start(bf16[512,8,192]{0,2,1:T(8,128)(2,1)} %param.7) | copy-start | bytes 4718596
  68.1 17.3 %collective-permute-start.1 = (f32[128,576]{1,0:T(8,128)}, f32[128,576]{1,0:T(8,128)}, u32[]{:S(2)}, u32[]{:S(2)}) collective-permute-start(f32[128,576]{1,0:T(8,128)} %fusion.130), channel_id=1, source_target_pairs={{0,1},{1,0},{2,3},{3,2},{4,5},{5,4},{6,7},{7,6},{8,9},{9,8},{10,11... | collective-permute-start | bytes 884744 | tf_op jit(solution)/shard_map/ppermute | solution.py:84
  69.9 4.3 %copy-start.14 = (bf16[8,256,512]{1,2,0:T(8,128)(2,1)S(1)}, bf16[8,256,512]{1,2,0:T(8,128)(2,1)}, u32[]{:S(2)}) copy-start(bf16[8,256,512]{1,2,0:T(8,128)(2,1)} %copy-done.13) | copy-start | bytes 6291460
  73.0 2.6 %copy-start.5 = (bf16[8,256,512]{1,2,0:T(8,128)(2,1)S(1)}, bf16[8,256,512]{1,2,0:T(8,128)(2,1)}, u32[]{:S(2)}) copy-start(bf16[8,256,512]{1,2,0:T(8,128)(2,1)} %multiply_convert_fusion.1) | copy-start | bytes 6291460
  74.3 2.8 %copy-start.17 = (bf16[512,8,32]{0,2,1:T(8,128)(2,1)S(1)}, bf16[512,8,32]{0,2,1:T(8,128)(2,1)}, u32[]{:S(2)}) copy-start(bf16[512,8,32]{0,2,1:T(8,128)(2,1)} %copy-done.16) | copy-start | bytes 786436
  74.3 3.3 %copy-start.41 = (f32[32]{0:T(128)S(1)}, f32[32]{0:T(128)}, u32[]{:S(2)}) copy-start(f32[32]{0:T(128)} %copy-done.40) | copy-start | bytes 388
  78.8 2.1 %copy-start.15 = (f32[8,256,128]{2,1,0:T(8,128)S(1)}, f32[8,256,128]{2,1,0:T(8,128)}, u32[]{:S(2)}) copy-start(f32[8,256,128]{2,1,0:T(8,128)} %fusion.104) | copy-start | bytes 3145732
  78.8 4.2 %copy-start.33 = (bf16[256,8,128]{2,0,1:T(8,128)(2,1)S(1)}, bf16[256,8,128]{2,0,1:T(8,128)(2,1)}, u32[]{:S(2)}) copy-start(bf16[256,8,128]{2,0,1:T(8,128)(2,1)} %fusion.78) | copy-start | bytes 1572868
  78.8 4.2 %copy-start.34 = (bf16[256,8,128]{2,0,1:T(8,128)(2,1)S(1)}, bf16[256,8,128]{2,0,1:T(8,128)(2,1)}, u32[]{:S(2)}) copy-start(bf16[256,8,128]{2,0,1:T(8,128)(2,1)} %fusion.80) | copy-start | bytes 1572868
  78.8 4.2 %copy-start.43 = (bf16[256,8,128]{2,0,1:T(8,128)(2,1)S(1)}, bf16[256,8,128]{2,0,1:T(8,128)(2,1)}, u32[]{:S(2)}) copy-start(bf16[256,8,128]{2,0,1:T(8,128)(2,1)} %fusion.75) | copy-start | bytes 1572868
  78.8 4.2 %copy-start.44 = (bf16[256,8,128]{2,0,1:T(8,128)(2,1)S(1)}, bf16[256,8,128]{2,0,1:T(8,128)(2,1)}, u32[]{:S(2)}) copy-start(bf16[256,8,128]{2,0,1:T(8,128)(2,1)} %fusion.74) | copy-start | bytes 1572868
  80.9 3.4 %copy-start.35 = (bf16[256,8,128]{2,0,1:T(8,128)(2,1)}, bf16[256,8,128]{2,0,1:T(8,128)(2,1)S(1)}, u32[]{:S(2)}) copy-start(bf16[256,8,128]{2,0,1:T(8,128)(2,1)S(1)} %fusion.77) | copy-start | bytes 1572868
  83.0 1.4 copy-start.36
  83.0 1.4 copy-start.37
  83.0 2.4 %copy-start.19 = (f32[256,512]{1,0:T(8,128)S(1)}, f32[256,512]{1,0:T(8,128)}, u32[]{:S(2)}) copy-start(f32[256,512]{1,0:T(8,128)} %copy-done.18) | copy-start | bytes 1572868
  85.3 15.0 %collective-permute-start = (bf16[8,32,576]{2,1,0:T(8,128)(2,1)}, bf16[8,32,576]{2,1,0:T(8,128)(2,1)}, u32[]{:S(2)}, u32[]{:S(2)}) collective-permute-start(bf16[8,32,576]{2,1,0:T(8,128)(2,1)} %fusion.129), channel_id=1, source_target_pairs={{0,1},{1,0},{2,3},{3,2},{4,5},{5,4},{6,7},{7,6},{8,9},{9,8},{10,11... | collective-permute-start | bytes 884744 | tf_op jit(solution)/shard_map/ppermute | solution.py:84
  89.0 21.9 %all-to-all-start.2 = ((f32[64,2,576]{2,1,0:T(2,128)}), f32[64,2,576]{2,1,0:T(2,128)S(1)}, u32[]{:S(2)}, u32[]{:S(2)}) async-start(f32[64,2,576]{2,1,0:T(2,128)} %reshape.240), calls=%async_computation.2 | async-start | bytes 655360 | tf_op jit(solution)/shard_map/all_to_all | solution.py:201
  111.0 10.3 %all-to-all-start = ((bf16[8,32,576]{2,1,0:T(8,128)(2,1)}), bf16[8,32,576]{2,1,0:T(8,128)(2,1)S(1)}, u32[]{:S(2)}, u32[]{:S(2)}) async-start(bf16[8,32,576]{2,1,0:T(8,128)(2,1)} %fusion.116), calls=%async_computation | async-start | bytes 655360 | tf_op jit(solution)/shard_map/all_to_all | solution.py:189
  118.3 1.5 copy-start.30
  118.3 1.5 copy-start.32
  118.3 9.7 %copy-start.20 = (bf16[768,64,1]{1,0,2:T(8,128)(2,1)S(1)}, bf16[768,64,1]{1,0,2:T(8,128)(2,1)}, u32[]{:S(2)}) copy-start(bf16[768,64,1]{1,0,2:T(8,128)(2,1)} %maximum_bitcast_fusion) | copy-start | bytes 294916
  122.0 15.8 %all-to-all-start.3 = ((f32[64,2,576]{2,1,0:T(2,128)}), f32[64,2,576]{2,1,0:T(2,128)S(1)}, u32[]{:S(2)}, u32[]{:S(2)}) async-start(f32[64,2,576]{2,1,0:T(2,128)} %broadcast_in_dim.38), calls=%async_computation.3 | async-start | bytes 655360 | tf_op jit(solution)/shard_map/all_to_all | solution.py:206
  130.6 11.7 %copy-start.38 = (f32[256,32]{0,1:T(8,128)S(1)}, f32[256,32]{0,1:T(8,128)}, u32[]{:S(2)}) copy-start(f32[256,32]{0,1:T(8,128)} %get-tuple-element.27) | copy-start | bytes 98308
  130.6 11.7 %copy-start.39 = (f32[256,32]{0,1:T(8,128)S(1)}, f32[256,32]{0,1:T(8,128)}, u32[]{:S(2)}) copy-start(f32[256,32]{0,1:T(8,128)} %get-tuple-element.38) | copy-start | bytes 98308
  130.6 12.4 %copy-start.24 = (bf16[512,64,1]{1,0,2:T(8,128)(2,1)S(1)}, bf16[512,64,1]{1,0,2:T(8,128)(2,1)}, u32[]{:S(2)}) copy-start(bf16[512,64,1]{1,0,2:T(8,128)(2,1)} %copy-done.23) | copy-start | bytes 196612
  137.9 7.4 %copy-start.21 = (f32[64,2,576]{2,1,0:T(2,128)}, f32[64,2,576]{2,1,0:T(2,128)S(1)}, u32[]{:S(2)}) copy-start(f32[64,2,576]{2,1,0:T(2,128)S(1)} %all-to-all-done.3) | copy-start | bytes 884740
  137.9 33.0 %all-to-all-start.1 = ((bf16[8,64,8,256]{3,1,2,0:T(8,128)(2,1)}), bf16[8,64,8,256]{3,1,2,0:T(8,128)(2,1)}, u32[]{:S(2)}, u32[]{:S(2)}) async-start(bf16[8,64,8,256]{3,1,2,0:T(8,128)(2,1)} %copy.257), calls=%async_computation.1 | async-start | bytes 4194304 | tf_op jit(solution)/shard_map/all_to_all | solution.py:170
  142.2 3.8 %copy-start.6 = (bf16[8,256,512]{1,2,0:T(8,128)(2,1)S(1)}, bf16[8,256,512]{1,2,0:T(8,128)(2,1)}, u32[]{:S(2)}) copy-start(bf16[8,256,512]{1,2,0:T(8,128)(2,1)} %multiply_convert_fusion.1) | copy-start | bytes 6291460
  143.0 4.8 %copy-start.4 = (bf16[8,256,768]{1,2,0:T(8,128)(2,1)S(1)}, bf16[8,256,768]{1,2,0:T(8,128)(2,1)}, u32[]{:S(2)}) copy-start(bf16[8,256,768]{1,2,0:T(8,128)(2,1)} %multiply_convert_fusion) | copy-start | bytes 9437188
  151.9 6.4 %copy-start.22 = (f32[128,576]{1,0:T(8,128)S(1)}, f32[128,576]{1,0:T(8,128)}, u32[]{:S(2)}) copy-start(f32[128,576]{1,0:T(8,128)} %reshape.241) | copy-start | bytes 884740
  152.0 6.4 %collective-permute-start.2 = (f32[128,576]{1,0:T(8,128)}, f32[128,576]{1,0:T(8,128)S(1)}, u32[]{:S(2)}, u32[]{:S(2)}) collective-permute-start(f32[128,576]{1,0:T(8,128)} %reshape.241), channel_id=1, source_target_pairs={{0,1},{1,0},{2,3},{3,2},{4,5},{5,4},{6,7},{7,6},{8,9},{9,8},{10,11... | collective-permute-start | bytes 884744 | tf_op jit(solution)/shard_map/ppermute | solution.py:84

commit v5 on v2

--- a/solution.py
+++ b/solution.py
@@ -69,7 +69,7 @@
     return lax.ppermute(values, "core", [(0, 1), (1, 0)])
 
 
-def on_device(queries, latent, prefix, kv_up, out_grad, lengths, positions):
+def device_step(queries, latent, prefix, kv_up, out_grad, lengths, positions):
     seq_len = queries.shape[0]
     latent_dim = kv_up.shape[0]
     value_dim = out_grad.shape[2]
@@ -128,7 +128,9 @@
                 [
                     nope_query,
                     unrotate(
-                        rope_query, cosine[first_row:last_row, None], sine[first_row:last_row, None]
+                        rope_query,
+                        cosine[first_row:last_row, None],
+                        sine[first_row:last_row, None],
                     ),
                 ],
                 axis=-1,
@@ -207,7 +209,7 @@
         P("dp", None),
     )
     return jax.shard_map(
-        on_device,
+        device_step,
         mesh=split,
         in_specs=placed,
         out_specs=(P("dp", head, None), P(("dp",) + head, None), P("dp", head, None), P()),

time: 167 us -> 167 us (level)
  no operation moved by 1% of the time
where the time goes in v5:
time: 167 us; the launch traced here: 166 us
  matrix products  63.4 us (38%)
  starting transfers between devices  29.6 us (18%)
  waiting for transfers between devices  28 us (17%)
  other arithmetic  25.3 us (15%)
  local copies, waits for them, and re-layouts  17.5 us (10%)
  between operations  1.84 us (1%)
    sub x2, matrix products, block_gradients(): exponent = jnp.exp(scores - highest)  13.3 us
    all_to_all x1, starting transfers between devices, device_step(): lax.all_to_all(prefix_half.reshape((outer_size, -1) + prefix_half.shape[1...  11.5 us
    all_to_all x1, waiting for transfers between devices, device_step(): lax.all_to_all(up_part.astype(jnp.bfloat16).reshape((dp_size, -1) + up_pa...  11.2 us
    all_to_all x1, waiting for transfers between devices, device_step(): lax.all_to_all(prefix_half.reshape((outer_size, -1) + prefix_half.shape[1...  8.49 us
    unnamed x68, local copies, waits for them, and re-layouts  7.5 us
    all_to_all x1, waiting for transfers between devices, device_step(): lax.all_to_all(prefix_copies, outer, 0, 0, tiled=False)  7.26 us
    dot_general x2, matrix products, block_gradients(): jnp.einsum('hqk,qhd->khd', score_grad, query_nope, preferred_element_type...  6.79 us
    dot_general x2, matrix products, block_gradients(): jnp.einsum('qhd,khd->hqk', query_nope, key_nope, preferred_element_type=j...  6.38 us
  transfers between devices with their start and end apart: 7, of which 4 were waited for; matrix products, arithmetic and copies ran while one was open for 20% of the time, Pallas kernels for 0%

profile of v5, /device:TPU:1, one launch (start us, length us, event | category | flops | bytes accessed | tf_op | source)
XLA Modules:
  0.0 165.7 jit_solution(15621060437868061803)
XLA Ops:
  0.7 1.0 slice_convert_fusion.1
  1.7 1.9 %slice.226 = bf16[512,512]{0,1:T(8,128)(2,1)} slice(bf16[512,576]{0,1:T(8,128)(2,1)} %param.26), slice={[0:512], [0:512]} | slice | bytes 1048576 | tf_op jit(solution)/shard_map/slice | solution.py:89
  3.5 1.2 copy.178
  4.7 0.7 convert_element_type.66
  5.4 0.3 multiply_cosine_fusion
  6.0 1.3 copy.268
  7.5 0.7 maximum_bitcast_fusion.1
  8.3 0.8 copy-done.13
  9.2 1.8 %convolution_convert_fusion = bf16[768,8,256]{2,0,1:T(8,128)(2,1)S(1)} fusion(bf16[512,8,256]{2,1,0:T(8,128)(2,1)S(1)} %copy-done, bf16[768,576]{1,0:T(8,128)(2,1)S(1)} %maximum_maximum_fusion.1), kind=kOutput, calls=%fused_computation.25 | convolution fusion | flops 1612185600 | bytes 6029312 | tf_op jit(solution)/shard_map/kl,lhd->khd/dot_general | solution.py:98
  11.0 3.6 %fusion.24 = f32[8,768,256]{2,1,0:T(8,128)} fusion(bf16[768,8,256]{2,0,1:T(8,128)(2,1)S(1)} %convolution_convert_fusion, bf16[512,8,192]{0,2,1:T(8,128)(2,1)S(1)} %copy-done.13), kind=kOutput, calls=%fused_computation.43 | convolution fusion | flops 402653184 | bytes 8388608 | tf_op jit(solution)/shard_map/qhd,khd->hqk/dot_general | solution.py:37
  14.6 2.8 %fusion.63 = f32[8,512,256]{2,1,0:T(8,128)} fusion(bf16[768,8,256]{2,0,1:T(8,128)(2,1)S(1)} %convolution_convert_fusion, bf16[512,8,192]{0,2,1:T(8,128)(2,1)S(1)} %copy-done.13), kind=kOutput, calls=%fused_computation.69 | convolution fusion | flops 268435456 | bytes 5767168 | tf_op jit(solution)/shard_map/qhd,khd->hqk/dot_general | solution.py:37
  18.1 1.2 copy_select_fusion
  19.7 5.7 %fusion.112 = (f32[8,256]{1,0:T(8,128)S(1)}, f32[8,256,512]{1,2,0:T(8,128)}) fusion(f32[8,512,256]{2,1,0:T(8,128)} %fusion.63, bf16[512,64,1]{1,0,2:T(8,128)(2,1)S(1)} %copy-done.26, pred[256,512]{0,1:T(8,128)(4,1)S(1)} %fusion.67, bf16[512,8,32]{0,2,1:T(8,128)(2,1)S(1)} %get-tuple-element.112, bf16[512,8,32]{0,2,1:T(8,128)(2,1)S(1)} %get-tuple-element.113), kind=kOutput, calls=%fused_computation.149 | convolution fusion | flops 139985408 | bytes 9117696 | tf_op jit(solution)/shard_map/sub | solution.py:47
  25.5 2.7 %fusion.14 = bf16[8,256,512]{1,2,0:T(8,128)(2,1)S(1)} fusion(f32[8,256,512]{1,2,0:T(8,128)} %get-tuple-element.133, f32[8,256]{1,0:T(8,128)S(1)} %get-tuple-element.132), kind=kLoop, calls=%fused_computation.30 | loop fusion | flops 2097152 | bytes 6299648 | tf_op jit(solution)/shard_map/convert_element_type | solution.py:49
  28.2 2.2 %fusion.46 = f32[256,8]{0,1:T(8,128)S(1)} fusion(bf16[8,256,512]{1,2,0:T(8,128)(2,1)S(1)} %fusion.14, bf16[768,8,256]{2,0,1:T(8,128)(2,1)} %copy-done.9, bf16[512,8,128]{2,0,1:T(8,128)(2,1)S(1)} %copy-done.14), kind=kOutput, calls=%fused_computation.53 | convolution fusion | flops 269219840 | bytes 3678208 | tf_op jit(solution)/shard_map/hqk,khv->qhv/dot_general | solution.py:50
  30.4 2.0 %multiply_convert_fusion.1 = bf16[8,256,512]{1,2,0:T(8,128)(2,1)S(1)} fusion(f32[8,256]{1,0:T(8,128)S(1)} %bitcast.132, f32[8,256,512]{1,2,0:T(8,128)S(1)} %copy-done.6, f32[8,256]{1,0:T(8,128)S(1)} %get-tuple-element.132, bf16[768,8,256]{2,0,1:T(8,128)(2,1)} %copy-done.9, bf16[512,8,128]{2,0,1:T(8,128)(2,1)S(1)} %copy-done.14), kind=kOutput, calls=%fused_computation.11 | convolution fusion | flops 273678336 | bytes 7880704 | tf_op jit(solution)/shard_map/qhv,khv->hqk/dot_general | solution.py:52
  32.5 0.7 convolution_bitcast_fusion.6
  33.2 3.3 %convolution_bitcast_fusion.1 = f32[512,8,128]{0,2,1:T(8,128)} fusion(bf16[8,256,512]{1,2,0:T(8,128)(2,1)S(1)} %multiply_convert_fusion.1, bf16[512,8,192]{0,2,1:T(8,128)(2,1)} %param.25), kind=kOutput, calls=%fused_computation.32 | convolution fusion | flops 268435456 | bytes 4718592 | tf_op jit(solution)/shard_map/hqk,qhd->khd/dot_general | solution.py:60
  36.5 2.1 %convolution_bitcast_fusion = f32[512,8,128]{0,2,1:T(8,128)} fusion(bf16[8,256,512]{1,2,0:T(8,128)(2,1)S(1)} %fusion.14, bf16[512,8,128]{2,0,1:T(8,128)(2,1)S(1)} %copy-done.14), kind=kOutput, calls=%fused_computation.31 | convolution fusion | flops 268435456 | bytes 4718592 | tf_op jit(solution)/shard_map/hqk,qhv->khv/dot_general | solution.py:64
  38.6 0.7 and_or_fusion
  39.3 7.5 %fusion.111 = (f32[8,256]{1,0:T(8,128)S(1)}, f32[8,256,768]{1,2,0:T(8,128)}) fusion(f32[8,768,256]{2,1,0:T(8,128)} %fusion.24, pred[256,768]{0,1:T(8,128)(4,1)S(1)} %and_or_fusion, bf16[768,64,1]{1,0,2:T(8,128)(2,1)S(1)} %maximum_bitcast_fusion, bf16[512,8,32]{0,2,1:T(8,128)(2,1)S(1)} %get-tuple-element.113, bf16[512,8,32]{0,2,1:T(8,128)(2,1)S(1)} %get-tuple-element.112), kind=kOutput, calls=%fused_computation.148 | convolution fusion | flops 209715968 | bytes 13410304 | tf_op jit(solution)/shard_map/sub | solution.py:47
  46.9 3.5 %fusion.9 = bf16[8,256,768]{1,2,0:T(8,128)(2,1)S(1)} fusion(f32[8,256,768]{1,2,0:T(8,128)} %get-tuple-element.131, f32[8,256]{1,0:T(8,128)S(1)} %get-tuple-element.130), kind=kLoop, calls=%fused_computation.24 | loop fusion | flops 3145728 | bytes 9445376 | tf_op jit(solution)/shard_map/convert_element_type | solution.py:49
  50.4 1.7 %copy-done.7 = bf16[8,256,768]{1,2,0:T(8,128)(2,1)} copy-done((bf16[8,256,768]{1,2,0:T(8,128)(2,1)}, bf16[8,256,768]{1,2,0:T(8,128)(2,1)S(1)}, u32[]{:S(2)}) %copy-start.7) | copy-done | bytes 3145752
  52.0 2.7 %fusion.47 = f32[256,8]{0,1:T(8,128)S(1)} fusion(bf16[8,256,768]{1,2,0:T(8,128)(2,1)S(1)} %fusion.9, bf16[768,8,256]{2,0,1:T(8,128)(2,1)S(1)} %copy-done.10, bf16[512,8,128]{2,0,1:T(8,128)(2,1)} %copy_select_fusion), kind=kOutput, calls=%fused_computation.54 | convolution fusion | flops 403437568 | bytes 5251072 | tf_op jit(solution)/shard_map/hqk,khv->qhv/dot_general | solution.py:50
  54.8 2.9 %multiply_convert_fusion = bf16[8,256,768]{1,2,0:T(8,128)(2,1)} fusion(f32[8,256]{1,0:T(8,128)S(1)} %bitcast.133, f32[8,256,768]{1,2,0:T(8,128)S(1)} %copy-done.5, f32[8,256]{1,0:T(8,128)S(1)} %get-tuple-element.130, bf16[768,8,256]{2,0,1:T(8,128)(2,1)S(1)} %copy-done.10, bf16[512,8,128]{2,0,1:T(8,128)(2,1)S(1)} %copy-done.15), kind=kOutput, calls=%fused_computation.5 | convolution fusion | flops 410517504 | bytes 11550720 | tf_op jit(solution)/shard_map/qhv,khv->hqk/dot_general | solution.py:52
  57.7 3.1 %fusion.57 = f32[768,64]{0,1:T(8,128)S(1)} fusion(bf16[8,256,768]{1,2,0:T(8,128)(2,1)} %multiply_convert_fusion, f32[512,64]{0,1:T(8,128)S(1)} %convolution_bitcast_fusion.6, bf16[512,8,32]{0,2,1:T(8,128)(2,1)S(1)} %get-tuple-element.113, bf16[512,8,32]{0,2,1:T(8,128)(2,1)S(1)} %get-tuple-element.112), kind=kOutput, calls=%fused_computation.61 | convolution fusion | flops 201900032 | bytes 3997696 | tf_op jit(solution)/shard_map/hqk,qhr->kr/dot_general | solution.py:63
  60.8 0.4 copy-done.12
  61.2 3.5 %fusion.8 = bf16[768,8,128]{0,2,1:T(8,128)(2,1)} fusion(f32[512,8,128]{0,2,1:T(8,128)S(1)} %copy-done.12, bf16[8,256,768]{1,2,0:T(8,128)(2,1)S(1)} %copy-done.1, bf16[512,8,192]{0,2,1:T(8,128)(2,1)} %param.25), kind=kOutput, calls=%fused_computation.22 | convolution fusion | flops 404226048 | bytes 7340032 | tf_op jit(solution)/shard_map/hqk,qhd->khd/dot_general | solution.py:60
  64.7 2.3 %fusion.7 = bf16[768,8,128]{0,2,1:T(8,128)(2,1)} fusion(f32[512,8,128]{0,2,1:T(8,128)S(1)} %copy-done.11, bf16[8,256,768]{1,2,0:T(8,128)(2,1)S(1)} %copy-done.8, bf16[512,8,128]{2,0,1:T(8,128)(2,1)S(1)} %copy-done.16), kind=kOutput, calls=%fused_computation.20 | convolution fusion | flops 404226048 | bytes 7340032 | tf_op jit(solution)/shard_map/hqk,qhv->khv/dot_general | solution.py:64
  67.2 2.2 %fusion.51 = f32[256,512]{1,0:T(8,128)S(1)} fusion(bf16[512,8,256]{2,1,0:T(8,128)(2,1)S(1)} %copy-done, bf16[768,8,128]{0,2,1:T(8,128)(2,1)} %fusion.8, bf16[768,8,128]{0,2,1:T(8,128)(2,1)} %fusion.7), kind=kOutput, calls=%fused_computation.56 | convolution fusion | flops 538968064 | bytes 5767168 | tf_op jit(solution)/shard_map/khd,lhd->kl/dot_general | solution.py:171
  69.5 0.8 fusion.77
  70.2 1.4 collective-permute-start.1
  71.9 2.1 %fusion.38 = bf16[512,512]{1,0:T(8,128)(2,1)} fusion(bf16[512,8,256]{2,1,0:T(8,128)(2,1)S(1)} %copy-done, bf16[768,8,128]{0,2,1:T(8,128)(2,1)S(1)} %copy-done.17, bf16[768,8,128]{0,2,1:T(8,128)(2,1)S(1)} %copy-done.18), kind=kOutput, calls=%fused_computation.50 | convolution fusion | flops 1078198272 | bytes 5767168 | tf_op jit(solution)/shard_map/khd,lhd->kl/dot_general | solution.py:156
  74.0 0.7 copy.265
  74.8 0.8 copy.264
  75.6 1.3 pad_maximum_fusion.4
  76.9 0.8 fusion.76
  77.6 1.7 %fusion.79 = f32[128,576]{1,0:T(8,128)} fusion(f32[128,576]{1,0:T(8,128)} %collective-permute-done.1, s32[]{:T(128)S(6)} %select_n.50, f32[256,512]{1,0:T(8,128)S(1)} %fusion.51, f32[256,64]{1,0:T(8,128)} %copy-done.25), kind=kLoop, calls=%fused_computation.102 | loop fusion | flops 147456 | bytes 1179652 | tf_op jit(solution)/shard_map/add | solution.py:178
  79.4 1.9 %reshape.413 = f32[64,2,576]{2,1,0:T(2,128)} reshape(f32[128,576]{1,0:T(8,128)} %fusion.79) | data formatting | bytes 589824 | tf_op jit(solution)/shard_map/reshape | solution.py:182
  81.3 11.5 %all-to-all-start.2 = ((f32[64,2,576]{2,1,0:T(2,128)}), f32[64,2,576]{2,1,0:T(2,128)S(1)}, u32[]{:S(2)}, u32[]{:S(2)}) async-start(f32[64,2,576]{2,1,0:T(2,128)} %reshape.413), calls=%async_computation.2 | async-start | bytes 655360 | tf_op jit(solution)/shard_map/all_to_all | solution.py:181
  92.8 1.8 %fusion.65 = bf16[8,32,576]{2,1,0:T(8,128)(2,1)} fusion(bf16[8,32,576]{2,1,0:T(8,128)(2,1)} %collective-permute-done, pred[]{:T(512)S(6)} %eq.2, bf16[8,2,32,576]{3,2,1,0:T(8,128)(2,1)S(1)} %pad_maximum_fusion.4), kind=kLoop, calls=%fused_computation.80 | loop fusion | flops 737280 | bytes 1179649 | tf_op jit(solution)/shard_map/convert_element_type | solution.py:168
  94.6 8.5 %all-to-all-done.2 = f32[64,2,576]{2,1,0:T(2,128)S(1)} async-done(((f32[64,2,576]{2,1,0:T(2,128)}), f32[64,2,576]{2,1,0:T(2,128)S(1)}, u32[]{:S(2)}, u32[]{:S(2)}) %all-to-all-start.2) | async-done | bytes 294944 | tf_op jit(solution)/shard_map/all_to_all | solution.py:181
  103.1 3.4 %all-to-all-start = ((bf16[8,32,576]{2,1,0:T(8,128)(2,1)}), bf16[8,32,576]{2,1,0:T(8,128)(2,1)S(1)}, u32[]{:S(2)}, u32[]{:S(2)}) async-start(bf16[8,32,576]{2,1,0:T(8,128)(2,1)} %fusion.65), calls=%async_computation | async-start | bytes 655360 | tf_op jit(solution)/shard_map/all_to_all | solution.py:169
  106.5 4.0 %fusion.13 = bf16[512,8,256]{2,0,1:T(8,128)(2,1)S(1)} fusion(bf16[768,8,128]{0,2,1:T(8,128)(2,1)} %fusion.7, bf16[768,8,128]{0,2,1:T(8,128)(2,1)} %fusion.8, bf16[768,576]{1,0:T(8,128)(2,1)} %copy-done.29), kind=kOutput, calls=%fused_computation.29 | convolution fusion | flops 1617952768 | bytes 6029312 | tf_op jit(solution)/shard_map/kl,khd->lhd/dot_general | solution.py:140
  110.5 1.6 copy.221
  112.2 1.1 all-to-all-done
  113.3 0.8 broadcast_in_dim.38
  114.2 5.5 %all-to-all-start.3 = ((f32[64,2,576]{2,1,0:T(2,128)}), f32[64,2,576]{2,1,0:T(2,128)S(1)}, u32[]{:S(2)}, u32[]{:S(2)}) async-start(f32[64,2,576]{2,1,0:T(2,128)} %broadcast_in_dim.38), calls=%async_computation.3 | async-start | bytes 655360 | tf_op jit(solution)/shard_map/all_to_all | solution.py:186
  119.7 2.6 %convolution_bitcast_fusion.3 = f32[256,8,64]{0,2,1:T(8,128)S(1)} fusion(bf16[768,64,1]{1,0,2:T(8,128)(2,1)S(1)} %maximum_bitcast_fusion, bf16[8,256,768]{1,2,0:T(8,128)(2,1)} %multiply_convert_fusion), kind=kOutput, calls=%fused_computation.57 | convolution fusion | flops 201326592 | bytes 3768320 | tf_op jit(solution)/shard_map/hqk,kr->qhr/dot_general | solution.py:59
  122.3 7.3 %all-to-all-done.3 = f32[64,2,576]{2,1,0:T(2,128)S(1)} async-done(((f32[64,2,576]{2,1,0:T(2,128)}), f32[64,2,576]{2,1,0:T(2,128)S(1)}, u32[]{:S(2)}, u32[]{:S(2)}) %all-to-all-start.3) | async-done | bytes 294944 | tf_op jit(solution)/shard_map/all_to_all | solution.py:186
  129.6 4.4 %all-to-all-start.1 = ((bf16[8,64,8,256]{3,1,2,0:T(8,128)(2,1)}), bf16[8,64,8,256]{3,1,2,0:T(8,128)(2,1)}, u32[]{:S(2)}, u32[]{:S(2)}) async-start(bf16[8,64,8,256]{3,1,2,0:T(8,128)(2,1)} %copy.221), calls=%async_computation.1 | async-start | bytes 4194304 | tf_op jit(solution)/shard_map/all_to_all | solution.py:150
  133.9 0.8 add_convert_fusion.1
  134.7 2.2 %convolution_bitcast_fusion.4 = f32[256,8,64]{0,2,1:T(8,128)S(1)} fusion(bf16[512,64,1]{1,0,2:T(8,128)(2,1)S(1)} %copy-done.27, bf16[8,256,512]{1,2,0:T(8,128)(2,1)} %copy-done.3), kind=kOutput, calls=%fused_computation.58 | convolution fusion | flops 134217728 | bytes 2686976 | tf_op jit(solution)/shard_map/hqk,kr->qhr/dot_general | solution.py:59
  137.0 0.8 add_convert_fusion.2
  137.7 1.8 %fusion.50 = bf16[256,8,128]{0,2,1:T(8,128)(2,1)S(1)} fusion(bf16[8,256,512]{1,2,0:T(8,128)(2,1)S(1)} %copy-done.4, bf16[768,8,256]{2,0,1:T(8,128)(2,1)} %copy-done.9), kind=kOutput, calls=%fused_computation.55 | convolution fusion | flops 268697600 | bytes 3670016 | tf_op jit(solution)/shard_map/hqk,khd->qhd/dot_general | solution.py:56
  139.5 2.2 %fusion.54 = bf16[256,8,128]{0,2,1:T(8,128)(2,1)S(1)} fusion(bf16[8,256,768]{1,2,0:T(8,128)(2,1)S(1)} %copy-done.2, bf16[768,8,256]{2,0,1:T(8,128)(2,1)} %copy-done.9), kind=kOutput, calls=%fused_computation.59 | convolution fusion | flops 402915328 | bytes 5242880 | tf_op jit(solution)/shard_map/hqk,khd->qhd/dot_general | solution.py:56
  141.7 2.0 %reshape.414 = f32[128,576]{1,0:T(8,128)} reshape(f32[64,2,576]{2,1,0:T(2,128)} %copy-done.23) | data formatting | bytes 589824 | tf_op jit(solution)/shard_map/reshape | solution.py:186
  143.7 3.4 %collective-permute-start.2 = (f32[128,576]{1,0:T(8,128)}, f32[128,576]{1,0:T(8,128)S(1)}, u32[]{:S(2)}, u32[]{:S(2)}) collective-permute-start(f32[128,576]{1,0:T(8,128)} %reshape.414), channel_id=1, source_target_pairs={{0,1},{1,0},{2,3},{3,2},{4,5},{5,4},{6,7},{7,6},{8,9},{9,8},{10,11... | collective-permute-start | bytes 884744 | tf_op jit(solution)/shard_map/ppermute | solution.py:69
  147.1 2.5 %maximum_maximum_fusion = bf16[512,8,192]{0,2,1:T(8,128)(2,1)} fusion(bf16[256,8,32]{0,2,1:T(8,128)(2,1)} %get-tuple-element.117, bf16[256,8,32]{0,2,1:T(8,128)(2,1)} %get-tuple-element.116, bf16[256,8,128]{0,2,1:T(8,128)(2,1)S(1)} %fusion.54, bf16[256,8,32]{0,2,1:T(8,128)(2,1)} %get-tuple-element.115, bf16[256,8,32]{0,2,1:T(8,128)(2,1)} %get-tuple-element.114, ...), kind=kLoop, calls=%fused_computation.37 | loop fusion | flops 9437184 | bytes 3145728 | tf_op jit(solution)/shard_map/concatenate | solution.py:144
  149.6 0.7 convert_reduce_fusion.1
  150.3 1.0 copy.227
  151.4 11.2 %all-to-all-done.1 = bf16[8,64,8,256]{3,1,2,0:T(8,128)(2,1)} async-done(((bf16[8,64,8,256]{3,1,2,0:T(8,128)(2,1)}), bf16[8,64,8,256]{3,1,2,0:T(8,128)(2,1)}, u32[]{:S(2)}, u32[]{:S(2)}) %all-to-all-start.1) | async-done | bytes 2097184 | tf_op jit(solution)/shard_map/all_to_all | solution.py:150
  162.5 2.0 %convert_reduce_fusion = f32[64,8,256]{2,0,1:T(8,128)S(1)} fusion(bf16[8,64,8,256]{3,1,2,0:T(8,128)(2,1)} %all-to-all-done.1), kind=kLoop, calls=%fused_computation.10 | loop fusion | flops 1966080 | bytes 2621440 | tf_op jit(solution)/shard_map/reduce_sum | solution.py:153
  164.6 1.1 copy.226
  (85 shorter events, 1.8 us)
Async XLA Ops:
  0.6 8.5 %copy-start = (bf16[512,8,256]{2,1,0:T(8,128)(2,1)S(1)}, bf16[512,8,256]{2,1,0:T(8,128)(2,1)}, u32[]{:S(2)}) copy-start(bf16[512,8,256]{2,1,0:T(8,128)(2,1)} %param.28) | copy-start | bytes 6291460
  5.7 13.6 %copy-start.30 = (f32[512,32]{0,1:T(8,128)}, f32[512,32]{0,1:T(8,128)S(1)}, u32[]{:S(2)}) copy-start(f32[512,32]{0,1:T(8,128)S(1)} %get-tuple-element.127) | copy-start | bytes 196612
  7.2 1.8 %copy-start.13 = (bf16[512,8,192]{0,2,1:T(8,128)(2,1)S(1)}, bf16[512,8,192]{0,2,1:T(8,128)(2,1)}, u32[]{:S(2)}) copy-start(bf16[512,8,192]{0,2,1:T(8,128)(2,1)} %param.25) | copy-start | bytes 4718596
  7.5 3.5 %copy-start.29 = (bf16[768,576]{1,0:T(8,128)(2,1)}, bf16[768,576]{1,0:T(8,128)(2,1)S(1)}, u32[]{:S(2)}) copy-start(bf16[768,576]{1,0:T(8,128)(2,1)S(1)} %maximum_maximum_fusion.1) | copy-start | bytes 2654212
  11.0 3.6 %copy-start.9 = (bf16[768,8,256]{2,0,1:T(8,128)(2,1)}, bf16[768,8,256]{2,0,1:T(8,128)(2,1)S(1)}, u32[]{:S(2)}) copy-start(bf16[768,8,256]{2,0,1:T(8,128)(2,1)S(1)} %convolution_convert_fusion) | copy-start | bytes 9437188
  14.6 3.5 %copy-start.28 = (bf16[512,8,128]{2,1,0:T(8,128)(2,1)S(1)}, bf16[512,8,128]{2,1,0:T(8,128)(2,1)}, u32[]{:S(2)}) copy-start(bf16[512,8,128]{2,1,0:T(8,128)(2,1)} %param.29) | copy-start | bytes 3145732
  17.4 2.3 %copy-start.26 = (bf16[512,64,1]{1,0,2:T(8,128)(2,1)S(1)}, bf16[512,64,1]{1,0,2:T(8,128)(2,1)}, u32[]{:S(2)}) copy-start(bf16[512,64,1]{1,0,2:T(8,128)(2,1)} %maximum_bitcast_fusion.1) | copy-start | bytes 196612
  25.5 2.7 %copy-start.14 = (bf16[512,8,128]{2,0,1:T(8,128)(2,1)S(1)}, bf16[512,8,128]{2,0,1:T(8,128)(2,1)}, u32[]{:S(2)}) copy-start(bf16[512,8,128]{2,0,1:T(8,128)(2,1)} %copy_select_fusion) | copy-start | bytes 3145732
  25.5 4.9 %copy-start.6 = (f32[8,256,512]{1,2,0:T(8,128)S(1)}, f32[8,256,512]{1,2,0:T(8,128)}, u32[]{:S(2)}) copy-start(f32[8,256,512]{1,2,0:T(8,128)} %get-tuple-element.133) | copy-start | bytes 12582916
  32.4 4.0 %copy-start.3 = (bf16[8,256,512]{1,2,0:T(8,128)(2,1)}, bf16[8,256,512]{1,2,0:T(8,128)(2,1)S(1)}, u32[]{:S(2)}) copy-start(bf16[8,256,512]{1,2,0:T(8,128)(2,1)S(1)} %multiply_convert_fusion.1) | copy-start | bytes 6291460
  46.9 5.2 %copy-start.10 = (bf16[768,8,256]{2,0,1:T(8,128)(2,1)S(1)}, bf16[768,8,256]{2,0,1:T(8,128)(2,1)}, u32[]{:S(2)}) copy-start(bf16[768,8,256]{2,0,1:T(8,128)(2,1)} %copy-done.9) | copy-start | bytes 9437188
  46.9 7.9 %copy-start.5 = (f32[8,256,768]{1,2,0:T(8,128)S(1)}, f32[8,256,768]{1,2,0:T(8,128)}, u32[]{:S(2)}) copy-start(f32[8,256,768]{1,2,0:T(8,128)} %get-tuple-element.131) | copy-start | bytes 18874372
  50.4 1.7 %copy-start.7 = (bf16[8,256,768]{1,2,0:T(8,128)(2,1)}, bf16[8,256,768]{1,2,0:T(8,128)(2,1)S(1)}, u32[]{:S(2)}) copy-start(bf16[8,256,768]{1,2,0:T(8,128)(2,1)S(1)} %fusion.9) | copy-start | bytes 9437188
  52.0 2.8 %copy-start.15 = (bf16[512,8,128]{2,0,1:T(8,128)(2,1)S(1)}, bf16[512,8,128]{2,0,1:T(8,128)(2,1)}, u32[]{:S(2)}) copy-start(bf16[512,8,128]{2,0,1:T(8,128)(2,1)} %copy_select_fusion) | copy-start | bytes 3145732
  57.7 3.1 %copy-start.1 = (bf16[8,256,768]{1,2,0:T(8,128)(2,1)S(1)}, bf16[8,256,768]{1,2,0:T(8,128)(2,1)}, u32[]{:S(2)}) copy-start(bf16[8,256,768]{1,2,0:T(8,128)(2,1)} %multiply_convert_fusion) | copy-start | bytes 9437188
  57.7 3.5 %copy-start.12 = (f32[512,8,128]{0,2,1:T(8,128)S(1)}, f32[512,8,128]{0,2,1:T(8,128)}, u32[]{:S(2)}) copy-start(f32[512,8,128]{0,2,1:T(8,128)} %convolution_bitcast_fusion.1) | copy-start | bytes 6291460
  61.2 5.9 %copy-start.19 = (f32[768,64]{0,1:T(8,128)}, f32[768,64]{0,1:T(8,128)S(1)}, u32[]{:S(2)}) copy-start(f32[768,64]{0,1:T(8,128)S(1)} %fusion.57) | copy-start | bytes 589828
  61.2 3.5 %copy-start.8 = (bf16[8,256,768]{1,2,0:T(8,128)(2,1)S(1)}, bf16[8,256,768]{1,2,0:T(8,128)(2,1)}, u32[]{:S(2)}) copy-start(bf16[8,256,768]{1,2,0:T(8,128)(2,1)} %copy-done.7) | copy-start | bytes 9437188
  61.2 3.5 %copy-start.11 = (f32[512,8,128]{0,2,1:T(8,128)S(1)}, f32[512,8,128]{0,2,1:T(8,128)}, u32[]{:S(2)}) copy-start(f32[512,8,128]{0,2,1:T(8,128)} %convolution_bitcast_fusion) | copy-start | bytes 6291460
  61.2 3.5 %copy-start.16 = (bf16[512,8,128]{2,0,1:T(8,128)(2,1)S(1)}, bf16[512,8,128]{2,0,1:T(8,128)(2,1)}, u32[]{:S(2)}) copy-start(bf16[512,8,128]{2,0,1:T(8,128)(2,1)} %copy_select_fusion) | copy-start | bytes 3145732
  67.2 2.3 %copy-start.25 = (f32[256,64]{1,0:T(8,128)}, f32[256,64]{1,0:T(8,128)S(1)}, u32[]{:S(2)}) copy-start(f32[256,64]{1,0:T(8,128)S(1)} %copy.225) | copy-start | bytes 196612
  67.2 4.4 %copy-start.20 = (f32[768,64]{0,1:T(8,128)S(1)}, f32[768,64]{0,1:T(8,128)}, u32[]{:S(2)}) copy-start(f32[768,64]{0,1:T(8,128)} %copy-done.19) | copy-start | bytes 589828
  67.2 4.7 %copy-start.17 = (bf16[768,8,128]{0,2,1:T(8,128)(2,1)S(1)}, bf16[768,8,128]{0,2,1:T(8,128)(2,1)}, u32[]{:S(2)}) copy-start(bf16[768,8,128]{0,2,1:T(8,128)(2,1)} %fusion.8) | copy-start | bytes 4718596
  67.2 4.7 %copy-start.18 = (bf16[768,8,128]{0,2,1:T(8,128)(2,1)S(1)}, bf16[768,8,128]{0,2,1:T(8,128)(2,1)}, u32[]{:S(2)}) copy-start(bf16[768,8,128]{0,2,1:T(8,128)(2,1)} %fusion.7) | copy-start | bytes 4718596
  70.2 7.4 %collective-permute-start.1 = (f32[128,576]{1,0:T(8,128)}, f32[128,576]{1,0:T(8,128)}, u32[]{:S(2)}, u32[]{:S(2)}) collective-permute-start(f32[128,576]{1,0:T(8,128)} %fusion.77), channel_id=1, source_target_pairs={{0,1},{1,0},{2,3},{3,2},{4,5},{5,4},{6,7},{7,6},{8,9},{9,8},{10,11... | collective-permute-start | bytes 884744 | tf_op jit(solution)/shard_map/ppermute | solution.py:69
  77.6 15.1 %collective-permute-start = (bf16[8,32,576]{2,1,0:T(8,128)(2,1)}, bf16[8,32,576]{2,1,0:T(8,128)(2,1)}, u32[]{:S(2)}, u32[]{:S(2)}) collective-permute-start(bf16[8,32,576]{2,1,0:T(8,128)(2,1)} %fusion.76), channel_id=1, source_target_pairs={{0,1},{1,0},{2,3},{3,2},{4,5},{5,4},{6,7},{7,6},{8,9},{9,8},{10,11... | collective-permute-start | bytes 884744 | tf_op jit(solution)/shard_map/ppermute | solution.py:69
  81.3 21.8 %all-to-all-start.2 = ((f32[64,2,576]{2,1,0:T(2,128)}), f32[64,2,576]{2,1,0:T(2,128)S(1)}, u32[]{:S(2)}, u32[]{:S(2)}) async-start(f32[64,2,576]{2,1,0:T(2,128)} %reshape.413), calls=%async_computation.2 | async-start | bytes 655360 | tf_op jit(solution)/shard_map/all_to_all | solution.py:181
  103.1 10.2 %all-to-all-start = ((bf16[8,32,576]{2,1,0:T(8,128)(2,1)}), bf16[8,32,576]{2,1,0:T(8,128)(2,1)S(1)}, u32[]{:S(2)}, u32[]{:S(2)}) async-start(bf16[8,32,576]{2,1,0:T(8,128)(2,1)} %fusion.65), calls=%async_computation | async-start | bytes 655360 | tf_op jit(solution)/shard_map/all_to_all | solution.py:169
  110.5 1.6 copy-start.31
  113.3 0.8 copy-start.21
  114.2 15.4 %all-to-all-start.3 = ((f32[64,2,576]{2,1,0:T(2,128)}), f32[64,2,576]{2,1,0:T(2,128)S(1)}, u32[]{:S(2)}, u32[]{:S(2)}) async-start(f32[64,2,576]{2,1,0:T(2,128)} %broadcast_in_dim.38), calls=%async_computation.3 | async-start | bytes 655360 | tf_op jit(solution)/shard_map/all_to_all | solution.py:186
  122.3 12.4 %copy-start.27 = (bf16[512,64,1]{1,0,2:T(8,128)(2,1)S(1)}, bf16[512,64,1]{1,0,2:T(8,128)(2,1)}, u32[]{:S(2)}) copy-start(bf16[512,64,1]{1,0,2:T(8,128)(2,1)} %maximum_bitcast_fusion.1) | copy-start | bytes 196612
  129.6 7.4 %copy-start.23 = (f32[64,2,576]{2,1,0:T(2,128)}, f32[64,2,576]{2,1,0:T(2,128)S(1)}, u32[]{:S(2)}) copy-start(f32[64,2,576]{2,1,0:T(2,128)S(1)} %all-to-all-done.3) | copy-start | bytes 884740
  129.6 33.0 %all-to-all-start.1 = ((bf16[8,64,8,256]{3,1,2,0:T(8,128)(2,1)}), bf16[8,64,8,256]{3,1,2,0:T(8,128)(2,1)}, u32[]{:S(2)}, u32[]{:S(2)}) async-start(bf16[8,64,8,256]{3,1,2,0:T(8,128)(2,1)} %copy.221), calls=%async_computation.1 | async-start | bytes 4194304 | tf_op jit(solution)/shard_map/all_to_all | solution.py:150
  133.9 3.8 %copy-start.4 = (bf16[8,256,512]{1,2,0:T(8,128)(2,1)S(1)}, bf16[8,256,512]{1,2,0:T(8,128)(2,1)}, u32[]{:S(2)}) copy-start(bf16[8,256,512]{1,2,0:T(8,128)(2,1)} %copy-done.3) | copy-start | bytes 6291460
  134.7 4.8 %copy-start.2 = (bf16[8,256,768]{1,2,0:T(8,128)(2,1)S(1)}, bf16[8,256,768]{1,2,0:T(8,128)(2,1)}, u32[]{:S(2)}) copy-start(bf16[8,256,768]{1,2,0:T(8,128)(2,1)} %multiply_convert_fusion) | copy-start | bytes 9437188
  141.7 7.9 %copy-start.22 = (bf16[8,32,576]{2,1,0:T(8,128)(2,1)S(1)}, bf16[8,32,576]{2,1,0:T(8,128)(2,1)}, u32[]{:S(2)}) copy-start(bf16[8,32,576]{2,1,0:T(8,128)(2,1)} %copy-done.21) | copy-start | bytes 884740
  143.7 6.6 %copy-start.24 = (f32[128,576]{1,0:T(8,128)S(1)}, f32[128,576]{1,0:T(8,128)}, u32[]{:S(2)}) copy-start(f32[128,576]{1,0:T(8,128)} %reshape.414) | copy-start | bytes 884740
  143.7 6.6 %collective-permute-start.2 = (f32[128,576]{1,0:T(8,128)}, f32[128,576]{1,0:T(8,128)S(1)}, u32[]{:S(2)}, u32[]{:S(2)}) collective-permute-start(f32[128,576]{1,0:T(8,128)} %reshape.414), channel_id=1, source_target_pairs={{0,1},{1,0},{2,3},{3,2},{4,5},{5,4},{6,7},{7,6},{8,9},{9,8},{10,11... | collective-permute-start | bytes 884744 | tf_op jit(solution)/shard_map/ppermute | solution.py:69

commit v6 on v3

--- a/solution.py
+++ b/solution.py
@@ -67,12 +67,6 @@
 
 def swap_pair(values):
     return lax.ppermute(values, "core", [(0, 1), (1, 0)])
-
-
-def gather_copies(values, axis, size):
-    copies = jnp.broadcast_to(values[None], (size,) + values.shape)
-    gathered = lax.all_to_all(copies, axis, 0, 0, tiled=False)
-    return gathered.reshape((size * values.shape[0],) + values.shape[1:])
 
 
 def on_device(queries, latent, prefix, kv_up, out_grad, lengths, positions):
@@ -188,7 +182,7 @@
     )
     prefix_own = jnp.sum(
         lax.all_to_all(
-            prefix_rows_part.reshape((dp_size, -1) + prefix_rows_part.shape[1:]),
+            jnp.broadcast_to(prefix_rows_part[None], (dp_size,) + prefix_rows_part.shape),
             "dp",
             0,
             0,
@@ -196,8 +190,10 @@
         ),
         axis=0,
     )
-    prefix_rows_full = gather_copies(prefix_own, "dp", dp_size)
-    prefix_gathered = gather_copies(prefix_rows_full, "hr", row_size)
+    prefix_copies = jnp.broadcast_to(prefix_own[None], (row_size,) + prefix_own.shape)
+    prefix_gathered = lax.all_to_all(prefix_copies, "hr", 0, 0, tiled=False).reshape(
+        prefix_half.shape
+    )
     prefix_partner = swap_pair(prefix_gathered)
     prefix_grad = jnp.where(
         core == 0,

time: 174 us -> 166 us (0.954)
  blocking collectives: 26.7 us -> 13.1 us
  waiting for transfers between devices: 20.5 us -> 24.2 us
  starting transfers between devices: 22.4 us -> 24.6 us
    all_to_all x1 -> x0, blocking collectives: 13.6 us -> none  [on_device(): lax.all_to_all(prefix_rows_part.reshape((dp_size, -1) + prefix_rows_part....]
    all_to_all x2, starting transfers between devices: 7.37 us -> 11.2 us  [the longest x1 7.2 us: on_device(): lax.all_to_all(jnp.broadcast_to(prefix_rows_part[None], (dp_size,) + pref...]
    all_to_all x2, waiting for transfers between devices: 6.34 us -> 8.21 us  [the longest x1 6.56 us: on_device(): lax.all_to_all(jnp.broadcast_to(prefix_rows_part[None], (dp_size,) + pref...]
    all_to_all x1, waiting for transfers between devices: 13.3 us -> 15.1 us  [on_device(): lax.all_to_all(up_part.astype(jnp.bfloat16).reshape((dp_size, -1) + up_pa...]
  transfers between devices with their start and end apart: 7 -> 7, of which waited for: 4 -> 4; matrix products, arithmetic and copies ran while one was open for 17% -> 18% of each run, Pallas kernels for 0% -> 0%
where the time goes in v6:
time: 166 us; the launch traced here: 165 us
  matrix products  64.9 us (39%)
  starting transfers between devices  24.6 us (15%)
  waiting for transfers between devices  24.2 us (15%)
  other arithmetic  21.9 us (13%)
  local copies, waits for them, and re-layouts  14.8 us (9%)
  blocking collectives  13.1 us (8%)
  between operations  1.84 us (1%)
    all_to_all x1, waiting for transfers between devices, on_device(): lax.all_to_all(up_part.astype(jnp.bfloat16).reshape((dp_size, -1) + up_pa...  15.1 us
    sub x2, matrix products, block_gradients(): exponent = jnp.exp(scores - highest)  13.3 us
    all_to_all x1, blocking collectives, on_device(): lax.all_to_all(prefix_half.reshape((row_size, -1) + prefix_half.shape[1:]...  13.1 us
    unnamed x66, local copies, waits for them, and re-layouts  7.49 us
    all_to_all x1, starting transfers between devices, on_device(): lax.all_to_all(jnp.broadcast_to(prefix_rows_part[None], (dp_size,) + pref...  7.2 us
    dot_general x2, matrix products, block_gradients(): jnp.einsum('hqk,qhd->khd', score_grad, query_nope, preferred_element_type...  6.77 us
    all_to_all x1, waiting for transfers between devices, on_device(): lax.all_to_all(jnp.broadcast_to(prefix_rows_part[None], (dp_size,) + pref...  6.56 us
    dot_general x2, matrix products, block_gradients(): jnp.einsum('qhd,khd->hqk', query_nope, key_nope, preferred_element_type=j...  6.37 us
  transfers between devices with their start and end apart: 7, of which 4 were waited for; matrix products, arithmetic and copies ran while one was open for 18% of the time, Pallas kernels for 0%

profile of v6, /device:TPU:1, one launch (start us, length us, event | category | flops | bytes accessed | tf_op | source)
XLA Modules:
  0.0 165.3 jit_solution(3196999254175690209)
XLA Ops:
  0.7 1.0 slice_convert_fusion.1
  1.7 1.9 %slice.226 = bf16[512,512]{0,1:T(8,128)(2,1)} slice(bf16[512,576]{0,1:T(8,128)(2,1)} %param.26), slice={[0:512], [0:512]} | slice | bytes 1048576 | tf_op jit(solution)/shard_map/slice | solution.py:89
  3.5 1.2 copy.235
  4.7 0.7 convert_element_type.66
  5.4 0.3 multiply_cosine_fusion
  6.0 1.3 copy.325
  7.5 0.7 maximum_bitcast_fusion.1
  8.3 0.8 copy-done.13
  9.2 1.8 %convolution_convert_fusion = bf16[768,8,256]{2,0,1:T(8,128)(2,1)S(1)} fusion(bf16[512,8,256]{2,1,0:T(8,128)(2,1)S(1)} %copy-done, bf16[768,576]{1,0:T(8,128)(2,1)S(1)} %maximum_maximum_fusion.1), kind=kOutput, calls=%fused_computation.25 | convolution fusion | flops 1612185600 | bytes 6029312 | tf_op jit(solution)/shard_map/kl,lhd->khd/dot_general | solution.py:98
  11.0 3.6 %fusion.24 = f32[8,768,256]{2,1,0:T(8,128)} fusion(bf16[768,8,256]{2,0,1:T(8,128)(2,1)S(1)} %convolution_convert_fusion, bf16[512,8,192]{0,2,1:T(8,128)(2,1)S(1)} %copy-done.13), kind=kOutput, calls=%fused_computation.43 | convolution fusion | flops 402653184 | bytes 8388608 | tf_op jit(solution)/shard_map/qhd,khd->hqk/dot_general | solution.py:37
  14.6 2.7 %fusion.63 = f32[8,512,256]{2,1,0:T(8,128)} fusion(bf16[768,8,256]{2,0,1:T(8,128)(2,1)S(1)} %convolution_convert_fusion, bf16[512,8,192]{0,2,1:T(8,128)(2,1)S(1)} %copy-done.13), kind=kOutput, calls=%fused_computation.69 | convolution fusion | flops 268435456 | bytes 5767168 | tf_op jit(solution)/shard_map/qhd,khd->hqk/dot_general | solution.py:37
  18.1 1.2 copy_select_fusion
  19.8 5.7 %fusion.112 = (f32[8,256]{1,0:T(8,128)S(1)}, f32[8,256,512]{1,2,0:T(8,128)}) fusion(f32[8,512,256]{2,1,0:T(8,128)} %fusion.63, bf16[512,64,1]{1,0,2:T(8,128)(2,1)S(1)} %copy-done.23, pred[256,512]{0,1:T(8,128)(4,1)S(1)} %fusion.67, bf16[512,8,32]{0,2,1:T(8,128)(2,1)S(1)} %get-tuple-element.116, bf16[512,8,32]{0,2,1:T(8,128)(2,1)S(1)} %get-tuple-element.117), kind=kOutput, calls=%fused_computation.149 | convolution fusion | flops 139985408 | bytes 9117696 | tf_op jit(solution)/shard_map/sub | solution.py:47
  25.5 2.7 %fusion.14 = bf16[8,256,512]{1,2,0:T(8,128)(2,1)S(1)} fusion(f32[8,256,512]{1,2,0:T(8,128)} %get-tuple-element.137, f32[8,256]{1,0:T(8,128)S(1)} %get-tuple-element.136), kind=kLoop, calls=%fused_computation.30 | loop fusion | flops 2097152 | bytes 6299648 | tf_op jit(solution)/shard_map/convert_element_type | solution.py:49
  28.2 2.2 %fusion.46 = f32[256,8]{0,1:T(8,128)S(1)} fusion(bf16[8,256,512]{1,2,0:T(8,128)(2,1)S(1)} %fusion.14, bf16[768,8,256]{2,0,1:T(8,128)(2,1)} %copy-done.9, bf16[512,8,128]{2,0,1:T(8,128)(2,1)S(1)} %copy-done.14), kind=kOutput, calls=%fused_computation.53 | convolution fusion | flops 269219840 | bytes 3678208 | tf_op jit(solution)/shard_map/hqk,khv->qhv/dot_general | solution.py:50
  30.4 2.0 %multiply_convert_fusion.1 = bf16[8,256,512]{1,2,0:T(8,128)(2,1)S(1)} fusion(f32[8,256]{1,0:T(8,128)S(1)} %bitcast.137, f32[8,256,512]{1,2,0:T(8,128)S(1)} %copy-done.6, f32[8,256]{1,0:T(8,128)S(1)} %get-tuple-element.136, bf16[768,8,256]{2,0,1:T(8,128)(2,1)} %copy-done.9, bf16[512,8,128]{2,0,1:T(8,128)(2,1)S(1)} %copy-done.14), kind=kOutput, calls=%fused_computation.11 | convolution fusion | flops 273678336 | bytes 7880704 | tf_op jit(solution)/shard_map/qhv,khv->hqk/dot_general | solution.py:52
  32.5 0.7 convolution_bitcast_fusion.6
  33.2 3.2 %convolution_bitcast_fusion.1 = f32[512,8,128]{0,2,1:T(8,128)} fusion(bf16[8,256,512]{1,2,0:T(8,128)(2,1)S(1)} %multiply_convert_fusion.1, bf16[512,8,192]{0,2,1:T(8,128)(2,1)} %param.25), kind=kOutput, calls=%fused_computation.32 | convolution fusion | flops 268435456 | bytes 4718592 | tf_op jit(solution)/shard_map/hqk,qhd->khd/dot_general | solution.py:60
  36.5 2.1 %convolution_bitcast_fusion = f32[512,8,128]{0,2,1:T(8,128)} fusion(bf16[8,256,512]{1,2,0:T(8,128)(2,1)S(1)} %fusion.14, bf16[512,8,128]{2,0,1:T(8,128)(2,1)S(1)} %copy-done.14), kind=kOutput, calls=%fused_computation.31 | convolution fusion | flops 268435456 | bytes 4718592 | tf_op jit(solution)/shard_map/hqk,qhv->khv/dot_general | solution.py:64
  38.6 0.7 and_or_fusion
  39.3 7.5 %fusion.111 = (f32[8,256]{1,0:T(8,128)S(1)}, f32[8,256,768]{1,2,0:T(8,128)}) fusion(f32[8,768,256]{2,1,0:T(8,128)} %fusion.24, pred[256,768]{0,1:T(8,128)(4,1)S(1)} %and_or_fusion, bf16[768,64,1]{1,0,2:T(8,128)(2,1)S(1)} %maximum_bitcast_fusion, bf16[512,8,32]{0,2,1:T(8,128)(2,1)S(1)} %get-tuple-element.117, bf16[512,8,32]{0,2,1:T(8,128)(2,1)S(1)} %get-tuple-element.116), kind=kOutput, calls=%fused_computation.148 | convolution fusion | flops 209715968 | bytes 13410304 | tf_op jit(solution)/shard_map/sub | solution.py:47
  46.9 3.5 %fusion.9 = bf16[8,256,768]{1,2,0:T(8,128)(2,1)S(1)} fusion(f32[8,256,768]{1,2,0:T(8,128)} %get-tuple-element.135, f32[8,256]{1,0:T(8,128)S(1)} %get-tuple-element.134), kind=kLoop, calls=%fused_computation.24 | loop fusion | flops 3145728 | bytes 9445376 | tf_op jit(solution)/shard_map/convert_element_type | solution.py:49
  50.4 1.7 %copy-done.7 = bf16[8,256,768]{1,2,0:T(8,128)(2,1)} copy-done((bf16[8,256,768]{1,2,0:T(8,128)(2,1)}, bf16[8,256,768]{1,2,0:T(8,128)(2,1)S(1)}, u32[]{:S(2)}) %copy-start.7) | copy-done | bytes 3145752
  52.0 2.8 %fusion.47 = f32[256,8]{0,1:T(8,128)S(1)} fusion(bf16[8,256,768]{1,2,0:T(8,128)(2,1)S(1)} %fusion.9, bf16[768,8,256]{2,0,1:T(8,128)(2,1)S(1)} %copy-done.10, bf16[512,8,128]{2,0,1:T(8,128)(2,1)} %copy_select_fusion), kind=kOutput, calls=%fused_computation.54 | convolution fusion | flops 403437568 | bytes 5251072 | tf_op jit(solution)/shard_map/hqk,khv->qhv/dot_general | solution.py:50
  54.8 2.9 %multiply_convert_fusion = bf16[8,256,768]{1,2,0:T(8,128)(2,1)} fusion(f32[8,256]{1,0:T(8,128)S(1)} %bitcast.138, f32[8,256,768]{1,2,0:T(8,128)S(1)} %copy-done.5, f32[8,256]{1,0:T(8,128)S(1)} %get-tuple-element.134, bf16[768,8,256]{2,0,1:T(8,128)(2,1)S(1)} %copy-done.10, bf16[512,8,128]{2,0,1:T(8,128)(2,1)S(1)} %copy-done.15), kind=kOutput, calls=%fused_computation.5 | convolution fusion | flops 410517504 | bytes 11550720 | tf_op jit(solution)/shard_map/qhv,khv->hqk/dot_general | solution.py:52
  57.7 3.1 %fusion.57 = f32[768,64]{0,1:T(8,128)S(1)} fusion(bf16[8,256,768]{1,2,0:T(8,128)(2,1)} %multiply_convert_fusion, f32[512,64]{0,1:T(8,128)S(1)} %convolution_bitcast_fusion.6, bf16[512,8,32]{0,2,1:T(8,128)(2,1)S(1)} %get-tuple-element.117, bf16[512,8,32]{0,2,1:T(8,128)(2,1)S(1)} %get-tuple-element.116), kind=kOutput, calls=%fused_computation.61 | convolution fusion | flops 201900032 | bytes 3997696 | tf_op jit(solution)/shard_map/hqk,qhr->kr/dot_general | solution.py:63
  60.8 0.4 copy-done.12
  61.2 3.5 %fusion.8 = bf16[768,8,128]{0,2,1:T(8,128)(2,1)} fusion(f32[512,8,128]{0,2,1:T(8,128)S(1)} %copy-done.12, bf16[8,256,768]{1,2,0:T(8,128)(2,1)S(1)} %copy-done.1, bf16[512,8,192]{0,2,1:T(8,128)(2,1)} %param.25), kind=kOutput, calls=%fused_computation.22 | convolution fusion | flops 404226048 | bytes 7340032 | tf_op jit(solution)/shard_map/hqk,qhd->khd/dot_general | solution.py:60
  64.7 2.3 %fusion.7 = bf16[768,8,128]{0,2,1:T(8,128)(2,1)} fusion(f32[512,8,128]{0,2,1:T(8,128)S(1)} %copy-done.11, bf16[8,256,768]{1,2,0:T(8,128)(2,1)S(1)} %copy-done.8, bf16[512,8,128]{2,0,1:T(8,128)(2,1)S(1)} %copy-done.16), kind=kOutput, calls=%fused_computation.20 | convolution fusion | flops 404226048 | bytes 7340032 | tf_op jit(solution)/shard_map/hqk,qhv->khv/dot_general | solution.py:64
  67.2 2.2 %fusion.51 = f32[256,512]{1,0:T(8,128)S(1)} fusion(bf16[512,8,256]{2,1,0:T(8,128)(2,1)S(1)} %copy-done, bf16[768,8,128]{0,2,1:T(8,128)(2,1)} %fusion.8, bf16[768,8,128]{0,2,1:T(8,128)(2,1)} %fusion.7), kind=kOutput, calls=%fused_computation.56 | convolution fusion | flops 538968064 | bytes 5767168 | tf_op jit(solution)/shard_map/khd,lhd->kl/dot_general | solution.py:169
  69.5 0.8 fusion.77
  70.2 1.4 collective-permute-start.1
  71.6 0.3 fusion.95
  71.9 2.1 %fusion.38 = bf16[512,512]{1,0:T(8,128)(2,1)} fusion(bf16[512,8,256]{2,1,0:T(8,128)(2,1)S(1)} %copy-done, bf16[768,8,128]{0,2,1:T(8,128)(2,1)S(1)} %copy-done.18, bf16[768,8,128]{0,2,1:T(8,128)(2,1)S(1)} %copy-done.19), kind=kOutput, calls=%fused_computation.50 | convolution fusion | flops 1078198272 | bytes 5767168 | tf_op jit(solution)/shard_map/khd,lhd->kl/dot_general | solution.py:154
  74.1 0.8 copy.322
  74.8 0.8 copy.321
  75.6 1.3 pad_maximum_fusion.4
  76.9 0.8 fusion.76
  77.7 1.0 fusion.79
  78.7 13.1 %all_to_all.25 = f32[8,16,576]{2,1,0:T(8,128)S(1)} all-to-all(f32[8,16,576]{2,1,0:T(8,128)S(1)} %bitcast.131), channel_id=1, replica_groups=mesh['dp'=8,'hr'=8,'core'=2] {'hr'}, dimensions={0} | all-to-all | bytes 589824 | tf_op jit(solution)/shard_map/all_to_all | solution.py:178
  91.7 0.7 broadcast_in_dim.44
  92.5 7.2 %all-to-all-start.3 = ((f32[8,16,576]{2,1,0:T(8,128)}), f32[8,16,576]{2,1,0:T(8,128)S(1)}, u32[]{:S(2)}, u32[]{:S(2)}) async-start(f32[8,16,576]{2,1,0:T(8,128)} %broadcast_in_dim.44), calls=%async_computation.3 | async-start | bytes 655360 | tf_op jit(solution)/shard_map/all_to_all | solution.py:184
  99.7 1.8 %fusion.65 = bf16[8,32,576]{2,1,0:T(8,128)(2,1)} fusion(bf16[8,32,576]{2,1,0:T(8,128)(2,1)} %collective-permute-done, pred[]{:T(512)S(6)} %eq.2, bf16[8,2,32,576]{3,2,1,0:T(8,128)(2,1)S(1)} %pad_maximum_fusion.4), kind=kLoop, calls=%fused_computation.80 | loop fusion | flops 737280 | bytes 1179649 | tf_op jit(solution)/shard_map/convert_element_type | solution.py:166
  101.5 6.6 %all-to-all-done.3 = f32[8,16,576]{2,1,0:T(8,128)S(1)} async-done(((f32[8,16,576]{2,1,0:T(8,128)}), f32[8,16,576]{2,1,0:T(8,128)S(1)}, u32[]{:S(2)}, u32[]{:S(2)}) %all-to-all-start.3) | async-done | bytes 294944 | tf_op jit(solution)/shard_map/all_to_all | solution.py:184
  108.1 3.7 %all-to-all-start = ((bf16[8,32,576]{2,1,0:T(8,128)(2,1)}), bf16[8,32,576]{2,1,0:T(8,128)(2,1)S(1)}, u32[]{:S(2)}, u32[]{:S(2)}) async-start(bf16[8,32,576]{2,1,0:T(8,128)(2,1)} %fusion.65), calls=%async_computation | async-start | bytes 655360 | tf_op jit(solution)/shard_map/all_to_all | solution.py:167
  111.7 5.3 %fusion.13 = bf16[512,8,256]{2,0,1:T(8,128)(2,1)} fusion(bf16[768,8,128]{0,2,1:T(8,128)(2,1)} %fusion.7, bf16[768,8,128]{0,2,1:T(8,128)(2,1)} %fusion.8, bf16[768,576]{1,0:T(8,128)(2,1)} %copy-done.26), kind=kOutput, calls=%fused_computation.29 | convolution fusion | flops 1617952768 | bytes 6029312 | tf_op jit(solution)/shard_map/kl,khd->lhd/dot_general | solution.py:138
  117.1 0.9 all-to-all-done
  118.0 0.7 broadcast_in_dim.45
  118.7 4.0 %all-to-all-start.4 = ((f32[8,16,576]{2,1,0:T(8,128)}), f32[8,16,576]{2,1,0:T(8,128)S(1)}, u32[]{:S(2)}, u32[]{:S(2)}) async-start(f32[8,16,576]{2,1,0:T(8,128)} %broadcast_in_dim.45), calls=%async_computation.4 | async-start | bytes 655360 | tf_op jit(solution)/shard_map/all_to_all | solution.py:194
  122.7 2.7 %convolution_bitcast_fusion.3 = f32[256,8,64]{0,2,1:T(8,128)S(1)} fusion(bf16[768,64,1]{1,0,2:T(8,128)(2,1)S(1)} %maximum_bitcast_fusion, bf16[8,256,768]{1,2,0:T(8,128)(2,1)} %multiply_convert_fusion), kind=kOutput, calls=%fused_computation.57 | convolution fusion | flops 201326592 | bytes 3768320 | tf_op jit(solution)/shard_map/hqk,kr->qhr/dot_general | solution.py:59
  125.5 1.5 copy.278
  127.0 0.6 fusion.109
  127.6 1.6 all-to-all-done.4
  129.2 4.3 %all-to-all-start.1 = ((bf16[8,64,8,256]{3,1,2,0:T(8,128)(2,1)}), bf16[8,64,8,256]{3,1,2,0:T(8,128)(2,1)}, u32[]{:S(2)}, u32[]{:S(2)}) async-start(bf16[8,64,8,256]{3,1,2,0:T(8,128)(2,1)} %copy.278), calls=%async_computation.1 | async-start | bytes 4194304 | tf_op jit(solution)/shard_map/all_to_all | solution.py:148
  133.7 2.2 %convolution_bitcast_fusion.4 = f32[256,8,64]{0,2,1:T(8,128)S(1)} fusion(bf16[512,64,1]{1,0,2:T(8,128)(2,1)S(1)} %copy-done.24, bf16[8,256,512]{1,2,0:T(8,128)(2,1)} %copy-done.3), kind=kOutput, calls=%fused_computation.58 | convolution fusion | flops 134217728 | bytes 2686976 | tf_op jit(solution)/shard_map/hqk,kr->qhr/dot_general | solution.py:59
  136.1 1.8 %fusion.50 = bf16[256,8,128]{0,2,1:T(8,128)(2,1)S(1)} fusion(bf16[8,256,512]{1,2,0:T(8,128)(2,1)S(1)} %copy-done.4, bf16[768,8,256]{2,0,1:T(8,128)(2,1)} %copy-done.9), kind=kOutput, calls=%fused_computation.55 | convolution fusion | flops 268697600 | bytes 3670016 | tf_op jit(solution)/shard_map/hqk,khd->qhd/dot_general | solution.py:56
  137.9 2.2 %fusion.54 = bf16[256,8,128]{0,2,1:T(8,128)(2,1)S(1)} fusion(bf16[8,256,768]{1,2,0:T(8,128)(2,1)S(1)} %copy-done.2, bf16[768,8,256]{2,0,1:T(8,128)(2,1)} %copy-done.9), kind=kOutput, calls=%fused_computation.59 | convolution fusion | flops 402915328 | bytes 5242880 | tf_op jit(solution)/shard_map/hqk,khd->qhd/dot_general | solution.py:56
  140.0 4.0 %collective-permute-start.2 = (f32[128,576]{1,0:T(8,128)S(1)}, f32[128,576]{1,0:T(8,128)S(1)}, u32[]{:S(2)}, u32[]{:S(2)}) collective-permute-start(f32[128,576]{1,0:T(8,128)S(1)} %bitcast.129), channel_id=1, source_target_pairs={{0,1},{1,0},{2,3},{3,2},{4,5},{5,4},{6,7},{7,6},{8,9},{9,8},{10,11... | collective-permute-start | bytes 884744 | tf_op jit(solution)/shard_map/ppermute | solution.py:69
  144.1 1.3 maximum_maximum_fusion
  145.3 0.7 convert_reduce_fusion.1
  146.1 1.0 copy.284
  147.1 15.1 %all-to-all-done.1 = bf16[8,64,8,256]{3,1,2,0:T(8,128)(2,1)} async-done(((bf16[8,64,8,256]{3,1,2,0:T(8,128)(2,1)}), bf16[8,64,8,256]{3,1,2,0:T(8,128)(2,1)}, u32[]{:S(2)}, u32[]{:S(2)}) %all-to-all-start.1) | async-done | bytes 2097184 | tf_op jit(solution)/shard_map/all_to_all | solution.py:148
  162.2 2.0 %convert_reduce_fusion = f32[64,8,256]{2,0,1:T(8,128)S(1)} fusion(bf16[8,64,8,256]{3,1,2,0:T(8,128)(2,1)} %all-to-all-done.1), kind=kLoop, calls=%fused_computation.10 | loop fusion | flops 1966080 | bytes 2621440 | tf_op jit(solution)/shard_map/reduce_sum | solution.py:151
  164.2 1.1 copy.283
  (84 shorter events, 1.6 us)
Async XLA Ops:
  0.6 8.5 %copy-start = (bf16[512,8,256]{2,1,0:T(8,128)(2,1)S(1)}, bf16[512,8,256]{2,1,0:T(8,128)(2,1)}, u32[]{:S(2)}) copy-start(bf16[512,8,256]{2,1,0:T(8,128)(2,1)} %param.28) | copy-start | bytes 6291460
  5.7 13.6 %copy-start.27 = (f32[512,32]{0,1:T(8,128)}, f32[512,32]{0,1:T(8,128)S(1)}, u32[]{:S(2)}) copy-start(f32[512,32]{0,1:T(8,128)S(1)} %get-tuple-element.131) | copy-start | bytes 196612
  7.2 1.8 %copy-start.13 = (bf16[512,8,192]{0,2,1:T(8,128)(2,1)S(1)}, bf16[512,8,192]{0,2,1:T(8,128)(2,1)}, u32[]{:S(2)}) copy-start(bf16[512,8,192]{0,2,1:T(8,128)(2,1)} %param.25) | copy-start | bytes 4718596
  7.5 3.5 %copy-start.26 = (bf16[768,576]{1,0:T(8,128)(2,1)}, bf16[768,576]{1,0:T(8,128)(2,1)S(1)}, u32[]{:S(2)}) copy-start(bf16[768,576]{1,0:T(8,128)(2,1)S(1)} %maximum_maximum_fusion.1) | copy-start | bytes 2654212
  11.0 3.6 %copy-start.9 = (bf16[768,8,256]{2,0,1:T(8,128)(2,1)}, bf16[768,8,256]{2,0,1:T(8,128)(2,1)S(1)}, u32[]{:S(2)}) copy-start(bf16[768,8,256]{2,0,1:T(8,128)(2,1)S(1)} %convolution_convert_fusion) | copy-start | bytes 9437188
  14.6 3.5 %copy-start.25 = (bf16[512,8,128]{2,1,0:T(8,128)(2,1)S(1)}, bf16[512,8,128]{2,1,0:T(8,128)(2,1)}, u32[]{:S(2)}) copy-start(bf16[512,8,128]{2,1,0:T(8,128)(2,1)} %param.29) | copy-start | bytes 3145732
  17.4 2.4 %copy-start.23 = (bf16[512,64,1]{1,0,2:T(8,128)(2,1)S(1)}, bf16[512,64,1]{1,0,2:T(8,128)(2,1)}, u32[]{:S(2)}) copy-start(bf16[512,64,1]{1,0,2:T(8,128)(2,1)} %maximum_bitcast_fusion.1) | copy-start | bytes 196612
  25.5 2.7 %copy-start.14 = (bf16[512,8,128]{2,0,1:T(8,128)(2,1)S(1)}, bf16[512,8,128]{2,0,1:T(8,128)(2,1)}, u32[]{:S(2)}) copy-start(bf16[512,8,128]{2,0,1:T(8,128)(2,1)} %copy_select_fusion) | copy-start | bytes 3145732
  25.5 4.9 %copy-start.6 = (f32[8,256,512]{1,2,0:T(8,128)S(1)}, f32[8,256,512]{1,2,0:T(8,128)}, u32[]{:S(2)}) copy-start(f32[8,256,512]{1,2,0:T(8,128)} %get-tuple-element.137) | copy-start | bytes 12582916
  32.5 4.0 %copy-start.3 = (bf16[8,256,512]{1,2,0:T(8,128)(2,1)}, bf16[8,256,512]{1,2,0:T(8,128)(2,1)S(1)}, u32[]{:S(2)}) copy-start(bf16[8,256,512]{1,2,0:T(8,128)(2,1)S(1)} %multiply_convert_fusion.1) | copy-start | bytes 6291460
  46.9 5.2 %copy-start.10 = (bf16[768,8,256]{2,0,1:T(8,128)(2,1)S(1)}, bf16[768,8,256]{2,0,1:T(8,128)(2,1)}, u32[]{:S(2)}) copy-start(bf16[768,8,256]{2,0,1:T(8,128)(2,1)} %copy-done.9) | copy-start | bytes 9437188
  46.9 7.9 %copy-start.5 = (f32[8,256,768]{1,2,0:T(8,128)S(1)}, f32[8,256,768]{1,2,0:T(8,128)}, u32[]{:S(2)}) copy-start(f32[8,256,768]{1,2,0:T(8,128)} %get-tuple-element.135) | copy-start | bytes 18874372
  50.4 1.7 %copy-start.7 = (bf16[8,256,768]{1,2,0:T(8,128)(2,1)}, bf16[8,256,768]{1,2,0:T(8,128)(2,1)S(1)}, u32[]{:S(2)}) copy-start(bf16[8,256,768]{1,2,0:T(8,128)(2,1)S(1)} %fusion.9) | copy-start | bytes 9437188
  52.0 2.8 %copy-start.15 = (bf16[512,8,128]{2,0,1:T(8,128)(2,1)S(1)}, bf16[512,8,128]{2,0,1:T(8,128)(2,1)}, u32[]{:S(2)}) copy-start(bf16[512,8,128]{2,0,1:T(8,128)(2,1)} %copy_select_fusion) | copy-start | bytes 3145732
  57.7 3.1 %copy-start.1 = (bf16[8,256,768]{1,2,0:T(8,128)(2,1)S(1)}, bf16[8,256,768]{1,2,0:T(8,128)(2,1)}, u32[]{:S(2)}) copy-start(bf16[8,256,768]{1,2,0:T(8,128)(2,1)} %multiply_convert_fusion) | copy-start | bytes 9437188
  57.7 3.5 %copy-start.12 = (f32[512,8,128]{0,2,1:T(8,128)S(1)}, f32[512,8,128]{0,2,1:T(8,128)}, u32[]{:S(2)}) copy-start(f32[512,8,128]{0,2,1:T(8,128)} %convolution_bitcast_fusion.1) | copy-start | bytes 6291460
  61.2 5.9 %copy-start.20 = (f32[768,64]{0,1:T(8,128)}, f32[768,64]{0,1:T(8,128)S(1)}, u32[]{:S(2)}) copy-start(f32[768,64]{0,1:T(8,128)S(1)} %fusion.57) | copy-start | bytes 589828
  61.2 3.5 %copy-start.8 = (bf16[8,256,768]{1,2,0:T(8,128)(2,1)S(1)}, bf16[8,256,768]{1,2,0:T(8,128)(2,1)}, u32[]{:S(2)}) copy-start(bf16[8,256,768]{1,2,0:T(8,128)(2,1)} %copy-done.7) | copy-start | bytes 9437188
  61.2 3.5 %copy-start.11 = (f32[512,8,128]{0,2,1:T(8,128)S(1)}, f32[512,8,128]{0,2,1:T(8,128)}, u32[]{:S(2)}) copy-start(f32[512,8,128]{0,2,1:T(8,128)} %convolution_bitcast_fusion) | copy-start | bytes 6291460
  61.2 3.5 %copy-start.16 = (bf16[512,8,128]{2,0,1:T(8,128)(2,1)S(1)}, bf16[512,8,128]{2,0,1:T(8,128)(2,1)}, u32[]{:S(2)}) copy-start(bf16[512,8,128]{2,0,1:T(8,128)(2,1)} %copy_select_fusion) | copy-start | bytes 3145732
  67.2 2.3 %copy-start.22 = (f32[256,64]{1,0:T(8,128)}, f32[256,64]{1,0:T(8,128)S(1)}, u32[]{:S(2)}) copy-start(f32[256,64]{1,0:T(8,128)S(1)} %copy.282) | copy-start | bytes 196612
  67.2 4.4 %copy-start.21 = (f32[768,64]{0,1:T(8,128)S(1)}, f32[768,64]{0,1:T(8,128)}, u32[]{:S(2)}) copy-start(f32[768,64]{0,1:T(8,128)} %copy-done.20) | copy-start | bytes 589828
  67.2 4.7 %copy-start.18 = (bf16[768,8,128]{0,2,1:T(8,128)(2,1)S(1)}, bf16[768,8,128]{0,2,1:T(8,128)(2,1)}, u32[]{:S(2)}) copy-start(bf16[768,8,128]{0,2,1:T(8,128)(2,1)} %fusion.8) | copy-start | bytes 4718596
  67.2 4.7 %copy-start.19 = (bf16[768,8,128]{0,2,1:T(8,128)(2,1)S(1)}, bf16[768,8,128]{0,2,1:T(8,128)(2,1)}, u32[]{:S(2)}) copy-start(bf16[768,8,128]{0,2,1:T(8,128)(2,1)} %fusion.7) | copy-start | bytes 4718596
  70.2 7.4 %collective-permute-start.1 = (f32[128,576]{1,0:T(8,128)}, f32[128,576]{1,0:T(8,128)}, u32[]{:S(2)}, u32[]{:S(2)}) collective-permute-start(f32[128,576]{1,0:T(8,128)} %fusion.77), channel_id=1, source_target_pairs={{0,1},{1,0},{2,3},{3,2},{4,5},{5,4},{6,7},{7,6},{8,9},{9,8},{10,11... | collective-permute-start | bytes 884744 | tf_op jit(solution)/shard_map/ppermute | solution.py:69
  77.6 22.1 %collective-permute-start = (bf16[8,32,576]{2,1,0:T(8,128)(2,1)}, bf16[8,32,576]{2,1,0:T(8,128)(2,1)}, u32[]{:S(2)}, u32[]{:S(2)}) collective-permute-start(bf16[8,32,576]{2,1,0:T(8,128)(2,1)} %fusion.76), channel_id=1, source_target_pairs={{0,1},{1,0},{2,3},{3,2},{4,5},{5,4},{6,7},{7,6},{8,9},{9,8},{10,11... | collective-permute-start | bytes 884744 | tf_op jit(solution)/shard_map/ppermute | solution.py:69
  92.5 15.6 %all-to-all-start.3 = ((f32[8,16,576]{2,1,0:T(8,128)}), f32[8,16,576]{2,1,0:T(8,128)S(1)}, u32[]{:S(2)}, u32[]{:S(2)}) async-start(f32[8,16,576]{2,1,0:T(8,128)} %broadcast_in_dim.44), calls=%async_computation.3 | async-start | bytes 655360 | tf_op jit(solution)/shard_map/all_to_all | solution.py:184
  108.1 9.9 %all-to-all-start = ((bf16[8,32,576]{2,1,0:T(8,128)(2,1)}), bf16[8,32,576]{2,1,0:T(8,128)(2,1)S(1)}, u32[]{:S(2)}, u32[]{:S(2)}) async-start(bf16[8,32,576]{2,1,0:T(8,128)(2,1)} %fusion.65), calls=%async_computation | async-start | bytes 655360 | tf_op jit(solution)/shard_map/all_to_all | solution.py:167
  118.7 10.5 %all-to-all-start.4 = ((f32[8,16,576]{2,1,0:T(8,128)}), f32[8,16,576]{2,1,0:T(8,128)S(1)}, u32[]{:S(2)}, u32[]{:S(2)}) async-start(f32[8,16,576]{2,1,0:T(8,128)} %broadcast_in_dim.45), calls=%async_computation.4 | async-start | bytes 655360 | tf_op jit(solution)/shard_map/all_to_all | solution.py:194
  122.7 2.7 %copy-start.17 = (bf16[512,8,256]{2,0,1:T(8,128)(2,1)S(1)}, bf16[512,8,256]{2,0,1:T(8,128)(2,1)}, u32[]{:S(2)}) copy-start(bf16[512,8,256]{2,0,1:T(8,128)(2,1)} %fusion.13) | copy-start | bytes 6291460
  122.7 4.2 %copy-start.28 = (f32[512,32]{0,1:T(8,128)S(1)}, f32[512,32]{0,1:T(8,128)}, u32[]{:S(2)}) copy-start(f32[512,32]{0,1:T(8,128)} %copy-done.27) | copy-start | bytes 196612
  127.0 6.7 %copy-start.24 = (bf16[512,64,1]{1,0,2:T(8,128)(2,1)S(1)}, bf16[512,64,1]{1,0,2:T(8,128)(2,1)}, u32[]{:S(2)}) copy-start(bf16[512,64,1]{1,0,2:T(8,128)(2,1)} %maximum_bitcast_fusion.1) | copy-start | bytes 196612
  127.6 6.0 %copy-start.29 = (f32[256,32]{0,1:T(8,128)S(1)}, f32[256,32]{0,1:T(8,128)}, u32[]{:S(2)}) copy-start(f32[256,32]{0,1:T(8,128)} %get-tuple-element.127) | copy-start | bytes 98308
  127.6 6.0 %copy-start.30 = (f32[256,32]{0,1:T(8,128)S(1)}, f32[256,32]{0,1:T(8,128)}, u32[]{:S(2)}) copy-start(f32[256,32]{0,1:T(8,128)} %get-tuple-element.138) | copy-start | bytes 98308
  129.2 33.0 %all-to-all-start.1 = ((bf16[8,64,8,256]{3,1,2,0:T(8,128)(2,1)}), bf16[8,64,8,256]{3,1,2,0:T(8,128)(2,1)}, u32[]{:S(2)}, u32[]{:S(2)}) async-start(bf16[8,64,8,256]{3,1,2,0:T(8,128)(2,1)} %copy.278), calls=%async_computation.1 | async-start | bytes 4194304 | tf_op jit(solution)/shard_map/all_to_all | solution.py:148
  133.6 2.5 %copy-start.4 = (bf16[8,256,512]{1,2,0:T(8,128)(2,1)S(1)}, bf16[8,256,512]{1,2,0:T(8,128)(2,1)}, u32[]{:S(2)}) copy-start(bf16[8,256,512]{1,2,0:T(8,128)(2,1)} %copy-done.3) | copy-start | bytes 6291460
  133.7 4.1 %copy-start.2 = (bf16[8,256,768]{1,2,0:T(8,128)(2,1)S(1)}, bf16[8,256,768]{1,2,0:T(8,128)(2,1)}, u32[]{:S(2)}) copy-start(bf16[8,256,768]{1,2,0:T(8,128)(2,1)} %multiply_convert_fusion) | copy-start | bytes 9437188
  140.0 6.0 %collective-permute-start.2 = (f32[128,576]{1,0:T(8,128)S(1)}, f32[128,576]{1,0:T(8,128)S(1)}, u32[]{:S(2)}, u32[]{:S(2)}) collective-permute-start(f32[128,576]{1,0:T(8,128)S(1)} %bitcast.129), channel_id=1, source_target_pairs={{0,1},{1,0},{2,3},{3,2},{4,5},{5,4},{6,7},{7,6},{8,9},{9,8},{10,11... | collective-permute-start | bytes 884744 | tf_op jit(solution)/shard_map/ppermute | solution.py:69

commit v7 on v6

--- a/solution.py
+++ b/solution.py
@@ -180,16 +180,12 @@
         ),
         axis=0,
     )
-    prefix_own = jnp.sum(
-        lax.all_to_all(
-            jnp.broadcast_to(prefix_rows_part[None], (dp_size,) + prefix_rows_part.shape),
-            "dp",
-            0,
-            0,
-            tiled=False,
-        ),
-        axis=0,
-    )
+    prefix_own = prefix_rows_part
+    stride = 1
+    while stride < dp_size:
+        partners = [(i, i ^ stride) for i in range(dp_size)]
+        prefix_own = prefix_own + lax.ppermute(prefix_own, "dp", partners)
+        stride *= 2
     prefix_copies = jnp.broadcast_to(prefix_own[None], (row_size,) + prefix_own.shape)
     prefix_gathered = lax.all_to_all(prefix_copies, "hr", 0, 0, tiled=False).reshape(
         prefix_half.shape

time: 166 us -> 163 us (0.982)
  blocking collectives: 13.1 us -> 0 us
  starting transfers between devices: 24.6 us -> 31.5 us
    all_to_all x1 -> x0, blocking collectives: 13.1 us -> none  [on_device(): lax.all_to_all(prefix_half.reshape((row_size, -1) + prefix_half.shape[1:]...]
    ppermute x0 -> x3, starting transfers between devices: none -> 7.91 us  [on_device(): prefix_own = prefix_own + lax.ppermute(prefix_own, 'dp', partners)]
    all_to_all x1, starting transfers between devices: 7.2 us -> 5.48 us  [on_device(): lax.all_to_all(prefix_half.reshape((row_size, -1) + prefix_half.shape[1:]...]
    unnamed x66 -> x62, local copies, waits for them, and re-layouts: 7.49 us -> 7.48 us
  transfers between devices with their start and end apart: 7 -> 10, of which waited for: 4 -> 4; matrix products, arithmetic and copies ran while one was open for 18% -> 18% of each run, Pallas kernels for 0% -> 0%
where the time goes in v7:
time: 163 us; the launch traced here: 162 us
  matrix products  66.4 us (41%)
  starting transfers between devices  31.5 us (19%)
  waiting for transfers between devices  25.2 us (15%)
  other arithmetic  22.6 us (14%)
  local copies, waits for them, and re-layouts  14.1 us (9%)
  between operations  1.83 us (1%)
    all_to_all x1, waiting for transfers between devices, on_device(): lax.all_to_all(up_part.astype(jnp.bfloat16).reshape((dp_size, -1) + up_pa...  14.9 us
    sub x2, matrix products, block_gradients(): exponent = jnp.exp(scores - highest)  13.3 us
    ppermute x3, starting transfers between devices, on_device(): prefix_own = prefix_own + lax.ppermute(prefix_own, 'dp', partners)  7.91 us
    unnamed x62, local copies, waits for them, and re-layouts  7.48 us
    all_to_all x1, waiting for transfers between devices, on_device(): lax.all_to_all(prefix_half.reshape((row_size, -1) + prefix_half.shape[1:]...  7.1 us
    dot_general x2, matrix products, block_gradients(): jnp.einsum('hqk,qhd->khd', score_grad, query_nope, preferred_element_type...  6.79 us
    dot_general x2, matrix products, block_gradients(): jnp.einsum('qhd,khd->hqk', query_nope, key_nope, preferred_element_type=j...  6.38 us
    convert_element_type x2, other arithmetic, block_gradients(): weights = probability.astype(jnp.bfloat16)  6.2 us
  transfers between devices with their start and end apart: 10, of which 4 were waited for; matrix products, arithmetic and copies ran while one was open for 18% of the time, Pallas kernels for 0%

profile of v7, /device:TPU:1, one launch (start us, length us, event | category | flops | bytes accessed | tf_op | source)
XLA Modules:
  0.0 161.7 jit_solution(497156254131194225)
XLA Ops:
  0.7 1.0 slice_convert_fusion.1
  1.7 1.9 %slice.226 = bf16[512,512]{0,1:T(8,128)(2,1)} slice(bf16[512,576]{0,1:T(8,128)(2,1)} %param.26), slice={[0:512], [0:512]} | slice | bytes 1048576 | tf_op jit(solution)/shard_map/slice | solution.py:89
  3.5 1.2 copy.178
  4.7 0.7 convert_element_type.66
  5.4 0.3 multiply_cosine_fusion
  6.0 1.3 copy.268
  7.5 0.7 maximum_bitcast_fusion.1
  8.3 0.8 copy-done.13
  9.2 1.8 %convolution_convert_fusion = bf16[768,8,256]{2,0,1:T(8,128)(2,1)S(1)} fusion(bf16[512,8,256]{2,1,0:T(8,128)(2,1)S(1)} %copy-done, bf16[768,576]{1,0:T(8,128)(2,1)S(1)} %maximum_maximum_fusion.1), kind=kOutput, calls=%fused_computation.25 | convolution fusion | flops 1612185600 | bytes 6029312 | tf_op jit(solution)/shard_map/kl,lhd->khd/dot_general | solution.py:98
  11.0 3.6 %fusion.24 = f32[8,768,256]{2,1,0:T(8,128)} fusion(bf16[768,8,256]{2,0,1:T(8,128)(2,1)S(1)} %convolution_convert_fusion, bf16[512,8,192]{0,2,1:T(8,128)(2,1)S(1)} %copy-done.13), kind=kOutput, calls=%fused_computation.43 | convolution fusion | flops 402653184 | bytes 8388608 | tf_op jit(solution)/shard_map/qhd,khd->hqk/dot_general | solution.py:37
  14.6 2.8 %fusion.63 = f32[8,512,256]{2,1,0:T(8,128)} fusion(bf16[768,8,256]{2,0,1:T(8,128)(2,1)S(1)} %convolution_convert_fusion, bf16[512,8,192]{0,2,1:T(8,128)(2,1)S(1)} %copy-done.13), kind=kOutput, calls=%fused_computation.69 | convolution fusion | flops 268435456 | bytes 5767168 | tf_op jit(solution)/shard_map/qhd,khd->hqk/dot_general | solution.py:37
  18.1 1.2 copy_select_fusion
  19.7 5.7 %fusion.112 = (f32[8,256]{1,0:T(8,128)S(1)}, f32[8,256,512]{1,2,0:T(8,128)}) fusion(f32[8,512,256]{2,1,0:T(8,128)} %fusion.63, bf16[512,64,1]{1,0,2:T(8,128)(2,1)S(1)} %copy-done.21, pred[256,512]{0,1:T(8,128)(4,1)S(1)} %fusion.67, bf16[512,8,32]{0,2,1:T(8,128)(2,1)S(1)} %get-tuple-element.112, bf16[512,8,32]{0,2,1:T(8,128)(2,1)S(1)} %get-tuple-element.113), kind=kOutput, calls=%fused_computation.149 | convolution fusion | flops 139985408 | bytes 9117696 | tf_op jit(solution)/shard_map/sub | solution.py:47
  25.5 2.7 %fusion.14 = bf16[8,256,512]{1,2,0:T(8,128)(2,1)S(1)} fusion(f32[8,256,512]{1,2,0:T(8,128)} %get-tuple-element.133, f32[8,256]{1,0:T(8,128)S(1)} %get-tuple-element.132), kind=kLoop, calls=%fused_computation.30 | loop fusion | flops 2097152 | bytes 6299648 | tf_op jit(solution)/shard_map/convert_element_type | solution.py:49
  28.2 2.2 %fusion.46 = f32[256,8]{0,1:T(8,128)S(1)} fusion(bf16[8,256,512]{1,2,0:T(8,128)(2,1)S(1)} %fusion.14, bf16[768,8,256]{2,0,1:T(8,128)(2,1)} %copy-done.9, bf16[512,8,128]{2,0,1:T(8,128)(2,1)S(1)} %copy-done.14), kind=kOutput, calls=%fused_computation.53 | convolution fusion | flops 269219840 | bytes 3678208 | tf_op jit(solution)/shard_map/hqk,khv->qhv/dot_general | solution.py:50
  30.4 2.0 %multiply_convert_fusion.1 = bf16[8,256,512]{1,2,0:T(8,128)(2,1)S(1)} fusion(f32[8,256]{1,0:T(8,128)S(1)} %bitcast.137, f32[8,256,512]{1,2,0:T(8,128)S(1)} %copy-done.6, f32[8,256]{1,0:T(8,128)S(1)} %get-tuple-element.132, bf16[768,8,256]{2,0,1:T(8,128)(2,1)} %copy-done.9, bf16[512,8,128]{2,0,1:T(8,128)(2,1)S(1)} %copy-done.14), kind=kOutput, calls=%fused_computation.11 | convolution fusion | flops 273678336 | bytes 7880704 | tf_op jit(solution)/shard_map/qhv,khv->hqk/dot_general | solution.py:52
  32.5 0.7 convolution_bitcast_fusion.6
  33.2 3.3 %convolution_bitcast_fusion.1 = f32[512,8,128]{0,2,1:T(8,128)} fusion(bf16[8,256,512]{1,2,0:T(8,128)(2,1)S(1)} %multiply_convert_fusion.1, bf16[512,8,192]{0,2,1:T(8,128)(2,1)} %param.25), kind=kOutput, calls=%fused_computation.32 | convolution fusion | flops 268435456 | bytes 4718592 | tf_op jit(solution)/shard_map/hqk,qhd->khd/dot_general | solution.py:60
  36.5 2.1 %convolution_bitcast_fusion = f32[512,8,128]{0,2,1:T(8,128)} fusion(bf16[8,256,512]{1,2,0:T(8,128)(2,1)S(1)} %fusion.14, bf16[512,8,128]{2,0,1:T(8,128)(2,1)S(1)} %copy-done.14), kind=kOutput, calls=%fused_computation.31 | convolution fusion | flops 268435456 | bytes 4718592 | tf_op jit(solution)/shard_map/hqk,qhv->khv/dot_general | solution.py:64
  38.6 0.7 and_or_fusion
  39.3 7.5 %fusion.111 = (f32[8,256]{1,0:T(8,128)S(1)}, f32[8,256,768]{1,2,0:T(8,128)}) fusion(f32[8,768,256]{2,1,0:T(8,128)} %fusion.24, pred[256,768]{0,1:T(8,128)(4,1)S(1)} %and_or_fusion, bf16[768,64,1]{1,0,2:T(8,128)(2,1)S(1)} %maximum_bitcast_fusion, bf16[512,8,32]{0,2,1:T(8,128)(2,1)S(1)} %get-tuple-element.113, bf16[512,8,32]{0,2,1:T(8,128)(2,1)S(1)} %get-tuple-element.112), kind=kOutput, calls=%fused_computation.148 | convolution fusion | flops 209715968 | bytes 13410304 | tf_op jit(solution)/shard_map/sub | solution.py:47
  46.9 3.5 %fusion.9 = bf16[8,256,768]{1,2,0:T(8,128)(2,1)S(1)} fusion(f32[8,256,768]{1,2,0:T(8,128)} %get-tuple-element.131, f32[8,256]{1,0:T(8,128)S(1)} %get-tuple-element.130), kind=kLoop, calls=%fused_computation.24 | loop fusion | flops 3145728 | bytes 9445376 | tf_op jit(solution)/shard_map/convert_element_type | solution.py:49
  50.4 1.7 %copy-done.7 = bf16[8,256,768]{1,2,0:T(8,128)(2,1)} copy-done((bf16[8,256,768]{1,2,0:T(8,128)(2,1)}, bf16[8,256,768]{1,2,0:T(8,128)(2,1)S(1)}, u32[]{:S(2)}) %copy-start.7) | copy-done | bytes 3145752
  52.0 2.7 %fusion.47 = f32[256,8]{0,1:T(8,128)S(1)} fusion(bf16[8,256,768]{1,2,0:T(8,128)(2,1)S(1)} %fusion.9, bf16[768,8,256]{2,0,1:T(8,128)(2,1)S(1)} %copy-done.10, bf16[512,8,128]{2,0,1:T(8,128)(2,1)} %copy_select_fusion), kind=kOutput, calls=%fused_computation.54 | convolution fusion | flops 403437568 | bytes 5251072 | tf_op jit(solution)/shard_map/hqk,khv->qhv/dot_general | solution.py:50
  54.8 2.9 %multiply_convert_fusion = bf16[8,256,768]{1,2,0:T(8,128)(2,1)} fusion(f32[8,256]{1,0:T(8,128)S(1)} %bitcast.138, f32[8,256,768]{1,2,0:T(8,128)S(1)} %copy-done.5, f32[8,256]{1,0:T(8,128)S(1)} %get-tuple-element.130, bf16[768,8,256]{2,0,1:T(8,128)(2,1)S(1)} %copy-done.10, bf16[512,8,128]{2,0,1:T(8,128)(2,1)S(1)} %copy-done.15), kind=kOutput, calls=%fused_computation.5 | convolution fusion | flops 410517504 | bytes 11550720 | tf_op jit(solution)/shard_map/qhv,khv->hqk/dot_general | solution.py:52
  57.7 3.1 %fusion.57 = f32[768,64]{0,1:T(8,128)S(1)} fusion(bf16[8,256,768]{1,2,0:T(8,128)(2,1)} %multiply_convert_fusion, f32[512,64]{0,1:T(8,128)S(1)} %convolution_bitcast_fusion.6, bf16[512,8,32]{0,2,1:T(8,128)(2,1)S(1)} %get-tuple-element.113, bf16[512,8,32]{0,2,1:T(8,128)(2,1)S(1)} %get-tuple-element.112), kind=kOutput, calls=%fused_computation.61 | convolution fusion | flops 201900032 | bytes 3997696 | tf_op jit(solution)/shard_map/hqk,qhr->kr/dot_general | solution.py:63
  60.8 0.4 copy-done.12
  61.2 3.5 %fusion.8 = bf16[768,8,128]{0,2,1:T(8,128)(2,1)} fusion(f32[512,8,128]{0,2,1:T(8,128)S(1)} %copy-done.12, bf16[8,256,768]{1,2,0:T(8,128)(2,1)S(1)} %copy-done.1, bf16[512,8,192]{0,2,1:T(8,128)(2,1)} %param.25), kind=kOutput, calls=%fused_computation.22 | convolution fusion | flops 404226048 | bytes 7340032 | tf_op jit(solution)/shard_map/hqk,qhd->khd/dot_general | solution.py:60
  64.7 2.3 %fusion.7 = bf16[768,8,128]{0,2,1:T(8,128)(2,1)} fusion(f32[512,8,128]{0,2,1:T(8,128)S(1)} %copy-done.11, bf16[8,256,768]{1,2,0:T(8,128)(2,1)S(1)} %copy-done.8, bf16[512,8,128]{2,0,1:T(8,128)(2,1)S(1)} %copy-done.16), kind=kOutput, calls=%fused_computation.20 | convolution fusion | flops 404226048 | bytes 7340032 | tf_op jit(solution)/shard_map/hqk,qhv->khv/dot_general | solution.py:64
  67.2 2.1 %fusion.51 = f32[256,512]{1,0:T(8,128)S(1)} fusion(bf16[512,8,256]{2,1,0:T(8,128)(2,1)S(1)} %copy-done, bf16[768,8,128]{0,2,1:T(8,128)(2,1)} %fusion.8, bf16[768,8,128]{0,2,1:T(8,128)(2,1)} %fusion.7), kind=kOutput, calls=%fused_computation.56 | convolution fusion | flops 538968064 | bytes 5767168 | tf_op jit(solution)/shard_map/khd,lhd->kl/dot_general | solution.py:169
  69.3 0.8 fusion.77
  70.0 1.4 collective-permute-start.1
  71.4 3.7 %fusion.38 = bf16[512,512]{1,0:T(8,128)(2,1)} fusion(bf16[512,8,256]{2,1,0:T(8,128)(2,1)S(1)} %copy-done, bf16[768,8,128]{0,2,1:T(8,128)(2,1)} %fusion.8, bf16[768,8,128]{0,2,1:T(8,128)(2,1)} %fusion.7), kind=kOutput, calls=%fused_computation.50 | convolution fusion | flops 1078198272 | bytes 5767168 | tf_op jit(solution)/shard_map/khd,lhd->kl/dot_general | solution.py:154
  75.5 0.8 copy.265
  76.2 0.8 copy.264
  77.0 1.3 pad_maximum_fusion.4
  78.3 1.7 %fusion.79 = f32[128,576]{1,0:T(8,128)} fusion(f32[128,576]{1,0:T(8,128)} %collective-permute-done.1, s32[]{:T(128)S(6)} %select_n.50, f32[256,512]{1,0:T(8,128)S(1)} %fusion.51, f32[256,64]{1,0:T(8,128)} %copy-done.20), kind=kLoop, calls=%fused_computation.102 | loop fusion | flops 147456 | bytes 1179652 | tf_op jit(solution)/shard_map/add | solution.py:176
  80.1 5.5 %all-to-all-start.2 = ((f32[8,16,576]{2,1,0:T(8,128)}), f32[8,16,576]{2,1,0:T(8,128)S(1)}, u32[]{:S(2)}, u32[]{:S(2)}) async-start(f32[8,16,576]{2,1,0:T(8,128)} %bitcast.131), calls=%async_computation.2 | async-start | bytes 655360 | tf_op jit(solution)/shard_map/all_to_all | solution.py:178
  85.5 0.8 fusion.76
  86.6 7.1 %all-to-all-done.2 = f32[8,16,576]{2,1,0:T(8,128)S(1)} async-done(((f32[8,16,576]{2,1,0:T(8,128)}), f32[8,16,576]{2,1,0:T(8,128)S(1)}, u32[]{:S(2)}, u32[]{:S(2)}) %all-to-all-start.2) | async-done | bytes 294944 | tf_op jit(solution)/shard_map/all_to_all | solution.py:178
  93.7 1.4 collective-permute-start.2
  95.1 1.5 collective-permute-done.2
  96.6 2.9 %collective-permute-start.3 = (f32[16,576]{1,0:T(8,128)S(1)}, f32[16,576]{1,0:T(8,128)S(1)}, u32[]{:S(2)}, u32[]{:S(2)}) collective-permute-start(f32[16,576]{1,0:T(8,128)S(1)} %add.144), channel_id=1, source_target_pairs={{0,32},{16,48},{32,0},{48,16},{64,96},{80,112},{96,64},{112,80},{1... | collective-permute-start | bytes 110600 | tf_op jit(solution)/shard_map/ppermute | solution.py:187
  99.6 1.8 %fusion.65 = bf16[8,32,576]{2,1,0:T(8,128)(2,1)} fusion(bf16[8,32,576]{2,1,0:T(8,128)(2,1)} %collective-permute-done, pred[]{:T(512)S(6)} %eq.2, bf16[8,2,32,576]{3,2,1,0:T(8,128)(2,1)S(1)} %pad_maximum_fusion.4), kind=kLoop, calls=%fused_computation.80 | loop fusion | flops 737280 | bytes 1179649 | tf_op jit(solution)/shard_map/convert_element_type | solution.py:166
  101.4 3.4 %all-to-all-start = ((bf16[8,32,576]{2,1,0:T(8,128)(2,1)}), bf16[8,32,576]{2,1,0:T(8,128)(2,1)S(1)}, u32[]{:S(2)}, u32[]{:S(2)}) async-start(bf16[8,32,576]{2,1,0:T(8,128)(2,1)} %fusion.65), calls=%async_computation | async-start | bytes 655360 | tf_op jit(solution)/shard_map/all_to_all | solution.py:167
  104.8 3.6 %collective-permute-start.4 = (f32[16,576]{1,0:T(8,128)S(1)}, f32[16,576]{1,0:T(8,128)S(1)}, u32[]{:S(2)}, u32[]{:S(2)}) collective-permute-start(f32[16,576]{1,0:T(8,128)S(1)} %add.145), channel_id=1, source_target_pairs={{0,64},{16,80},{32,96},{48,112},{64,0},{80,16},{96,32},{112,48},{1... | collective-permute-start | bytes 110600 | tf_op jit(solution)/shard_map/ppermute | solution.py:187
  108.4 5.4 %fusion.13 = bf16[512,8,256]{2,0,1:T(8,128)(2,1)} fusion(bf16[768,8,128]{0,2,1:T(8,128)(2,1)} %fusion.7, bf16[768,8,128]{0,2,1:T(8,128)(2,1)} %fusion.8, bf16[768,576]{1,0:T(8,128)(2,1)} %copy-done.24), kind=kOutput, calls=%fused_computation.29 | convolution fusion | flops 1617952768 | bytes 6029312 | tf_op jit(solution)/shard_map/kl,khd->lhd/dot_general | solution.py:138
  113.8 0.7 broadcast_in_dim.38
  114.6 4.5 %all-to-all-start.3 = ((f32[8,16,576]{2,1,0:T(8,128)}), f32[8,16,576]{2,1,0:T(8,128)S(1)}, u32[]{:S(2)}, u32[]{:S(2)}) async-start(f32[8,16,576]{2,1,0:T(8,128)} %broadcast_in_dim.38), calls=%async_computation.3 | async-start | bytes 655360 | tf_op jit(solution)/shard_map/all_to_all | solution.py:190
  119.0 2.7 %convolution_bitcast_fusion.3 = f32[256,8,64]{0,2,1:T(8,128)S(1)} fusion(bf16[768,64,1]{1,0,2:T(8,128)(2,1)S(1)} %maximum_bitcast_fusion, bf16[8,256,768]{1,2,0:T(8,128)(2,1)} %multiply_convert_fusion), kind=kOutput, calls=%fused_computation.57 | convolution fusion | flops 201326592 | bytes 3768320 | tf_op jit(solution)/shard_map/hqk,kr->qhr/dot_general | solution.py:59
  121.8 1.5 copy.221
  123.2 0.6 fusion.109
  123.9 1.7 %all-to-all-done.3 = f32[8,16,576]{2,1,0:T(8,128)S(1)} async-done(((f32[8,16,576]{2,1,0:T(8,128)}), f32[8,16,576]{2,1,0:T(8,128)S(1)}, u32[]{:S(2)}, u32[]{:S(2)}) %all-to-all-start.3) | async-done | bytes 294944 | tf_op jit(solution)/shard_map/all_to_all | solution.py:190
  125.5 4.4 %all-to-all-start.1 = ((bf16[8,64,8,256]{3,1,2,0:T(8,128)(2,1)}), bf16[8,64,8,256]{3,1,2,0:T(8,128)(2,1)}, u32[]{:S(2)}, u32[]{:S(2)}) async-start(bf16[8,64,8,256]{3,1,2,0:T(8,128)(2,1)} %copy.221), calls=%async_computation.1 | async-start | bytes 4194304 | tf_op jit(solution)/shard_map/all_to_all | solution.py:148
  130.0 2.2 %convolution_bitcast_fusion.4 = f32[256,8,64]{0,2,1:T(8,128)S(1)} fusion(bf16[512,64,1]{1,0,2:T(8,128)(2,1)S(1)} %copy-done.22, bf16[8,256,512]{1,2,0:T(8,128)(2,1)} %copy-done.3), kind=kOutput, calls=%fused_computation.58 | convolution fusion | flops 134217728 | bytes 2686976 | tf_op jit(solution)/shard_map/hqk,kr->qhr/dot_general | solution.py:59
  132.4 1.8 %fusion.50 = bf16[256,8,128]{0,2,1:T(8,128)(2,1)S(1)} fusion(bf16[8,256,512]{1,2,0:T(8,128)(2,1)S(1)} %copy-done.4, bf16[768,8,256]{2,0,1:T(8,128)(2,1)} %copy-done.9), kind=kOutput, calls=%fused_computation.55 | convolution fusion | flops 268697600 | bytes 3670016 | tf_op jit(solution)/shard_map/hqk,khd->qhd/dot_general | solution.py:56
  134.2 2.2 %fusion.54 = bf16[256,8,128]{0,2,1:T(8,128)(2,1)S(1)} fusion(bf16[8,256,768]{1,2,0:T(8,128)(2,1)S(1)} %copy-done.2, bf16[768,8,256]{2,0,1:T(8,128)(2,1)} %copy-done.9), kind=kOutput, calls=%fused_computation.59 | convolution fusion | flops 402915328 | bytes 5242880 | tf_op jit(solution)/shard_map/hqk,khd->qhd/dot_general | solution.py:56
  136.3 4.3 %collective-permute-start.5 = (f32[128,576]{1,0:T(8,128)S(1)}, f32[128,576]{1,0:T(8,128)S(1)}, u32[]{:S(2)}, u32[]{:S(2)}) collective-permute-start(f32[128,576]{1,0:T(8,128)S(1)} %bitcast.129), channel_id=1, source_target_pairs={{0,1},{1,0},{2,3},{3,2},{4,5},{5,4},{6,7},{7,6},{8,9},{9,8},{10,11... | collective-permute-start | bytes 884744 | tf_op jit(solution)/shard_map/ppermute | solution.py:69
  140.6 1.3 maximum_maximum_fusion
  141.9 0.7 convert_reduce_fusion.1
  142.6 1.0 copy.227
  143.6 14.9 %all-to-all-done.1 = bf16[8,64,8,256]{3,1,2,0:T(8,128)(2,1)} async-done(((bf16[8,64,8,256]{3,1,2,0:T(8,128)(2,1)}), bf16[8,64,8,256]{3,1,2,0:T(8,128)(2,1)}, u32[]{:S(2)}, u32[]{:S(2)}) %all-to-all-start.1) | async-done | bytes 2097184 | tf_op jit(solution)/shard_map/all_to_all | solution.py:148
  158.5 2.0 %convert_reduce_fusion = f32[64,8,256]{2,0,1:T(8,128)S(1)} fusion(bf16[8,64,8,256]{3,1,2,0:T(8,128)(2,1)} %all-to-all-done.1), kind=kLoop, calls=%fused_computation.10 | loop fusion | flops 1966080 | bytes 2621440 | tf_op jit(solution)/shard_map/reduce_sum | solution.py:151
  160.6 1.1 copy.226
  (86 shorter events, 2.2 us)
Async XLA Ops:
  0.6 8.5 %copy-start = (bf16[512,8,256]{2,1,0:T(8,128)(2,1)S(1)}, bf16[512,8,256]{2,1,0:T(8,128)(2,1)}, u32[]{:S(2)}) copy-start(bf16[512,8,256]{2,1,0:T(8,128)(2,1)} %param.28) | copy-start | bytes 6291460
  5.7 13.6 %copy-start.25 = (f32[512,32]{0,1:T(8,128)}, f32[512,32]{0,1:T(8,128)S(1)}, u32[]{:S(2)}) copy-start(f32[512,32]{0,1:T(8,128)S(1)} %get-tuple-element.127) | copy-start | bytes 196612
  7.2 1.8 %copy-start.13 = (bf16[512,8,192]{0,2,1:T(8,128)(2,1)S(1)}, bf16[512,8,192]{0,2,1:T(8,128)(2,1)}, u32[]{:S(2)}) copy-start(bf16[512,8,192]{0,2,1:T(8,128)(2,1)} %param.25) | copy-start | bytes 4718596
  7.5 3.5 %copy-start.24 = (bf16[768,576]{1,0:T(8,128)(2,1)}, bf16[768,576]{1,0:T(8,128)(2,1)S(1)}, u32[]{:S(2)}) copy-start(bf16[768,576]{1,0:T(8,128)(2,1)S(1)} %maximum_maximum_fusion.1) | copy-start | bytes 2654212
  11.0 3.6 %copy-start.9 = (bf16[768,8,256]{2,0,1:T(8,128)(2,1)}, bf16[768,8,256]{2,0,1:T(8,128)(2,1)S(1)}, u32[]{:S(2)}) copy-start(bf16[768,8,256]{2,0,1:T(8,128)(2,1)S(1)} %convolution_convert_fusion) | copy-start | bytes 9437188
  14.6 3.5 %copy-start.23 = (bf16[512,8,128]{2,1,0:T(8,128)(2,1)S(1)}, bf16[512,8,128]{2,1,0:T(8,128)(2,1)}, u32[]{:S(2)}) copy-start(bf16[512,8,128]{2,1,0:T(8,128)(2,1)} %param.29) | copy-start | bytes 3145732
  17.4 2.3 %copy-start.21 = (bf16[512,64,1]{1,0,2:T(8,128)(2,1)S(1)}, bf16[512,64,1]{1,0,2:T(8,128)(2,1)}, u32[]{:S(2)}) copy-start(bf16[512,64,1]{1,0,2:T(8,128)(2,1)} %maximum_bitcast_fusion.1) | copy-start | bytes 196612
  25.5 2.7 %copy-start.14 = (bf16[512,8,128]{2,0,1:T(8,128)(2,1)S(1)}, bf16[512,8,128]{2,0,1:T(8,128)(2,1)}, u32[]{:S(2)}) copy-start(bf16[512,8,128]{2,0,1:T(8,128)(2,1)} %copy_select_fusion) | copy-start | bytes 3145732
  25.5 4.9 %copy-start.6 = (f32[8,256,512]{1,2,0:T(8,128)S(1)}, f32[8,256,512]{1,2,0:T(8,128)}, u32[]{:S(2)}) copy-start(f32[8,256,512]{1,2,0:T(8,128)} %get-tuple-element.133) | copy-start | bytes 12582916
  32.4 4.0 %copy-start.3 = (bf16[8,256,512]{1,2,0:T(8,128)(2,1)}, bf16[8,256,512]{1,2,0:T(8,128)(2,1)S(1)}, u32[]{:S(2)}) copy-start(bf16[8,256,512]{1,2,0:T(8,128)(2,1)S(1)} %multiply_convert_fusion.1) | copy-start | bytes 6291460
  46.9 5.2 %copy-start.10 = (bf16[768,8,256]{2,0,1:T(8,128)(2,1)S(1)}, bf16[768,8,256]{2,0,1:T(8,128)(2,1)}, u32[]{:S(2)}) copy-start(bf16[768,8,256]{2,0,1:T(8,128)(2,1)} %copy-done.9) | copy-start | bytes 9437188
  46.9 7.9 %copy-start.5 = (f32[8,256,768]{1,2,0:T(8,128)S(1)}, f32[8,256,768]{1,2,0:T(8,128)}, u32[]{:S(2)}) copy-start(f32[8,256,768]{1,2,0:T(8,128)} %get-tuple-element.131) | copy-start | bytes 18874372
  50.4 1.7 %copy-start.7 = (bf16[8,256,768]{1,2,0:T(8,128)(2,1)}, bf16[8,256,768]{1,2,0:T(8,128)(2,1)S(1)}, u32[]{:S(2)}) copy-start(bf16[8,256,768]{1,2,0:T(8,128)(2,1)S(1)} %fusion.9) | copy-start | bytes 9437188
  52.0 2.8 %copy-start.15 = (bf16[512,8,128]{2,0,1:T(8,128)(2,1)S(1)}, bf16[512,8,128]{2,0,1:T(8,128)(2,1)}, u32[]{:S(2)}) copy-start(bf16[512,8,128]{2,0,1:T(8,128)(2,1)} %copy_select_fusion) | copy-start | bytes 3145732
  57.7 3.1 %copy-start.1 = (bf16[8,256,768]{1,2,0:T(8,128)(2,1)S(1)}, bf16[8,256,768]{1,2,0:T(8,128)(2,1)}, u32[]{:S(2)}) copy-start(bf16[8,256,768]{1,2,0:T(8,128)(2,1)} %multiply_convert_fusion) | copy-start | bytes 9437188
  57.7 3.5 %copy-start.12 = (f32[512,8,128]{0,2,1:T(8,128)S(1)}, f32[512,8,128]{0,2,1:T(8,128)}, u32[]{:S(2)}) copy-start(f32[512,8,128]{0,2,1:T(8,128)} %convolution_bitcast_fusion.1) | copy-start | bytes 6291460
  61.2 5.9 %copy-start.18 = (f32[768,64]{0,1:T(8,128)}, f32[768,64]{0,1:T(8,128)S(1)}, u32[]{:S(2)}) copy-start(f32[768,64]{0,1:T(8,128)S(1)} %fusion.57) | copy-start | bytes 589828
  61.2 3.5 %copy-start.8 = (bf16[8,256,768]{1,2,0:T(8,128)(2,1)S(1)}, bf16[8,256,768]{1,2,0:T(8,128)(2,1)}, u32[]{:S(2)}) copy-start(bf16[8,256,768]{1,2,0:T(8,128)(2,1)} %copy-done.7) | copy-start | bytes 9437188
  61.2 3.5 %copy-start.11 = (f32[512,8,128]{0,2,1:T(8,128)S(1)}, f32[512,8,128]{0,2,1:T(8,128)}, u32[]{:S(2)}) copy-start(f32[512,8,128]{0,2,1:T(8,128)} %convolution_bitcast_fusion) | copy-start | bytes 6291460
  61.2 3.5 %copy-start.16 = (bf16[512,8,128]{2,0,1:T(8,128)(2,1)S(1)}, bf16[512,8,128]{2,0,1:T(8,128)(2,1)}, u32[]{:S(2)}) copy-start(bf16[512,8,128]{2,0,1:T(8,128)(2,1)} %copy_select_fusion) | copy-start | bytes 3145732
  67.2 2.1 %copy-start.20 = (f32[256,64]{1,0:T(8,128)}, f32[256,64]{1,0:T(8,128)S(1)}, u32[]{:S(2)}) copy-start(f32[256,64]{1,0:T(8,128)S(1)} %copy.225) | copy-start | bytes 196612
  70.0 8.2 %collective-permute-start.1 = (f32[128,576]{1,0:T(8,128)}, f32[128,576]{1,0:T(8,128)}, u32[]{:S(2)}, u32[]{:S(2)}) collective-permute-start(f32[128,576]{1,0:T(8,128)} %fusion.77), channel_id=1, source_target_pairs={{0,1},{1,0},{2,3},{3,2},{4,5},{5,4},{6,7},{7,6},{8,9},{9,8},{10,11... | collective-permute-start | bytes 884744 | tf_op jit(solution)/shard_map/ppermute | solution.py:69
  71.4 3.7 %copy-start.19 = (f32[768,64]{0,1:T(8,128)S(1)}, f32[768,64]{0,1:T(8,128)}, u32[]{:S(2)}) copy-start(f32[768,64]{0,1:T(8,128)} %copy-done.18) | copy-start | bytes 589828
  80.1 13.6 %all-to-all-start.2 = ((f32[8,16,576]{2,1,0:T(8,128)}), f32[8,16,576]{2,1,0:T(8,128)S(1)}, u32[]{:S(2)}, u32[]{:S(2)}) async-start(f32[8,16,576]{2,1,0:T(8,128)} %bitcast.131), calls=%async_computation.2 | async-start | bytes 655360 | tf_op jit(solution)/shard_map/all_to_all | solution.py:178
  86.3 13.3 %collective-permute-start = (bf16[8,32,576]{2,1,0:T(8,128)(2,1)}, bf16[8,32,576]{2,1,0:T(8,128)(2,1)}, u32[]{:S(2)}, u32[]{:S(2)}) collective-permute-start(bf16[8,32,576]{2,1,0:T(8,128)(2,1)} %fusion.76), channel_id=1, source_target_pairs={{0,1},{1,0},{2,3},{3,2},{4,5},{5,4},{6,7},{7,6},{8,9},{9,8},{10,11... | collective-permute-start | bytes 884744 | tf_op jit(solution)/shard_map/ppermute | solution.py:69
  93.7 2.9 %collective-permute-start.2 = (f32[16,576]{1,0:T(8,128)S(1)}, f32[16,576]{1,0:T(8,128)S(1)}, u32[]{:S(2)}, u32[]{:S(2)}) collective-permute-start(f32[16,576]{1,0:T(8,128)S(1)} %reduce_sum.69), channel_id=1, source_target_pairs={{0,16},{16,0},{32,48},{48,32},{64,80},{80,64},{96,112},{112,96},{1... | collective-permute-start | bytes 110600 | tf_op jit(solution)/shard_map/ppermute | solution.py:187
  96.6 8.2 %collective-permute-start.3 = (f32[16,576]{1,0:T(8,128)S(1)}, f32[16,576]{1,0:T(8,128)S(1)}, u32[]{:S(2)}, u32[]{:S(2)}) collective-permute-start(f32[16,576]{1,0:T(8,128)S(1)} %add.144), channel_id=1, source_target_pairs={{0,32},{16,48},{32,0},{48,16},{64,96},{80,112},{96,64},{112,80},{1... | collective-permute-start | bytes 110600 | tf_op jit(solution)/shard_map/ppermute | solution.py:187
  101.4 12.4 %all-to-all-start = ((bf16[8,32,576]{2,1,0:T(8,128)(2,1)}), bf16[8,32,576]{2,1,0:T(8,128)(2,1)S(1)}, u32[]{:S(2)}, u32[]{:S(2)}) async-start(bf16[8,32,576]{2,1,0:T(8,128)(2,1)} %fusion.65), calls=%async_computation | async-start | bytes 655360 | tf_op jit(solution)/shard_map/all_to_all | solution.py:167
  104.8 9.0 %collective-permute-start.4 = (f32[16,576]{1,0:T(8,128)S(1)}, f32[16,576]{1,0:T(8,128)S(1)}, u32[]{:S(2)}, u32[]{:S(2)}) collective-permute-start(f32[16,576]{1,0:T(8,128)S(1)} %add.145), channel_id=1, source_target_pairs={{0,64},{16,80},{32,96},{48,112},{64,0},{80,16},{96,32},{112,48},{1... | collective-permute-start | bytes 110600 | tf_op jit(solution)/shard_map/ppermute | solution.py:187
  114.6 11.0 %all-to-all-start.3 = ((f32[8,16,576]{2,1,0:T(8,128)}), f32[8,16,576]{2,1,0:T(8,128)S(1)}, u32[]{:S(2)}, u32[]{:S(2)}) async-start(f32[8,16,576]{2,1,0:T(8,128)} %broadcast_in_dim.38), calls=%async_computation.3 | async-start | bytes 655360 | tf_op jit(solution)/shard_map/all_to_all | solution.py:190
  119.0 2.7 %copy-start.17 = (bf16[512,8,256]{2,0,1:T(8,128)(2,1)S(1)}, bf16[512,8,256]{2,0,1:T(8,128)(2,1)}, u32[]{:S(2)}) copy-start(bf16[512,8,256]{2,0,1:T(8,128)(2,1)} %fusion.13) | copy-start | bytes 6291460
  119.0 4.2 %copy-start.26 = (f32[512,32]{0,1:T(8,128)S(1)}, f32[512,32]{0,1:T(8,128)}, u32[]{:S(2)}) copy-start(f32[512,32]{0,1:T(8,128)} %copy-done.25) | copy-start | bytes 196612
  123.2 6.8 %copy-start.22 = (bf16[512,64,1]{1,0,2:T(8,128)(2,1)S(1)}, bf16[512,64,1]{1,0,2:T(8,128)(2,1)}, u32[]{:S(2)}) copy-start(bf16[512,64,1]{1,0,2:T(8,128)(2,1)} %maximum_bitcast_fusion.1) | copy-start | bytes 196612
  123.9 6.0 %copy-start.27 = (f32[256,32]{0,1:T(8,128)S(1)}, f32[256,32]{0,1:T(8,128)}, u32[]{:S(2)}) copy-start(f32[256,32]{0,1:T(8,128)} %get-tuple-element.123) | copy-start | bytes 98308
  123.9 6.0 %copy-start.28 = (f32[256,32]{0,1:T(8,128)S(1)}, f32[256,32]{0,1:T(8,128)}, u32[]{:S(2)}) copy-start(f32[256,32]{0,1:T(8,128)} %get-tuple-element.134) | copy-start | bytes 98308
  125.5 33.0 %all-to-all-start.1 = ((bf16[8,64,8,256]{3,1,2,0:T(8,128)(2,1)}), bf16[8,64,8,256]{3,1,2,0:T(8,128)(2,1)}, u32[]{:S(2)}, u32[]{:S(2)}) async-start(bf16[8,64,8,256]{3,1,2,0:T(8,128)(2,1)} %copy.221), calls=%async_computation.1 | async-start | bytes 4194304 | tf_op jit(solution)/shard_map/all_to_all | solution.py:148
  129.9 2.5 %copy-start.4 = (bf16[8,256,512]{1,2,0:T(8,128)(2,1)S(1)}, bf16[8,256,512]{1,2,0:T(8,128)(2,1)}, u32[]{:S(2)}) copy-start(bf16[8,256,512]{1,2,0:T(8,128)(2,1)} %copy-done.3) | copy-start | bytes 6291460
  130.0 4.1 %copy-start.2 = (bf16[8,256,768]{1,2,0:T(8,128)(2,1)S(1)}, bf16[8,256,768]{1,2,0:T(8,128)(2,1)}, u32[]{:S(2)}) copy-start(bf16[8,256,768]{1,2,0:T(8,128)(2,1)} %multiply_convert_fusion) | copy-start | bytes 9437188
  136.3 6.2 %collective-permute-start.5 = (f32[128,576]{1,0:T(8,128)S(1)}, f32[128,576]{1,0:T(8,128)S(1)}, u32[]{:S(2)}, u32[]{:S(2)}) collective-permute-start(f32[128,576]{1,0:T(8,128)S(1)} %bitcast.129), channel_id=1, source_target_pairs={{0,1},{1,0},{2,3},{3,2},{4,5},{5,4},{6,7},{7,6},{8,9},{9,8},{10,11... | collective-permute-start | bytes 884744 | tf_op jit(solution)/shard_map/ppermute | solution.py:69

commit v8 on v7

--- a/solution.py
+++ b/solution.py
@@ -29,16 +29,15 @@
     )
 
 
-def block_gradients(
-    query_nope, query_rope, key_nope, key_rope, values, cotangent, first_row, length, prefix_rows
-):
-    score_scale = (query_nope.shape[-1] + query_rope.shape[-1]) ** (-0.5)
+def block_gradients(query_used, key_used, values, cotangent, first_row, length, prefix_rows):
+    nope_dim = values.shape[-1]
+    score_scale = query_used.shape[-1] ** (-0.5)
     scores = (
-        jnp.einsum("qhd,khd->hqk", query_nope, key_nope, preferred_element_type=jnp.float32)
-        + jnp.einsum("qhr,kr->hqk", query_rope, key_rope, preferred_element_type=jnp.float32)
-    ) * score_scale
-    row_index = first_row + jnp.arange(query_nope.shape[0])
-    col_index = jnp.arange(key_nope.shape[0]) - prefix_rows
+        jnp.einsum("qhd,khd->hqk", query_used, key_used, preferred_element_type=jnp.float32)
+        * score_scale
+    )
+    row_index = first_row + jnp.arange(query_used.shape[0])
+    col_index = jnp.arange(key_used.shape[0]) - prefix_rows
     allowed = (col_index[None, :] < 0) | (col_index[None, :] <= row_index[:, None]) & (
         col_index[None, :] < length
     )
@@ -53,14 +52,12 @@
     score_grad = (
         probability * (prob_grad - jnp.transpose(row_delta)[:, :, None]) * score_scale
     ).astype(jnp.bfloat16)
-    nope_query = jnp.einsum(
-        "hqk,khd->qhd", score_grad, key_nope, preferred_element_type=jnp.float32
-    )
-    rope_query = jnp.einsum("hqk,kr->qhr", score_grad, key_rope, preferred_element_type=jnp.float32)
-    nope_key = jnp.einsum(
-        "hqk,qhd->khd", score_grad, query_nope, preferred_element_type=jnp.float32
-    )
-    rope_key = jnp.einsum("hqk,qhr->kr", score_grad, query_rope, preferred_element_type=jnp.float32)
+    query_part = jnp.einsum("hqk,khd->qhd", score_grad, key_used, preferred_element_type=jnp.float32)
+    key_part = jnp.einsum("hqk,qhd->khd", score_grad, query_used, preferred_element_type=jnp.float32)
+    nope_query = query_part[:, :, :nope_dim]
+    rope_query = query_part[:, :, nope_dim:]
+    nope_key = key_part[:, :, :nope_dim]
+    rope_key = jnp.sum(key_part[:, :, nope_dim:], axis=1)
     value_grad = jnp.einsum("hqk,qhv->khv", weights, cotangent, preferred_element_type=jnp.float32)
     return (nope_query, rope_query, nope_key, rope_key, value_grad)
 
@@ -100,6 +97,11 @@
     ).astype(jnp.bfloat16)
     key_nope = projected[:, :, :nope_dim]
     values = projected[:, :, nope_dim:]
+    query_used = jnp.concatenate([query_nope, query_rope], axis=-1)
+    key_used = jnp.concatenate(
+        [key_nope, jnp.broadcast_to(key_rope[:, None, :], key_rope.shape[:1] + (head_part,) + key_rope.shape[1:])],
+        axis=-1,
+    )
     nope_total = jnp.zeros((key_total, head_part, nope_dim), jnp.float32)
     rope_total = jnp.zeros((key_total, rope_dim), jnp.float32)
     value_total = jnp.zeros((key_total, head_part, value_dim), jnp.float32)
@@ -109,10 +111,8 @@
         last_row = first_row + block_rows
         seen = prefix_rows + last_row
         pieces = block_gradients(
-            query_nope[first_row:last_row],
-            query_rope[first_row:last_row],
-            key_nope[:seen],
-            key_rope[:seen],
+            query_used[first_row:last_row],
+            key_used[:seen],
             values[:seen],
             cotangent[first_row:last_row],
             first_row,

time: 163 us -> 138 us (0.85)
  matrix products: 66.4 us -> 30.9 us
  starting transfers between devices: 31.5 us -> 35.8 us
  other arithmetic: 22.6 us -> 26.3 us
  local copies, waits for them, and re-layouts: 14.1 us -> 15.9 us
    dot_general x10 -> x6, matrix products: 25.9 us -> 10 us  [the longest x2 4.51 us: block_gradients(): jnp.einsum('hqk,khd->qhd', score_grad, key_used, preferred_element_type=j...]
    sub x2 -> x0, matrix products: 13.3 us -> none  [block_gradients(): exponent = jnp.exp(scores - highest)]
    convert_element_type x2, other arithmetic: 6.2 us -> 0.84 us  [block_gradients(): weights = probability.astype(jnp.bfloat16)]
    sub x2 -> x4, other arithmetic: 0.01 us -> 4.94 us  [the longest x2 4.93 us: block_gradients(): exponent = jnp.exp(scores - highest)]
    ppermute x3, waiting for transfers between devices: 1.55 us -> 4.7 us  [on_device(): prefix_own = prefix_own + lax.ppermute(prefix_own, 'dp', partners)]
    dot_general x2, matrix products: 4.95 us -> 1.88 us  [block_gradients(): jnp.einsum('hqk,khv->qhv', weights, values, preferred_element_type=jnp.fl...]
    all_to_all x1, starting transfers between devices: 4.35 us -> 7.2 us  [on_device(): lax.all_to_all(up_part.astype(jnp.bfloat16).reshape((dp_size, -1) + up_pa...]
    concatenate x1, other arithmetic: 0.14 us -> 2.06 us  [on_device(): jnp.concatenate([prefix, jnp.concatenate([latent[:, :latent_dim], token_r...]
  transfers between devices with their start and end apart: 10 -> 10, of which waited for: 4 -> 6; matrix products, arithmetic and copies ran while one was open for 18% -> 17% of each run, Pallas kernels for 0% -> 0%
where the time goes in v8:
time: 138 us
  starting transfers between devices  35.8 us (26%)
  matrix products  30.9 us (22%)
  waiting for transfers between devices  26.7 us (19%)
  other arithmetic  26.3 us (19%)
  local copies, waits for them, and re-layouts  15.9 us (12%)
  between operations  1.9 us (1%)
    all_to_all x1, waiting for transfers between devices, on_device(): lax.all_to_all(up_part.astype(jnp.bfloat16).reshape((dp_size, -1) + up_pa...  14.7 us
    unnamed x48, local copies, waits for them, and re-layouts  8.17 us
    ppermute x3, starting transfers between devices, on_device(): prefix_own = prefix_own + lax.ppermute(prefix_own, 'dp', partners)  7.57 us
    ppermute x3, starting transfers between devices, swap_pair(): return lax.ppermute(values, 'core', [(0, 1), (1, 0)])  7.4 us
    all_to_all x1, starting transfers between devices, on_device(): lax.all_to_all(up_part.astype(jnp.bfloat16).reshape((dp_size, -1) + up_pa...  7.2 us
    all_to_all x1, waiting for transfers between devices, on_device(): lax.all_to_all(prefix_half.reshape((row_size, -1) + prefix_half.shape[1:]...  6.42 us
    all_to_all x1, starting transfers between devices, on_device(): lax.all_to_all(prefix_half.reshape((row_size, -1) + prefix_half.shape[1:]...  5.49 us
    sub x2, other arithmetic, block_gradients(): exponent = jnp.exp(scores - highest)  4.93 us
  transfers between devices with their start and end apart: 10, of which 6 were waited for; matrix products, arithmetic and copies ran while one was open for 17% of the time, Pallas kernels for 0%

profile of v8, /device:TPU:1, one launch (start us, length us, event | category | flops | bytes accessed | tf_op | source)
XLA Modules:
  0.0 137.6 jit_solution(14593529317195478994)
XLA Ops:
  0.7 1.0 slice_convert_fusion.3
  1.7 1.1 slice.241
  2.7 1.2 copy.105
  3.9 0.7 convert_element_type.66
  4.6 1.0 multiply_cosine_fusion
  5.6 0.8 copy.104
  6.3 0.8 copy.103
  7.3 1.2 pad_maximum_fusion.14
  8.5 2.1 %maximum_maximum_fusion.1 = bf16[768,576]{1,0:T(8,128)(2,1)} fusion(bf16[512,32]{1,0:T(8,128)(2,1)} %copy.104, bf16[512,32]{1,0:T(8,128)(2,1)} %copy.103, bf16[512,512]{1,0:T(8,128)(2,1)S(1)} %copy.146, bf16[256,576]{1,0:T(8,128)(2,1)S(1)} %copy.105), kind=kLoop, calls=%fused_computation.69 | loop fusion | flops 3538944 | bytes 1769472 | tf_op jit(solution)/shard_map/concatenate | solution.py:85
  10.9 3.1 %convolution_convert_fusion = bf16[768,8,256]{0,2,1:T(8,128)(2,1)S(1)} fusion(bf16[512,8,256]{2,1,0:T(8,128)(2,1)S(1)} %copy-done, bf16[768,576]{1,0:T(8,128)(2,1)} %maximum_maximum_fusion.1), kind=kOutput, calls=%fused_computation.28 | convolution fusion | flops 1612185600 | bytes 6029312 | tf_op jit(solution)/shard_map/kl,lhd->khd/dot_general | solution.py:95
  14.1 0.7 copy-done.20
  14.9 0.7 slice-done.1
  15.9 1.0 fusion.17
  17.0 0.8 fusion.55
  18.8 2.1 %fusion.108 = (f32[8,256]{1,0:T(8,128)S(1)}, f32[8,256,512]{2,1,0:T(8,128)S(1)}) fusion(f32[8,256,512]{2,1,0:T(8,128)S(1)} %fusion.55, pred[256,512]{1,0:T(8,128)(4,1)S(1)} %fusion.64), kind=kOutput, calls=%fused_computation.152 | output fusion | flops 6291967 | bytes 8527872 | tf_op jit(solution)/shard_map/sub | solution.py:46
  21.3 0.8 fusion.46
  22.1 1.2 multiply_convert_fusion.1
  24.0 0.6 copy-done.7
  24.7 1.9 %convolution_bitcast_fusion.2 = f32[512,8,128]{0,2,1:T(8,128)} fusion(bf16[8,256,512]{2,1,0:T(8,128)(2,1)S(1)} %fusion.20, bf16[512,8,128]{2,0,1:T(8,128)(2,1)S(1)} %copy_select_fusion), kind=kOutput, calls=%fused_computation.40 | convolution fusion | flops 268435456 | bytes 4718592 | tf_op jit(solution)/shard_map/hqk,qhv->khv/dot_general | solution.py:61
  26.9 2.9 %fusion.107 = (f32[8,256]{1,0:T(8,128)S(1)}, f32[8,256,768]{2,1,0:T(8,128)S(1)}) fusion(f32[8,256,768]{2,1,0:T(8,128)S(1)} %fusion.17, pred[256,768]{1,0:T(8,128)(4,1)S(1)} %and_or_fusion), kind=kOutput, calls=%fused_computation.151 | output fusion | flops 9437951 | bytes 12787712 | tf_op jit(solution)/shard_map/sub | solution.py:46
  30.2 1.1 fusion.47
  31.3 0.6 copy-done.4
  31.9 2.6 %multiply_convert_fusion = bf16[8,256,768]{2,1,0:T(8,128)(2,1)} fusion(f32[8,256]{1,0:T(8,128)S(1)} %bitcast.87, f32[8,256,768]{2,1,0:T(8,128)S(1)} %get-tuple-element.131, f32[8,256]{1,0:T(8,128)S(1)} %get-tuple-element.130, bf16[768,8,256]{0,2,1:T(8,128)(2,1)S(1)} %convolution_convert_fusion, bf16[512,8,128]{2,0,1:T(8,128)(2,1)S(1)} %copy_select_fusion), kind=kOutput, calls=%fused_computation.2 | convolution fusion | flops 410517504 | bytes 11550720 | tf_op jit(solution)/shard_map/qhv,khv->hqk/dot_general | solution.py:51
  34.5 3.1 %convolution_bitcast_fusion = f32[768,8,192]{0,2,1:T(8,128)S(1)} fusion(bf16[8,256,768]{2,1,0:T(8,128)(2,1)} %multiply_convert_fusion, bf16[512,8,192]{0,2,1:T(8,128)(2,1)} %copy-done.3), kind=kOutput, calls=%fused_computation.27 | convolution fusion | flops 603979776 | bytes 8650752 | tf_op jit(solution)/shard_map/hqk,qhd->khd/dot_general | solution.py:56
  37.7 1.5 %fusion.5 = bf16[768,8,128]{0,2,1:T(8,128)(2,1)} fusion(f32[768,8,192]{0,2,1:T(8,128)S(1)} %convolution_bitcast_fusion, f32[512,8,128]{0,2,1:T(8,128)S(1)} %slice-done), kind=kLoop, calls=%fused_computation.18 | loop fusion | flops 1572864 | bytes 6815744 | tf_op jit(solution)/shard_map/convert.7
  39.2 1.0 copy-done.5
  40.2 0.7 copy-done.9
  41.1 1.9 %fusion.6 = bf16[768,8,128]{0,2,1:T(8,128)(2,1)} fusion(f32[512,8,128]{0,2,1:T(8,128)S(1)} %copy-done.9, bf16[8,256,768]{2,1,0:T(8,128)(2,1)S(1)} %copy-done.5, bf16[512,8,128]{2,0,1:T(8,128)(2,1)S(1)} %copy-done.11), kind=kOutput, calls=%fused_computation.20 | convolution fusion | flops 404226048 | bytes 7340032 | tf_op jit(solution)/shard_map/hqk,qhv->khv/dot_general | solution.py:61
  43.1 2.2 %fusion.50 = f32[256,512]{1,0:T(8,128)S(1)} fusion(bf16[512,8,256]{2,1,0:T(8,128)(2,1)S(1)} %copy-done, bf16[768,8,128]{0,2,1:T(8,128)(2,1)} %fusion.5, bf16[768,8,128]{0,2,1:T(8,128)(2,1)} %fusion.6), kind=kOutput, calls=%fused_computation.62 | convolution fusion | flops 538968064 | bytes 5767168 | tf_op jit(solution)/shard_map/khd,lhd->kl/dot_general | solution.py:169
  45.3 0.8 copy-done.13
  46.1 0.8 fusion.70
  46.8 1.4 %collective-permute-start.1 = (f32[128,576]{1,0:T(8,128)}, f32[128,576]{1,0:T(8,128)}, u32[]{:S(2)}, u32[]{:S(2)}) collective-permute-start(f32[128,576]{1,0:T(8,128)} %fusion.70), channel_id=1, source_target_pairs={{0,1},{1,0},{2,3},{3,2},{4,5},{5,4},{6,7},{7,6},{8,9},{9,8},{10,11... | collective-permute-start | bytes 884744 | tf_op jit(solution)/shard_map/ppermute | solution.py:66
  48.6 2.1 %fusion.41 = bf16[512,512]{1,0:T(8,128)(2,1)} fusion(bf16[512,8,256]{2,1,0:T(8,128)(2,1)S(1)} %copy-done, bf16[768,8,128]{0,2,1:T(8,128)(2,1)S(1)} %copy-done.15, bf16[768,8,128]{0,2,1:T(8,128)(2,1)S(1)} %copy-done.14), kind=kOutput, calls=%fused_computation.59 | convolution fusion | flops 1078198272 | bytes 5767168 | tf_op jit(solution)/shard_map/khd,lhd->kl/dot_general | solution.py:154
  50.7 0.8 copy.143
  51.4 0.8 copy.142
  52.2 1.3 pad_maximum_fusion.13
  53.5 0.8 fusion.69
  54.3 1.8 %fusion.72 = f32[128,576]{1,0:T(8,128)} fusion(f32[128,576]{1,0:T(8,128)} %collective-permute-done.1, s32[]{:T(128)S(6)} %select_n.50, f32[256,512]{1,0:T(8,128)} %copy-done.13, f32[256,64]{1,0:T(8,128)} %copy-done.16), kind=kLoop, calls=%fused_computation.101 | loop fusion | flops 147456 | bytes 1179652 | tf_op jit(solution)/shard_map/add | solution.py:176
  56.1 5.5 %all-to-all-start.2 = ((f32[8,16,576]{2,1,0:T(8,128)}), f32[8,16,576]{2,1,0:T(8,128)}, u32[]{:S(2)}, u32[]{:S(2)}) async-start(f32[8,16,576]{2,1,0:T(8,128)} %bitcast.81), calls=%async_computation.2 | async-start | bytes 655360 | tf_op jit(solution)/shard_map/all_to_all | solution.py:178
  61.6 1.8 %fusion.62 = bf16[8,32,576]{2,1,0:T(8,128)(2,1)} fusion(bf16[8,32,576]{2,1,0:T(8,128)(2,1)} %collective-permute-done, pred[]{:T(512)S(6)} %eq.2, bf16[8,2,32,576]{3,2,1,0:T(8,128)(2,1)S(1)} %pad_maximum_fusion.13), kind=kLoop, calls=%fused_computation.85 | loop fusion | flops 737280 | bytes 1179649 | tf_op jit(solution)/shard_map/convert_element_type | solution.py:166
  63.4 6.4 %all-to-all-done.2 = f32[8,16,576]{2,1,0:T(8,128)} async-done(((f32[8,16,576]{2,1,0:T(8,128)}), f32[8,16,576]{2,1,0:T(8,128)}, u32[]{:S(2)}, u32[]{:S(2)}) %all-to-all-start.2) | async-done | bytes 294944 | tf_op jit(solution)/shard_map/all_to_all | solution.py:178
  69.8 3.4 %all-to-all-start = ((bf16[8,32,576]{2,1,0:T(8,128)(2,1)}), bf16[8,32,576]{2,1,0:T(8,128)(2,1)S(1)}, u32[]{:S(2)}, u32[]{:S(2)}) async-start(bf16[8,32,576]{2,1,0:T(8,128)(2,1)} %fusion.62), calls=%async_computation | async-start | bytes 655360 | tf_op jit(solution)/shard_map/all_to_all | solution.py:167
  73.3 1.0 reduce_sum.89
  74.3 1.4 collective-permute-start.2
  75.6 1.9 %collective-permute-done.2 = f32[16,576]{1,0:T(8,128)S(1)} collective-permute-done((f32[16,576]{1,0:T(8,128)S(1)}, f32[16,576]{1,0:T(8,128)S(1)}, u32[]{:S(2)}, u32[]{:S(2)}) %collective-permute-start.2) | collective-permute-done | bytes 36896 | tf_op jit(solution)/shard_map/ppermute | solution.py:187
  77.5 2.9 %collective-permute-start.3 = (f32[16,576]{1,0:T(8,128)S(1)}, f32[16,576]{1,0:T(8,128)S(1)}, u32[]{:S(2)}, u32[]{:S(2)}) collective-permute-start(f32[16,576]{1,0:T(8,128)S(1)} %add.133), channel_id=1, source_target_pairs={{0,32},{16,48},{32,0},{48,16},{64,96},{80,112},{96,64},{112,80},{1... | collective-permute-start | bytes 110600 | tf_op jit(solution)/shard_map/ppermute | solution.py:187
  80.4 1.4 %collective-permute-done.3 = f32[16,576]{1,0:T(8,128)S(1)} collective-permute-done((f32[16,576]{1,0:T(8,128)S(1)}, f32[16,576]{1,0:T(8,128)S(1)}, u32[]{:S(2)}, u32[]{:S(2)}) %collective-permute-start.3) | collective-permute-done | bytes 36896 | tf_op jit(solution)/shard_map/ppermute | solution.py:187
  81.9 3.3 %collective-permute-start.4 = (f32[16,576]{1,0:T(8,128)S(1)}, f32[16,576]{1,0:T(8,128)S(1)}, u32[]{:S(2)}, u32[]{:S(2)}) collective-permute-start(f32[16,576]{1,0:T(8,128)S(1)} %add.134), channel_id=1, source_target_pairs={{0,64},{16,80},{32,96},{48,112},{64,0},{80,16},{96,32},{112,48},{1... | collective-permute-start | bytes 110600 | tf_op jit(solution)/shard_map/ppermute | solution.py:187
  85.2 1.4 %collective-permute-done.4 = f32[16,576]{1,0:T(8,128)S(1)} collective-permute-done((f32[16,576]{1,0:T(8,128)S(1)}, f32[16,576]{1,0:T(8,128)S(1)}, u32[]{:S(2)}, u32[]{:S(2)}) %collective-permute-start.4) | collective-permute-done | bytes 36896 | tf_op jit(solution)/shard_map/ppermute | solution.py:187
  86.6 0.7 broadcast_in_dim.41
  87.3 4.7 %all-to-all-start.3 = ((f32[8,16,576]{2,1,0:T(8,128)}), f32[8,16,576]{2,1,0:T(8,128)S(1)}, u32[]{:S(2)}, u32[]{:S(2)}) async-start(f32[8,16,576]{2,1,0:T(8,128)} %broadcast_in_dim.41), calls=%async_computation.3 | async-start | bytes 655360 | tf_op jit(solution)/shard_map/all_to_all | solution.py:190
  92.1 4.0 %fusion.19 = bf16[512,8,256]{2,0,1:T(8,128)(2,1)S(1)} fusion(bf16[768,8,128]{0,2,1:T(8,128)(2,1)} %fusion.6, bf16[768,8,128]{0,2,1:T(8,128)(2,1)} %fusion.5, bf16[768,576]{1,0:T(8,128)(2,1)} %maximum_maximum_fusion.1), kind=kOutput, calls=%fused_computation.37 | convolution fusion | flops 1617952768 | bytes 6029312 | tf_op jit(solution)/shard_map/kl,khd->lhd/dot_general | solution.py:138
  96.0 1.6 %copy.125 = bf16[8,64,8,256]{3,1,2,0:T(8,128)(2,1)} copy(bf16[8,64,8,256]{3,1,0,2:T(8,128)(2,1)S(1)} %bitcast.78) | data formatting | bytes 4194304 | tf_op jit(solution)/shard_map/reshape | solution.py:149
  97.7 0.9 all-to-all-done.3
  98.5 7.2 %all-to-all-start.1 = ((bf16[8,64,8,256]{3,1,2,0:T(8,128)(2,1)}), bf16[8,64,8,256]{3,1,2,0:T(8,128)(2,1)}, u32[]{:S(2)}, u32[]{:S(2)}) async-start(bf16[8,64,8,256]{3,1,2,0:T(8,128)(2,1)} %copy.125), calls=%async_computation.1 | async-start | bytes 4194304 | tf_op jit(solution)/shard_map/all_to_all | solution.py:148
  105.8 3.7 %fusion.25 = f32[256,8,192]{0,2,1:T(8,128)S(1)} fusion(bf16[8,256,768]{2,1,0:T(8,128)(2,1)} %multiply_convert_fusion, bf16[768,8,64]{0,2,1:T(8,128)(2,1)S(1)} %broadcast_in_dim.34, bf16[768,8,128]{0,2,1:T(8,128)(2,1)} %copy-done.1), kind=kOutput, calls=%fused_computation.49 | convolution fusion | flops 608698368 | bytes 7077888 | tf_op jit(solution)/shard_map/hqk,khd->qhd/dot_general | solution.py:55
  109.6 0.8 convolution_bitcast_fusion.3
  110.7 6.0 %collective-permute-start.5 = (f32[128,576]{1,0:T(8,128)S(1)}, f32[128,576]{1,0:T(8,128)S(1)}, u32[]{:S(2)}, u32[]{:S(2)}) collective-permute-start(f32[128,576]{1,0:T(8,128)S(1)} %bitcast.79), channel_id=1, source_target_pairs={{0,1},{1,0},{2,3},{3,2},{4,5},{5,4},{6,7},{7,6},{8,9},{9,8},{10,11... | collective-permute-start | bytes 884744 | tf_op jit(solution)/shard_map/ppermute | solution.py:66
  116.7 1.3 maximum_maximum_fusion
  117.9 0.7 convert_reduce_fusion.1
  118.7 1.0 copy.131
  119.7 14.7 %all-to-all-done.1 = bf16[8,64,8,256]{3,1,2,0:T(8,128)(2,1)} async-done(((bf16[8,64,8,256]{3,1,2,0:T(8,128)(2,1)}), bf16[8,64,8,256]{3,1,2,0:T(8,128)(2,1)}, u32[]{:S(2)}, u32[]{:S(2)}) %all-to-all-start.1) | async-done | bytes 2097184 | tf_op jit(solution)/shard_map/all_to_all | solution.py:148
  134.4 2.0 %convert_reduce_fusion = f32[64,8,256]{2,0,1:T(8,128)S(1)} fusion(bf16[8,64,8,256]{3,1,2,0:T(8,128)(2,1)} %all-to-all-done.1), kind=kLoop, calls=%fused_computation.6 | loop fusion | flops 1966080 | bytes 2621440 | tf_op jit(solution)/shard_map/reduce_sum | solution.py:151
  136.4 1.1 copy.130
  (81 shorter events, 4.2 us)
Async XLA Ops:
  0.6 10.2 %copy-start = (bf16[512,8,256]{2,1,0:T(8,128)(2,1)S(1)}, bf16[512,8,256]{2,1,0:T(8,128)(2,1)}, u32[]{:S(2)}) copy-start(bf16[512,8,256]{2,1,0:T(8,128)(2,1)} %param.28) | copy-start | bytes 6291460
  5.6 8.5 %copy-start.18 = (f32[512,32]{0,1:T(8,128)}, f32[512,32]{0,1:T(8,128)S(1)}, u32[]{:S(2)}) copy-start(f32[512,32]{0,1:T(8,128)S(1)} %get-tuple-element.126) | copy-start | bytes 196612
  7.3 3.3 %copy-start.12 = (bf16[512,8,192]{0,2,1:T(8,128)(2,1)S(1)}, bf16[512,8,192]{0,2,1:T(8,128)(2,1)}, u32[]{:S(2)}) copy-start(bf16[512,8,192]{0,2,1:T(8,128)(2,1)} %param.25) | copy-start | bytes 4718596
  13.9 0.8 copy-start.20
  13.9 1.7 %slice-start.1 = ((bf16[512,8,192]{0,2,1:T(8,128)(2,1)}), bf16[512,8,128]{0,2,1:T(8,128)(2,1)S(1)}, s32[]{:S(2)}) async-start(bf16[512,8,192]{0,2,1:T(8,128)(2,1)} %param.25), calls=%async_computation.5 | async-start | bytes 2097152 | tf_op jit(solution)/shard_map/slice | solution.py:78
  14.1 2.9 %copy-start.1 = (bf16[768,8,128]{0,2,1:T(8,128)(2,1)}, bf16[768,8,128]{0,2,1:T(8,128)(2,1)S(1)}, u32[]{:S(2)}) copy-start(bf16[768,8,128]{0,2,1:T(8,128)(2,1)S(1)} %slice.283) | copy-start | bytes 4718596
  15.8 7.5 %copy-start.3 = (bf16[512,8,192]{0,2,1:T(8,128)(2,1)}, bf16[512,8,192]{0,2,1:T(8,128)(2,1)S(1)}, u32[]{:S(2)}) copy-start(bf16[512,8,192]{0,2,1:T(8,128)(2,1)S(1)} %pad_maximum_fusion.8) | copy-start | bytes 4718596
  17.0 1.5 %copy-start.17 = (bf16[512,8,128]{2,1,0:T(8,128)(2,1)S(1)}, bf16[512,8,128]{2,1,0:T(8,128)(2,1)}, u32[]{:S(2)}) copy-start(bf16[512,8,128]{2,1,0:T(8,128)(2,1)} %param.29) | copy-start | bytes 3145732
  18.7 13.2 %copy-start.10 = (bf16[512,8,128]{2,0,1:T(8,128)(2,1)}, bf16[512,8,128]{2,0,1:T(8,128)(2,1)S(1)}, u32[]{:S(2)}) copy-start(bf16[512,8,128]{2,0,1:T(8,128)(2,1)S(1)} %copy_select_fusion) | copy-start | bytes 3145732
  23.3 1.3 copy-start.7
  23.9 2.7 %copy-start.6 = (f32[512,8,192]{0,2,1:T(8,128)}, f32[512,8,192]{0,2,1:T(8,128)S(1)}, u32[]{:S(2)}) copy-start(f32[512,8,192]{0,2,1:T(8,128)S(1)} %convolution_bitcast_fusion.1) | copy-start | bytes 9437188
  30.2 1.7 %copy-start.4 = (bf16[8,256,768]{2,1,0:T(8,128)(2,1)}, bf16[8,256,768]{2,1,0:T(8,128)(2,1)S(1)}, u32[]{:S(2)}) copy-start(bf16[8,256,768]{2,1,0:T(8,128)(2,1)S(1)} %fusion.10) | copy-start | bytes 9437188
  34.5 3.2 %slice-start = ((f32[512,8,192]{0,2,1:T(8,128)}), f32[512,8,128]{0,2,1:T(8,128)S(1)}, s32[]{:S(2)}) async-start(f32[512,8,192]{0,2,1:T(8,128)} %copy-done.6), calls=%async_computation.4 | async-start | bytes 4194304 | tf_op jit(solution)/shard_map/slice | solution.py:59
  37.7 2.5 %copy-start.5 = (bf16[8,256,768]{2,1,0:T(8,128)(2,1)S(1)}, bf16[8,256,768]{2,1,0:T(8,128)(2,1)}, u32[]{:S(2)}) copy-start(bf16[8,256,768]{2,1,0:T(8,128)(2,1)} %copy-done.4) | copy-start | bytes 9437188
  37.7 3.1 %copy-start.9 = (f32[512,8,128]{0,2,1:T(8,128)S(1)}, f32[512,8,128]{0,2,1:T(8,128)}, u32[]{:S(2)}) copy-start(f32[512,8,128]{0,2,1:T(8,128)} %convolution_bitcast_fusion.2) | copy-start | bytes 6291460
  37.7 3.3 %copy-start.11 = (bf16[512,8,128]{2,0,1:T(8,128)(2,1)S(1)}, bf16[512,8,128]{2,0,1:T(8,128)(2,1)}, u32[]{:S(2)}) copy-start(bf16[512,8,128]{2,0,1:T(8,128)(2,1)} %copy-done.10) | copy-start | bytes 3145732
  43.0 2.2 %copy-start.16 = (f32[256,64]{1,0:T(8,128)}, f32[256,64]{1,0:T(8,128)S(1)}, u32[]{:S(2)}) copy-start(f32[256,64]{1,0:T(8,128)S(1)} %copy.129) | copy-start | bytes 196612
  43.1 5.5 %copy-start.14 = (bf16[768,8,128]{0,2,1:T(8,128)(2,1)S(1)}, bf16[768,8,128]{0,2,1:T(8,128)(2,1)}, u32[]{:S(2)}) copy-start(bf16[768,8,128]{0,2,1:T(8,128)(2,1)} %fusion.6) | copy-start | bytes 4718596
  43.1 5.5 %copy-start.15 = (bf16[768,8,128]{0,2,1:T(8,128)(2,1)S(1)}, bf16[768,8,128]{0,2,1:T(8,128)(2,1)}, u32[]{:S(2)}) copy-start(bf16[768,8,128]{0,2,1:T(8,128)(2,1)} %fusion.5) | copy-start | bytes 4718596
  45.3 0.8 copy-start.13
  46.8 7.4 %collective-permute-start.1 = (f32[128,576]{1,0:T(8,128)}, f32[128,576]{1,0:T(8,128)}, u32[]{:S(2)}, u32[]{:S(2)}) collective-permute-start(f32[128,576]{1,0:T(8,128)} %fusion.70), channel_id=1, source_target_pairs={{0,1},{1,0},{2,3},{3,2},{4,5},{5,4},{6,7},{7,6},{8,9},{9,8},{10,11... | collective-permute-start | bytes 884744 | tf_op jit(solution)/shard_map/ppermute | solution.py:66
  54.3 7.3 %collective-permute-start = (bf16[8,32,576]{2,1,0:T(8,128)(2,1)}, bf16[8,32,576]{2,1,0:T(8,128)(2,1)}, u32[]{:S(2)}, u32[]{:S(2)}) collective-permute-start(bf16[8,32,576]{2,1,0:T(8,128)(2,1)} %fusion.69), channel_id=1, source_target_pairs={{0,1},{1,0},{2,3},{3,2},{4,5},{5,4},{6,7},{7,6},{8,9},{9,8},{10,11... | collective-permute-start | bytes 884744 | tf_op jit(solution)/shard_map/ppermute | solution.py:66
  56.1 13.7 %all-to-all-start.2 = ((f32[8,16,576]{2,1,0:T(8,128)}), f32[8,16,576]{2,1,0:T(8,128)}, u32[]{:S(2)}, u32[]{:S(2)}) async-start(f32[8,16,576]{2,1,0:T(8,128)} %bitcast.81), calls=%async_computation.2 | async-start | bytes 655360 | tf_op jit(solution)/shard_map/all_to_all | solution.py:178
  69.8 16.7 %all-to-all-start = ((bf16[8,32,576]{2,1,0:T(8,128)(2,1)}), bf16[8,32,576]{2,1,0:T(8,128)(2,1)S(1)}, u32[]{:S(2)}, u32[]{:S(2)}) async-start(bf16[8,32,576]{2,1,0:T(8,128)(2,1)} %fusion.62), calls=%async_computation | async-start | bytes 655360 | tf_op jit(solution)/shard_map/all_to_all | solution.py:167
  74.3 3.2 %collective-permute-start.2 = (f32[16,576]{1,0:T(8,128)S(1)}, f32[16,576]{1,0:T(8,128)S(1)}, u32[]{:S(2)}, u32[]{:S(2)}) collective-permute-start(f32[16,576]{1,0:T(8,128)S(1)} %reduce_sum.89), channel_id=1, source_target_pairs={{0,16},{16,0},{32,48},{48,32},{64,80},{80,64},{96,112},{112,96},{1... | collective-permute-start | bytes 110600 | tf_op jit(solution)/shard_map/ppermute | solution.py:187
  77.5 4.4 %collective-permute-start.3 = (f32[16,576]{1,0:T(8,128)S(1)}, f32[16,576]{1,0:T(8,128)S(1)}, u32[]{:S(2)}, u32[]{:S(2)}) collective-permute-start(f32[16,576]{1,0:T(8,128)S(1)} %add.133), channel_id=1, source_target_pairs={{0,32},{16,48},{32,0},{48,16},{64,96},{80,112},{96,64},{112,80},{1... | collective-permute-start | bytes 110600 | tf_op jit(solution)/shard_map/ppermute | solution.py:187
  81.9 4.7 %collective-permute-start.4 = (f32[16,576]{1,0:T(8,128)S(1)}, f32[16,576]{1,0:T(8,128)S(1)}, u32[]{:S(2)}, u32[]{:S(2)}) collective-permute-start(f32[16,576]{1,0:T(8,128)S(1)} %add.134), channel_id=1, source_target_pairs={{0,64},{16,80},{32,96},{48,112},{64,0},{80,16},{96,32},{112,48},{1... | collective-permute-start | bytes 110600 | tf_op jit(solution)/shard_map/ppermute | solution.py:187
  87.3 11.2 %all-to-all-start.3 = ((f32[8,16,576]{2,1,0:T(8,128)}), f32[8,16,576]{2,1,0:T(8,128)S(1)}, u32[]{:S(2)}, u32[]{:S(2)}) async-start(f32[8,16,576]{2,1,0:T(8,128)} %broadcast_in_dim.41), calls=%async_computation.3 | async-start | bytes 655360 | tf_op jit(solution)/shard_map/all_to_all | solution.py:190
  98.5 35.9 %all-to-all-start.1 = ((bf16[8,64,8,256]{3,1,2,0:T(8,128)(2,1)}), bf16[8,64,8,256]{3,1,2,0:T(8,128)(2,1)}, u32[]{:S(2)}, u32[]{:S(2)}) async-start(bf16[8,64,8,256]{3,1,2,0:T(8,128)(2,1)} %copy.125), calls=%async_computation.1 | async-start | bytes 4194304 | tf_op jit(solution)/shard_map/all_to_all | solution.py:148
  105.8 3.8 %copy-start.2 = (bf16[768,8,128]{0,2,1:T(8,128)(2,1)S(1)}, bf16[768,8,128]{0,2,1:T(8,128)(2,1)}, u32[]{:S(2)}) copy-start(bf16[768,8,128]{0,2,1:T(8,128)(2,1)} %copy-done.1) | copy-start | bytes 4718596
  105.8 3.8 %copy-start.8 = (bf16[8,256,512]{2,1,0:T(8,128)(2,1)S(1)}, bf16[8,256,512]{2,1,0:T(8,128)(2,1)}, u32[]{:S(2)}) copy-start(bf16[8,256,512]{2,1,0:T(8,128)(2,1)} %copy-done.7) | copy-start | bytes 6291460
  109.5 0.9 copy-start.19
  109.5 0.9 copy-start.21
  110.7 8.0 %collective-permute-start.5 = (f32[128,576]{1,0:T(8,128)S(1)}, f32[128,576]{1,0:T(8,128)S(1)}, u32[]{:S(2)}, u32[]{:S(2)}) collective-permute-start(f32[128,576]{1,0:T(8,128)S(1)} %bitcast.79), channel_id=1, source_target_pairs={{0,1},{1,0},{2,3},{3,2},{4,5},{5,4},{6,7},{7,6},{8,9},{9,8},{10,11... | collective-permute-start | bytes 884744 | tf_op jit(solution)/shard_map/ppermute | solution.py:66

commit v9 on v8

--- a/solution.py
+++ b/solution.py
@@ -66,7 +66,7 @@
     return lax.ppermute(values, "core", [(0, 1), (1, 0)])
 
 
-def on_device(queries, latent, prefix, kv_up, out_grad, lengths, positions):
+def device_step(queries, latent, prefix, kv_up, out_grad, lengths, positions):
     seq_len = queries.shape[0]
     latent_dim = kv_up.shape[0]
     value_dim = out_grad.shape[2]
@@ -146,7 +146,11 @@
     )
     dp_size = lax.axis_size("dp")
     up_pieces = lax.all_to_all(
-        up_part.astype(jnp.bfloat16).reshape((dp_size, -1) + up_part.shape[1:]), "dp", 0, 0, tiled=False
+        up_part.astype(jnp.bfloat16).reshape((dp_size, -1) + up_part.shape[1:]),
+        "dp",
+        0,
+        0,
+        tiled=False,
     )
     up_grad = jnp.sum(up_pieces.astype(jnp.float32), axis=0)
     token_grad = projected_grad[prefix_rows:]
@@ -213,7 +217,7 @@
         P("dp", None),
     )
     return jax.shard_map(
-        on_device,
+        device_step,
         mesh=split,
         in_specs=placed,
         out_specs=(P("dp", head, None), P(("dp",) + head, None), P("dp", head, None), P()),

time: 138 us -> 138 us (level)
  no operation moved by 1% of the time
where the time goes in v9:
time: 138 us
  starting transfers between devices  35.8 us (26%)
  matrix products  30.9 us (22%)
  waiting for transfers between devices  26.7 us (19%)
  other arithmetic  26.3 us (19%)
  local copies, waits for them, and re-layouts  15.9 us (12%)
  between operations  1.9 us (1%)
    all_to_all x1, waiting for transfers between devices, device_step(): lax.all_to_all(up_part.astype(jnp.bfloat16).reshape((dp_size, -1) + up_pa...  14.7 us
    unnamed x48, local copies, waits for them, and re-layouts  8.17 us
    ppermute x3, starting transfers between devices, device_step(): prefix_own = prefix_own + lax.ppermute(prefix_own, 'dp', partners)  7.57 us
    ppermute x3, starting transfers between devices, swap_pair(): return lax.ppermute(values, 'core', [(0, 1), (1, 0)])  7.4 us
    all_to_all x1, starting transfers between devices, device_step(): lax.all_to_all(up_part.astype(jnp.bfloat16).reshape((dp_size, -1) + up_pa...  7.2 us
    all_to_all x1, waiting for transfers between devices, device_step(): lax.all_to_all(prefix_half.reshape((row_size, -1) + prefix_half.shape[1:]...  6.42 us
    all_to_all x1, starting transfers between devices, device_step(): lax.all_to_all(prefix_half.reshape((row_size, -1) + prefix_half.shape[1:]...  5.49 us
    sub x2, other arithmetic, block_gradients(): exponent = jnp.exp(scores - highest)  4.93 us
  transfers between devices with their start and end apart: 10, of which 6 were waited for; matrix products, arithmetic and copies ran while one was open for 17% of the time, Pallas kernels for 0%

profile of v9, /device:TPU:1, one launch (start us, length us, event | category | flops | bytes accessed | tf_op | source)
XLA Modules:
  0.0 137.6 jit_solution(14593529317195478994)
XLA Ops:
  0.7 1.0 slice_convert_fusion.3
  1.7 1.1 slice.241
  2.7 1.2 copy.105
  3.9 0.7 convert_element_type.66
  4.6 1.0 multiply_cosine_fusion
  5.6 0.8 copy.104
  6.3 0.8 copy.103
  7.3 1.2 pad_maximum_fusion.14
  8.5 2.1 %maximum_maximum_fusion.1 = bf16[768,576]{1,0:T(8,128)(2,1)} fusion(bf16[512,32]{1,0:T(8,128)(2,1)} %copy.104, bf16[512,32]{1,0:T(8,128)(2,1)} %copy.103, bf16[512,512]{1,0:T(8,128)(2,1)S(1)} %copy.146, bf16[256,576]{1,0:T(8,128)(2,1)S(1)} %copy.105), kind=kLoop, calls=%fused_computation.69 | loop fusion | flops 3538944 | bytes 1769472 | tf_op jit(solution)/shard_map/concatenate | solution.py:85
  10.9 3.1 %convolution_convert_fusion = bf16[768,8,256]{0,2,1:T(8,128)(2,1)S(1)} fusion(bf16[512,8,256]{2,1,0:T(8,128)(2,1)S(1)} %copy-done, bf16[768,576]{1,0:T(8,128)(2,1)} %maximum_maximum_fusion.1), kind=kOutput, calls=%fused_computation.28 | convolution fusion | flops 1612185600 | bytes 6029312 | tf_op jit(solution)/shard_map/kl,lhd->khd/dot_general | solution.py:95
  14.1 0.7 copy-done.20
  14.9 0.7 slice-done.1
  15.9 1.0 fusion.17
  17.0 0.8 fusion.55
  18.8 2.1 %fusion.108 = (f32[8,256]{1,0:T(8,128)S(1)}, f32[8,256,512]{2,1,0:T(8,128)S(1)}) fusion(f32[8,256,512]{2,1,0:T(8,128)S(1)} %fusion.55, pred[256,512]{1,0:T(8,128)(4,1)S(1)} %fusion.64), kind=kOutput, calls=%fused_computation.152 | output fusion | flops 6291967 | bytes 8527872 | tf_op jit(solution)/shard_map/sub | solution.py:46
  21.3 0.8 fusion.46
  22.1 1.2 multiply_convert_fusion.1
  24.0 0.6 copy-done.7
  24.7 1.9 %convolution_bitcast_fusion.2 = f32[512,8,128]{0,2,1:T(8,128)} fusion(bf16[8,256,512]{2,1,0:T(8,128)(2,1)S(1)} %fusion.20, bf16[512,8,128]{2,0,1:T(8,128)(2,1)S(1)} %copy_select_fusion), kind=kOutput, calls=%fused_computation.40 | convolution fusion | flops 268435456 | bytes 4718592 | tf_op jit(solution)/shard_map/hqk,qhv->khv/dot_general | solution.py:61
  26.9 2.9 %fusion.107 = (f32[8,256]{1,0:T(8,128)S(1)}, f32[8,256,768]{2,1,0:T(8,128)S(1)}) fusion(f32[8,256,768]{2,1,0:T(8,128)S(1)} %fusion.17, pred[256,768]{1,0:T(8,128)(4,1)S(1)} %and_or_fusion), kind=kOutput, calls=%fused_computation.151 | output fusion | flops 9437951 | bytes 12787712 | tf_op jit(solution)/shard_map/sub | solution.py:46
  30.2 1.1 fusion.47
  31.3 0.6 copy-done.4
  31.9 2.6 %multiply_convert_fusion = bf16[8,256,768]{2,1,0:T(8,128)(2,1)} fusion(f32[8,256]{1,0:T(8,128)S(1)} %bitcast.87, f32[8,256,768]{2,1,0:T(8,128)S(1)} %get-tuple-element.131, f32[8,256]{1,0:T(8,128)S(1)} %get-tuple-element.130, bf16[768,8,256]{0,2,1:T(8,128)(2,1)S(1)} %convolution_convert_fusion, bf16[512,8,128]{2,0,1:T(8,128)(2,1)S(1)} %copy_select_fusion), kind=kOutput, calls=%fused_computation.2 | convolution fusion | flops 410517504 | bytes 11550720 | tf_op jit(solution)/shard_map/qhv,khv->hqk/dot_general | solution.py:51
  34.5 3.1 %convolution_bitcast_fusion = f32[768,8,192]{0,2,1:T(8,128)S(1)} fusion(bf16[8,256,768]{2,1,0:T(8,128)(2,1)} %multiply_convert_fusion, bf16[512,8,192]{0,2,1:T(8,128)(2,1)} %copy-done.3), kind=kOutput, calls=%fused_computation.27 | convolution fusion | flops 603979776 | bytes 8650752 | tf_op jit(solution)/shard_map/hqk,qhd->khd/dot_general | solution.py:56
  37.7 1.5 %fusion.5 = bf16[768,8,128]{0,2,1:T(8,128)(2,1)} fusion(f32[768,8,192]{0,2,1:T(8,128)S(1)} %convolution_bitcast_fusion, f32[512,8,128]{0,2,1:T(8,128)S(1)} %slice-done), kind=kLoop, calls=%fused_computation.18 | loop fusion | flops 1572864 | bytes 6815744 | tf_op jit(solution)/shard_map/convert.7
  39.2 1.0 copy-done.5
  40.2 0.7 copy-done.9
  41.1 1.9 %fusion.6 = bf16[768,8,128]{0,2,1:T(8,128)(2,1)} fusion(f32[512,8,128]{0,2,1:T(8,128)S(1)} %copy-done.9, bf16[8,256,768]{2,1,0:T(8,128)(2,1)S(1)} %copy-done.5, bf16[512,8,128]{2,0,1:T(8,128)(2,1)S(1)} %copy-done.11), kind=kOutput, calls=%fused_computation.20 | convolution fusion | flops 404226048 | bytes 7340032 | tf_op jit(solution)/shard_map/hqk,qhv->khv/dot_general | solution.py:61
  43.1 2.2 %fusion.50 = f32[256,512]{1,0:T(8,128)S(1)} fusion(bf16[512,8,256]{2,1,0:T(8,128)(2,1)S(1)} %copy-done, bf16[768,8,128]{0,2,1:T(8,128)(2,1)} %fusion.5, bf16[768,8,128]{0,2,1:T(8,128)(2,1)} %fusion.6), kind=kOutput, calls=%fused_computation.62 | convolution fusion | flops 538968064 | bytes 5767168 | tf_op jit(solution)/shard_map/khd,lhd->kl/dot_general | solution.py:173
  45.3 0.8 copy-done.13
  46.1 0.8 fusion.70
  46.8 1.4 %collective-permute-start.1 = (f32[128,576]{1,0:T(8,128)}, f32[128,576]{1,0:T(8,128)}, u32[]{:S(2)}, u32[]{:S(2)}) collective-permute-start(f32[128,576]{1,0:T(8,128)} %fusion.70), channel_id=1, source_target_pairs={{0,1},{1,0},{2,3},{3,2},{4,5},{5,4},{6,7},{7,6},{8,9},{9,8},{10,11... | collective-permute-start | bytes 884744 | tf_op jit(solution)/shard_map/ppermute | solution.py:66
  48.6 2.1 %fusion.41 = bf16[512,512]{1,0:T(8,128)(2,1)} fusion(bf16[512,8,256]{2,1,0:T(8,128)(2,1)S(1)} %copy-done, bf16[768,8,128]{0,2,1:T(8,128)(2,1)S(1)} %copy-done.15, bf16[768,8,128]{0,2,1:T(8,128)(2,1)S(1)} %copy-done.14), kind=kOutput, calls=%fused_computation.59 | convolution fusion | flops 1078198272 | bytes 5767168 | tf_op jit(solution)/shard_map/khd,lhd->kl/dot_general | solution.py:158
  50.7 0.8 copy.143
  51.4 0.8 copy.142
  52.2 1.3 pad_maximum_fusion.13
  53.5 0.8 fusion.69
  54.3 1.8 %fusion.72 = f32[128,576]{1,0:T(8,128)} fusion(f32[128,576]{1,0:T(8,128)} %collective-permute-done.1, s32[]{:T(128)S(6)} %select_n.50, f32[256,512]{1,0:T(8,128)} %copy-done.13, f32[256,64]{1,0:T(8,128)} %copy-done.16), kind=kLoop, calls=%fused_computation.101 | loop fusion | flops 147456 | bytes 1179652 | tf_op jit(solution)/shard_map/add | solution.py:180
  56.1 5.5 %all-to-all-start.2 = ((f32[8,16,576]{2,1,0:T(8,128)}), f32[8,16,576]{2,1,0:T(8,128)}, u32[]{:S(2)}, u32[]{:S(2)}) async-start(f32[8,16,576]{2,1,0:T(8,128)} %bitcast.81), calls=%async_computation.2 | async-start | bytes 655360 | tf_op jit(solution)/shard_map/all_to_all | solution.py:182
  61.6 1.8 %fusion.62 = bf16[8,32,576]{2,1,0:T(8,128)(2,1)} fusion(bf16[8,32,576]{2,1,0:T(8,128)(2,1)} %collective-permute-done, pred[]{:T(512)S(6)} %eq.2, bf16[8,2,32,576]{3,2,1,0:T(8,128)(2,1)S(1)} %pad_maximum_fusion.13), kind=kLoop, calls=%fused_computation.85 | loop fusion | flops 737280 | bytes 1179649 | tf_op jit(solution)/shard_map/convert_element_type | solution.py:170
  63.4 6.4 %all-to-all-done.2 = f32[8,16,576]{2,1,0:T(8,128)} async-done(((f32[8,16,576]{2,1,0:T(8,128)}), f32[8,16,576]{2,1,0:T(8,128)}, u32[]{:S(2)}, u32[]{:S(2)}) %all-to-all-start.2) | async-done | bytes 294944 | tf_op jit(solution)/shard_map/all_to_all | solution.py:182
  69.8 3.4 %all-to-all-start = ((bf16[8,32,576]{2,1,0:T(8,128)(2,1)}), bf16[8,32,576]{2,1,0:T(8,128)(2,1)S(1)}, u32[]{:S(2)}, u32[]{:S(2)}) async-start(bf16[8,32,576]{2,1,0:T(8,128)(2,1)} %fusion.62), calls=%async_computation | async-start | bytes 655360 | tf_op jit(solution)/shard_map/all_to_all | solution.py:171
  73.3 1.0 reduce_sum.89
  74.3 1.4 collective-permute-start.2
  75.6 1.9 %collective-permute-done.2 = f32[16,576]{1,0:T(8,128)S(1)} collective-permute-done((f32[16,576]{1,0:T(8,128)S(1)}, f32[16,576]{1,0:T(8,128)S(1)}, u32[]{:S(2)}, u32[]{:S(2)}) %collective-permute-start.2) | collective-permute-done | bytes 36896 | tf_op jit(solution)/shard_map/ppermute | solution.py:191
  77.5 2.9 %collective-permute-start.3 = (f32[16,576]{1,0:T(8,128)S(1)}, f32[16,576]{1,0:T(8,128)S(1)}, u32[]{:S(2)}, u32[]{:S(2)}) collective-permute-start(f32[16,576]{1,0:T(8,128)S(1)} %add.133), channel_id=1, source_target_pairs={{0,32},{16,48},{32,0},{48,16},{64,96},{80,112},{96,64},{112,80},{1... | collective-permute-start | bytes 110600 | tf_op jit(solution)/shard_map/ppermute | solution.py:191
  80.4 1.4 %collective-permute-done.3 = f32[16,576]{1,0:T(8,128)S(1)} collective-permute-done((f32[16,576]{1,0:T(8,128)S(1)}, f32[16,576]{1,0:T(8,128)S(1)}, u32[]{:S(2)}, u32[]{:S(2)}) %collective-permute-start.3) | collective-permute-done | bytes 36896 | tf_op jit(solution)/shard_map/ppermute | solution.py:191
  81.9 3.3 %collective-permute-start.4 = (f32[16,576]{1,0:T(8,128)S(1)}, f32[16,576]{1,0:T(8,128)S(1)}, u32[]{:S(2)}, u32[]{:S(2)}) collective-permute-start(f32[16,576]{1,0:T(8,128)S(1)} %add.134), channel_id=1, source_target_pairs={{0,64},{16,80},{32,96},{48,112},{64,0},{80,16},{96,32},{112,48},{1... | collective-permute-start | bytes 110600 | tf_op jit(solution)/shard_map/ppermute | solution.py:191
  85.2 1.4 %collective-permute-done.4 = f32[16,576]{1,0:T(8,128)S(1)} collective-permute-done((f32[16,576]{1,0:T(8,128)S(1)}, f32[16,576]{1,0:T(8,128)S(1)}, u32[]{:S(2)}, u32[]{:S(2)}) %collective-permute-start.4) | collective-permute-done | bytes 36896 | tf_op jit(solution)/shard_map/ppermute | solution.py:191
  86.6 0.7 broadcast_in_dim.41
  87.3 4.7 %all-to-all-start.3 = ((f32[8,16,576]{2,1,0:T(8,128)}), f32[8,16,576]{2,1,0:T(8,128)S(1)}, u32[]{:S(2)}, u32[]{:S(2)}) async-start(f32[8,16,576]{2,1,0:T(8,128)} %broadcast_in_dim.41), calls=%async_computation.3 | async-start | bytes 655360 | tf_op jit(solution)/shard_map/all_to_all | solution.py:194
  92.1 4.0 %fusion.19 = bf16[512,8,256]{2,0,1:T(8,128)(2,1)S(1)} fusion(bf16[768,8,128]{0,2,1:T(8,128)(2,1)} %fusion.6, bf16[768,8,128]{0,2,1:T(8,128)(2,1)} %fusion.5, bf16[768,576]{1,0:T(8,128)(2,1)} %maximum_maximum_fusion.1), kind=kOutput, calls=%fused_computation.37 | convolution fusion | flops 1617952768 | bytes 6029312 | tf_op jit(solution)/shard_map/kl,khd->lhd/dot_general | solution.py:138
  96.0 1.6 %copy.125 = bf16[8,64,8,256]{3,1,2,0:T(8,128)(2,1)} copy(bf16[8,64,8,256]{3,1,0,2:T(8,128)(2,1)S(1)} %bitcast.78) | data formatting | bytes 4194304 | tf_op jit(solution)/shard_map/reshape | solution.py:149
  97.7 0.9 all-to-all-done.3
  98.5 7.2 %all-to-all-start.1 = ((bf16[8,64,8,256]{3,1,2,0:T(8,128)(2,1)}), bf16[8,64,8,256]{3,1,2,0:T(8,128)(2,1)}, u32[]{:S(2)}, u32[]{:S(2)}) async-start(bf16[8,64,8,256]{3,1,2,0:T(8,128)(2,1)} %copy.125), calls=%async_computation.1 | async-start | bytes 4194304 | tf_op jit(solution)/shard_map/all_to_all | solution.py:148
  105.8 3.7 %fusion.25 = f32[256,8,192]{0,2,1:T(8,128)S(1)} fusion(bf16[8,256,768]{2,1,0:T(8,128)(2,1)} %multiply_convert_fusion, bf16[768,8,64]{0,2,1:T(8,128)(2,1)S(1)} %broadcast_in_dim.34, bf16[768,8,128]{0,2,1:T(8,128)(2,1)} %copy-done.1), kind=kOutput, calls=%fused_computation.49 | convolution fusion | flops 608698368 | bytes 7077888 | tf_op jit(solution)/shard_map/hqk,khd->qhd/dot_general | solution.py:55
  109.6 0.8 convolution_bitcast_fusion.3
  110.7 6.0 %collective-permute-start.5 = (f32[128,576]{1,0:T(8,128)S(1)}, f32[128,576]{1,0:T(8,128)S(1)}, u32[]{:S(2)}, u32[]{:S(2)}) collective-permute-start(f32[128,576]{1,0:T(8,128)S(1)} %bitcast.79), channel_id=1, source_target_pairs={{0,1},{1,0},{2,3},{3,2},{4,5},{5,4},{6,7},{7,6},{8,9},{9,8},{10,11... | collective-permute-start | bytes 884744 | tf_op jit(solution)/shard_map/ppermute | solution.py:66
  116.7 1.3 maximum_maximum_fusion
  117.9 0.7 convert_reduce_fusion.1
  118.7 1.0 copy.131
  119.7 14.7 %all-to-all-done.1 = bf16[8,64,8,256]{3,1,2,0:T(8,128)(2,1)} async-done(((bf16[8,64,8,256]{3,1,2,0:T(8,128)(2,1)}), bf16[8,64,8,256]{3,1,2,0:T(8,128)(2,1)}, u32[]{:S(2)}, u32[]{:S(2)}) %all-to-all-start.1) | async-done | bytes 2097184 | tf_op jit(solution)/shard_map/all_to_all | solution.py:148
  134.4 2.0 %convert_reduce_fusion = f32[64,8,256]{2,0,1:T(8,128)S(1)} fusion(bf16[8,64,8,256]{3,1,2,0:T(8,128)(2,1)} %all-to-all-done.1), kind=kLoop, calls=%fused_computation.6 | loop fusion | flops 1966080 | bytes 2621440 | tf_op jit(solution)/shard_map/reduce_sum | solution.py:155
  136.4 1.1 copy.130
  (81 shorter events, 4.2 us)
Async XLA Ops:
  0.6 10.2 %copy-start = (bf16[512,8,256]{2,1,0:T(8,128)(2,1)S(1)}, bf16[512,8,256]{2,1,0:T(8,128)(2,1)}, u32[]{:S(2)}) copy-start(bf16[512,8,256]{2,1,0:T(8,128)(2,1)} %param.28) | copy-start | bytes 6291460
  5.6 8.5 %copy-start.18 = (f32[512,32]{0,1:T(8,128)}, f32[512,32]{0,1:T(8,128)S(1)}, u32[]{:S(2)}) copy-start(f32[512,32]{0,1:T(8,128)S(1)} %get-tuple-element.126) | copy-start | bytes 196612
  7.3 3.3 %copy-start.12 = (bf16[512,8,192]{0,2,1:T(8,128)(2,1)S(1)}, bf16[512,8,192]{0,2,1:T(8,128)(2,1)}, u32[]{:S(2)}) copy-start(bf16[512,8,192]{0,2,1:T(8,128)(2,1)} %param.25) | copy-start | bytes 4718596
  13.9 0.8 copy-start.20
  13.9 1.7 %slice-start.1 = ((bf16[512,8,192]{0,2,1:T(8,128)(2,1)}), bf16[512,8,128]{0,2,1:T(8,128)(2,1)S(1)}, s32[]{:S(2)}) async-start(bf16[512,8,192]{0,2,1:T(8,128)(2,1)} %param.25), calls=%async_computation.5 | async-start | bytes 2097152 | tf_op jit(solution)/shard_map/slice | solution.py:78
  14.1 2.9 %copy-start.1 = (bf16[768,8,128]{0,2,1:T(8,128)(2,1)}, bf16[768,8,128]{0,2,1:T(8,128)(2,1)S(1)}, u32[]{:S(2)}) copy-start(bf16[768,8,128]{0,2,1:T(8,128)(2,1)S(1)} %slice.283) | copy-start | bytes 4718596
  15.8 7.5 %copy-start.3 = (bf16[512,8,192]{0,2,1:T(8,128)(2,1)}, bf16[512,8,192]{0,2,1:T(8,128)(2,1)S(1)}, u32[]{:S(2)}) copy-start(bf16[512,8,192]{0,2,1:T(8,128)(2,1)S(1)} %pad_maximum_fusion.8) | copy-start | bytes 4718596
  17.0 1.5 %copy-start.17 = (bf16[512,8,128]{2,1,0:T(8,128)(2,1)S(1)}, bf16[512,8,128]{2,1,0:T(8,128)(2,1)}, u32[]{:S(2)}) copy-start(bf16[512,8,128]{2,1,0:T(8,128)(2,1)} %param.29) | copy-start | bytes 3145732
  18.7 13.2 %copy-start.10 = (bf16[512,8,128]{2,0,1:T(8,128)(2,1)}, bf16[512,8,128]{2,0,1:T(8,128)(2,1)S(1)}, u32[]{:S(2)}) copy-start(bf16[512,8,128]{2,0,1:T(8,128)(2,1)S(1)} %copy_select_fusion) | copy-start | bytes 3145732
  23.3 1.3 copy-start.7
  23.9 2.7 %copy-start.6 = (f32[512,8,192]{0,2,1:T(8,128)}, f32[512,8,192]{0,2,1:T(8,128)S(1)}, u32[]{:S(2)}) copy-start(f32[512,8,192]{0,2,1:T(8,128)S(1)} %convolution_bitcast_fusion.1) | copy-start | bytes 9437188
  30.2 1.7 %copy-start.4 = (bf16[8,256,768]{2,1,0:T(8,128)(2,1)}, bf16[8,256,768]{2,1,0:T(8,128)(2,1)S(1)}, u32[]{:S(2)}) copy-start(bf16[8,256,768]{2,1,0:T(8,128)(2,1)S(1)} %fusion.10) | copy-start | bytes 9437188
  34.5 3.2 %slice-start = ((f32[512,8,192]{0,2,1:T(8,128)}), f32[512,8,128]{0,2,1:T(8,128)S(1)}, s32[]{:S(2)}) async-start(f32[512,8,192]{0,2,1:T(8,128)} %copy-done.6), calls=%async_computation.4 | async-start | bytes 4194304 | tf_op jit(solution)/shard_map/slice | solution.py:59
  37.7 2.5 %copy-start.5 = (bf16[8,256,768]{2,1,0:T(8,128)(2,1)S(1)}, bf16[8,256,768]{2,1,0:T(8,128)(2,1)}, u32[]{:S(2)}) copy-start(bf16[8,256,768]{2,1,0:T(8,128)(2,1)} %copy-done.4) | copy-start | bytes 9437188
  37.7 3.1 %copy-start.9 = (f32[512,8,128]{0,2,1:T(8,128)S(1)}, f32[512,8,128]{0,2,1:T(8,128)}, u32[]{:S(2)}) copy-start(f32[512,8,128]{0,2,1:T(8,128)} %convolution_bitcast_fusion.2) | copy-start | bytes 6291460
  37.7 3.3 %copy-start.11 = (bf16[512,8,128]{2,0,1:T(8,128)(2,1)S(1)}, bf16[512,8,128]{2,0,1:T(8,128)(2,1)}, u32[]{:S(2)}) copy-start(bf16[512,8,128]{2,0,1:T(8,128)(2,1)} %copy-done.10) | copy-start | bytes 3145732
  43.0 2.2 %copy-start.16 = (f32[256,64]{1,0:T(8,128)}, f32[256,64]{1,0:T(8,128)S(1)}, u32[]{:S(2)}) copy-start(f32[256,64]{1,0:T(8,128)S(1)} %copy.129) | copy-start | bytes 196612
  43.1 5.5 %copy-start.14 = (bf16[768,8,128]{0,2,1:T(8,128)(2,1)S(1)}, bf16[768,8,128]{0,2,1:T(8,128)(2,1)}, u32[]{:S(2)}) copy-start(bf16[768,8,128]{0,2,1:T(8,128)(2,1)} %fusion.6) | copy-start | bytes 4718596
  43.1 5.5 %copy-start.15 = (bf16[768,8,128]{0,2,1:T(8,128)(2,1)S(1)}, bf16[768,8,128]{0,2,1:T(8,128)(2,1)}, u32[]{:S(2)}) copy-start(bf16[768,8,128]{0,2,1:T(8,128)(2,1)} %fusion.5) | copy-start | bytes 4718596
  45.3 0.8 copy-start.13
  46.8 7.4 %collective-permute-start.1 = (f32[128,576]{1,0:T(8,128)}, f32[128,576]{1,0:T(8,128)}, u32[]{:S(2)}, u32[]{:S(2)}) collective-permute-start(f32[128,576]{1,0:T(8,128)} %fusion.70), channel_id=1, source_target_pairs={{0,1},{1,0},{2,3},{3,2},{4,5},{5,4},{6,7},{7,6},{8,9},{9,8},{10,11... | collective-permute-start | bytes 884744 | tf_op jit(solution)/shard_map/ppermute | solution.py:66
  54.3 7.3 %collective-permute-start = (bf16[8,32,576]{2,1,0:T(8,128)(2,1)}, bf16[8,32,576]{2,1,0:T(8,128)(2,1)}, u32[]{:S(2)}, u32[]{:S(2)}) collective-permute-start(bf16[8,32,576]{2,1,0:T(8,128)(2,1)} %fusion.69), channel_id=1, source_target_pairs={{0,1},{1,0},{2,3},{3,2},{4,5},{5,4},{6,7},{7,6},{8,9},{9,8},{10,11... | collective-permute-start | bytes 884744 | tf_op jit(solution)/shard_map/ppermute | solution.py:66
  56.1 13.7 %all-to-all-start.2 = ((f32[8,16,576]{2,1,0:T(8,128)}), f32[8,16,576]{2,1,0:T(8,128)}, u32[]{:S(2)}, u32[]{:S(2)}) async-start(f32[8,16,576]{2,1,0:T(8,128)} %bitcast.81), calls=%async_computation.2 | async-start | bytes 655360 | tf_op jit(solution)/shard_map/all_to_all | solution.py:182
  69.8 16.7 %all-to-all-start = ((bf16[8,32,576]{2,1,0:T(8,128)(2,1)}), bf16[8,32,576]{2,1,0:T(8,128)(2,1)S(1)}, u32[]{:S(2)}, u32[]{:S(2)}) async-start(bf16[8,32,576]{2,1,0:T(8,128)(2,1)} %fusion.62), calls=%async_computation | async-start | bytes 655360 | tf_op jit(solution)/shard_map/all_to_all | solution.py:171
  74.3 3.2 %collective-permute-start.2 = (f32[16,576]{1,0:T(8,128)S(1)}, f32[16,576]{1,0:T(8,128)S(1)}, u32[]{:S(2)}, u32[]{:S(2)}) collective-permute-start(f32[16,576]{1,0:T(8,128)S(1)} %reduce_sum.89), channel_id=1, source_target_pairs={{0,16},{16,0},{32,48},{48,32},{64,80},{80,64},{96,112},{112,96},{1... | collective-permute-start | bytes 110600 | tf_op jit(solution)/shard_map/ppermute | solution.py:191
  77.5 4.4 %collective-permute-start.3 = (f32[16,576]{1,0:T(8,128)S(1)}, f32[16,576]{1,0:T(8,128)S(1)}, u32[]{:S(2)}, u32[]{:S(2)}) collective-permute-start(f32[16,576]{1,0:T(8,128)S(1)} %add.133), channel_id=1, source_target_pairs={{0,32},{16,48},{32,0},{48,16},{64,96},{80,112},{96,64},{112,80},{1... | collective-permute-start | bytes 110600 | tf_op jit(solution)/shard_map/ppermute | solution.py:191
  81.9 4.7 %collective-permute-start.4 = (f32[16,576]{1,0:T(8,128)S(1)}, f32[16,576]{1,0:T(8,128)S(1)}, u32[]{:S(2)}, u32[]{:S(2)}) collective-permute-start(f32[16,576]{1,0:T(8,128)S(1)} %add.134), channel_id=1, source_target_pairs={{0,64},{16,80},{32,96},{48,112},{64,0},{80,16},{96,32},{112,48},{1... | collective-permute-start | bytes 110600 | tf_op jit(solution)/shard_map/ppermute | solution.py:191
  87.3 11.2 %all-to-all-start.3 = ((f32[8,16,576]{2,1,0:T(8,128)}), f32[8,16,576]{2,1,0:T(8,128)S(1)}, u32[]{:S(2)}, u32[]{:S(2)}) async-start(f32[8,16,576]{2,1,0:T(8,128)} %broadcast_in_dim.41), calls=%async_computation.3 | async-start | bytes 655360 | tf_op jit(solution)/shard_map/all_to_all | solution.py:194
  98.5 35.9 %all-to-all-start.1 = ((bf16[8,64,8,256]{3,1,2,0:T(8,128)(2,1)}), bf16[8,64,8,256]{3,1,2,0:T(8,128)(2,1)}, u32[]{:S(2)}, u32[]{:S(2)}) async-start(bf16[8,64,8,256]{3,1,2,0:T(8,128)(2,1)} %copy.125), calls=%async_computation.1 | async-start | bytes 4194304 | tf_op jit(solution)/shard_map/all_to_all | solution.py:148
  105.8 3.8 %copy-start.2 = (bf16[768,8,128]{0,2,1:T(8,128)(2,1)S(1)}, bf16[768,8,128]{0,2,1:T(8,128)(2,1)}, u32[]{:S(2)}) copy-start(bf16[768,8,128]{0,2,1:T(8,128)(2,1)} %copy-done.1) | copy-start | bytes 4718596
  105.8 3.8 %copy-start.8 = (bf16[8,256,512]{2,1,0:T(8,128)(2,1)S(1)}, bf16[8,256,512]{2,1,0:T(8,128)(2,1)}, u32[]{:S(2)}) copy-start(bf16[8,256,512]{2,1,0:T(8,128)(2,1)} %copy-done.7) | copy-start | bytes 6291460
  109.5 0.9 copy-start.19
  109.5 0.9 copy-start.21
  110.7 8.0 %collective-permute-start.5 = (f32[128,576]{1,0:T(8,128)S(1)}, f32[128,576]{1,0:T(8,128)S(1)}, u32[]{:S(2)}, u32[]{:S(2)}) collective-permute-start(f32[128,576]{1,0:T(8,128)S(1)} %bitcast.79), channel_id=1, source_target_pairs={{0,1},{1,0},{2,3},{3,2},{4,5},{5,4},{6,7},{7,6},{8,9},{9,8},{10,11... | collective-permute-start | bytes 884744 | tf_op jit(solution)/shard_map/ppermute | solution.py:66

commit v10 on v8

--- a/solution.py
+++ b/solution.py
@@ -90,7 +90,7 @@
     key_total = source.shape[0]
     live_rows = jnp.arange(seq_len) < length
     cotangent = jnp.where(live_rows[:, None, None], out_grad, jnp.zeros_like(out_grad))
-    block_rows = min(seq_len, 256)
+    block_rows = seq_len
     head_part = kv_up.shape[1]
     projected = jnp.einsum(
         "kl,lhd->khd", source_latent, kv_up, preferred_element_type=jnp.float32

time: 138 us -> 157 us (1.14)
  other arithmetic: 26.3 us -> 39.7 us
  local copies, waits for them, and re-layouts: 15.9 us -> 20.2 us
  matrix products: 30.9 us -> 33 us
    sub x2 -> x1, other arithmetic: 4.93 us -> 16.6 us  [block_gradients(): exponent = jnp.exp(scores - highest)]
    convert_element_type x2 -> x1, other arithmetic: 0.84 us -> 6.28 us  [block_gradients(): weights = probability.astype(jnp.bfloat16)]
    unnamed x48 -> x44, local copies, waits for them, and re-layouts: 8.17 us -> 12 us
    dot_general x2 -> x1, matrix products: 1.86 us -> 5.54 us  [block_gradients(): jnp.einsum('qhd,khd->hqk', query_used, key_used, preferred_element_type=j...]
    dot_general x2 -> x1, matrix products: 3.64 us -> 1.4 us  [block_gradients(): jnp.einsum('hqk,qhd->khd', score_grad, query_used, preferred_element_type...]
    concatenate x1, other arithmetic: 2.06 us -> 0.14 us  [on_device(): jnp.concatenate([prefix, jnp.concatenate([latent[:, :latent_dim], token_r...]
    dot_general x2 -> x1, matrix products: 3.79 us -> 2.25 us  [block_gradients(): jnp.einsum('hqk,qhv->khv', weights, cotangent, preferred_element_type=jnp...]
    dot_general x2 -> x1, matrix products: 4.51 us -> 5.47 us  [block_gradients(): jnp.einsum('hqk,khd->qhd', score_grad, key_used, preferred_element_type=j...]
  transfers between devices with their start and end apart: 10 -> 10, of which waited for: 6 -> 6; matrix products, arithmetic and copies ran while one was open for 17% -> 16% of each run, Pallas kernels for 0% -> 0%
where the time goes in v10:
time: 157 us; the launch traced here: 156 us
  other arithmetic  39.7 us (25%)
  starting transfers between devices  35.9 us (23%)
  matrix products  33 us (21%)
  waiting for transfers between devices  25.7 us (16%)
  local copies, waits for them, and re-layouts  20.2 us (13%)
  between operations  1.73 us (1%)
    sub x1, other arithmetic, block_gradients(): exponent = jnp.exp(scores - highest)  16.6 us
    all_to_all x1, waiting for transfers between devices, on_device(): lax.all_to_all(up_part.astype(jnp.bfloat16).reshape((dp_size, -1) + up_pa...  13.8 us
    unnamed x44, local copies, waits for them, and re-layouts  12 us
    ppermute x3, starting transfers between devices, on_device(): prefix_own = prefix_own + lax.ppermute(prefix_own, 'dp', partners)  7.6 us
    ppermute x3, starting transfers between devices, swap_pair(): return lax.ppermute(values, 'core', [(0, 1), (1, 0)])  7.4 us
    all_to_all x1, starting transfers between devices, on_device(): lax.all_to_all(up_part.astype(jnp.bfloat16).reshape((dp_size, -1) + up_pa...  7.21 us
    all_to_all x1, waiting for transfers between devices, on_device(): lax.all_to_all(prefix_half.reshape((row_size, -1) + prefix_half.shape[1:]...  6.31 us
    convert_element_type x1, other arithmetic, block_gradients(): weights = probability.astype(jnp.bfloat16)  6.28 us
  transfers between devices with their start and end apart: 10, of which 6 were waited for; matrix products, arithmetic and copies ran while one was open for 16% of the time, Pallas kernels for 0%

profile of v10, /device:TPU:1, one launch (start us, length us, event | category | flops | bytes accessed | tf_op | source)
XLA Modules:
  0.0 156.1 jit_solution(18017133611357922955)
XLA Ops:
  0.7 1.0 slice_convert_fusion.3
  1.7 1.1 slice.134
  2.7 0.7 convert_element_type.56
  3.4 0.3 multiply_cosine_fusion
  3.9 0.1 copy.81
  4.0 0.2 copy.115
  4.3 1.2 copy.82
  5.4 0.1 maximum_maximum_fusion
  5.6 0.8 pad_maximum_fusion.14
  6.4 0.9 copy-done.6
  7.3 1.1 slice_convert_fusion.2
  8.5 1.9 %convolution_convert_fusion = bf16[768,8,256]{0,2,1:T(8,128)(2,1)S(1)} fusion(bf16[512,8,256]{2,1,0:T(8,128)(2,1)S(1)} %copy-done, bf16[768,576]{1,0:T(8,128)(2,1)S(1)} %maximum_maximum_fusion), kind=kOutput, calls=%fused_computation.20 | convolution fusion | flops 1612185600 | bytes 6029312 | tf_op jit(solution)/shard_map/kl,lhd->khd/dot_general | solution.py:95
  10.4 1.7 %copy-done.9 = bf16[768,8,256]{0,2,1:T(8,128)(2,1)} copy-done((bf16[768,8,256]{0,2,1:T(8,128)(2,1)}, bf16[768,8,256]{0,2,1:T(8,128)(2,1)S(1)}, u32[]{:S(2)}) %copy-start.9) | copy-done | bytes 3145752
  12.1 1.2 slice.161
  13.4 0.8 copy.84
  14.9 2.6 %copy.85 = bf16[512,8,128]{0,2,1:T(8,128)(2,1)} copy(bf16[512,8,128]{2,1,0:T(8,128)(2,1)} %param.23) | data formatting | bytes 2097152 | tf_op args[4]
  17.5 1.5 subtract_convert_fusion.1
  19.0 0.3 fusion.20
  19.4 0.9 copy-done.4
  20.3 5.5 %fusion.12 = f32[8,512,768]{2,1,0:T(8,128)} fusion(bf16[768,8,64]{0,2,1:T(8,128)(2,1)S(1)} %broadcast_in_dim.22, bf16[768,8,128]{0,2,1:T(8,128)(2,1)S(1)} %copy-done.2, bf16[512,8,32]{0,2,1:T(8,128)(2,1)S(1)} %get-tuple-element.79, bf16[512,8,32]{0,2,1:T(8,128)(2,1)S(1)} %get-tuple-element.78, bf16[512,8,128]{0,2,1:T(8,128)(2,1)S(1)} %slice.141), kind=kOutput, calls=%fused_computation.27 | convolution fusion | flops 1217396736 | bytes 16515072 | tf_op jit(solution)/shard_map/qhd,khd->hqk/dot_general | solution.py:36
  25.8 16.6 %fusion.75 = (f32[8,512]{1,0:T(8,128)S(1)}, f32[8,512,768]{2,1,0:T(8,128)}) fusion(f32[8,512,768]{2,1,0:T(8,128)} %fusion.12, pred[512,768]{1,0:T(8,128)(4,1)S(1)} %fusion.20), kind=kOutput, calls=%fused_computation.109 | output fusion | flops 18875136 | bytes 25575424 | tf_op jit(solution)/shard_map/sub | solution.py:46
  42.4 6.3 %fusion.5 = bf16[8,512,768]{2,1,0:T(8,128)(2,1)S(1)} fusion(f32[8,512,768]{2,1,0:T(8,128)} %get-tuple-element.89, f32[8,512]{1,0:T(8,128)S(1)} %get-tuple-element.88), kind=kLoop, calls=%fused_computation.9 | loop fusion | flops 6291456 | bytes 18890752 | tf_op jit(solution)/shard_map/convert_element_type | solution.py:48
  48.7 2.2 %fusion.10 = f32[512,8]{0,1:T(8,128)S(1)} fusion(bf16[8,512,768]{2,1,0:T(8,128)(2,1)S(1)} %fusion.5, bf16[768,8,256]{0,2,1:T(8,128)(2,1)S(1)} %copy-done.10, bf16[512,8,128]{0,2,1:T(8,128)(2,1)S(1)} %copy-done.3, pred[512]{0:T(512)(128)(4,1)S(1)} %iota_compare_fusion.1), kind=kOutput, calls=%fused_computation.25 | convolution fusion | flops 807399424 | bytes 8929792 | tf_op jit(solution)/shard_map/hqk,khv->qhv/dot_general | solution.py:49
  50.9 2.3 %fusion.21 = bf16[768,8,128]{0,2,1:T(8,128)(2,1)} fusion(bf16[8,512,768]{2,1,0:T(8,128)(2,1)S(1)} %fusion.5, bf16[512,8,128]{0,2,1:T(8,128)(2,1)S(1)} %copy-done.3, pred[512]{0:T(512)(128)(4,1)S(1)} %iota_compare_fusion.1), kind=kOutput, calls=%fused_computation.41 | convolution fusion | flops 806617088 | bytes 8913408 | tf_op jit(solution)/shard_map/hqk,qhv->khv/dot_general | solution.py:61
  53.2 1.0 slice-done.2
  54.2 4.5 %multiply_convert_fusion = bf16[8,512,768]{2,1,0:T(8,128)(2,1)S(1)} fusion(f32[8,512]{1,0:T(8,128)S(1)} %bitcast.68, f32[8,512,768]{2,1,0:T(8,128)S(1)} %bitcast.58, f32[8,512]{1,0:T(8,128)S(1)} %get-tuple-element.88, bf16[768,8,256]{0,2,1:T(8,128)(2,1)} %copy-done.9, bf16[512,8,128]{0,2,1:T(8,128)(2,1)S(1)} %copy-done.3, ...), kind=kOutput, calls=%fused_computation.1 | convolution fusion | flops 821559296 | bytes 21529088 | tf_op jit(solution)/shard_map/qhv,khv->hqk/dot_general | solution.py:51
  58.7 1.4 convolution_bitcast_fusion
  60.1 1.2 copy-done.1
  61.4 1.3 slice.235
  62.9 2.1 %fusion.34 = f32[256,512]{1,0:T(8,128)S(1)} fusion(bf16[512,8,256]{2,1,0:T(8,128)(2,1)S(1)} %copy-done, bf16[768,8,128]{0,2,1:T(8,128)(2,1)} %slice.235, bf16[768,8,128]{0,2,1:T(8,128)(2,1)} %fusion.21), kind=kOutput, calls=%fused_computation.46 | convolution fusion | flops 538968064 | bytes 5767168 | tf_op jit(solution)/shard_map/khd,lhd->kl/dot_general | solution.py:169
  64.9 0.8 fusion.43
  65.7 1.4 collective-permute-start.1
  67.1 3.7 %fusion.29 = bf16[512,512]{1,0:T(8,128)(2,1)} fusion(bf16[512,8,256]{2,1,0:T(8,128)(2,1)S(1)} %copy-done, bf16[768,8,128]{0,2,1:T(8,128)(2,1)} %slice.235, bf16[768,8,128]{0,2,1:T(8,128)(2,1)} %fusion.21), kind=kOutput, calls=%fused_computation.45 | convolution fusion | flops 1078198272 | bytes 5767168 | tf_op jit(solution)/shard_map/khd,lhd->kl/dot_general | solution.py:154
  70.7 0.3 fusion.60
  71.2 0.8 copy.112
  72.0 1.2 pad_maximum_fusion.11
  73.2 0.8 fusion.42
  74.0 1.7 %fusion.45 = f32[128,576]{1,0:T(8,128)} fusion(f32[128,576]{1,0:T(8,128)} %collective-permute-done.1, s32[]{:T(128)S(6)} %select_n.45, f32[256,512]{1,0:T(8,128)S(1)} %fusion.34, f32[256,64]{1,0:T(8,128)S(1)} %copy.117), kind=kLoop, calls=%fused_computation.71 | loop fusion | flops 147456 | bytes 1179652 | tf_op jit(solution)/shard_map/add | solution.py:176
  75.7 5.5 %all-to-all-start.2 = ((f32[8,16,576]{2,1,0:T(8,128)}), f32[8,16,576]{2,1,0:T(8,128)S(1)}, u32[]{:S(2)}, u32[]{:S(2)}) async-start(f32[8,16,576]{2,1,0:T(8,128)} %bitcast.62), calls=%async_computation.2 | async-start | bytes 655360 | tf_op jit(solution)/shard_map/all_to_all | solution.py:178
  81.2 1.8 %fusion.39 = bf16[8,32,576]{2,1,0:T(8,128)(2,1)} fusion(bf16[8,32,576]{2,1,0:T(8,128)(2,1)} %collective-permute-done, pred[]{:T(512)S(6)} %eq.2, bf16[8,2,32,576]{3,2,1,0:T(8,128)(2,1)S(1)} %pad_maximum_fusion.11), kind=kLoop, calls=%fused_computation.58 | loop fusion | flops 737280 | bytes 1179649 | tf_op jit(solution)/shard_map/convert_element_type | solution.py:166
  83.0 6.3 %all-to-all-done.2 = f32[8,16,576]{2,1,0:T(8,128)S(1)} async-done(((f32[8,16,576]{2,1,0:T(8,128)}), f32[8,16,576]{2,1,0:T(8,128)S(1)}, u32[]{:S(2)}, u32[]{:S(2)}) %all-to-all-start.2) | async-done | bytes 294944 | tf_op jit(solution)/shard_map/all_to_all | solution.py:178
  89.3 3.4 %all-to-all-start = ((bf16[8,32,576]{2,1,0:T(8,128)(2,1)}), bf16[8,32,576]{2,1,0:T(8,128)(2,1)S(1)}, u32[]{:S(2)}, u32[]{:S(2)}) async-start(bf16[8,32,576]{2,1,0:T(8,128)(2,1)} %fusion.39), calls=%async_computation | async-start | bytes 655360 | tf_op jit(solution)/shard_map/all_to_all | solution.py:167
  92.8 1.4 collective-permute-start.2
  94.2 1.6 collective-permute-done.2
  95.7 2.9 %collective-permute-start.3 = (f32[16,576]{1,0:T(8,128)S(1)}, f32[16,576]{1,0:T(8,128)S(1)}, u32[]{:S(2)}, u32[]{:S(2)}) collective-permute-start(f32[16,576]{1,0:T(8,128)S(1)} %add.73), channel_id=1, source_target_pairs={{0,32},{16,48},{32,0},{48,16},{64,96},{80,112},{96,64},{112,80},{1... | collective-permute-start | bytes 110600 | tf_op jit(solution)/shard_map/ppermute | solution.py:187
  98.7 1.7 %collective-permute-done.3 = f32[16,576]{1,0:T(8,128)S(1)} collective-permute-done((f32[16,576]{1,0:T(8,128)S(1)}, f32[16,576]{1,0:T(8,128)S(1)}, u32[]{:S(2)}, u32[]{:S(2)}) %collective-permute-start.3) | collective-permute-done | bytes 36896 | tf_op jit(solution)/shard_map/ppermute | solution.py:187
  100.4 3.3 %collective-permute-start.4 = (f32[16,576]{1,0:T(8,128)S(1)}, f32[16,576]{1,0:T(8,128)S(1)}, u32[]{:S(2)}, u32[]{:S(2)}) collective-permute-start(f32[16,576]{1,0:T(8,128)S(1)} %add.74), channel_id=1, source_target_pairs={{0,64},{16,80},{32,96},{48,112},{64,0},{80,16},{96,32},{112,48},{1... | collective-permute-start | bytes 110600 | tf_op jit(solution)/shard_map/ppermute | solution.py:187
  103.7 1.4 collective-permute-done.4
  105.1 0.7 broadcast_in_dim.31
  105.8 4.7 %all-to-all-start.3 = ((f32[8,16,576]{2,1,0:T(8,128)}), f32[8,16,576]{2,1,0:T(8,128)S(1)}, u32[]{:S(2)}, u32[]{:S(2)}) async-start(f32[8,16,576]{2,1,0:T(8,128)} %broadcast_in_dim.31), calls=%async_computation.3 | async-start | bytes 655360 | tf_op jit(solution)/shard_map/all_to_all | solution.py:190
  110.6 4.0 %fusion.14 = bf16[512,8,256]{2,0,1:T(8,128)(2,1)S(1)} fusion(bf16[768,8,128]{0,2,1:T(8,128)(2,1)} %fusion.21, bf16[768,8,128]{0,2,1:T(8,128)(2,1)} %slice.235, bf16[768,576]{1,0:T(8,128)(2,1)} %copy-done.7), kind=kOutput, calls=%fused_computation.29 | convolution fusion | flops 1617952768 | bytes 6029312 | tf_op jit(solution)/shard_map/kl,khd->lhd/dot_general | solution.py:138
  114.6 1.6 %copy.98 = bf16[8,64,8,256]{3,1,2,0:T(8,128)(2,1)} copy(bf16[8,64,8,256]{3,1,0,2:T(8,128)(2,1)S(1)} %bitcast.59) | data formatting | bytes 4194304 | tf_op jit(solution)/shard_map/reshape | solution.py:149
  116.2 0.9 all-to-all-done.3
  117.1 7.2 %all-to-all-start.1 = ((bf16[8,64,8,256]{3,1,2,0:T(8,128)(2,1)}), bf16[8,64,8,256]{3,1,2,0:T(8,128)(2,1)}, u32[]{:S(2)}, u32[]{:S(2)}) async-start(bf16[8,64,8,256]{3,1,2,0:T(8,128)(2,1)} %copy.98), calls=%async_computation.1 | async-start | bytes 4194304 | tf_op jit(solution)/shard_map/all_to_all | solution.py:148
  124.3 5.5 %fusion.13 = f32[512,8,192]{0,2,1:T(8,128)S(1)} fusion(bf16[8,512,768]{2,1,0:T(8,128)(2,1)} %copy-done.1, bf16[768,8,64]{0,2,1:T(8,128)(2,1)S(1)} %copy-done.5, bf16[768,8,128]{0,2,1:T(8,128)(2,1)} %slice.161), kind=kOutput, calls=%fused_computation.28 | convolution fusion | flops 1212678144 | bytes 11796480 | tf_op jit(solution)/shard_map/hqk,khd->qhd/dot_general | solution.py:55
  129.8 6.0 %collective-permute-start.5 = (f32[128,576]{1,0:T(8,128)S(1)}, f32[128,576]{1,0:T(8,128)S(1)}, u32[]{:S(2)}, u32[]{:S(2)}) collective-permute-start(f32[128,576]{1,0:T(8,128)S(1)} %bitcast.60), channel_id=1, source_target_pairs={{0,1},{1,0},{2,3},{3,2},{4,5},{5,4},{6,7},{7,6},{8,9},{9,8},{10,11... | collective-permute-start | bytes 884744 | tf_op jit(solution)/shard_map/ppermute | solution.py:66
  135.8 0.2 add_convert_fusion
  136.0 0.1 slice.236
  136.1 1.2 pad_maximum_fusion.10
  137.4 0.7 convert_reduce_fusion.1
  138.1 1.0 copy.104
  139.2 13.8 %all-to-all-done.1 = bf16[8,64,8,256]{3,1,2,0:T(8,128)(2,1)} async-done(((bf16[8,64,8,256]{3,1,2,0:T(8,128)(2,1)}), bf16[8,64,8,256]{3,1,2,0:T(8,128)(2,1)}, u32[]{:S(2)}, u32[]{:S(2)}) %all-to-all-start.1) | async-done | bytes 2097184 | tf_op jit(solution)/shard_map/all_to_all | solution.py:148
  152.9 2.0 %convert_reduce_fusion = f32[64,8,256]{2,0,1:T(8,128)S(1)} fusion(bf16[8,64,8,256]{3,1,2,0:T(8,128)(2,1)} %all-to-all-done.1), kind=kLoop, calls=%fused_computation.10 | loop fusion | flops 1966080 | bytes 2621440 | tf_op jit(solution)/shard_map/reduce_sum | solution.py:151
  155.0 1.1 copy.103
  (55 shorter events, 0.8 us)
Async XLA Ops:
  0.6 7.8 %copy-start = (bf16[512,8,256]{2,1,0:T(8,128)(2,1)S(1)}, bf16[512,8,256]{2,1,0:T(8,128)(2,1)}, u32[]{:S(2)}) copy-start(bf16[512,8,256]{2,1,0:T(8,128)(2,1)} %param.22) | copy-start | bytes 6291460
  3.8 13.7 %copy-start.11 = (f32[512,32]{0,1:T(8,128)}, f32[512,32]{0,1:T(8,128)S(1)}, u32[]{:S(2)}) copy-start(f32[512,32]{0,1:T(8,128)S(1)} %get-tuple-element.84) | copy-start | bytes 196612
  3.8 13.7 %copy-start.13 = (f32[512,32]{0,1:T(8,128)}, f32[512,32]{0,1:T(8,128)S(1)}, u32[]{:S(2)}) copy-start(f32[512,32]{0,1:T(8,128)S(1)} %get-tuple-element.85) | copy-start | bytes 196612
  5.4 1.8 %copy-start.6 = (bf16[512,8,192]{0,2,1:T(8,128)(2,1)S(1)}, bf16[512,8,192]{0,2,1:T(8,128)(2,1)}, u32[]{:S(2)}) copy-start(bf16[512,8,192]{0,2,1:T(8,128)(2,1)} %param.19) | copy-start | bytes 4718596
  5.6 4.8 %copy-start.7 = (bf16[768,576]{1,0:T(8,128)(2,1)}, bf16[768,576]{1,0:T(8,128)(2,1)S(1)}, u32[]{:S(2)}) copy-start(bf16[768,576]{1,0:T(8,128)(2,1)S(1)} %maximum_maximum_fusion) | copy-start | bytes 2654212
  10.4 1.7 %copy-start.9 = (bf16[768,8,256]{0,2,1:T(8,128)(2,1)}, bf16[768,8,256]{0,2,1:T(8,128)(2,1)S(1)}, u32[]{:S(2)}) copy-start(bf16[768,8,256]{0,2,1:T(8,128)(2,1)S(1)} %convolution_convert_fusion) | copy-start | bytes 9437188
  12.1 1.2 copy-start.8
  14.1 5.2 %copy-start.15 = (bf16[768,64]{0,1:T(8,128)(2,1)S(1)}, bf16[768,64]{0,1:T(8,128)(2,1)}, u32[]{:S(2)}) copy-start(bf16[768,64]{0,1:T(8,128)(2,1)} %copy.84) | copy-start | bytes 294916
  17.5 2.8 %copy-start.2 = (bf16[768,8,128]{0,2,1:T(8,128)(2,1)S(1)}, bf16[768,8,128]{0,2,1:T(8,128)(2,1)}, u32[]{:S(2)}) copy-start(bf16[768,8,128]{0,2,1:T(8,128)(2,1)} %slice.161) | copy-start | bytes 4718596
  19.4 0.9 copy-start.4
  42.4 6.3 %copy-start.3 = (bf16[512,8,128]{0,2,1:T(8,128)(2,1)S(1)}, bf16[512,8,128]{0,2,1:T(8,128)(2,1)}, u32[]{:S(2)}) copy-start(bf16[512,8,128]{0,2,1:T(8,128)(2,1)} %copy.85) | copy-start | bytes 3145732
  42.4 6.3 %copy-start.10 = (bf16[768,8,256]{0,2,1:T(8,128)(2,1)S(1)}, bf16[768,8,256]{0,2,1:T(8,128)(2,1)}, u32[]{:S(2)}) copy-start(bf16[768,8,256]{0,2,1:T(8,128)(2,1)} %copy-done.9) | copy-start | bytes 9437188
  48.7 4.5 %slice-start = ((s8[12582912]{0:T(1024)(128)(4,1)}), s8[4194304]{0:T(1024)(128)(4,1)S(1)}, s32[]{:S(2)}) async-start(s8[12582912]{0:T(1024)(128)(4,1)} %bitcast.57), calls=%async_computation.4 | async-start | bytes 8388608
  48.7 4.5 %slice-start.1 = ((s8[12582912]{0:T(1024)(128)(4,1)}), s8[4194304]{0:T(1024)(128)(4,1)S(1)}, s32[]{:S(2)}) async-start(s8[12582912]{0:T(1024)(128)(4,1)} %bitcast.57), calls=%async_computation.5 | async-start | bytes 8388608
  50.9 3.2 %slice-start.2 = ((s8[12582912]{0:T(1024)(128)(4,1)}), s8[4194304]{0:T(1024)(128)(4,1)S(1)}, s32[]{:S(2)}) async-start(s8[12582912]{0:T(1024)(128)(4,1)} %bitcast.57), calls=%async_computation.6 | async-start | bytes 8388608
  58.7 2.7 %copy-start.1 = (bf16[8,512,768]{2,1,0:T(8,128)(2,1)}, bf16[8,512,768]{2,1,0:T(8,128)(2,1)S(1)}, u32[]{:S(2)}) copy-start(bf16[8,512,768]{2,1,0:T(8,128)(2,1)S(1)} %multiply_convert_fusion) | copy-start | bytes 18874372
  65.7 8.3 %collective-permute-start.1 = (f32[128,576]{1,0:T(8,128)}, f32[128,576]{1,0:T(8,128)}, u32[]{:S(2)}, u32[]{:S(2)}) collective-permute-start(f32[128,576]{1,0:T(8,128)} %fusion.43), channel_id=1, source_target_pairs={{0,1},{1,0},{2,3},{3,2},{4,5},{5,4},{6,7},{7,6},{8,9},{9,8},{10,11... | collective-permute-start | bytes 884744 | tf_op jit(solution)/shard_map/ppermute | solution.py:66
  74.0 7.2 %collective-permute-start = (bf16[8,32,576]{2,1,0:T(8,128)(2,1)}, bf16[8,32,576]{2,1,0:T(8,128)(2,1)}, u32[]{:S(2)}, u32[]{:S(2)}) collective-permute-start(bf16[8,32,576]{2,1,0:T(8,128)(2,1)} %fusion.42), channel_id=1, source_target_pairs={{0,1},{1,0},{2,3},{3,2},{4,5},{5,4},{6,7},{7,6},{8,9},{9,8},{10,11... | collective-permute-start | bytes 884744 | tf_op jit(solution)/shard_map/ppermute | solution.py:66
  75.7 13.6 %all-to-all-start.2 = ((f32[8,16,576]{2,1,0:T(8,128)}), f32[8,16,576]{2,1,0:T(8,128)S(1)}, u32[]{:S(2)}, u32[]{:S(2)}) async-start(f32[8,16,576]{2,1,0:T(8,128)} %bitcast.62), calls=%async_computation.2 | async-start | bytes 655360 | tf_op jit(solution)/shard_map/all_to_all | solution.py:178
  89.3 15.8 %all-to-all-start = ((bf16[8,32,576]{2,1,0:T(8,128)(2,1)}), bf16[8,32,576]{2,1,0:T(8,128)(2,1)S(1)}, u32[]{:S(2)}, u32[]{:S(2)}) async-start(bf16[8,32,576]{2,1,0:T(8,128)(2,1)} %fusion.39), calls=%async_computation | async-start | bytes 655360 | tf_op jit(solution)/shard_map/all_to_all | solution.py:167
  92.8 2.9 %collective-permute-start.2 = (f32[16,576]{1,0:T(8,128)S(1)}, f32[16,576]{1,0:T(8,128)S(1)}, u32[]{:S(2)}, u32[]{:S(2)}) collective-permute-start(f32[16,576]{1,0:T(8,128)S(1)} %reduce_sum.59), channel_id=1, source_target_pairs={{0,16},{16,0},{32,48},{48,32},{64,80},{80,64},{96,112},{112,96},{1... | collective-permute-start | bytes 110600 | tf_op jit(solution)/shard_map/ppermute | solution.py:187
  95.7 4.7 %collective-permute-start.3 = (f32[16,576]{1,0:T(8,128)S(1)}, f32[16,576]{1,0:T(8,128)S(1)}, u32[]{:S(2)}, u32[]{:S(2)}) collective-permute-start(f32[16,576]{1,0:T(8,128)S(1)} %add.73), channel_id=1, source_target_pairs={{0,32},{16,48},{32,0},{48,16},{64,96},{80,112},{96,64},{112,80},{1... | collective-permute-start | bytes 110600 | tf_op jit(solution)/shard_map/ppermute | solution.py:187
  100.4 4.7 %collective-permute-start.4 = (f32[16,576]{1,0:T(8,128)S(1)}, f32[16,576]{1,0:T(8,128)S(1)}, u32[]{:S(2)}, u32[]{:S(2)}) collective-permute-start(f32[16,576]{1,0:T(8,128)S(1)} %add.74), channel_id=1, source_target_pairs={{0,64},{16,80},{32,96},{48,112},{64,0},{80,16},{96,32},{112,48},{1... | collective-permute-start | bytes 110600 | tf_op jit(solution)/shard_map/ppermute | solution.py:187
  105.8 11.2 %all-to-all-start.3 = ((f32[8,16,576]{2,1,0:T(8,128)}), f32[8,16,576]{2,1,0:T(8,128)S(1)}, u32[]{:S(2)}, u32[]{:S(2)}) async-start(f32[8,16,576]{2,1,0:T(8,128)} %broadcast_in_dim.31), calls=%async_computation.3 | async-start | bytes 655360 | tf_op jit(solution)/shard_map/all_to_all | solution.py:190
  116.2 8.1 %copy-start.5 = (bf16[768,8,64]{0,2,1:T(8,128)(2,1)S(1)}, bf16[768,8,64]{0,2,1:T(8,128)(2,1)}, u32[]{:S(2)}) copy-start(bf16[768,8,64]{0,2,1:T(8,128)(2,1)} %copy-done.4) | copy-start | bytes 2359300
  117.1 35.9 %all-to-all-start.1 = ((bf16[8,64,8,256]{3,1,2,0:T(8,128)(2,1)}), bf16[8,64,8,256]{3,1,2,0:T(8,128)(2,1)}, u32[]{:S(2)}, u32[]{:S(2)}) async-start(bf16[8,64,8,256]{3,1,2,0:T(8,128)(2,1)} %copy.98), calls=%async_computation.1 | async-start | bytes 4194304 | tf_op jit(solution)/shard_map/all_to_all | solution.py:148
  124.3 11.5 %copy-start.12 = (f32[512,32]{0,1:T(8,128)S(1)}, f32[512,32]{0,1:T(8,128)}, u32[]{:S(2)}) copy-start(f32[512,32]{0,1:T(8,128)} %copy-done.11) | copy-start | bytes 196612
  124.3 11.5 %copy-start.14 = (f32[512,32]{0,1:T(8,128)S(1)}, f32[512,32]{0,1:T(8,128)}, u32[]{:S(2)}) copy-start(f32[512,32]{0,1:T(8,128)} %copy-done.13) | copy-start | bytes 196612
  129.8 8.3 %collective-permute-start.5 = (f32[128,576]{1,0:T(8,128)S(1)}, f32[128,576]{1,0:T(8,128)S(1)}, u32[]{:S(2)}, u32[]{:S(2)}) collective-permute-start(f32[128,576]{1,0:T(8,128)S(1)} %bitcast.60), channel_id=1, source_target_pairs={{0,1},{1,0},{2,3},{3,2},{4,5},{5,4},{6,7},{7,6},{8,9},{9,8},{10,11... | collective-permute-start | bytes 884744 | tf_op jit(solution)/shard_map/ppermute | solution.py:66

commit v11 on v10

--- a/solution.py
+++ b/solution.py
@@ -90,7 +90,7 @@
     key_total = source.shape[0]
     live_rows = jnp.arange(seq_len) < length
     cotangent = jnp.where(live_rows[:, None, None], out_grad, jnp.zeros_like(out_grad))
-    block_rows = seq_len
+    block_rows = min(seq_len, 128)
     head_part = kv_up.shape[1]
     projected = jnp.einsum(
         "kl,lhd->khd", source_latent, kv_up, preferred_element_type=jnp.float32

time: 157 us -> 225 us (1.43)
  matrix products: 33 us -> 69.6 us
  local copies, waits for them, and re-layouts: 20.2 us -> 42.8 us
  other arithmetic: 39.7 us -> 56.1 us
  starting transfers between devices: 35.9 us -> 30.3 us
  waiting for transfers between devices: 25.7 us -> 22.2 us
    slice x0 -> x10, local copies, waits for them, and re-layouts: none -> 8.82 us  [the longest x5 5.29 us: on_device(): cosine[first_row:last_row, None]]
    dot_general x1 -> x4, matrix products: 2.25 us -> 10.9 us  [block_gradients(): jnp.einsum('hqk,qhv->khv', weights, cotangent, preferred_element_type=jnp...]
    scatter-add x0 -> x4, other arithmetic: none -> 8.26 us  [the longest x2 7.16 us: on_device(): nope_total = nope_total.at[:seen].add(nope_key)]
    sub x1 -> x2, other arithmetic: 16.6 us -> 8.53 us  [block_gradients(): exponent = jnp.exp(scores - highest)]
    dot_general x1 -> x4, matrix products: 2.17 us -> 10.1 us  [block_gradients(): jnp.einsum('hqk,khv->qhv', weights, values, preferred_element_type=jnp.fl...]
    sub x0 -> x2, matrix products: none -> 6.9 us  [block_gradients(): exponent = jnp.exp(scores - highest)]
    dot_general x1 -> x4, matrix products: 5.47 us -> 11.9 us  [block_gradients(): jnp.einsum('hqk,khd->qhd', score_grad, key_used, preferred_element_type=j...]
    convert_element_type x1 -> x0, other arithmetic: 6.28 us -> none  [block_gradients(): weights = probability.astype(jnp.bfloat16)]
  transfers between devices with their start and end apart: 10 -> 10, of which waited for: 6 -> 3; matrix products, arithmetic and copies ran while one was open for 16% -> 22% of each run, Pallas kernels for 0% -> 0%
where the time goes in v11:
time: 225 us; the launch traced here: 223 us
  matrix products  69.6 us (31%)
  other arithmetic  56.1 us (25%)
  local copies, waits for them, and re-layouts  42.8 us (19%)
  starting transfers between devices  30.3 us (13%)
  waiting for transfers between devices  22.2 us (10%)
    all_to_all x1, waiting for transfers between devices, on_device(): lax.all_to_all(up_part.astype(jnp.bfloat16).reshape((dp_size, -1) + up_pa...  15.9 us
    dot_general x4, matrix products, block_gradients(): jnp.einsum('hqk,khd->qhd', score_grad, key_used, preferred_element_type=j...  11.9 us
    dot_general x4, matrix products, block_gradients(): jnp.einsum('hqk,qhv->khv', weights, cotangent, preferred_element_type=jnp...  10.9 us
    unnamed x109, local copies, waits for them, and re-layouts  10.5 us
    dot_general x4, matrix products, block_gradients(): jnp.einsum('hqk,khv->qhv', weights, values, preferred_element_type=jnp.fl...  10.1 us
    sub x2, other arithmetic, block_gradients(): exponent = jnp.exp(scores - highest)  8.53 us
    another operation x7, other arithmetic  7.82 us
    ppermute x3, starting transfers between devices, on_device(): prefix_own = prefix_own + lax.ppermute(prefix_own, 'dp', partners)  7.32 us
  transfers between devices with their start and end apart: 10, of which 3 were waited for; matrix products, arithmetic and copies ran while one was open for 22% of the time, Pallas kernels for 0%

profile of v11, /device:TPU:1, one launch (start us, length us, event | category | flops | bytes accessed | tf_op | source)
XLA Modules:
  0.0 222.9 jit_solution(13534962652546092977)
XLA Ops:
  5.3 1.2 copy.90
  6.7 2.9 %multiply_cosine_fusion = (f32[512,32]{1,0:T(8,128)S(1)}, f32[512,32]{1,0:T(8,128)}, bf16[512,32]{1,0:T(8,128)(2,1)S(1)}, bf16[512,32]{1,0:T(8,128)(2,1)S(1)}) fusion(f32[32]{0:T(128)S(1)} %negate_power_fusion, f32[512]{0:T(512)S(1)} %bitcast.115, f32[512,64]{1,0:T(8,128)} %convert_element_type.85), kind=kLoop, calls=%fused_computation.140 | loop fusion | flops 147456 | bytes 329856 | tf_op jit(solution)/shard_map/cos | solution.py:11
  14.1 1.7 copy.92
  15.8 3.1 %convolution_convert_fusion = bf16[768,8,256]{0,2,1:T(8,128)(2,1)S(1)} fusion(bf16[512,8,256]{2,1,0:T(8,128)(2,1)S(1)} %copy-done, bf16[768,576]{1,0:T(8,128)(2,1)} %maximum_maximum_fusion.1), kind=kOutput, calls=%fused_computation.34 | convolution fusion | flops 1612185600 | bytes 6029312 | tf_op jit(solution)/shard_map/kl,lhd->khd/dot_general | solution.py:95
  18.9 1.2 slice.521
  20.9 1.2 copy_select_fusion
  22.9 1.2 pad_maximum_fusion.7
  24.2 3.3 %fusion.200 = (f32[8,128]{1,0:T(8,128)S(1)}, f32[8,128,384]{2,1,0:T(8,128)}) fusion(pred[128,384]{1,0:T(8,128)(4,1)S(1)} %copy-done.41, bf16[512,8,192]{0,2,1:T(8,128)(2,1)} %pad_maximum_fusion.7, bf16[768,8,128]{0,2,1:T(8,128)(2,1)} %slice.521, bf16[768,8,64]{0,2,1:T(8,128)(2,1)S(1)} %broadcast_in_dim.54), kind=kOutput, calls=%fused_computation.240 | convolution fusion | flops 154927488 | bytes 4378624 | tf_op jit(solution)/shard_map/sub | solution.py:46
  27.5 2.4 %fusion.64 = f32[128,8]{0,1:T(8,128)S(1)} fusion(bf16[768,8,256]{0,2,1:T(8,128)(2,1)} %copy-done.30, bf16[512,8,128]{2,0,1:T(8,128)(2,1)} %copy_select_fusion, f32[8,128,384]{2,1,0:T(8,128)} %get-tuple-element.213, f32[8,128]{1,0:T(8,128)S(1)} %get-tuple-element.212), kind=kOutput, calls=%fused_computation.97 | convolution fusion | flops 101841920 | bytes 2629632 | tf_op jit(solution)/shard_map/hqk,khv->qhv/dot_general | solution.py:49
  30.0 1.7 convolution_bitcast_fusion.4
  31.7 1.7 multiply_convert_fusion.3
  34.3 1.2 slice.562
  35.6 2.1 fusion.80
  37.7 2.3 %fusion.17 = f32[8,128,768]{2,1,0:T(8,128)} fusion(bf16[768,8,64]{0,2,1:T(8,128)(2,1)S(1)} %broadcast_in_dim.54, bf16[768,8,128]{0,2,1:T(8,128)(2,1)S(1)} %copy-done.2, bf16[512,8,192]{0,2,1:T(8,128)(2,1)S(1)} %copy-done.1), kind=kOutput, calls=%fused_computation.47 | convolution fusion | flops 306708480 | bytes 5898240 | tf_op jit(solution)/shard_map/qhd,khd->hqk/dot_general | solution.py:36
  41.3 3.5 %scatter-add.30 = f32[768,8,128]{0,2,1:T(8,128)} pad(f32[384,8,128]{0,2,1:T(8,128)} %slice.562, f32[]{:T(128)} %constant.342.clone.1), padding=0_384x0_0x0_0 | pad | bytes 4718596 | tf_op jit(solution)/shard_map/scatter-add | solution.py:123
  44.8 1.9 scatter-add.35
  46.9 3.6 %fusion.195 = (f32[8,128]{1,0:T(8,128)S(1)}, f32[8,128,512]{2,1,0:T(8,128)}) fusion(pred[128,512]{1,0:T(8,128)(4,1)S(1)} %and_or_fusion.2, bf16[768,8,128]{0,2,1:T(8,128)(2,1)} %slice.521, bf16[768,8,64]{0,2,1:T(8,128)(2,1)S(1)} %broadcast_in_dim.54, bf16[512,8,192]{0,2,1:T(8,128)(2,1)} %pad_maximum_fusion.7), kind=kOutput, calls=%fused_computation.239 | convolution fusion | flops 206569984 | bytes 4919296 | tf_op jit(solution)/shard_map/sub | solution.py:46
  50.6 2.6 %fusion.62 = f32[128,8]{0,1:T(8,128)S(1)} fusion(bf16[768,8,256]{0,2,1:T(8,128)(2,1)} %copy-done.30, bf16[512,8,128]{2,0,1:T(8,128)(2,1)} %copy_select_fusion, f32[8,128,512]{2,1,0:T(8,128)} %get-tuple-element.211, f32[8,128]{1,0:T(8,128)S(1)} %get-tuple-element.210), kind=kOutput, calls=%fused_computation.95 | convolution fusion | flops 135658496 | bytes 3416064 | tf_op jit(solution)/shard_map/hqk,khv->qhv/dot_general | solution.py:49
  55.4 1.7 copy-done.5
  57.0 1.7 multiply_convert_fusion.2
  58.8 1.9 convolution_bitcast_fusion.2
  61.4 3.5 %fusion.13 = f32[768,8,128]{0,2,1:T(8,128)} fusion(f32[768,8,128]{0,2,1:T(8,128)} %scatter-add.30, f32[512,8,192]{0,2,1:T(8,128)S(1)} %convolution_bitcast_fusion.2), kind=kLoop, calls=%fused_computation.38 | loop fusion | flops 524288 | bytes 6291456 | tf_op jit(solution)/shard_map/scatter-add | solution.py:123
  66.7 4.1 %fusion.194 = (f32[8,128]{1,0:T(8,128)S(1)}, f32[8,128,640]{2,1,0:T(8,128)}) fusion(f32[8,128,640]{2,1,0:T(8,128)} %fusion.80, pred[128,640]{1,0:T(8,128)(4,1)S(1)} %and_or_fusion.1), kind=kOutput, calls=%fused_computation.238 | output fusion | flops 2622079 | bytes 5328896 | tf_op jit(solution)/shard_map/sub | solution.py:46
  70.9 4.2 %fusion.63 = f32[128,8]{0,1:T(8,128)S(1)} fusion(bf16[768,8,256]{0,2,1:T(8,128)(2,1)} %copy-done.30, bf16[512,8,128]{2,0,1:T(8,128)(2,1)} %copy_select_fusion, f32[8,128]{1,0:T(8,128)S(1)} %get-tuple-element.208, f32[8,128,640]{2,1,0:T(8,128)} %fusion.80, pred[128,640]{1,0:T(8,128)(4,1)} %copy-done.33), kind=kOutput, calls=%fused_computation.96 | convolution fusion | flops 171442816 | bytes 4284416 | tf_op jit(solution)/shard_map/hqk,khv->qhv/dot_general | solution.py:49
  75.2 6.3 %fusion.7 = f32[768,8,128]{0,2,1:T(8,128)} fusion(f32[768,8,128]{0,2,1:T(8,128)} %copy-done.5, bf16[512,8,128]{2,0,1:T(8,128)(2,1)} %copy_select_fusion, f32[8,128]{1,0:T(8,128)S(1)} %get-tuple-element.208, f32[8,128,640]{2,1,0:T(8,128)} %fusion.80, pred[128,640]{1,0:T(8,128)(4,1)} %copy-done.33), kind=kOutput, calls=%fused_computation.26 | convolution fusion | flops 171705984 | bytes 8212480 | tf_op jit(solution)/shard_map/hqk,qhv->khv/dot_general | solution.py:61
  81.5 2.8 %multiply_convert_fusion.1 = bf16[8,128,640]{2,1,0:T(8,128)(2,1)S(1)} fusion(f32[8,128]{1,0:T(8,128)S(1)} %bitcast.117, bf16[768,8,256]{0,2,1:T(8,128)(2,1)} %copy-done.30, f32[8,128,640]{2,1,0:T(8,128)} %get-tuple-element.209, f32[8,128]{1,0:T(8,128)S(1)} %get-tuple-element.208, bf16[512,8,128]{2,0,1:T(8,128)(2,1)} %copy_select_fusion), kind=kOutput, calls=%fused_computation.29 | convolution fusion | flops 171048960 | bytes 5513216 | tf_op jit(solution)/shard_map/qhv,khv->hqk/dot_general | solution.py:51
  84.3 2.0 convolution_bitcast_fusion.1
  87.0 3.7 %fusion.8 = f32[768,8,128]{0,2,1:T(8,128)} fusion(f32[768,8,128]{0,2,1:T(8,128)} %fusion.13, f32[640,8,192]{0,2,1:T(8,128)S(1)} %convolution_bitcast_fusion.1), kind=kLoop, calls=%fused_computation.28 | loop fusion | flops 655360 | bytes 7864320 | tf_op jit(solution)/shard_map/scatter-add | solution.py:123
  90.7 1.8 copy.120
  93.3 4.4 %fusion.193 = (f32[8,128]{1,0:T(8,128)S(1)}, f32[8,128,768]{2,1,0:T(8,128)S(1)}) fusion(f32[8,128,768]{2,1,0:T(8,128)} %fusion.17, pred[128,768]{1,0:T(8,128)(4,1)S(1)} %and_or_fusion), kind=kOutput, calls=%fused_computation.237 | output fusion | flops 4719359 | bytes 6393856 | tf_op jit(solution)/shard_map/sub | solution.py:46
  99.6 1.9 fusion.6
  102.3 2.1 convolution_bitcast_fusion
  105.1 3.3 %fusion.5 = bf16[768,8,128]{0,2,1:T(8,128)(2,1)} fusion(f32[768,8,128]{0,2,1:T(8,128)} %fusion.8, f32[768,8,192]{0,2,1:T(8,128)S(1)} %convolution_bitcast_fusion), kind=kLoop, calls=%fused_computation.16 | loop fusion | flops 1572864 | bytes 7864320 | tf_op jit(solution)/shard_map/convert.7
  108.5 1.8 copy.121
  113.3 2.1 fusion.50
  116.9 1.4 collective-permute-start.1
  118.3 1.2 fusion.116
  119.5 2.9 %fusion.42 = bf16[512,512]{1,0:T(8,128)(2,1)S(1)} fusion(bf16[512,8,256]{2,1,0:T(8,128)(2,1)S(1)} %copy-done, bf16[768,8,128]{0,2,1:T(8,128)(2,1)} %fusion.5, bf16[768,8,128]{0,2,1:T(8,128)(2,1)} %fusion.6), kind=kOutput, calls=%fused_computation.79 | convolution fusion | flops 1078198272 | bytes 5767168 | tf_op jit(solution)/shard_map/khd,lhd->kl/dot_general | solution.py:154
  123.5 3.4 %convolution_bitcast_fusion.5 = f32[128,8,192]{0,2,1:T(8,128)} fusion(bf16[8,128,640]{2,1,0:T(8,128)(2,1)} %copy-done.18, bf16[768,8,128]{0,2,1:T(8,128)(2,1)} %slice.521, bf16[768,8,64]{0,2,1:T(8,128)(2,1)S(1)} %broadcast_in_dim.54), kind=kOutput, calls=%fused_computation.80 | convolution fusion | flops 255590400 | bytes 4456448 | tf_op jit(solution)/shard_map/hqk,khd->qhd/dot_general | solution.py:55
  126.9 1.8 fusion.108
  128.7 5.5 %all-to-all-start.2 = ((f32[8,16,576]{2,1,0:T(8,128)}), f32[8,16,576]{2,1,0:T(8,128)}, u32[]{:S(2)}, u32[]{:S(2)}) async-start(f32[8,16,576]{2,1,0:T(8,128)} %bitcast.111), calls=%async_computation.2 | async-start | bytes 655360 | tf_op jit(solution)/shard_map/all_to_all | solution.py:178
  134.2 3.0 %convolution_bitcast_fusion.6 = f32[128,8,192]{0,2,1:T(8,128)} fusion(bf16[8,128,512]{2,1,0:T(8,128)(2,1)} %copy-done.28, bf16[768,8,128]{0,2,1:T(8,128)(2,1)} %slice.521, bf16[768,8,64]{0,2,1:T(8,128)(2,1)S(1)} %broadcast_in_dim.54), kind=kOutput, calls=%fused_computation.82 | convolution fusion | flops 204472320 | bytes 4194304 | tf_op jit(solution)/shard_map/hqk,khd->qhd/dot_general | solution.py:55
  137.2 5.2 %all-to-all-done.2 = f32[8,16,576]{2,1,0:T(8,128)} async-done(((f32[8,16,576]{2,1,0:T(8,128)}), f32[8,16,576]{2,1,0:T(8,128)}, u32[]{:S(2)}, u32[]{:S(2)}) %all-to-all-start.2) | async-done | bytes 294944 | tf_op jit(solution)/shard_map/all_to_all | solution.py:178
  142.4 1.6 reduce_sum.149
  144.0 1.3 collective-permute-start.2
  145.3 1.8 fusion.84
  147.2 3.4 %all-to-all-start = ((bf16[8,32,576]{2,1,0:T(8,128)(2,1)}), bf16[8,32,576]{2,1,0:T(8,128)(2,1)S(1)}, u32[]{:S(2)}, u32[]{:S(2)}) async-start(bf16[8,32,576]{2,1,0:T(8,128)(2,1)} %fusion.84), calls=%async_computation | async-start | bytes 655360 | tf_op jit(solution)/shard_map/all_to_all | solution.py:167
  151.4 2.7 %collective-permute-start.3 = (f32[16,576]{1,0:T(8,128)S(1)}, f32[16,576]{1,0:T(8,128)S(1)}, u32[]{:S(2)}, u32[]{:S(2)}) collective-permute-start(f32[16,576]{1,0:T(8,128)S(1)} %add.235), channel_id=1, source_target_pairs={{0,32},{16,48},{32,0},{48,16},{64,96},{80,112},{96,64},{112,80},{1... | collective-permute-start | bytes 110600 | tf_op jit(solution)/shard_map/ppermute | solution.py:187
  154.1 2.8 %convolution_bitcast_fusion.7 = f32[128,8,192]{0,2,1:T(8,128)} fusion(bf16[8,128,384]{2,1,0:T(8,128)(2,1)} %copy-done.29, bf16[768,8,128]{0,2,1:T(8,128)(2,1)} %slice.521, bf16[768,8,64]{0,2,1:T(8,128)(2,1)S(1)} %broadcast_in_dim.54), kind=kOutput, calls=%fused_computation.83 | convolution fusion | flops 153354240 | bytes 3932160 | tf_op jit(solution)/shard_map/hqk,khd->qhd/dot_general | solution.py:55
  157.5 3.3 %collective-permute-start.4 = (f32[16,576]{1,0:T(8,128)}, f32[16,576]{1,0:T(8,128)}, u32[]{:S(2)}, u32[]{:S(2)}) collective-permute-start(f32[16,576]{1,0:T(8,128)} %add.236), channel_id=1, source_target_pairs={{0,64},{16,80},{32,96},{48,112},{64,0},{80,16},{96,32},{112,48},{1... | collective-permute-start | bytes 110600 | tf_op jit(solution)/shard_map/ppermute | solution.py:187
  161.5 1.5 copy.98
  163.0 1.5 copy.102
  168.8 1.8 slice.790
  170.6 1.8 slice.789
  172.4 1.8 slice.788
  175.8 4.5 %all-to-all-start.3 = ((f32[8,16,576]{2,1,0:T(8,128)}), f32[8,16,576]{2,1,0:T(8,128)S(1)}, u32[]{:S(2)}, u32[]{:S(2)}) async-start(f32[8,16,576]{2,1,0:T(8,128)} %broadcast_in_dim.69), calls=%async_computation.3 | async-start | bytes 655360 | tf_op jit(solution)/shard_map/all_to_all | solution.py:190
  180.2 4.0 %fusion.19 = bf16[512,8,256]{2,0,1:T(8,128)(2,1)S(1)} fusion(bf16[768,8,128]{0,2,1:T(8,128)(2,1)} %fusion.6, bf16[768,8,128]{0,2,1:T(8,128)(2,1)} %fusion.5, bf16[768,576]{1,0:T(8,128)(2,1)} %maximum_maximum_fusion.1), kind=kOutput, calls=%fused_computation.49 | convolution fusion | flops 1617952768 | bytes 6029312 | tf_op jit(solution)/shard_map/kl,khd->lhd/dot_general | solution.py:138
  184.2 1.5 copy.128
  186.8 4.3 %all-to-all-start.1 = ((bf16[8,64,8,256]{3,1,2,0:T(8,128)(2,1)}), bf16[8,64,8,256]{3,1,2,0:T(8,128)(2,1)}, u32[]{:S(2)}, u32[]{:S(2)}) async-start(bf16[8,64,8,256]{3,1,2,0:T(8,128)(2,1)} %copy.128), calls=%async_computation.1 | async-start | bytes 4194304 | tf_op jit(solution)/shard_map/all_to_all | solution.py:148
  191.2 2.7 %fusion.47 = f32[128,8,192]{0,2,1:T(8,128)S(1)} fusion(bf16[8,128,768]{2,1,0:T(8,128)(2,1)} %copy-done.15, bf16[768,8,64]{0,2,1:T(8,128)(2,1)S(1)} %broadcast_in_dim.54, bf16[768,8,128]{0,2,1:T(8,128)(2,1)} %slice.521), kind=kOutput, calls=%fused_computation.81 | convolution fusion | flops 306708480 | bytes 4718592 | tf_op jit(solution)/shard_map/hqk,khd->qhd/dot_general | solution.py:55
  197.2 3.6 %collective-permute-start.5 = (f32[128,576]{1,0:T(8,128)S(1)}, f32[128,576]{1,0:T(8,128)S(1)}, u32[]{:S(2)}, u32[]{:S(2)}) collective-permute-start(f32[128,576]{1,0:T(8,128)S(1)} %bitcast.109), channel_id=1, source_target_pairs={{0,1},{1,0},{2,3},{3,2},{4,5},{5,4},{6,7},{7,6},{8,9},{9,8},{10,11... | collective-permute-start | bytes 884744 | tf_op jit(solution)/shard_map/ppermute | solution.py:66
  200.8 1.3 maximum_maximum_fusion
  203.9 15.9 %all-to-all-done.1 = bf16[8,64,8,256]{3,1,2,0:T(8,128)(2,1)} async-done(((bf16[8,64,8,256]{3,1,2,0:T(8,128)(2,1)}), bf16[8,64,8,256]{3,1,2,0:T(8,128)(2,1)}, u32[]{:S(2)}, u32[]{:S(2)}) %all-to-all-start.1) | async-done | bytes 2097184 | tf_op jit(solution)/shard_map/all_to_all | solution.py:148
  219.7 2.0 convert_reduce_fusion
  (183 shorter events, 43.0 us)
Async XLA Ops:
  0.6 15.2 %copy-start = (bf16[512,8,256]{2,1,0:T(8,128)(2,1)S(1)}, bf16[512,8,256]{2,1,0:T(8,128)(2,1)}, u32[]{:S(2)}) copy-start(bf16[512,8,256]{2,1,0:T(8,128)(2,1)} %param.40) | copy-start | bytes 6291460
  0.6 5.8 %slice-start.1 = ((bf16[512,576]{0,1:T(8,128)(2,1)}), bf16[512,512]{0,1:T(8,128)(2,1)S(1)}, s32[]{:S(2)}) async-start(bf16[512,576]{0,1:T(8,128)(2,1)} %param.38), calls=%async_computation.5 | async-start | bytes 1048576 | tf_op jit(solution)/shard_map/slice | solution.py:86
  0.7 9.0 %copy-start.45 = (f32[32]{0:T(128)}, f32[32]{0:T(128)S(1)}, u32[]{:S(2)}) copy-start(f32[32]{0:T(128)S(1)} %negate_power_fusion) | copy-start | bytes 388
  6.7 4.8 %copy-start.3 = (bf16[512,8,192]{0,2,1:T(8,128)(2,1)S(1)}, bf16[512,8,192]{0,2,1:T(8,128)(2,1)}, u32[]{:S(2)}) copy-start(bf16[512,8,192]{0,2,1:T(8,128)(2,1)} %param.37) | copy-start | bytes 4718596
  9.6 3.3 %copy-start.9 = (f32[512,32]{1,0:T(8,128)}, f32[512,32]{1,0:T(8,128)S(1)}, u32[]{:S(2)}) copy-start(f32[512,32]{1,0:T(8,128)S(1)} %get-tuple-element.202) | copy-start | bytes 196612
  18.9 3.2 %copy-start.30 = (bf16[768,8,256]{0,2,1:T(8,128)(2,1)}, bf16[768,8,256]{0,2,1:T(8,128)(2,1)S(1)}, u32[]{:S(2)}) copy-start(bf16[768,8,256]{0,2,1:T(8,128)(2,1)S(1)} %convolution_convert_fusion) | copy-start | bytes 9437188
  18.9 2.0 copy-start.21
  20.1 2.8 %slice-start = ((bf16[512,8,192]{0,2,1:T(8,128)(2,1)}), bf16[512,8,128]{0,2,1:T(8,128)(2,1)S(1)}, s32[]{:S(2)}) async-start(bf16[512,8,192]{0,2,1:T(8,128)(2,1)} %param.37), calls=%async_computation.4 | async-start | bytes 2097152 | tf_op jit(solution)/shard_map/slice | solution.py:78
  22.7 1.4 copy-start.32
  22.9 1.3 copy-start.41
  27.5 2.4 %copy-start.22 = (bf16[512,8,128]{2,0,1:T(8,128)(2,1)S(1)}, bf16[512,8,128]{2,0,1:T(8,128)(2,1)}, u32[]{:S(2)}) copy-start(bf16[512,8,128]{2,0,1:T(8,128)(2,1)} %copy_select_fusion) | copy-start | bytes 3145732
  27.5 2.5 %copy-start.50 = (f32[8,128,384]{2,1,0:T(8,128)S(1)}, f32[8,128,384]{2,1,0:T(8,128)}, u32[]{:S(2)}) copy-start(f32[8,128,384]{2,1,0:T(8,128)} %get-tuple-element.213) | copy-start | bytes 4718596
  31.7 1.7 copy-start.1
  33.4 0.9 copy-start.29
  33.9 1.7 copy-start.2
  41.3 3.5 %copy-start.14 = (f32[384,8,128]{0,2,1:T(8,128)S(1)}, f32[384,8,128]{0,2,1:T(8,128)}, u32[]{:S(2)}) copy-start(f32[384,8,128]{0,2,1:T(8,128)} %convolution_bitcast_fusion.4) | copy-start | bytes 4718596
  44.8 2.0 copy-start.47
  44.8 2.0 copy-start.48
  44.8 2.0 copy-start.49
  50.5 2.9 %copy-start.4 = (f32[768,8,128]{0,2,1:T(8,128)S(1)}, f32[768,8,128]{0,2,1:T(8,128)}, u32[]{:S(2)}) copy-start(f32[768,8,128]{0,2,1:T(8,128)} %scatter-add.35) | copy-start | bytes 9437188
  50.5 3.2 %copy-start.23 = (bf16[512,8,128]{2,0,1:T(8,128)(2,1)S(1)}, bf16[512,8,128]{2,0,1:T(8,128)(2,1)}, u32[]{:S(2)}) copy-start(bf16[512,8,128]{2,0,1:T(8,128)(2,1)} %copy_select_fusion) | copy-start | bytes 3145732
  50.6 3.9 %copy-start.51 = (f32[8,128,512]{2,1,0:T(8,128)S(1)}, f32[8,128,512]{2,1,0:T(8,128)}, u32[]{:S(2)}) copy-start(f32[8,128,512]{2,1,0:T(8,128)} %get-tuple-element.211) | copy-start | bytes 6291460
  55.4 1.7 copy-start.5
  58.8 1.9 copy-start.28
  61.4 4.5 %copy-start.44 = (pred[640]{0:T(1024)(128)(4,1)S(1)}, pred[640]{0:T(1024)(128)(4,1)}, u32[]{:S(2)}) copy-start(pred[640]{0:T(1024)(128)(4,1)} %get-tuple-element.222) | copy-start | bytes 1924
  66.7 4.2 %copy-start.33 = (pred[128,640]{1,0:T(8,128)(4,1)}, pred[128,640]{1,0:T(8,128)(4,1)S(1)}, u32[]{:S(2)}) copy-start(pred[128,640]{1,0:T(8,128)(4,1)S(1)} %and_or_fusion.1) | copy-start | bytes 245764
  84.3 2.0 copy-start.18
  87.0 5.5 %copy-start.42 = (pred[768]{0:T(1024)(128)(4,1)S(1)}, pred[768]{0:T(1024)(128)(4,1)}, u32[]{:S(2)}) copy-start(pred[768]{0:T(1024)(128)(4,1)} %get-tuple-element.220) | copy-start | bytes 2308
  87.0 5.5 %copy-start.43 = (pred[768]{0:T(1024)(128)(4,1)S(1)}, pred[768]{0:T(1024)(128)(4,1)}, u32[]{:S(2)}) copy-start(pred[768]{0:T(1024)(128)(4,1)} %get-tuple-element.221) | copy-start | bytes 2308
  93.3 4.4 %copy-start.24 = (bf16[512,8,128]{2,0,1:T(8,128)(2,1)S(1)}, bf16[512,8,128]{2,0,1:T(8,128)(2,1)}, u32[]{:S(2)}) copy-start(bf16[512,8,128]{2,0,1:T(8,128)(2,1)} %copy_select_fusion) | copy-start | bytes 3145732
  93.3 4.4 %copy-start.31 = (bf16[768,8,256]{0,2,1:T(8,128)(2,1)S(1)}, bf16[768,8,256]{0,2,1:T(8,128)(2,1)}, u32[]{:S(2)}) copy-start(bf16[768,8,256]{0,2,1:T(8,128)(2,1)} %copy-done.30) | copy-start | bytes 9437188
  97.7 1.9 copy-start.6
  102.3 2.1 copy-start.15
  112.5 0.7 copy-start.7
  113.2 2.2 copy-start.19
  113.2 5.1 %copy-start.8 = (f32[768,64]{1,0:T(8,128)S(1)}, f32[768,64]{1,0:T(8,128)}, u32[]{:S(2)}) copy-start(f32[768,64]{1,0:T(8,128)} %copy-done.7) | copy-start | bytes 589828
  113.2 5.1 %copy-start.46 = (f32[32]{0:T(128)S(1)}, f32[32]{0:T(128)}, u32[]{:S(2)}) copy-start(f32[32]{0:T(128)} %copy-done.45) | copy-start | bytes 388
  115.4 0.8 copy-start.12
  116.9 10.0 %collective-permute-start.1 = (f32[128,576]{1,0:T(8,128)}, f32[128,576]{1,0:T(8,128)}, u32[]{:S(2)}, u32[]{:S(2)}) collective-permute-start(f32[128,576]{1,0:T(8,128)} %fusion.106), channel_id=1, source_target_pairs={{0,1},{1,0},{2,3},{3,2},{4,5},{5,4},{6,7},{7,6},{8,9},{9,8},{10,11... | collective-permute-start | bytes 884744 | tf_op jit(solution)/shard_map/ppermute | solution.py:66
  123.3 22.1 %collective-permute-start = (bf16[8,32,576]{2,1,0:T(8,128)(2,1)}, bf16[8,32,576]{2,1,0:T(8,128)(2,1)}, u32[]{:S(2)}, u32[]{:S(2)}) collective-permute-start(bf16[8,32,576]{2,1,0:T(8,128)(2,1)} %fusion.105), channel_id=1, source_target_pairs={{0,1},{1,0},{2,3},{3,2},{4,5},{5,4},{6,7},{7,6},{8,9},{9,8},{10,11... | collective-permute-start | bytes 884744 | tf_op jit(solution)/shard_map/ppermute | solution.py:66
  123.5 3.4 %copy-start.13 = (f32[256,512]{1,0:T(8,128)S(1)}, f32[256,512]{1,0:T(8,128)}, u32[]{:S(2)}) copy-start(f32[256,512]{1,0:T(8,128)} %copy-done.12) | copy-start | bytes 1572868
  123.5 3.4 %copy-start.20 = (f32[256,64]{1,0:T(8,128)S(1)}, f32[256,64]{1,0:T(8,128)}, u32[]{:S(2)}) copy-start(f32[256,64]{1,0:T(8,128)} %copy-done.19) | copy-start | bytes 196612
  128.7 13.7 %all-to-all-start.2 = ((f32[8,16,576]{2,1,0:T(8,128)}), f32[8,16,576]{2,1,0:T(8,128)}, u32[]{:S(2)}, u32[]{:S(2)}) async-start(f32[8,16,576]{2,1,0:T(8,128)} %bitcast.111), calls=%async_computation.2 | async-start | bytes 655360 | tf_op jit(solution)/shard_map/all_to_all | solution.py:178
  144.0 6.6 %collective-permute-start.2 = (f32[16,576]{1,0:T(8,128)}, f32[16,576]{1,0:T(8,128)}, u32[]{:S(2)}, u32[]{:S(2)}) collective-permute-start(f32[16,576]{1,0:T(8,128)} %reduce_sum.149), channel_id=1, source_target_pairs={{0,16},{16,0},{32,48},{48,32},{64,80},{80,64},{96,112},{112,96},{1... | collective-permute-start | bytes 110600 | tf_op jit(solution)/shard_map/ppermute | solution.py:187
  147.2 27.9 %all-to-all-start = ((bf16[8,32,576]{2,1,0:T(8,128)(2,1)}), bf16[8,32,576]{2,1,0:T(8,128)(2,1)S(1)}, u32[]{:S(2)}, u32[]{:S(2)}) async-start(bf16[8,32,576]{2,1,0:T(8,128)(2,1)} %fusion.84), calls=%async_computation | async-start | bytes 655360 | tf_op jit(solution)/shard_map/all_to_all | solution.py:167
  151.4 9.4 %copy-start.10 = (f32[512,32]{1,0:T(8,128)S(1)}, f32[512,32]{1,0:T(8,128)}, u32[]{:S(2)}) copy-start(f32[512,32]{1,0:T(8,128)} %copy-done.9) | copy-start | bytes 196612
  151.4 9.4 %copy-start.11 = (f32[512,32]{1,0:T(8,128)S(1)}, f32[512,32]{1,0:T(8,128)}, u32[]{:S(2)}) copy-start(f32[512,32]{1,0:T(8,128)} %get-tuple-element.203) | copy-start | bytes 196612
  151.4 5.5 %collective-permute-start.3 = (f32[16,576]{1,0:T(8,128)S(1)}, f32[16,576]{1,0:T(8,128)S(1)}, u32[]{:S(2)}, u32[]{:S(2)}) collective-permute-start(f32[16,576]{1,0:T(8,128)S(1)} %add.235), channel_id=1, source_target_pairs={{0,32},{16,48},{32,0},{48,16},{64,96},{80,112},{96,64},{112,80},{1... | collective-permute-start | bytes 110600 | tf_op jit(solution)/shard_map/ppermute | solution.py:187
  157.5 16.7 %collective-permute-start.4 = (f32[16,576]{1,0:T(8,128)}, f32[16,576]{1,0:T(8,128)}, u32[]{:S(2)}, u32[]{:S(2)}) collective-permute-start(f32[16,576]{1,0:T(8,128)} %add.236), channel_id=1, source_target_pairs={{0,64},{16,80},{32,96},{48,112},{64,0},{80,16},{96,32},{112,48},{1... | collective-permute-start | bytes 110600 | tf_op jit(solution)/shard_map/ppermute | solution.py:187
  175.8 11.0 %all-to-all-start.3 = ((f32[8,16,576]{2,1,0:T(8,128)}), f32[8,16,576]{2,1,0:T(8,128)S(1)}, u32[]{:S(2)}, u32[]{:S(2)}) async-start(f32[8,16,576]{2,1,0:T(8,128)} %broadcast_in_dim.69), calls=%async_computation.3 | async-start | bytes 655360 | tf_op jit(solution)/shard_map/all_to_all | solution.py:190
  186.8 10.4 %copy-start.16 = (f32[8,16,576]{2,1,0:T(8,128)}, f32[8,16,576]{2,1,0:T(8,128)S(1)}, u32[]{:S(2)}) copy-start(f32[8,16,576]{2,1,0:T(8,128)S(1)} %all-to-all-done.3) | copy-start | bytes 884740
  186.8 33.0 %all-to-all-start.1 = ((bf16[8,64,8,256]{3,1,2,0:T(8,128)(2,1)}), bf16[8,64,8,256]{3,1,2,0:T(8,128)(2,1)}, u32[]{:S(2)}, u32[]{:S(2)}) async-start(bf16[8,64,8,256]{3,1,2,0:T(8,128)(2,1)} %copy.128), calls=%async_computation.1 | async-start | bytes 4194304 | tf_op jit(solution)/shard_map/all_to_all | solution.py:148
  191.1 2.8 %copy-start.38 = (f32[128,32]{0,1:T(8,128)S(1)}, f32[128,32]{0,1:T(8,128)}, u32[]{:S(2)}) copy-start(f32[128,32]{0,1:T(8,128)} %copy.98) | copy-start | bytes 49156
  191.1 2.8 %copy-start.40 = (f32[128,32]{0,1:T(8,128)S(1)}, f32[128,32]{0,1:T(8,128)}, u32[]{:S(2)}) copy-start(f32[128,32]{0,1:T(8,128)} %copy.99) | copy-start | bytes 49156
  191.1 3.9 %copy-start.37 = (f32[128,32]{0,1:T(8,128)S(1)}, f32[128,32]{0,1:T(8,128)}, u32[]{:S(2)}) copy-start(f32[128,32]{0,1:T(8,128)} %copy.102) | copy-start | bytes 49156
  191.2 3.9 %copy-start.39 = (f32[128,32]{0,1:T(8,128)S(1)}, f32[128,32]{0,1:T(8,128)}, u32[]{:S(2)}) copy-start(f32[128,32]{0,1:T(8,128)} %copy.103) | copy-start | bytes 49156
  191.2 4.9 %copy-start.35 = (f32[128,32]{0,1:T(8,128)S(1)}, f32[128,32]{0,1:T(8,128)}, u32[]{:S(2)}) copy-start(f32[128,32]{0,1:T(8,128)} %copy.106) | copy-start | bytes 49156
  191.2 4.9 %copy-start.36 = (f32[128,32]{0,1:T(8,128)S(1)}, f32[128,32]{0,1:T(8,128)}, u32[]{:S(2)}) copy-start(f32[128,32]{0,1:T(8,128)} %copy.107) | copy-start | bytes 49156
  191.2 6.0 %copy-start.34 = (f32[128,32]{0,1:T(8,128)S(1)}, f32[128,32]{0,1:T(8,128)}, u32[]{:S(2)}) copy-start(f32[128,32]{0,1:T(8,128)} %copy.111) | copy-start | bytes 49156
  193.9 6.9 %copy-start.25 = (bf16[128,8,128]{0,2,1:T(8,128)(2,1)S(1)}, bf16[128,8,128]{0,2,1:T(8,128)(2,1)}, u32[]{:S(2)}) copy-start(bf16[128,8,128]{0,2,1:T(8,128)(2,1)} %slice.790) | copy-start | bytes 786436
  193.9 6.9 %copy-start.26 = (bf16[128,8,128]{0,2,1:T(8,128)(2,1)S(1)}, bf16[128,8,128]{0,2,1:T(8,128)(2,1)}, u32[]{:S(2)}) copy-start(bf16[128,8,128]{0,2,1:T(8,128)(2,1)} %slice.789) | copy-start | bytes 786436
  193.9 6.9 %copy-start.27 = (bf16[128,8,128]{0,2,1:T(8,128)(2,1)S(1)}, bf16[128,8,128]{0,2,1:T(8,128)(2,1)}, u32[]{:S(2)}) copy-start(bf16[128,8,128]{0,2,1:T(8,128)(2,1)} %slice.788) | copy-start | bytes 786436
  197.2 5.6 %collective-permute-start.5 = (f32[128,576]{1,0:T(8,128)S(1)}, f32[128,576]{1,0:T(8,128)S(1)}, u32[]{:S(2)}, u32[]{:S(2)}) collective-permute-start(f32[128,576]{1,0:T(8,128)S(1)} %bitcast.109), channel_id=1, source_target_pairs={{0,1},{1,0},{2,3},{3,2},{4,5},{5,4},{6,7},{7,6},{8,9},{9,8},{10,11... | collective-permute-start | bytes 884744 | tf_op jit(solution)/shard_map/ppermute | solution.py:66
  200.8 2.0 copy-start.17

commit v12 on v8

--- a/solution.py
+++ b/solution.py
@@ -106,9 +106,8 @@
     rope_total = jnp.zeros((key_total, rope_dim), jnp.float32)
     value_total = jnp.zeros((key_total, head_part, value_dim), jnp.float32)
     query_pieces = []
-    for block_number in range(seq_len // block_rows):
-        first_row = block_number * block_rows
-        last_row = first_row + block_rows
+    bounds = (0, seq_len // 2, 3 * seq_len // 4, seq_len)
+    for first_row, last_row in zip(bounds[:-1], bounds[1:]):
         seen = prefix_rows + last_row
         pieces = block_gradients(
             query_used[first_row:last_row],

time: 138 us -> 180 us (1.30)
  local copies, waits for them, and re-layouts: 15.9 us -> 45.2 us
  waiting for transfers between devices: 26.7 us -> 10.4 us
  matrix products: 30.9 us -> 45.8 us
  blocking collectives: 0 us -> 13.2 us
  other arithmetic: 26.3 us -> 37.4 us
  starting transfers between devices: 35.8 us -> 24.9 us
    all_to_all x0 -> x1, blocking collectives: none -> 13.2 us  [on_device(): lax.all_to_all(prefix_half.reshape((row_size, -1) + prefix_half.shape[1:]...]
    unnamed x48 -> x87, local copies, waits for them, and re-layouts: 8.17 us -> 20.7 us
    all_to_all x1 -> x0, waiting for transfers between devices: 6.42 us -> none  [on_device(): lax.all_to_all(prefix_half.reshape((row_size, -1) + prefix_half.shape[1:]...]
    all_to_all x1 -> x0, starting transfers between devices: 5.49 us -> none  [on_device(): lax.all_to_all(prefix_half.reshape((row_size, -1) + prefix_half.shape[1:]...]
    all_to_all x1, waiting for transfers between devices: 14.7 us -> 9.4 us  [on_device(): lax.all_to_all(up_part.astype(jnp.bfloat16).reshape((dp_size, -1) + up_pa...]
    ppermute x3, waiting for transfers between devices: 4.7 us -> 0.01 us  [on_device(): prefix_own = prefix_own + lax.ppermute(prefix_own, 'dp', partners)]
    dot_general x2 -> x3, matrix products: 4.51 us -> 8.78 us  [block_gradients(): jnp.einsum('hqk,khd->qhd', score_grad, key_used, preferred_element_type=j...]
    sub x0 -> x1, matrix products: none -> 4.15 us  [block_gradients(): exponent = jnp.exp(scores - highest)]
  transfers between devices with their start and end apart: 10 -> 9, of which waited for: 6 -> 2; matrix products, arithmetic and copies ran while one was open for 17% -> 21% of each run, Pallas kernels for 0% -> 0%
where the time goes in v12:
time: 180 us; the launch traced here: 179 us
  matrix products  45.8 us (25%)
  local copies, waits for them, and re-layouts  45.2 us (25%)
  other arithmetic  37.4 us (21%)
  starting transfers between devices  24.9 us (14%)
  blocking collectives  13.2 us (7%)
  waiting for transfers between devices  10.4 us (6%)
  between operations  2.02 us (1%)
    unnamed x87, local copies, waits for them, and re-layouts  20.7 us
    all_to_all x1, blocking collectives, on_device(): lax.all_to_all(prefix_half.reshape((row_size, -1) + prefix_half.shape[1:]...  13.2 us
    all_to_all x1, waiting for transfers between devices, on_device(): lax.all_to_all(up_part.astype(jnp.bfloat16).reshape((dp_size, -1) + up_pa...  9.4 us
    dot_general x3, matrix products, block_gradients(): jnp.einsum('hqk,khd->qhd', score_grad, key_used, preferred_element_type=j...  8.78 us
    ppermute x3, starting transfers between devices, on_device(): prefix_own = prefix_own + lax.ppermute(prefix_own, 'dp', partners)  7.38 us
    dot_general x3, matrix products, block_gradients(): jnp.einsum('qhv,khv->hqk', cotangent, values, preferred_element_type=jnp....  6.29 us
    another operation x6, other arithmetic  6.21 us
    ppermute x3, starting transfers between devices, swap_pair(): return lax.ppermute(values, 'core', [(0, 1), (1, 0)])  5.23 us
  transfers between devices with their start and end apart: 9, of which 2 were waited for; matrix products, arithmetic and copies ran while one was open for 21% of the time, Pallas kernels for 0%

profile of v12, /device:TPU:1, one launch (start us, length us, event | category | flops | bytes accessed | tf_op | source)
XLA Modules:
  0.0 178.9 jit_solution(17620701230263781347)
XLA Ops:
  0.7 2.0 %slice.346 = bf16[512,512]{0,1:T(8,128)(2,1)} slice(bf16[512,576]{0,1:T(8,128)(2,1)} %param.32), slice={[0:512], [0:512]} | slice | bytes 1048576 | tf_op jit(solution)/shard_map/slice | solution.py:86
  2.7 2.1 %slice_convert_fusion.3 = f32[512,8,64]{0,2,1:T(8,128)} fusion(bf16[512,8,192]{0,2,1:T(8,128)(2,1)} %param.31), kind=kLoop, calls=%fused_computation.116 | loop fusion | flops 262144 | bytes 1572864 | tf_op jit(solution)/shard_map/convert_element_type | solution.py:80
  5.8 2.0 %copy.133 = bf16[512,512]{1,0:T(8,128)(2,1)} copy(bf16[512,512]{0,1:T(8,128)(2,1)} %slice.346) | data formatting | bytes 1048576
  7.9 1.2 copy.80
  9.0 2.9 %multiply_cosine_fusion = (f32[512,32]{1,0:T(8,128)}, f32[512,32]{1,0:T(8,128)}, bf16[512,32]{1,0:T(8,128)(2,1)S(1)}, bf16[512,32]{1,0:T(8,128)(2,1)S(1)}) fusion(f32[32]{0:T(128)S(1)} %negate_power_fusion, f32[512]{0:T(512)S(1)} %bitcast.107, f32[512,64]{1,0:T(8,128)} %convert_element_type.75), kind=kLoop, calls=%fused_computation.126 | loop fusion | flops 147456 | bytes 329856 | tf_op jit(solution)/shard_map/cos | solution.py:11
  12.0 2.2 %maximum_maximum_fusion.1 = bf16[768,576]{1,0:T(8,128)(2,1)} fusion(bf16[512,32]{1,0:T(8,128)(2,1)S(1)} %get-tuple-element.164, bf16[512,32]{1,0:T(8,128)(2,1)S(1)} %get-tuple-element.165, bf16[512,512]{1,0:T(8,128)(2,1)} %copy.133, bf16[256,576]{1,0:T(8,128)(2,1)S(1)} %copy.80), kind=kLoop, calls=%fused_computation.94 | loop fusion | flops 3538944 | bytes 1769472 | tf_op jit(solution)/shard_map/concatenate | solution.py:85
  16.0 1.0 copy.84
  17.1 1.1 copy.83
  18.1 1.4 subtract_convert_fusion
  20.4 1.3 pad_maximum_fusion.7
  22.4 1.0 copy.82
  23.5 3.1 %convolution_convert_fusion = bf16[768,8,256]{0,2,1:T(8,128)(2,1)S(1)} fusion(bf16[512,8,256]{2,1,0:T(8,128)(2,1)S(1)} %copy-done, bf16[768,576]{1,0:T(8,128)(2,1)} %maximum_maximum_fusion.1), kind=kOutput, calls=%fused_computation.35 | convolution fusion | flops 1612185600 | bytes 6029312 | tf_op jit(solution)/shard_map/kl,lhd->khd/dot_general | solution.py:95
  26.7 1.9 %copy-done.19 = bf16[512,8,128]{2,1,0:T(8,128)(2,1)S(1)} copy-done((bf16[512,8,128]{2,1,0:T(8,128)(2,1)S(1)}, bf16[512,8,128]{2,1,0:T(8,128)(2,1)}, u32[]{:S(2)}) %copy-start.19) | copy-done | bytes 1048600
  28.8 1.4 copy-done.6
  31.2 2.1 %fusion.148 = (f32[8,256]{1,0:T(8,128)S(1)}, f32[8,256,512]{2,1,0:T(8,128)S(1)}) fusion(f32[8,256,512]{2,1,0:T(8,128)S(1)} %fusion.75, pred[256,512]{1,0:T(8,128)(4,1)S(1)} %fusion.79), kind=kOutput, calls=%fused_computation.195 | output fusion | flops 6291967 | bytes 8527872 | tf_op jit(solution)/shard_map/sub | solution.py:46
  34.5 1.2 multiply_convert_fusion
  37.1 1.6 slice.431
  38.7 1.8 %convolution_bitcast_fusion.3 = f32[512,8,128]{0,2,1:T(8,128)} fusion(bf16[8,256,512]{2,1,0:T(8,128)(2,1)S(1)} %fusion.21, bf16[512,8,128]{2,0,1:T(8,128)(2,1)S(1)} %copy_select_fusion), kind=kOutput, calls=%fused_computation.50 | convolution fusion | flops 268435456 | bytes 4718592 | tf_op jit(solution)/shard_map/hqk,qhv->khv/dot_general | solution.py:61
  41.3 1.5 fusion.144
  44.4 1.9 %multiply_convert_fusion.1 = bf16[8,128,768]{2,1,0:T(8,128)(2,1)} fusion(f32[8,128]{1,0:T(8,128)S(1)} %bitcast.111, bf16[768,8,256]{0,2,1:T(8,128)(2,1)S(1)} %convolution_convert_fusion, f32[8,128,768]{2,1,0:T(8,128)S(1)} %get-tuple-element.167, f32[8,128]{1,0:T(8,128)S(1)} %get-tuple-element.166, bf16[512,8,128]{2,0,1:T(8,128)(2,1)S(1)} %copy_select_fusion), kind=kOutput, calls=%fused_computation.21 | convolution fusion | flops 205258752 | bytes 6561792 | tf_op jit(solution)/shard_map/qhv,khv->hqk/dot_general | solution.py:51
  46.4 4.2 %fusion.145 = (f32[8,128]{1,0:T(8,128)S(1)}, f32[8,128,640]{2,1,0:T(8,128)}) fusion(pred[128,640]{1,0:T(8,128)(4,1)S(1)} %and_or_fusion.1, bf16[128,8,192]{0,2,1:T(8,128)(2,1)} %get-tuple-element.146, bf16[768,8,128]{0,2,1:T(8,128)(2,1)} %copy-done.4, bf16[768,8,64]{0,2,1:T(8,128)(2,1)S(1)} %broadcast_in_dim.42), kind=kOutput, calls=%fused_computation.194 | convolution fusion | flops 258212480 | bytes 5459968 | tf_op jit(solution)/shard_map/sub | solution.py:46
  50.6 3.0 %fusion.60 = f32[128,8]{0,1:T(8,128)S(1)} fusion(bf16[768,8,256]{0,2,1:T(8,128)(2,1)} %copy-done.22, bf16[512,8,128]{2,0,1:T(8,128)(2,1)} %copy-done.10, f32[8,128,640]{2,1,0:T(8,128)} %get-tuple-element.169, f32[8,128]{1,0:T(8,128)S(1)} %get-tuple-element.168), kind=kOutput, calls=%fused_computation.85 | convolution fusion | flops 169475072 | bytes 4202496 | tf_op jit(solution)/shard_map/hqk,khv->qhv/dot_general | solution.py:49
  53.6 3.2 %multiply_convert_fusion.2 = bf16[8,128,640]{2,1,0:T(8,128)(2,1)} fusion(f32[8,128]{1,0:T(8,128)S(1)} %bitcast.110, bf16[768,8,256]{0,2,1:T(8,128)(2,1)} %copy-done.22, f32[8,128,640]{2,1,0:T(8,128)S(1)} %copy-done.35, f32[8,128]{1,0:T(8,128)S(1)} %get-tuple-element.168, bf16[512,8,128]{2,0,1:T(8,128)(2,1)} %copy-done.10), kind=kOutput, calls=%fused_computation.28 | convolution fusion | flops 171048960 | bytes 5513216 | tf_op jit(solution)/shard_map/qhv,khv->hqk/dot_general | solution.py:51
  57.6 2.1 %convolution_bitcast_fusion.1 = f32[640,8,192]{0,2,1:T(8,128)S(1)} fusion(bf16[128,8,192]{0,2,1:T(8,128)(2,1)} %get-tuple-element.146, bf16[8,128,640]{2,1,0:T(8,128)(2,1)} %multiply_convert_fusion.2), kind=kOutput, calls=%fused_computation.43 | convolution fusion | flops 251658240 | bytes 5636096 | tf_op jit(solution)/shard_map/hqk,qhd->khd/dot_general | solution.py:56
  59.7 1.9 %copy-done.2 = f32[640,8,192]{0,2,1:T(8,128)} copy-done((f32[640,8,192]{0,2,1:T(8,128)}, f32[640,8,192]{0,2,1:T(8,128)S(1)}, u32[]{:S(2)}) %copy-start.2) | copy-done | bytes 3932184
  62.7 2.2 %convolution_bitcast_fusion = f32[768,8,192]{0,2,1:T(8,128)S(1)} fusion(bf16[128,8,192]{0,2,1:T(8,128)(2,1)S(1)} %get-tuple-element.147, bf16[8,128,768]{2,1,0:T(8,128)(2,1)} %multiply_convert_fusion.1), kind=kOutput, calls=%fused_computation.34 | convolution fusion | flops 301989888 | bytes 6684672 | tf_op jit(solution)/shard_map/hqk,qhd->khd/dot_general | solution.py:56
  64.8 2.1 %copy-done.1 = f32[768,8,192]{0,2,1:T(8,128)} copy-done((f32[768,8,192]{0,2,1:T(8,128)}, f32[768,8,192]{0,2,1:T(8,128)S(1)}, u32[]{:S(2)}) %copy-start.1) | copy-done | bytes 4718616
  68.0 1.1 scatter-add.26
  69.1 2.0 %scatter-add.20 = f32[768,8,128]{0,2,1:T(8,128)S(1)} pad(f32[512,8,128]{0,2,1:T(8,128)} %slice.431, f32[]{:T(128)} %constant.271.clone.1), padding=0_256x0_0x0_0 | pad | bytes 5242884 | tf_op jit(solution)/shard_map/scatter-add | solution.py:122
  72.4 1.5 fusion.5
  76.7 1.2 fusion.8
  78.5 2.1 %fusion.6 = bf16[768,8,128]{0,2,1:T(8,128)(2,1)} fusion(f32[768,8,128]{0,2,1:T(8,128)S(1)} %fusion.8, bf16[512,8,128]{2,0,1:T(8,128)(2,1)S(1)} %copy-done.11, f32[8,128,768]{2,1,0:T(8,128)S(1)} %copy-done.33, f32[8,128]{1,0:T(8,128)S(1)} %copy-done.38), kind=kOutput, calls=%fused_computation.20 | convolution fusion | flops 204472320 | bytes 8130560 | tf_op jit(solution)/shard_map/hqk,qhv->khv/dot_general | solution.py:61
  80.6 1.0 add_dynamic-update-slice_fusion
  81.7 1.0 add.178
  83.5 2.2 %fusion.50 = f32[256,512]{1,0:T(8,128)S(1)} fusion(bf16[512,8,256]{2,1,0:T(8,128)(2,1)S(1)} %copy-done, bf16[768,8,128]{0,2,1:T(8,128)(2,1)} %fusion.5, bf16[768,8,128]{0,2,1:T(8,128)(2,1)} %fusion.6), kind=kOutput, calls=%fused_computation.80 | convolution fusion | flops 538968064 | bytes 5767168 | tf_op jit(solution)/shard_map/khd,lhd->kl/dot_general | solution.py:168
  87.3 1.4 collective-permute-start.1
  88.7 1.2 fusion.102
  89.9 1.3 fusion.42
  92.1 1.1 fusion.95
  93.2 13.2 %all_to_all.20 = f32[8,16,576]{2,1,0:T(8,128)} all-to-all(f32[8,16,576]{2,1,0:T(8,128)S(1)} %bitcast.103), channel_id=1, replica_groups=mesh['dp'=8,'hr'=8,'core'=2] {'hr'}, dimensions={0} | all-to-all | bytes 589824 | tf_op jit(solution)/shard_map/all_to_all | solution.py:177
  106.4 1.6 reduce_sum.119
  108.0 1.3 collective-permute-start.2
  109.3 1.8 %fusion.77 = bf16[8,32,576]{2,1,0:T(8,128)(2,1)} fusion(bf16[8,32,576]{2,1,0:T(8,128)(2,1)} %collective-permute-done, pred[]{:T(512)S(6)} %eq.2, bf16[8,2,32,576]{3,2,1,0:T(8,128)(2,1)S(1)} %pad_maximum_fusion.10), kind=kLoop, calls=%fused_computation.109 | loop fusion | flops 737280 | bytes 1179649 | tf_op jit(solution)/shard_map/convert_element_type | solution.py:165
  111.1 3.4 %all-to-all-start = ((bf16[8,32,576]{2,1,0:T(8,128)(2,1)}), bf16[8,32,576]{2,1,0:T(8,128)(2,1)S(1)}, u32[]{:S(2)}, u32[]{:S(2)}) async-start(bf16[8,32,576]{2,1,0:T(8,128)(2,1)} %fusion.77), calls=%async_computation | async-start | bytes 655360 | tf_op jit(solution)/shard_map/all_to_all | solution.py:166
  115.4 2.7 %collective-permute-start.3 = (f32[16,576]{1,0:T(8,128)S(1)}, f32[16,576]{1,0:T(8,128)S(1)}, u32[]{:S(2)}, u32[]{:S(2)}) collective-permute-start(f32[16,576]{1,0:T(8,128)S(1)} %add.184), channel_id=1, source_target_pairs={{0,32},{16,48},{32,0},{48,16},{64,96},{80,112},{96,64},{112,80},{1... | collective-permute-start | bytes 110600 | tf_op jit(solution)/shard_map/ppermute | solution.py:186
  118.1 3.6 %fusion.47 = f32[128,8,192]{0,2,1:T(8,128)} fusion(bf16[8,128,768]{2,1,0:T(8,128)(2,1)} %multiply_convert_fusion.1, bf16[768,8,64]{0,2,1:T(8,128)(2,1)S(1)} %broadcast_in_dim.42, bf16[768,8,128]{0,2,1:T(8,128)(2,1)} %copy-done.4), kind=kOutput, calls=%fused_computation.77 | convolution fusion | flops 306708480 | bytes 4718592 | tf_op jit(solution)/shard_map/hqk,khd->qhd/dot_general | solution.py:55
  121.7 3.4 %collective-permute-start.4 = (f32[16,576]{1,0:T(8,128)S(1)}, f32[16,576]{1,0:T(8,128)}, u32[]{:S(2)}, u32[]{:S(2)}) collective-permute-start(f32[16,576]{1,0:T(8,128)S(1)} %add.185), channel_id=1, source_target_pairs={{0,64},{16,80},{32,96},{48,112},{64,0},{80,16},{96,32},{112,48},{1... | collective-permute-start | bytes 110600 | tf_op jit(solution)/shard_map/ppermute | solution.py:186
  127.1 1.8 slice.587
  131.8 4.5 %all-to-all-start.3 = ((f32[8,16,576]{2,1,0:T(8,128)}), f32[8,16,576]{2,1,0:T(8,128)S(1)}, u32[]{:S(2)}, u32[]{:S(2)}) async-start(f32[8,16,576]{2,1,0:T(8,128)} %broadcast_in_dim.55), calls=%async_computation.3 | async-start | bytes 655360 | tf_op jit(solution)/shard_map/all_to_all | solution.py:189
  136.3 4.0 %fusion.20 = bf16[512,8,256]{2,0,1:T(8,128)(2,1)S(1)} fusion(bf16[768,8,128]{0,2,1:T(8,128)(2,1)} %fusion.6, bf16[768,8,128]{0,2,1:T(8,128)(2,1)} %fusion.5, bf16[768,576]{1,0:T(8,128)(2,1)} %maximum_maximum_fusion.1), kind=kOutput, calls=%fused_computation.47 | convolution fusion | flops 1617952768 | bytes 6029312 | tf_op jit(solution)/shard_map/kl,khd->lhd/dot_general | solution.py:137
  140.3 1.5 copy.112
  142.8 4.3 %all-to-all-start.1 = ((bf16[8,64,8,256]{3,1,2,0:T(8,128)(2,1)}), bf16[8,64,8,256]{3,1,2,0:T(8,128)(2,1)}, u32[]{:S(2)}, u32[]{:S(2)}) async-start(bf16[8,64,8,256]{3,1,2,0:T(8,128)(2,1)} %copy.112), calls=%async_computation.1 | async-start | bytes 4194304 | tf_op jit(solution)/shard_map/all_to_all | solution.py:147
  147.2 2.4 %convolution_bitcast_fusion.6 = f32[128,8,192]{0,2,1:T(8,128)S(1)} fusion(bf16[8,128,640]{2,1,0:T(8,128)(2,1)} %multiply_convert_fusion.2, bf16[768,8,128]{0,2,1:T(8,128)(2,1)} %copy-done.4, bf16[768,8,64]{0,2,1:T(8,128)(2,1)S(1)} %broadcast_in_dim.42), kind=kOutput, calls=%fused_computation.76 | convolution fusion | flops 255590400 | bytes 4456448 | tf_op jit(solution)/shard_map/hqk,khd->qhd/dot_general | solution.py:55
  151.2 1.6 copy.89
  152.8 1.6 copy.88
  154.4 2.8 %convolution_bitcast_fusion.4 = f32[256,8,192]{0,2,1:T(8,128)S(1)} fusion(bf16[8,256,512]{2,1,0:T(8,128)(2,1)} %copy-done.14, bf16[768,8,128]{0,2,1:T(8,128)(2,1)} %copy-done.4, bf16[768,8,64]{0,2,1:T(8,128)(2,1)S(1)} %broadcast_in_dim.42), kind=kOutput, calls=%fused_computation.63 | convolution fusion | flops 405798912 | bytes 6029312 | tf_op jit(solution)/shard_map/hqk,khd->qhd/dot_general | solution.py:55
  157.3 1.1 add_convert_fusion.2
  158.4 1.0 add_convert_fusion.3
  159.5 3.9 %collective-permute-start.5 = (f32[128,576]{1,0:T(8,128)S(1)}, f32[128,576]{1,0:T(8,128)S(1)}, u32[]{:S(2)}, u32[]{:S(2)}) collective-permute-start(f32[128,576]{1,0:T(8,128)S(1)} %bitcast.101), channel_id=1, source_target_pairs={{0,1},{1,0},{2,3},{3,2},{4,5},{5,4},{6,7},{7,6},{8,9},{9,8},{10,11... | collective-permute-start | bytes 884744 | tf_op jit(solution)/shard_map/ppermute | solution.py:66
  163.4 1.2 maximum_maximum_fusion
  165.4 1.0 copy.117
  166.4 9.4 %all-to-all-done.1 = bf16[8,64,8,256]{3,1,2,0:T(8,128)(2,1)} async-done(((bf16[8,64,8,256]{3,1,2,0:T(8,128)(2,1)}), bf16[8,64,8,256]{3,1,2,0:T(8,128)(2,1)}, u32[]{:S(2)}, u32[]{:S(2)}) %all-to-all-start.1) | async-done | bytes 2097184 | tf_op jit(solution)/shard_map/all_to_all | solution.py:147
  175.8 2.0 %convert_reduce_fusion = f32[64,8,256]{2,0,1:T(8,128)S(1)} fusion(bf16[8,64,8,256]{3,1,2,0:T(8,128)(2,1)} %all-to-all-done.1), kind=kLoop, calls=%fused_computation.3 | loop fusion | flops 1966080 | bytes 2621440 | tf_op jit(solution)/shard_map/reduce_sum | solution.py:150
  177.8 1.1 copy.116
  (146 shorter events, 30.1 us)
Async XLA Ops:
  0.6 22.8 %copy-start = (bf16[512,8,256]{2,1,0:T(8,128)(2,1)S(1)}, bf16[512,8,256]{2,1,0:T(8,128)(2,1)}, u32[]{:S(2)}) copy-start(bf16[512,8,256]{2,1,0:T(8,128)(2,1)} %param.34) | copy-start | bytes 6291460
  0.6 4.3 %slice-start.2 = ((bf16[512,576]{0,1:T(8,128)(2,1)}), bf16[512,64]{0,1:T(8,128)(2,1)S(1)}, s32[]{:S(2)}) async-start(bf16[512,576]{0,1:T(8,128)(2,1)} %param.32), calls=%async_computation.6 | async-start | bytes 131072 | tf_op jit(solution)/shard_map/slice | solution.py:82
  0.7 4.2 %copy-start.16 = (bf16[512,8,192]{0,2,1:T(8,128)(2,1)S(1)}, bf16[512,8,192]{0,2,1:T(8,128)(2,1)}, u32[]{:S(2)}) copy-start(bf16[512,8,192]{0,2,1:T(8,128)(2,1)} %param.31) | copy-start | bytes 4718596
  0.7 4.3 %copy-start.29 = (s32[1,512]{1,0:T(1,128)S(1)}, s32[1,512]{1,0:T(1,128)}, u32[]{:S(2)}) copy-start(s32[1,512]{1,0:T(1,128)} %param.37) | copy-start | bytes 6148
  9.0 5.1 %copy-start.7 = (bf16[512,512]{1,0:T(8,128)(2,1)S(1)}, bf16[512,512]{1,0:T(8,128)(2,1)}, u32[]{:S(2)}) copy-start(bf16[512,512]{1,0:T(8,128)(2,1)} %copy.133) | copy-start | bytes 1572868
  26.5 17.1 %copy-start.22 = (bf16[768,8,256]{0,2,1:T(8,128)(2,1)}, bf16[768,8,256]{0,2,1:T(8,128)(2,1)S(1)}, u32[]{:S(2)}) copy-start(bf16[768,8,256]{0,2,1:T(8,128)(2,1)S(1)} %convolution_convert_fusion) | copy-start | bytes 9437188
  26.5 2.0 %copy-start.19 = (bf16[512,8,128]{2,1,0:T(8,128)(2,1)S(1)}, bf16[512,8,128]{2,1,0:T(8,128)(2,1)}, u32[]{:S(2)}) copy-start(bf16[512,8,128]{2,1,0:T(8,128)(2,1)} %param.35) | copy-start | bytes 3145732
  26.6 3.7 %copy-start.6 = (bf16[512,8,192]{0,2,1:T(8,128)(2,1)S(1)}, bf16[512,8,192]{0,2,1:T(8,128)(2,1)}, u32[]{:S(2)}) copy-start(bf16[512,8,192]{0,2,1:T(8,128)(2,1)} %pad_maximum_fusion.7) | copy-start | bytes 4718596
  26.7 13.8 %copy-start.4 = (bf16[768,8,128]{0,2,1:T(8,128)(2,1)}, bf16[768,8,128]{0,2,1:T(8,128)(2,1)S(1)}, u32[]{:S(2)}) copy-start(bf16[768,8,128]{0,2,1:T(8,128)(2,1)S(1)} %slice.402) | copy-start | bytes 4718596
  28.7 14.9 %copy-start.10 = (bf16[512,8,128]{2,0,1:T(8,128)(2,1)}, bf16[512,8,128]{2,0,1:T(8,128)(2,1)S(1)}, u32[]{:S(2)}) copy-start(bf16[512,8,128]{2,0,1:T(8,128)(2,1)S(1)} %copy_select_fusion) | copy-start | bytes 3145732
  35.7 1.3 copy-start.14
  40.5 0.7 copy-start.31
  42.8 1.6 copy-start.32
  42.8 1.6 copy-start.37
  44.4 1.9 %copy-start.30 = (s32[128]{0:T(128)S(1)}, s32[128]{0:T(128)}, u32[]{:S(2)}) copy-start(s32[128]{0:T(128)} %iota_add_fusion.4) | copy-start | bytes 1540
  50.6 3.0 %copy-start.35 = (f32[8,128,640]{2,1,0:T(8,128)S(1)}, f32[8,128,640]{2,1,0:T(8,128)}, u32[]{:S(2)}) copy-start(f32[8,128,640]{2,1,0:T(8,128)} %get-tuple-element.169) | copy-start | bytes 7864324
  59.7 2.0 %copy-start.2 = (f32[640,8,192]{0,2,1:T(8,128)}, f32[640,8,192]{0,2,1:T(8,128)S(1)}, u32[]{:S(2)}) copy-start(f32[640,8,192]{0,2,1:T(8,128)S(1)} %convolution_bitcast_fusion.1) | copy-start | bytes 11796484
  64.8 2.1 %copy-start.1 = (f32[768,8,192]{0,2,1:T(8,128)}, f32[768,8,192]{0,2,1:T(8,128)S(1)}, u32[]{:S(2)}) copy-start(f32[768,8,192]{0,2,1:T(8,128)S(1)} %convolution_bitcast_fusion) | copy-start | bytes 14155780
  68.0 3.2 %copy-start.3 = (f32[640,8,192]{0,2,1:T(8,128)S(1)}, f32[640,8,192]{0,2,1:T(8,128)}, u32[]{:S(2)}) copy-start(f32[640,8,192]{0,2,1:T(8,128)} %copy-done.2) | copy-start | bytes 11796484
  69.1 3.2 %slice-start = ((s8[4718592]{0:T(1024)(128)(4,1)}), s8[4194304]{0:T(1024)(128)(4,1)S(1)}, s32[]{:S(2)}) async-start(s8[4718592]{0:T(1024)(128)(4,1)} %bitcast.98), calls=%async_computation.4 | async-start | bytes 8388608
  71.2 1.3 slice-start.1
  72.4 2.2 %copy-start.5 = (f32[512,8,128]{0,2,1:T(8,128)S(1)}, f32[512,8,128]{0,2,1:T(8,128)}, u32[]{:S(2)}) copy-start(f32[512,8,128]{0,2,1:T(8,128)} %convolution_bitcast_fusion.3) | copy-start | bytes 6291460
  74.6 1.2 copy-start.11
  74.6 2.1 %copy-start.36 = (f32[8,128,640]{2,1,0:T(8,128)S(1)}, f32[8,128,640]{2,1,0:T(8,128)}, u32[]{:S(2)}) copy-start(f32[8,128,640]{2,1,0:T(8,128)} %get-tuple-element.169) | copy-start | bytes 7864324
  76.7 1.9 %copy-start.33 = (f32[8,128,768]{2,1,0:T(8,128)S(1)}, f32[8,128,768]{2,1,0:T(8,128)}, u32[]{:S(2)}) copy-start(f32[8,128,768]{2,1,0:T(8,128)} %copy-done.32) | copy-start | bytes 9437188
  76.7 1.9 %copy-start.38 = (f32[8,128]{1,0:T(8,128)S(1)}, f32[8,128]{1,0:T(8,128)}, u32[]{:S(2)}) copy-start(f32[8,128]{1,0:T(8,128)} %copy-done.37) | copy-start | bytes 12292
  82.7 0.7 copy-start.8
  83.5 2.3 %copy-start.18 = (f32[256,64]{1,0:T(8,128)}, f32[256,64]{1,0:T(8,128)S(1)}, u32[]{:S(2)}) copy-start(f32[256,64]{1,0:T(8,128)S(1)} %slice.445) | copy-start | bytes 196612
  83.5 5.2 %copy-start.9 = (f32[768,64]{1,0:T(8,128)S(1)}, f32[768,64]{1,0:T(8,128)}, u32[]{:S(2)}) copy-start(f32[768,64]{1,0:T(8,128)} %copy-done.8) | copy-start | bytes 589828
  83.5 6.4 %copy-start.17 = (bf16[768,8,128]{0,2,1:T(8,128)(2,1)S(1)}, bf16[768,8,128]{0,2,1:T(8,128)(2,1)}, u32[]{:S(2)}) copy-start(bf16[768,8,128]{0,2,1:T(8,128)(2,1)} %fusion.5) | copy-start | bytes 4718596
  83.5 6.4 %copy-start.34 = (bf16[768,8,128]{0,2,1:T(8,128)(2,1)S(1)}, bf16[768,8,128]{0,2,1:T(8,128)(2,1)}, u32[]{:S(2)}) copy-start(bf16[768,8,128]{0,2,1:T(8,128)(2,1)} %fusion.6) | copy-start | bytes 4718596
  85.7 0.8 copy-start.15
  87.3 4.8 %collective-permute-start.1 = (f32[128,576]{1,0:T(8,128)}, f32[128,576]{1,0:T(8,128)}, u32[]{:S(2)}, u32[]{:S(2)}) collective-permute-start(f32[128,576]{1,0:T(8,128)} %fusion.93), channel_id=1, source_target_pairs={{0,1},{1,0},{2,3},{3,2},{4,5},{5,4},{6,7},{7,6},{8,9},{9,8},{10,11... | collective-permute-start | bytes 884744 | tf_op jit(solution)/shard_map/ppermute | solution.py:66
  92.1 17.2 %collective-permute-start = (bf16[8,32,576]{2,1,0:T(8,128)(2,1)}, bf16[8,32,576]{2,1,0:T(8,128)(2,1)}, u32[]{:S(2)}, u32[]{:S(2)}) collective-permute-start(bf16[8,32,576]{2,1,0:T(8,128)(2,1)} %fusion.92), channel_id=1, source_target_pairs={{0,1},{1,0},{2,3},{3,2},{4,5},{5,4},{6,7},{7,6},{8,9},{9,8},{10,11... | collective-permute-start | bytes 884744 | tf_op jit(solution)/shard_map/ppermute | solution.py:66
  108.0 6.6 %collective-permute-start.2 = (f32[16,576]{1,0:T(8,128)}, f32[16,576]{1,0:T(8,128)}, u32[]{:S(2)}, u32[]{:S(2)}) collective-permute-start(f32[16,576]{1,0:T(8,128)} %reduce_sum.119), channel_id=1, source_target_pairs={{0,16},{16,0},{32,48},{48,32},{64,80},{80,64},{96,112},{112,96},{1... | collective-permute-start | bytes 110600 | tf_op jit(solution)/shard_map/ppermute | solution.py:186
  111.1 20.0 %all-to-all-start = ((bf16[8,32,576]{2,1,0:T(8,128)(2,1)}), bf16[8,32,576]{2,1,0:T(8,128)(2,1)S(1)}, u32[]{:S(2)}, u32[]{:S(2)}) async-start(bf16[8,32,576]{2,1,0:T(8,128)(2,1)} %fusion.77), calls=%async_computation | async-start | bytes 655360 | tf_op jit(solution)/shard_map/all_to_all | solution.py:166
  115.4 9.7 %copy-start.12 = (f32[512,32]{1,0:T(8,128)S(1)}, f32[512,32]{1,0:T(8,128)}, u32[]{:S(2)}) copy-start(f32[512,32]{1,0:T(8,128)} %get-tuple-element.162) | copy-start | bytes 196612
  115.4 9.7 %copy-start.13 = (f32[512,32]{1,0:T(8,128)S(1)}, f32[512,32]{1,0:T(8,128)}, u32[]{:S(2)}) copy-start(f32[512,32]{1,0:T(8,128)} %get-tuple-element.163) | copy-start | bytes 196612
  115.4 6.3 %collective-permute-start.3 = (f32[16,576]{1,0:T(8,128)S(1)}, f32[16,576]{1,0:T(8,128)S(1)}, u32[]{:S(2)}, u32[]{:S(2)}) collective-permute-start(f32[16,576]{1,0:T(8,128)S(1)} %add.184), channel_id=1, source_target_pairs={{0,32},{16,48},{32,0},{48,16},{64,96},{80,112},{96,64},{112,80},{1... | collective-permute-start | bytes 110600 | tf_op jit(solution)/shard_map/ppermute | solution.py:186
  121.7 8.6 %collective-permute-start.4 = (f32[16,576]{1,0:T(8,128)S(1)}, f32[16,576]{1,0:T(8,128)}, u32[]{:S(2)}, u32[]{:S(2)}) collective-permute-start(f32[16,576]{1,0:T(8,128)S(1)} %add.185), channel_id=1, source_target_pairs={{0,64},{16,80},{32,96},{48,112},{64,0},{80,16},{96,32},{112,48},{1... | collective-permute-start | bytes 110600 | tf_op jit(solution)/shard_map/ppermute | solution.py:186
  131.8 11.0 %all-to-all-start.3 = ((f32[8,16,576]{2,1,0:T(8,128)}), f32[8,16,576]{2,1,0:T(8,128)S(1)}, u32[]{:S(2)}, u32[]{:S(2)}) async-start(f32[8,16,576]{2,1,0:T(8,128)} %broadcast_in_dim.55), calls=%async_computation.3 | async-start | bytes 655360 | tf_op jit(solution)/shard_map/all_to_all | solution.py:189
  142.8 33.0 %all-to-all-start.1 = ((bf16[8,64,8,256]{3,1,2,0:T(8,128)(2,1)}), bf16[8,64,8,256]{3,1,2,0:T(8,128)(2,1)}, u32[]{:S(2)}, u32[]{:S(2)}) async-start(bf16[8,64,8,256]{3,1,2,0:T(8,128)(2,1)} %copy.112), calls=%async_computation.1 | async-start | bytes 4194304 | tf_op jit(solution)/shard_map/all_to_all | solution.py:147
  149.6 0.9 copy-start.23
  154.4 2.9 %copy-start.27 = (f32[128,32]{0,1:T(8,128)S(1)}, f32[128,32]{0,1:T(8,128)}, u32[]{:S(2)}) copy-start(f32[128,32]{0,1:T(8,128)} %copy.96) | copy-start | bytes 49156
  154.4 4.0 %copy-start.26 = (f32[128,32]{0,1:T(8,128)S(1)}, f32[128,32]{0,1:T(8,128)}, u32[]{:S(2)}) copy-start(f32[128,32]{0,1:T(8,128)} %copy.93) | copy-start | bytes 49156
  154.4 4.0 %copy-start.28 = (f32[128,32]{0,1:T(8,128)S(1)}, f32[128,32]{0,1:T(8,128)}, u32[]{:S(2)}) copy-start(f32[128,32]{0,1:T(8,128)} %copy.92) | copy-start | bytes 49156
  154.4 5.0 %copy-start.24 = (f32[256,32]{0,1:T(8,128)S(1)}, f32[256,32]{0,1:T(8,128)}, u32[]{:S(2)}) copy-start(f32[256,32]{0,1:T(8,128)} %copy.89) | copy-start | bytes 98308
  154.4 5.0 %copy-start.25 = (f32[256,32]{0,1:T(8,128)S(1)}, f32[256,32]{0,1:T(8,128)}, u32[]{:S(2)}) copy-start(f32[256,32]{0,1:T(8,128)} %copy.88) | copy-start | bytes 98308
  157.2 6.2 %copy-start.20 = (bf16[128,8,128]{0,2,1:T(8,128)(2,1)S(1)}, bf16[128,8,128]{0,2,1:T(8,128)(2,1)}, u32[]{:S(2)}) copy-start(bf16[128,8,128]{0,2,1:T(8,128)(2,1)} %slice.587) | copy-start | bytes 786436
  157.3 6.2 %copy-start.21 = (bf16[128,8,128]{0,2,1:T(8,128)(2,1)S(1)}, bf16[128,8,128]{0,2,1:T(8,128)(2,1)}, u32[]{:S(2)}) copy-start(bf16[128,8,128]{0,2,1:T(8,128)(2,1)} %slice.588) | copy-start | bytes 786436
  159.5 5.8 %collective-permute-start.5 = (f32[128,576]{1,0:T(8,128)S(1)}, f32[128,576]{1,0:T(8,128)S(1)}, u32[]{:S(2)}, u32[]{:S(2)}) collective-permute-start(f32[128,576]{1,0:T(8,128)S(1)} %bitcast.101), channel_id=1, source_target_pairs={{0,1},{1,0},{2,3},{3,2},{4,5},{5,4},{6,7},{7,6},{8,9},{9,8},{10,11... | collective-permute-start | bytes 884744 | tf_op jit(solution)/shard_map/ppermute | solution.py:66

commit v13 on v8

--- a/solution.py
+++ b/solution.py
@@ -186,7 +186,8 @@
         partners = [(i, i ^ stride) for i in range(dp_size)]
         prefix_own = prefix_own + lax.ppermute(prefix_own, "dp", partners)
         stride *= 2
-    prefix_copies = jnp.broadcast_to(prefix_own[None], (row_size,) + prefix_own.shape)
+    prefix_sent = prefix_own.astype(jnp.bfloat16)
+    prefix_copies = jnp.broadcast_to(prefix_sent[None], (row_size,) + prefix_sent.shape)
     prefix_gathered = lax.all_to_all(prefix_copies, "hr", 0, 0, tiled=False).reshape(
         prefix_half.shape
     )
@@ -195,7 +196,7 @@
         core == 0,
         jnp.concatenate([prefix_gathered, prefix_partner], axis=0),
         jnp.concatenate([prefix_partner, prefix_gathered], axis=0),
-    )
+    ).astype(jnp.float32)
     return (query_grad, latent_grad, up_grad, prefix_grad)
 
 

time: 138 us -> 143 us (1.036)
  waiting for transfers between devices: 26.7 us -> 30.9 us
  starting transfers between devices: 35.8 us -> 31.6 us
  other arithmetic: 26.3 us -> 29.1 us
  matrix products: 30.9 us -> 32.4 us
    all_to_all x1, waiting for transfers between devices: 0.01 us -> 5.6 us  [on_device(): token_pieces = lax.all_to_all(token_pair, 'hr', 0, 0, tiled=False)]
    all_to_all x1, starting transfers between devices: 7.2 us -> 4.36 us  [on_device(): lax.all_to_all(up_part.astype(jnp.bfloat16).reshape((dp_size, -1) + up_pa...]
    dot_general x1, matrix products: 2.1 us -> 3.67 us  [on_device(): jnp.einsum('khd,lhd->kl', token_grad, kv_up, preferred_element_type=jnp.f...]
    ppermute x3, waiting for transfers between devices: 4.7 us -> 3.22 us  [on_device(): prefix_own = prefix_own + lax.ppermute(prefix_own, 'dp', partners)]
    unnamed x48 -> x44, local copies, waits for them, and re-layouts: 8.17 us -> 8.16 us
  transfers between devices with their start and end apart: 10 -> 10, of which waited for: 6 -> 5; matrix products, arithmetic and copies ran while one was open for 17% -> 19% of each run, Pallas kernels for 0% -> 0%
where the time goes in v13:
time: 143 us; the launch traced here: 142 us
  matrix products  32.4 us (23%)
  starting transfers between devices  31.6 us (22%)
  waiting for transfers between devices  30.9 us (22%)
  other arithmetic  29.1 us (20%)
  local copies, waits for them, and re-layouts  15.8 us (11%)
  between operations  1.89 us (1%)
    all_to_all x1, waiting for transfers between devices, on_device(): lax.all_to_all(up_part.astype(jnp.bfloat16).reshape((dp_size, -1) + up_pa...  14.9 us
    unnamed x44, local copies, waits for them, and re-layouts  8.16 us
    ppermute x3, starting transfers between devices, on_device(): prefix_own = prefix_own + lax.ppermute(prefix_own, 'dp', partners)  7.51 us
    ppermute x3, starting transfers between devices, swap_pair(): return lax.ppermute(values, 'core', [(0, 1), (1, 0)])  7.24 us
    all_to_all x1, waiting for transfers between devices, on_device(): lax.all_to_all(prefix_half.reshape((row_size, -1) + prefix_half.shape[1:]...  7.2 us
    all_to_all x1, waiting for transfers between devices, on_device(): token_pieces = lax.all_to_all(token_pair, 'hr', 0, 0, tiled=False)  5.6 us
    all_to_all x1, starting transfers between devices, on_device(): lax.all_to_all(prefix_half.reshape((row_size, -1) + prefix_half.shape[1:]...  5.48 us
    sub x2, other arithmetic, block_gradients(): exponent = jnp.exp(scores - highest)  4.93 us
  transfers between devices with their start and end apart: 10, of which 5 were waited for; matrix products, arithmetic and copies ran while one was open for 19% of the time, Pallas kernels for 0%

profile of v13, /device:TPU:1, one launch (start us, length us, event | category | flops | bytes accessed | tf_op | source)
XLA Modules:
  0.0 141.7 jit_solution(12081859787343039266)
XLA Ops:
  0.7 1.0 slice_convert_fusion.3
  1.7 1.1 slice.241
  2.7 1.2 copy.105
  3.9 0.7 convert_element_type.72
  4.6 1.0 multiply_cosine_fusion
  5.6 0.8 copy.104
  6.3 0.8 copy.103
  7.3 1.2 pad_maximum_fusion.14
  8.5 2.1 %maximum_maximum_fusion.1 = bf16[768,576]{1,0:T(8,128)(2,1)} fusion(bf16[512,32]{1,0:T(8,128)(2,1)} %copy.104, bf16[512,32]{1,0:T(8,128)(2,1)} %copy.103, bf16[512,512]{1,0:T(8,128)(2,1)S(1)} %copy.146, bf16[256,576]{1,0:T(8,128)(2,1)S(1)} %copy.105), kind=kLoop, calls=%fused_computation.69 | loop fusion | flops 3538944 | bytes 1769472 | tf_op jit(solution)/shard_map/concatenate | solution.py:85
  10.9 3.1 %convolution_convert_fusion = bf16[768,8,256]{0,2,1:T(8,128)(2,1)S(1)} fusion(bf16[512,8,256]{2,1,0:T(8,128)(2,1)S(1)} %copy-done, bf16[768,576]{1,0:T(8,128)(2,1)} %maximum_maximum_fusion.1), kind=kOutput, calls=%fused_computation.28 | convolution fusion | flops 1612185600 | bytes 6029312 | tf_op jit(solution)/shard_map/kl,lhd->khd/dot_general | solution.py:95
  14.1 0.7 copy-done.18
  14.9 0.7 slice-done.1
  15.9 1.0 fusion.17
  17.0 0.8 fusion.55
  18.8 2.1 %fusion.109 = (f32[8,256]{1,0:T(8,128)S(1)}, f32[8,256,512]{2,1,0:T(8,128)S(1)}) fusion(f32[8,256,512]{2,1,0:T(8,128)S(1)} %fusion.55, pred[256,512]{1,0:T(8,128)(4,1)S(1)} %fusion.64), kind=kOutput, calls=%fused_computation.154 | output fusion | flops 6291967 | bytes 8527872 | tf_op jit(solution)/shard_map/sub | solution.py:46
  21.3 0.8 fusion.46
  22.1 1.2 multiply_convert_fusion.1
  24.0 0.6 copy-done.7
  24.7 1.9 %convolution_bitcast_fusion.2 = f32[512,8,128]{0,2,1:T(8,128)} fusion(bf16[8,256,512]{2,1,0:T(8,128)(2,1)S(1)} %fusion.20, bf16[512,8,128]{2,0,1:T(8,128)(2,1)S(1)} %copy_select_fusion), kind=kOutput, calls=%fused_computation.40 | convolution fusion | flops 268435456 | bytes 4718592 | tf_op jit(solution)/shard_map/hqk,qhv->khv/dot_general | solution.py:61
  26.9 2.9 %fusion.108 = (f32[8,256]{1,0:T(8,128)S(1)}, f32[8,256,768]{2,1,0:T(8,128)S(1)}) fusion(f32[8,256,768]{2,1,0:T(8,128)S(1)} %fusion.17, pred[256,768]{1,0:T(8,128)(4,1)S(1)} %and_or_fusion), kind=kOutput, calls=%fused_computation.153 | output fusion | flops 9437951 | bytes 12787712 | tf_op jit(solution)/shard_map/sub | solution.py:46
  30.2 1.1 fusion.47
  31.9 2.6 %multiply_convert_fusion = bf16[8,256,768]{2,1,0:T(8,128)(2,1)} fusion(f32[8,256]{1,0:T(8,128)S(1)} %bitcast.87, f32[8,256,768]{2,1,0:T(8,128)S(1)} %get-tuple-element.131, f32[8,256]{1,0:T(8,128)S(1)} %get-tuple-element.130, bf16[768,8,256]{0,2,1:T(8,128)(2,1)S(1)} %convolution_convert_fusion, bf16[512,8,128]{2,0,1:T(8,128)(2,1)S(1)} %copy_select_fusion), kind=kOutput, calls=%fused_computation.2 | convolution fusion | flops 410517504 | bytes 11550720 | tf_op jit(solution)/shard_map/qhv,khv->hqk/dot_general | solution.py:51
  34.5 3.1 %convolution_bitcast_fusion = f32[768,8,192]{0,2,1:T(8,128)S(1)} fusion(bf16[8,256,768]{2,1,0:T(8,128)(2,1)} %multiply_convert_fusion, bf16[512,8,192]{0,2,1:T(8,128)(2,1)} %copy-done.3), kind=kOutput, calls=%fused_computation.27 | convolution fusion | flops 603979776 | bytes 8650752 | tf_op jit(solution)/shard_map/hqk,qhd->khd/dot_general | solution.py:56
  37.7 1.5 %fusion.5 = bf16[768,8,128]{0,2,1:T(8,128)(2,1)} fusion(f32[768,8,192]{0,2,1:T(8,128)S(1)} %convolution_bitcast_fusion, f32[512,8,128]{0,2,1:T(8,128)S(1)} %slice-done), kind=kLoop, calls=%fused_computation.18 | loop fusion | flops 1572864 | bytes 6815744 | tf_op jit(solution)/shard_map/convert.7
  39.2 1.0 copy-done.5
  40.2 0.7 copy-done.9
  41.1 1.8 %fusion.6 = bf16[768,8,128]{0,2,1:T(8,128)(2,1)} fusion(f32[512,8,128]{0,2,1:T(8,128)S(1)} %copy-done.9, bf16[8,256,768]{2,1,0:T(8,128)(2,1)S(1)} %copy-done.5, bf16[512,8,128]{2,0,1:T(8,128)(2,1)S(1)} %copy-done.11), kind=kOutput, calls=%fused_computation.20 | convolution fusion | flops 404226048 | bytes 7340032 | tf_op jit(solution)/shard_map/hqk,qhv->khv/dot_general | solution.py:61
  43.1 2.1 %fusion.50 = f32[256,512]{1,0:T(8,128)S(1)} fusion(bf16[512,8,256]{2,1,0:T(8,128)(2,1)S(1)} %copy-done, bf16[768,8,128]{0,2,1:T(8,128)(2,1)} %fusion.5, bf16[768,8,128]{0,2,1:T(8,128)(2,1)} %fusion.6), kind=kOutput, calls=%fused_computation.62 | convolution fusion | flops 538968064 | bytes 5767168 | tf_op jit(solution)/shard_map/khd,lhd->kl/dot_general | solution.py:169
  45.2 0.8 copy-done.13
  46.0 0.7 fusion.70
  46.7 1.4 collective-permute-start.1
  48.1 3.7 %fusion.41 = bf16[512,512]{1,0:T(8,128)(2,1)} fusion(bf16[512,8,256]{2,1,0:T(8,128)(2,1)S(1)} %copy-done, bf16[768,8,128]{0,2,1:T(8,128)(2,1)} %fusion.5, bf16[768,8,128]{0,2,1:T(8,128)(2,1)} %fusion.6), kind=kOutput, calls=%fused_computation.59 | convolution fusion | flops 1078198272 | bytes 5767168 | tf_op jit(solution)/shard_map/khd,lhd->kl/dot_general | solution.py:154
  52.1 0.8 copy.143
  52.9 0.7 copy.142
  53.6 1.3 pad_maximum_fusion.13
  54.9 1.8 %fusion.72 = f32[128,576]{1,0:T(8,128)} fusion(f32[128,576]{1,0:T(8,128)} %collective-permute-done.1, s32[]{:T(128)S(6)} %select_n.50, f32[256,512]{1,0:T(8,128)} %copy-done.13, f32[256,64]{1,0:T(8,128)} %copy-done.14), kind=kLoop, calls=%fused_computation.100 | loop fusion | flops 147456 | bytes 1179652 | tf_op jit(solution)/shard_map/add | solution.py:176
  56.7 5.5 %all-to-all-start.2 = ((f32[8,16,576]{2,1,0:T(8,128)}), f32[8,16,576]{2,1,0:T(8,128)}, u32[]{:S(2)}, u32[]{:S(2)}) async-start(f32[8,16,576]{2,1,0:T(8,128)} %bitcast.79), calls=%async_computation.2 | async-start | bytes 655360 | tf_op jit(solution)/shard_map/all_to_all | solution.py:178
  62.2 0.8 fusion.69
  63.3 7.2 %all-to-all-done.2 = f32[8,16,576]{2,1,0:T(8,128)} async-done(((f32[8,16,576]{2,1,0:T(8,128)}), f32[8,16,576]{2,1,0:T(8,128)}, u32[]{:S(2)}, u32[]{:S(2)}) %all-to-all-start.2) | async-done | bytes 294944 | tf_op jit(solution)/shard_map/all_to_all | solution.py:178
  70.5 1.6 %reduce_sum.89 = f32[16,576]{1,0:T(8,128)} reduce(f32[8,16,576]{2,1,0:T(8,128)} %all-to-all-done.2, f32[]{:T(128)} %constant.200.clone.1), dimensions={0}, to_apply=%region_10.11 | reduce | flops 64512 | bytes 331780 | tf_op jit(solution)/shard_map/reduce_sum | solution.py:177
  72.1 1.3 collective-permute-start.2
  73.4 1.8 %collective-permute-done.2 = f32[16,576]{1,0:T(8,128)S(1)} collective-permute-done((f32[16,576]{1,0:T(8,128)}, f32[16,576]{1,0:T(8,128)S(1)}, u32[]{:S(2)}, u32[]{:S(2)}) %collective-permute-start.2) | collective-permute-done | bytes 36896 | tf_op jit(solution)/shard_map/ppermute | solution.py:187
  75.1 0.8 add.133
  75.9 2.9 %collective-permute-start.3 = (f32[16,576]{1,0:T(8,128)S(1)}, f32[16,576]{1,0:T(8,128)S(1)}, u32[]{:S(2)}, u32[]{:S(2)}) collective-permute-start(f32[16,576]{1,0:T(8,128)S(1)} %add.133), channel_id=1, source_target_pairs={{0,32},{16,48},{32,0},{48,16},{64,96},{80,112},{96,64},{112,80},{1... | collective-permute-start | bytes 110600 | tf_op jit(solution)/shard_map/ppermute | solution.py:187
  78.8 1.4 %collective-permute-done.3 = f32[16,576]{1,0:T(8,128)S(1)} collective-permute-done((f32[16,576]{1,0:T(8,128)S(1)}, f32[16,576]{1,0:T(8,128)S(1)}, u32[]{:S(2)}, u32[]{:S(2)}) %collective-permute-start.3) | collective-permute-done | bytes 36896 | tf_op jit(solution)/shard_map/ppermute | solution.py:187
  80.9 3.3 %collective-permute-start.4 = (f32[16,576]{1,0:T(8,128)}, f32[16,576]{1,0:T(8,128)}, u32[]{:S(2)}, u32[]{:S(2)}) collective-permute-start(f32[16,576]{1,0:T(8,128)} %add.134), channel_id=1, source_target_pairs={{0,64},{16,80},{32,96},{48,112},{64,0},{80,16},{96,32},{112,48},{1... | collective-permute-start | bytes 110600 | tf_op jit(solution)/shard_map/ppermute | solution.py:187
  84.2 1.8 %fusion.62 = bf16[8,32,576]{2,1,0:T(8,128)(2,1)} fusion(bf16[8,32,576]{2,1,0:T(8,128)(2,1)} %collective-permute-done, pred[]{:T(512)S(6)} %eq.2, bf16[8,2,32,576]{3,2,1,0:T(8,128)(2,1)S(1)} %pad_maximum_fusion.13), kind=kLoop, calls=%fused_computation.84 | loop fusion | flops 737280 | bytes 1179649 | tf_op jit(solution)/shard_map/convert_element_type | solution.py:166
  86.0 3.4 %all-to-all-start = ((bf16[8,32,576]{2,1,0:T(8,128)(2,1)}), bf16[8,32,576]{2,1,0:T(8,128)(2,1)S(1)}, u32[]{:S(2)}, u32[]{:S(2)}) async-start(bf16[8,32,576]{2,1,0:T(8,128)(2,1)} %fusion.62), calls=%async_computation | async-start | bytes 655360 | tf_op jit(solution)/shard_map/all_to_all | solution.py:167
  89.5 0.8 add_convert_fusion.3
  90.3 5.6 %all-to-all-done = bf16[8,32,576]{2,1,0:T(8,128)(2,1)S(1)} async-done(((bf16[8,32,576]{2,1,0:T(8,128)(2,1)}), bf16[8,32,576]{2,1,0:T(8,128)(2,1)S(1)}, u32[]{:S(2)}, u32[]{:S(2)}) %all-to-all-start) | async-done | bytes 294944 | tf_op jit(solution)/shard_map/all_to_all | solution.py:167
  95.9 0.7 broadcast_in_dim.41
  96.6 3.6 %all-to-all-start.3 = ((bf16[8,16,576]{2,1,0:T(8,128)(2,1)}), bf16[8,16,576]{2,1,0:T(8,128)(2,1)S(1)}, u32[]{:S(2)}, u32[]{:S(2)}) async-start(bf16[8,16,576]{2,1,0:T(8,128)(2,1)} %broadcast_in_dim.41), calls=%async_computation.3 | async-start | bytes 327680 | tf_op jit(solution)/shard_map/all_to_all | solution.py:191
  100.2 4.0 %fusion.19 = bf16[512,8,256]{2,0,1:T(8,128)(2,1)S(1)} fusion(bf16[768,8,128]{0,2,1:T(8,128)(2,1)} %fusion.6, bf16[768,8,128]{0,2,1:T(8,128)(2,1)} %fusion.5, bf16[768,576]{1,0:T(8,128)(2,1)} %maximum_maximum_fusion.1), kind=kOutput, calls=%fused_computation.37 | convolution fusion | flops 1617952768 | bytes 6029312 | tf_op jit(solution)/shard_map/kl,khd->lhd/dot_general | solution.py:138
  104.2 1.6 %copy.125 = bf16[8,64,8,256]{3,1,2,0:T(8,128)(2,1)} copy(bf16[8,64,8,256]{3,1,0,2:T(8,128)(2,1)S(1)} %bitcast.78) | data formatting | bytes 4194304 | tf_op jit(solution)/shard_map/reshape | solution.py:149
  105.8 4.4 %all-to-all-start.1 = ((bf16[8,64,8,256]{3,1,2,0:T(8,128)(2,1)}), bf16[8,64,8,256]{3,1,2,0:T(8,128)(2,1)}, u32[]{:S(2)}, u32[]{:S(2)}) async-start(bf16[8,64,8,256]{3,1,2,0:T(8,128)(2,1)} %copy.125), calls=%async_computation.1 | async-start | bytes 4194304 | tf_op jit(solution)/shard_map/all_to_all | solution.py:148
  110.2 3.7 %fusion.25 = f32[256,8,192]{0,2,1:T(8,128)S(1)} fusion(bf16[8,256,768]{2,1,0:T(8,128)(2,1)} %multiply_convert_fusion, bf16[768,8,64]{0,2,1:T(8,128)(2,1)S(1)} %broadcast_in_dim.34, bf16[768,8,128]{0,2,1:T(8,128)(2,1)} %copy-done.1), kind=kOutput, calls=%fused_computation.49 | convolution fusion | flops 608698368 | bytes 7077888 | tf_op jit(solution)/shard_map/hqk,khd->qhd/dot_general | solution.py:55
  114.0 0.8 convolution_bitcast_fusion.3
  115.1 5.6 %collective-permute-start.5 = (bf16[128,576]{1,0:T(8,128)(2,1)S(1)}, bf16[128,576]{1,0:T(8,128)(2,1)S(1)}, u32[]{:S(2)}, u32[]{:S(2)}) collective-permute-start(bf16[128,576]{1,0:T(8,128)(2,1)S(1)} %bitcast.80), channel_id=1, source_target_pairs={{0,1},{1,0},{2,3},{3,2},{4,5},{5,4},{6,7},{7,6},{8,9},{9,8},{10,11... | collective-permute-start | bytes 442376 | tf_op jit(solution)/shard_map/ppermute | solution.py:66
  120.6 1.3 maximum_maximum_fusion
  121.9 0.7 convert_reduce_fusion.1
  122.7 1.0 copy.131
  123.7 14.9 %all-to-all-done.1 = bf16[8,64,8,256]{3,1,2,0:T(8,128)(2,1)} async-done(((bf16[8,64,8,256]{3,1,2,0:T(8,128)(2,1)}), bf16[8,64,8,256]{3,1,2,0:T(8,128)(2,1)}, u32[]{:S(2)}, u32[]{:S(2)}) %all-to-all-start.1) | async-done | bytes 2097184 | tf_op jit(solution)/shard_map/all_to_all | solution.py:148
  138.6 2.0 %convert_reduce_fusion = f32[64,8,256]{2,0,1:T(8,128)S(1)} fusion(bf16[8,64,8,256]{3,1,2,0:T(8,128)(2,1)} %all-to-all-done.1), kind=kLoop, calls=%fused_computation.6 | loop fusion | flops 1966080 | bytes 2621440 | tf_op jit(solution)/shard_map/reduce_sum | solution.py:151
  140.6 1.1 copy.130
  (77 shorter events, 5.7 us)
Async XLA Ops:
  0.6 10.2 %copy-start = (bf16[512,8,256]{2,1,0:T(8,128)(2,1)S(1)}, bf16[512,8,256]{2,1,0:T(8,128)(2,1)}, u32[]{:S(2)}) copy-start(bf16[512,8,256]{2,1,0:T(8,128)(2,1)} %param.28) | copy-start | bytes 6291460
  5.6 8.5 %copy-start.16 = (f32[512,32]{0,1:T(8,128)}, f32[512,32]{0,1:T(8,128)S(1)}, u32[]{:S(2)}) copy-start(f32[512,32]{0,1:T(8,128)S(1)} %get-tuple-element.126) | copy-start | bytes 196612
  7.3 3.3 %copy-start.12 = (bf16[512,8,192]{0,2,1:T(8,128)(2,1)S(1)}, bf16[512,8,192]{0,2,1:T(8,128)(2,1)}, u32[]{:S(2)}) copy-start(bf16[512,8,192]{0,2,1:T(8,128)(2,1)} %param.25) | copy-start | bytes 4718596
  13.9 0.8 copy-start.18
  13.9 1.7 %slice-start.1 = ((bf16[512,8,192]{0,2,1:T(8,128)(2,1)}), bf16[512,8,128]{0,2,1:T(8,128)(2,1)S(1)}, s32[]{:S(2)}) async-start(bf16[512,8,192]{0,2,1:T(8,128)(2,1)} %param.25), calls=%async_computation.5 | async-start | bytes 2097152 | tf_op jit(solution)/shard_map/slice | solution.py:78
  14.1 2.9 %copy-start.1 = (bf16[768,8,128]{0,2,1:T(8,128)(2,1)}, bf16[768,8,128]{0,2,1:T(8,128)(2,1)S(1)}, u32[]{:S(2)}) copy-start(bf16[768,8,128]{0,2,1:T(8,128)(2,1)S(1)} %slice.283) | copy-start | bytes 4718596
  15.8 7.5 %copy-start.3 = (bf16[512,8,192]{0,2,1:T(8,128)(2,1)}, bf16[512,8,192]{0,2,1:T(8,128)(2,1)S(1)}, u32[]{:S(2)}) copy-start(bf16[512,8,192]{0,2,1:T(8,128)(2,1)S(1)} %pad_maximum_fusion.8) | copy-start | bytes 4718596
  17.0 1.5 %copy-start.15 = (bf16[512,8,128]{2,1,0:T(8,128)(2,1)S(1)}, bf16[512,8,128]{2,1,0:T(8,128)(2,1)}, u32[]{:S(2)}) copy-start(bf16[512,8,128]{2,1,0:T(8,128)(2,1)} %param.29) | copy-start | bytes 3145732
  18.7 13.2 %copy-start.10 = (bf16[512,8,128]{2,0,1:T(8,128)(2,1)}, bf16[512,8,128]{2,0,1:T(8,128)(2,1)S(1)}, u32[]{:S(2)}) copy-start(bf16[512,8,128]{2,0,1:T(8,128)(2,1)S(1)} %copy_select_fusion) | copy-start | bytes 3145732
  23.4 1.3 copy-start.7
  24.0 2.7 %copy-start.6 = (f32[512,8,192]{0,2,1:T(8,128)}, f32[512,8,192]{0,2,1:T(8,128)S(1)}, u32[]{:S(2)}) copy-start(f32[512,8,192]{0,2,1:T(8,128)S(1)} %convolution_bitcast_fusion.1) | copy-start | bytes 9437188
  30.2 1.7 %copy-start.4 = (bf16[8,256,768]{2,1,0:T(8,128)(2,1)}, bf16[8,256,768]{2,1,0:T(8,128)(2,1)S(1)}, u32[]{:S(2)}) copy-start(bf16[8,256,768]{2,1,0:T(8,128)(2,1)S(1)} %fusion.10) | copy-start | bytes 9437188
  34.5 3.2 %slice-start = ((f32[512,8,192]{0,2,1:T(8,128)}), f32[512,8,128]{0,2,1:T(8,128)S(1)}, s32[]{:S(2)}) async-start(f32[512,8,192]{0,2,1:T(8,128)} %copy-done.6), calls=%async_computation.4 | async-start | bytes 4194304 | tf_op jit(solution)/shard_map/slice | solution.py:59
  37.7 2.5 %copy-start.5 = (bf16[8,256,768]{2,1,0:T(8,128)(2,1)S(1)}, bf16[8,256,768]{2,1,0:T(8,128)(2,1)}, u32[]{:S(2)}) copy-start(bf16[8,256,768]{2,1,0:T(8,128)(2,1)} %copy-done.4) | copy-start | bytes 9437188
  37.7 3.1 %copy-start.9 = (f32[512,8,128]{0,2,1:T(8,128)S(1)}, f32[512,8,128]{0,2,1:T(8,128)}, u32[]{:S(2)}) copy-start(f32[512,8,128]{0,2,1:T(8,128)} %convolution_bitcast_fusion.2) | copy-start | bytes 6291460
  37.7 3.3 %copy-start.11 = (bf16[512,8,128]{2,0,1:T(8,128)(2,1)S(1)}, bf16[512,8,128]{2,0,1:T(8,128)(2,1)}, u32[]{:S(2)}) copy-start(bf16[512,8,128]{2,0,1:T(8,128)(2,1)} %copy-done.10) | copy-start | bytes 3145732
  43.0 2.1 %copy-start.14 = (f32[256,64]{1,0:T(8,128)}, f32[256,64]{1,0:T(8,128)S(1)}, u32[]{:S(2)}) copy-start(f32[256,64]{1,0:T(8,128)S(1)} %copy.129) | copy-start | bytes 196612
  45.2 0.8 copy-start.13
  46.7 8.2 %collective-permute-start.1 = (f32[128,576]{1,0:T(8,128)}, f32[128,576]{1,0:T(8,128)}, u32[]{:S(2)}, u32[]{:S(2)}) collective-permute-start(f32[128,576]{1,0:T(8,128)} %fusion.70), channel_id=1, source_target_pairs={{0,1},{1,0},{2,3},{3,2},{4,5},{5,4},{6,7},{7,6},{8,9},{9,8},{10,11... | collective-permute-start | bytes 884744 | tf_op jit(solution)/shard_map/ppermute | solution.py:66
  56.7 13.7 %all-to-all-start.2 = ((f32[8,16,576]{2,1,0:T(8,128)}), f32[8,16,576]{2,1,0:T(8,128)}, u32[]{:S(2)}, u32[]{:S(2)}) async-start(f32[8,16,576]{2,1,0:T(8,128)} %bitcast.79), calls=%async_computation.2 | async-start | bytes 655360 | tf_op jit(solution)/shard_map/all_to_all | solution.py:178
  63.0 21.2 %collective-permute-start = (bf16[8,32,576]{2,1,0:T(8,128)(2,1)}, bf16[8,32,576]{2,1,0:T(8,128)(2,1)}, u32[]{:S(2)}, u32[]{:S(2)}) collective-permute-start(bf16[8,32,576]{2,1,0:T(8,128)(2,1)} %fusion.69), channel_id=1, source_target_pairs={{0,1},{1,0},{2,3},{3,2},{4,5},{5,4},{6,7},{7,6},{8,9},{9,8},{10,11... | collective-permute-start | bytes 884744 | tf_op jit(solution)/shard_map/ppermute | solution.py:66
  72.1 3.1 %collective-permute-start.2 = (f32[16,576]{1,0:T(8,128)}, f32[16,576]{1,0:T(8,128)S(1)}, u32[]{:S(2)}, u32[]{:S(2)}) collective-permute-start(f32[16,576]{1,0:T(8,128)} %reduce_sum.89), channel_id=1, source_target_pairs={{0,16},{16,0},{32,48},{48,32},{64,80},{80,64},{96,112},{112,96},{1... | collective-permute-start | bytes 110600 | tf_op jit(solution)/shard_map/ppermute | solution.py:187
  75.9 4.4 %collective-permute-start.3 = (f32[16,576]{1,0:T(8,128)S(1)}, f32[16,576]{1,0:T(8,128)S(1)}, u32[]{:S(2)}, u32[]{:S(2)}) collective-permute-start(f32[16,576]{1,0:T(8,128)S(1)} %add.133), channel_id=1, source_target_pairs={{0,32},{16,48},{32,0},{48,16},{64,96},{80,112},{96,64},{112,80},{1... | collective-permute-start | bytes 110600 | tf_op jit(solution)/shard_map/ppermute | solution.py:187
  80.9 8.6 %collective-permute-start.4 = (f32[16,576]{1,0:T(8,128)}, f32[16,576]{1,0:T(8,128)}, u32[]{:S(2)}, u32[]{:S(2)}) collective-permute-start(f32[16,576]{1,0:T(8,128)} %add.134), channel_id=1, source_target_pairs={{0,64},{16,80},{32,96},{48,112},{64,0},{80,16},{96,32},{112,48},{1... | collective-permute-start | bytes 110600 | tf_op jit(solution)/shard_map/ppermute | solution.py:187
  86.0 9.9 %all-to-all-start = ((bf16[8,32,576]{2,1,0:T(8,128)(2,1)}), bf16[8,32,576]{2,1,0:T(8,128)(2,1)S(1)}, u32[]{:S(2)}, u32[]{:S(2)}) async-start(bf16[8,32,576]{2,1,0:T(8,128)(2,1)} %fusion.62), calls=%async_computation | async-start | bytes 655360 | tf_op jit(solution)/shard_map/all_to_all | solution.py:167
  96.6 9.2 %all-to-all-start.3 = ((bf16[8,16,576]{2,1,0:T(8,128)(2,1)}), bf16[8,16,576]{2,1,0:T(8,128)(2,1)S(1)}, u32[]{:S(2)}, u32[]{:S(2)}) async-start(bf16[8,16,576]{2,1,0:T(8,128)(2,1)} %broadcast_in_dim.41), calls=%async_computation.3 | async-start | bytes 327680 | tf_op jit(solution)/shard_map/all_to_all | solution.py:191
  105.8 32.8 %all-to-all-start.1 = ((bf16[8,64,8,256]{3,1,2,0:T(8,128)(2,1)}), bf16[8,64,8,256]{3,1,2,0:T(8,128)(2,1)}, u32[]{:S(2)}, u32[]{:S(2)}) async-start(bf16[8,64,8,256]{3,1,2,0:T(8,128)(2,1)} %copy.125), calls=%async_computation.1 | async-start | bytes 4194304 | tf_op jit(solution)/shard_map/all_to_all | solution.py:148
  110.2 3.8 %copy-start.2 = (bf16[768,8,128]{0,2,1:T(8,128)(2,1)S(1)}, bf16[768,8,128]{0,2,1:T(8,128)(2,1)}, u32[]{:S(2)}) copy-start(bf16[768,8,128]{0,2,1:T(8,128)(2,1)} %copy-done.1) | copy-start | bytes 4718596
  110.2 3.8 %copy-start.8 = (bf16[8,256,512]{2,1,0:T(8,128)(2,1)S(1)}, bf16[8,256,512]{2,1,0:T(8,128)(2,1)}, u32[]{:S(2)}) copy-start(bf16[8,256,512]{2,1,0:T(8,128)(2,1)} %copy-done.7) | copy-start | bytes 6291460
  113.9 0.9 copy-start.17
  114.0 0.9 copy-start.19
  115.1 7.5 %collective-permute-start.5 = (bf16[128,576]{1,0:T(8,128)(2,1)S(1)}, bf16[128,576]{1,0:T(8,128)(2,1)S(1)}, u32[]{:S(2)}, u32[]{:S(2)}) collective-permute-start(bf16[128,576]{1,0:T(8,128)(2,1)S(1)} %bitcast.80), channel_id=1, source_target_pairs={{0,1},{1,0},{2,3},{3,2},{4,5},{5,4},{6,7},{7,6},{8,9},{9,8},{10,11... | collective-permute-start | bytes 442376 | tf_op jit(solution)/shard_map/ppermute | solution.py:66
